TPU v7x, 32 devices: a whole 2x2x4 slice. The times are simulated.
32 devices in a mesh: groups: 2 (over x), ctx: 8 (over z, y), heads: 2 (over core).
Axes of the slice: x: 2, y: 2, z: 4, core: 2. Of those that a mesh axis runs over, the one named last changes fastest.
Arguments:
- ssm_input: bfloat16 [4, 2048, 8192], P('groups', 'ctx', 'heads'), parts along dimension 0, may hold values from -6 to 6
- b_proj: bfloat16 [4, 2048, 512], P('groups', 'ctx', 'heads'), parts along dimension 0, may hold values from -600 to 600
- c_proj: bfloat16 [4, 2048, 512], P('groups', 'ctx', 'heads'), parts along dimension 0, may hold values from -6 to 6
- step_size: float32 [4, 128, 2048], P('groups', 'heads', 'ctx'), parts along dimension 0, may hold values from 0.01 to 0.04
- log_decay: float32 [4, 128, 2048], P('groups', 'heads', 'ctx'), parts along dimension 0, may hold values from -1 to 0
- skip_gain: float32 [128], P('heads'), may hold values from 0.5 to 1.5
- request_of_slot: int32 [16], P(('groups', 'ctx')), parts along dimension 0, may hold values from 0 to 1, as said below
- new_input: bfloat16 [16, 4, 8192], P(('groups', 'ctx'), None, 'heads'), parts along dimension 0, may hold values from -6 to 6
- new_b: bfloat16 [16, 4, 512], P(('groups', 'ctx'), None, 'heads'), parts along dimension 0, may hold values from -0.5 to 0.5
- new_c: bfloat16 [16, 4, 512], P(('groups', 'ctx'), None, 'heads'), parts along dimension 0, may hold values from -6 to 6
- new_step: float32 [16, 4, 128], P(('groups', 'ctx'), None, 'heads'), parts along dimension 0, may hold values from 0.2 to 1
- new_log_decay: float32 [16, 4, 128], P(('groups', 'ctx'), None, 'heads'), parts along dimension 0, may hold values from -0.3 to -0.02
- out_weight: bfloat16 [8192, 8192], P('heads', 'ctx'), may hold values from -0.0625 to 0.0625
Outputs:
- prefill_out: bfloat16 [4, 2048, 8192], P('groups', 'ctx', 'heads'), parts along dimension 0
- decoded: bfloat16 [16, 4, 8192], P('groups', None, 'ctx'), parts along dimension 0
There are 2 independent parts, one for each index of `groups`. A program takes and returns all parts, laid end to end along the dimension named above; an argument that names none is the same for every part. Nothing has to cross between parts.
Inputs may be any that keep to these rules, and one draw needn't show every extreme that they name: `request_of_slot`: every prompt is named by at least one slot.
All inputs are finite; a program needn't handle non-finite values.
Results may differ from a plain program's by a relative error of at most 0.008.
Values may be sent and summed in bfloat16 or wider, within the bound.
No kernel may reach another device: no remote copies, remote signals or barrier semaphores. Data moves between devices by JAX's collectives and lax.ppermute only.
A program may use at most 320 MiB of HBM per device.

v0:
```python
import jax
import jax.numpy as jnp
from jax import lax
from jax.sharding import PartitionSpec as P

HEADS = 128
HEAD_DIM = 64
STATE = 128
GROUPS = 4


def entering_2(value, axis, join, neutral):
    place = lax.axis_index(axis)
    gathered = jax.tree.map(
        lambda a, kind: lax.all_gather(a.astype(kind), axis), value, (jnp.bfloat16, jnp.bfloat16)
    )
    state = jax.tree.map(lambda a, e: jnp.zeros_like(a) + jnp.asarray(e, a.dtype), value, neutral)

    def one(step, state):
        return join(
            state,
            jax.tree.map(
                lambda a, own: lax.dynamic_index_in_dim(a, step, 0, False).astype(own.dtype),
                gathered,
                value,
            ),
        )

    return lax.fori_loop(0, place, one, state)


def as_sent(value):

    def short(part):
        return part.astype(jnp.bfloat16) if part.dtype == jnp.float32 else part

    return jax.tree.map(short, value)


def spread(block, axis, source):
    block = jnp.where(lax.axis_index(axis) == source, block, jnp.zeros_like(block))
    return lax.psum(block, axis)


def block_terms(block_input, block_b, block_c, block_step, block_logd):
    block_size = block_input.shape[0]
    head_count = block_step.shape[0]
    per_group = HEADS // GROUPS
    group_count = head_count // per_group
    cumulative = jnp.cumsum(block_logd, axis=1)
    block_total = cumulative[:, -1]
    inputs_head = block_input.reshape(block_size, group_count, per_group, HEAD_DIM)
    b_groups = block_b.reshape(block_size, group_count, STATE)
    c_groups = block_c.reshape(block_size, group_count, STATE)
    scores = jnp.einsum("tgn,sgn->gts", c_groups, b_groups, preferred_element_type=jnp.float32)
    row_index = lax.broadcasted_iota(jnp.int32, (block_size, block_size), 0)
    col_index = lax.broadcasted_iota(jnp.int32, (block_size, block_size), 1)
    causal = row_index >= col_index
    log_gap = cumulative[:, :, None] - cumulative[:, None, :]
    decay_rate = (
        jnp.where(causal, jnp.exp(jnp.where(causal, log_gap, 0.0)), 0.0) * block_step[:, None, :]
    )
    mixing = (
        scores[:, None, :, :] * decay_rate.reshape(group_count, per_group, block_size, block_size)
    ).astype(jnp.bfloat16)
    local_out = jnp.einsum(
        "gkts,sgkp->tgkp", mixing, inputs_head, preferred_element_type=jnp.float32
    )
    weighting = jnp.exp(block_total[:, None] - cumulative) * block_step
    weighted = (weighting.T.reshape(block_size, group_count, per_group, 1) * inputs_head).astype(
        jnp.bfloat16
    )
    block_state = jnp.einsum(
        "sgkp,sgn->gkpn", weighted, b_groups, preferred_element_type=jnp.float32
    )
    return (cumulative, block_total.reshape(group_count, per_group), local_out, block_state)


def finish(local_out, cumulative, block_c, entering, block_input, skip_gain):
    block_size = block_input.shape[0]
    group_count, per_group = (entering.shape[0], entering.shape[1])
    c_groups = block_c.reshape(block_size, group_count, STATE).astype(jnp.float32)
    carried = jnp.einsum("tgn,gkpn->tgkp", c_groups, entering, precision=lax.Precision.HIGHEST)
    carried = carried * jnp.exp(cumulative).T.reshape(block_size, group_count, per_group, 1)
    inputs_head = block_input.reshape(block_size, group_count, per_group, HEAD_DIM)
    skipped = skip_gain.reshape(group_count, per_group, 1) * inputs_head
    return (
        (local_out + carried + skipped)
        .reshape(block_size, group_count * per_group * HEAD_DIM)
        .astype(jnp.bfloat16)
    )


def decode_step(carry_state, row_input, row_b, row_c, row_step, row_logd, skip_gain):
    group_count, per_group = (carry_state.shape[0], carry_state.shape[1])
    inputs_head = row_input.reshape(group_count, per_group, HEAD_DIM).astype(jnp.float32)
    b_groups = row_b.reshape(group_count, STATE).astype(jnp.float32)
    c_groups = row_c.reshape(group_count, STATE).astype(jnp.float32)
    scaled = row_step.reshape(group_count, per_group, 1) * inputs_head
    carry_state = (
        jnp.exp(row_logd).reshape(group_count, per_group, 1, 1) * carry_state
        + scaled[:, :, :, None] * b_groups[:, None, None, :]
    )
    output = jnp.einsum("gkpn,gn->gkp", carry_state, c_groups, precision=lax.Precision.HIGHEST)
    output = output + skip_gain.reshape(group_count, per_group, 1) * inputs_head
    return (carry_state, output.reshape(group_count * per_group * HEAD_DIM).astype(jnp.bfloat16))


def shards(
    ssm_input,
    b_proj,
    c_proj,
    step_size,
    log_decay,
    skip_gain,
    request_of_slot,
    new_input,
    new_b,
    new_c,
    new_step,
    new_log_decay,
    out_weight,
):
    request_count = ssm_input.shape[0]
    terms = []
    for request in range(request_count):
        terms.append(
            block_terms(
                ssm_input[request],
                b_proj[request],
                c_proj[request],
                step_size[request],
                log_decay[request],
            )
        )
    totals = jnp.stack([term[1] for term in terms])
    states = jnp.stack([term[3] for term in terms])

    def combine(earlier, later):
        return (
            earlier[0] + later[0],
            jnp.exp(later[0])[:, :, :, None, None] * earlier[1] + later[1],
        )

    identity = (jnp.zeros_like(totals), jnp.zeros_like(states))
    before_totals, entering = entering_2((totals, states), "ctx", combine, identity)
    prefill_rows = []
    for request in range(request_count):
        prefill_rows.append(
            finish(
                terms[request][2],
                terms[request][0],
                c_proj[request],
                entering[request],
                ssm_input[request],
                skip_gain,
            )
        )
    prefill_out = jnp.stack(prefill_rows)
    request_numbers = lax.broadcasted_iota(jnp.int32, (request_count,), 0)
    leaving = jnp.exp(totals)[:, :, :, None, None] * entering + states
    finals = spread(as_sent(leaving), "ctx", lax.axis_size("ctx") - 1).astype(leaving.dtype)
    chosen = (request_numbers == request_of_slot[0]).astype(jnp.float32)
    carry_state = jnp.einsum("r,rgkpn->gkpn", chosen, finals, precision=lax.Precision.HIGHEST)
    results = []
    for position in range(new_input.shape[1]):
        carry_state, output = decode_step(
            carry_state,
            new_input[0, position],
            new_b[0, position],
            new_c[0, position],
            new_step[0, position],
            new_log_decay[0, position],
            skip_gain,
        )
        results.append(output)
    new_output = jnp.stack(results)[None]
    partial_value = jnp.einsum(
        "jup,pd->jud",
        lax.all_gather(new_output, "ctx", axis=0, tiled=True),
        out_weight,
        preferred_element_type=jnp.float32,
    )
    decoded = lax.psum(partial_value, "heads").astype(jnp.bfloat16)
    return (prefill_out, decoded)


def solution(mesh):
    in_specs = (
        P("groups", "ctx", "heads"),
        P("groups", "ctx", "heads"),
        P("groups", "ctx", "heads"),
        P("groups", "heads", "ctx"),
        P("groups", "heads", "ctx"),
        P("heads"),
        P(("groups", "ctx")),
        P(("groups", "ctx"), None, "heads"),
        P(("groups", "ctx"), None, "heads"),
        P(("groups", "ctx"), None, "heads"),
        P(("groups", "ctx"), None, "heads"),
        P(("groups", "ctx"), None, "heads"),
        P("heads", "ctx"),
    )
    out_specs = (P("groups", "ctx", "heads"), P("groups", None, "ctx"))
    return jax.shard_map(shards, mesh=mesh, in_specs=in_specs, out_specs=out_specs, check_vma=False)
```

profile of v0, /device:TPU:18, one launch (start us, length us, event | category | flops | bytes accessed | tf_op | source)
XLA Modules:
  0.0 468.9 jit_solution(9860267805544068038)
XLA Ops:
  10.1 4.1 fusion.76
  14.1 2.5 copy.53
  18.4 2.3 fusion.26
  20.9 4.1 copy.48
  26.0 2.3 fusion.28
  29.9 1.5 pad_maximum_fusion.1
  45.4 15.6 %all_gather.11 = bf16[8,2,2,32]{3,2,1,0:T(2,128)(2,1)S(1)} all-gather(bf16[1,2,2,32]{3,2,1,0:T(2,128)(2,1)S(1)} %pad_maximum_fusion.2), channel_id=1, replica_groups=mesh['groups'=2,'ctx'=8,'heads'=2] {'ctx'}, dimensions={0}, use_global_device_ids=true | all-gather | bytes 2304 | tf_op jit(solution)/shard_map/all_gather | solution.py:15
  65.1 1.3 broadcast_multiply_fusion
  68.4 191.0 %all-gather.4.cloned.1.call-done = bf16[8,2,2,32,64,128]{5,4,3,2,1,0:T(8,128)(2,1)} async-done(((bf16[1,2,2,32,64,128]{5,4,3,2,1,0:T(8,128)(2,1)}), bf16[8,2,2,32,64,128]{5,4,3,2,1,0:T(8,128)(2,1)}) %all-gather.4.cloned.1.call-update) | async-done | bytes 16777232 | tf_op jit(solution)/shard_map/all_gather | solution.py:15
  259.5 2.5 broadcast_in_dim.49
  262.0 21.5 %while.12 = (s32[]{:T(128)}, f32[2,2,32,64,128]{4,3,2,1,0:T(8,128)}, s32[]{:T(128)}, bf16[8,2,2,32]{3,2,1,0:T(2,128)(2,1)S(1)}, bf16[8,2,2,32,64,128]{5,4,3,2,1,...) while((s32[]{:T(128)}, f32[2,2,32,64,128]{4,3,2,1,0:T(8,128)}, s32[]{:T(128)}, ...), condition=%wide.region_5.6_spmd, body=%wide.region_4.5_spmd.sunk | while | flops 3145861 | bytes 10487167 | solution.py:29
  262.0 5.4 %convert_add_fusion.2 = f32[2,2,32,64,128]{4,3,2,1,0:T(8,128)} fusion(f32[2,2,32,64,128]{4,3,2,1,0:T(8,128)} %get-tuple-element.144, bf16[8,2,2,32,64,128]{5,4,3,2,1,0:T(8,128)(2,1)} %get-tuple-element.155, s32[]{:T(128)S(6)} %select_n.57, f32[2,2,32]{2,1,0:T(2,128)S(1)} %exponential_bitcast_fusion.2), kind=kLoop, calls=%fused_computation.clone.1 | loop fusion | flops 3145728 | bytes 10486276 | tf_op jit(solution)/shard_map/while/body/add | solution.py:142
  267.4 5.4 %convert_add_fusion.2 = f32[2,2,32,64,128]{4,3,2,1,0:T(8,128)} fusion(f32[2,2,32,64,128]{4,3,2,1,0:T(8,128)} %get-tuple-element.144, bf16[8,2,2,32,64,128]{5,4,3,2,1,0:T(8,128)(2,1)} %get-tuple-element.155, s32[]{:T(128)S(6)} %select_n.57, f32[2,2,32]{2,1,0:T(2,128)S(1)} %exponential_bitcast_fusion.2), kind=kLoop, calls=%fused_computation.clone.1 | loop fusion | flops 3145728 | bytes 10486276 | tf_op jit(solution)/shard_map/while/body/add | solution.py:142
  272.8 5.4 %convert_add_fusion.2 = f32[2,2,32,64,128]{4,3,2,1,0:T(8,128)} fusion(f32[2,2,32,64,128]{4,3,2,1,0:T(8,128)} %get-tuple-element.144, bf16[8,2,2,32,64,128]{5,4,3,2,1,0:T(8,128)(2,1)} %get-tuple-element.155, s32[]{:T(128)S(6)} %select_n.57, f32[2,2,32]{2,1,0:T(2,128)S(1)} %exponential_bitcast_fusion.2), kind=kLoop, calls=%fused_computation.clone.1 | loop fusion | flops 3145728 | bytes 10486276 | tf_op jit(solution)/shard_map/while/body/add | solution.py:142
  278.1 5.4 %convert_add_fusion.2 = f32[2,2,32,64,128]{4,3,2,1,0:T(8,128)} fusion(f32[2,2,32,64,128]{4,3,2,1,0:T(8,128)} %get-tuple-element.144, bf16[8,2,2,32,64,128]{5,4,3,2,1,0:T(8,128)(2,1)} %get-tuple-element.155, s32[]{:T(128)S(6)} %select_n.57, f32[2,2,32]{2,1,0:T(2,128)S(1)} %exponential_bitcast_fusion.2), kind=kLoop, calls=%fused_computation.clone.1 | loop fusion | flops 3145728 | bytes 10486276 | tf_op jit(solution)/shard_map/while/body/add | solution.py:142
  283.5 4.8 %fusion.25 = bf16[2,2,32,64,128]{4,3,2,1,0:T(8,128)(2,1)} fusion(f32[1,2,32,64,128]{4,3,2,1,0:T(8,128)S(1)} %bitcast.147, f32[1,2,32,64,128]{4,3,2,1,0:T(8,128)} %bitcast.148, f32[2,2,32,64,128]{4,3,2,1,0:T(8,128)} %get-tuple-element.46, f32[2,2,32]{2,1,0:T(2,128)S(1)} %maximum_exponential_fusion, pred[]{:T(512)S(6)} %eq.11), kind=kLoop, calls=%fused_computation.37 | loop fusion | flops 5242880 | bytes 10486273 | tf_op jit(solution)/shard_map/jit(_where)/select_n | solution.py:41
  288.4 3.6 fusion.32
  292.1 7.2 %fusion.18 = bf16[256,2,32,64]{0,3,2,1:T(8,128)(2,1)} fusion(bf16[256,2,32,64]{0,3,2,1:T(8,128)(2,1)S(1)} %bitcast.152, f32[2,32,64,256]{3,2,1,0:T(8,128)S(1)} %fusion.32, f32[2,32,256]{2,1,0:T(8,128)S(1)} %bitcast.171, f32[2,32,256]{2,1,0:T(8,128)S(1)} %copy-done.13, f32[2,256,256]{2,1,0:T(8,128)S(1)} %copy-done.5, ...), kind=kOutput, calls=%fused_computation.26 | convolution fusion | flops 568328192 | bytes 9175296 | tf_op jit(solution)/shard_map/gkts,sgkp->tgkp/dot_general | solution.py:66
  299.2 3.8 fusion.30
  303.0 4.3 copy.62
  307.3 9.5 %fusion.21 = bf16[256,2,32,64]{0,3,2,1:T(8,128)(2,1)} fusion(bf16[256,2,32,64]{0,3,2,1:T(8,128)(2,1)S(1)} %bitcast.150, f32[2,32,64,256]{3,2,1,0:T(8,128)} %fusion.30, f32[2,32,256]{2,1,0:T(8,128)S(1)} %bitcast.170, f32[2,32,256]{2,1,0:T(8,128)S(1)} %reduce_window_sum.52, f32[2,256,256]{2,1,0:T(8,128)S(1)} %fusion.82, ...), kind=kOutput, calls=%fused_computation.29 | convolution fusion | flops 568328192 | bytes 9175296 | tf_op jit(solution)/shard_map/gkts,sgkp->tgkp/dot_general | solution.py:66
  316.8 4.3 copy.63
  321.1 4.0 pad_maximum_fusion
  325.2 80.0 %all-reduce.3.cloned.1.call-done = bf16[2,2,32,64,128]{4,3,2,1,0:T(8,128)(2,1)} async-done(((bf16[2,2,32,64,128]{4,3,2,1,0:T(8,128)(2,1)}), bf16[2,2,32,64,128]{4,3,2,1,0:T(8,128)(2,1)}) %all-reduce.3.cloned.1.call-update) | async-done | bytes 2097168 | tf_op jit(solution)/shard_map/psum | solution.py:42
  405.1 3.9 fusion.42
  409.1 2.8 fusion.44
  412.0 3.6 fusion.58
  415.7 4.2 fusion.45
  420.0 5.6 %fusion.34 = f32[2,1,32,64]{3,1,2,0:T(1,128)S(1)} fusion(f32[2,128]{1,0:T(2,128)S(1)} %bitcast.184, f32[2,32,64]{2,1,0:T(8,128)S(1)} %copy-done.18, f32[2,32]{1,0:T(2,128)S(1)} %copy-done.36, f32[2,128]{1,0:T(2,128)S(1)} %bitcast.186, f32[2,32,64]{2,1,0:T(8,128)S(1)} %copy-done.17, f32[2,32]{1,0:T(2,128)S(1)} %copy-done.35, ...), kind=kOutput, calls=%fused_computation.45 | convolution fusion | flops 12582912 | bytes 2253824 | tf_op jit(solution)/shard_map/gkpn,gn->gkp/dot_general | solution.py:104
  426.1 26.6 %all-gather.1 = bf16[8,4,4096]{2,1,0:T(4,128)(2,1)S(1)} all-gather(bf16[1,4,4096]{2,1,0:T(4,128)(2,1)S(1)} %maximum_bitcast_fusion), channel_id=2, replica_groups=mesh['groups'=2,'ctx'=8,'heads'=2] {'ctx'}, dimensions={0}, use_global_device_ids=true | all-gather | bytes 294912 | tf_op jit(solution)/shard_map/all_gather | solution.py:180
  452.7 4.8 %fusion.2 = f32[8,4,1024]{2,0,1:T(8,128)S(1)} fusion(bf16[4096,1024]{1,0:T(8,128)(2,1)} %param.27, bf16[8,4,4096]{2,1,0:T(4,128)(2,1)S(1)} %all-gather.1), kind=kOutput, calls=%fused_computation.6 | convolution fusion | flops 268435456 | bytes 8781824 | tf_op jit(solution)/shard_map/jup,pd->jud/dot_general | solution.py:178
  457.5 3.8 all-reduce.4
  (151 shorter events, 28.0 us)
Async XLA Ops:
  7.2 252.3 %all-gather.4.cloned.1.call-start = ((), (), s32[]{:S(2)}) async-start(), calls=%async_computation | async-start | bytes 18874368 | tf_op jit(solution)/shard_map/all_gather | solution.py:15
  9.1 8.3 %copy-start.10 = (f32[64,256]{1,0:T(8,128)}, f32[64,256]{1,0:T(8,128)S(1)}, u32[]{:S(2)}) copy-start(f32[64,256]{1,0:T(8,128)S(1)} %copy_bitcast_fusion) | copy-start | bytes 196612
  10.1 7.3 %copy-start.11 = (f32[64,256]{1,0:T(8,128)}, f32[64,256]{1,0:T(8,128)S(1)}, u32[]{:S(2)}) copy-start(f32[64,256]{1,0:T(8,128)S(1)} %copy_bitcast_fusion.1) | copy-start | bytes 196612
  14.1 3.5 copy-start.6
  17.6 3.1 copy-start.23
  31.4 5.7 %copy-start.21 = (f32[1,4,64]{2,1,0:T(4,128)S(1)}, f32[1,4,64]{2,1,0:T(4,128)}, u32[]{:S(2)}) copy-start(f32[1,4,64]{2,1,0:T(4,128)} %param.25) | copy-start | bytes 3076
  31.4 5.7 %copy-start.22 = (f32[1,4,64]{2,1,0:T(4,128)S(1)}, f32[1,4,64]{2,1,0:T(4,128)}, u32[]{:S(2)}) copy-start(f32[1,4,64]{2,1,0:T(4,128)} %param.26) | copy-start | bytes 3076
  31.4 6.4 %copy-start.12 = (bf16[1,4,4096]{2,1,0:T(4,128)(2,1)S(1)}, bf16[1,4,4096]{2,1,0:T(4,128)(2,1)}, u32[]{:S(2)}) copy-start(bf16[1,4,4096]{2,1,0:T(4,128)(2,1)} %param.22) | copy-start | bytes 98308
  31.4 11.4 %copy-start.33 = (f32[64]{0:T(128)S(1)}, f32[64]{0:T(128)}, u32[]{:S(2)}) copy-start(f32[64]{0:T(128)} %param.20) | copy-start | bytes 772
  31.4 12.1 %copy-start.9 = (bf16[2,256,256]{2,1,0:T(8,128)(2,1)S(1)}, bf16[2,256,256]{2,1,0:T(8,128)(2,1)}, u32[]{:S(2)}) copy-start(bf16[2,256,256]{2,1,0:T(8,128)(2,1)} %param.17) | copy-start | bytes 786436
  31.4 30.3 %copy-start.19 = (bf16[1,4,256]{2,1,0:T(4,128)(2,1)S(1)}, bf16[1,4,256]{2,1,0:T(4,128)(2,1)}, u32[]{:S(2)}) copy-start(bf16[1,4,256]{2,1,0:T(4,128)(2,1)} %param.23) | copy-start | bytes 6148
  31.4 35.0 %copy-start.7 = (f32[2,64,256]{2,1,0:T(8,128)S(1)}, f32[2,64,256]{2,1,0:T(8,128)}, u32[]{:S(2)}) copy-start(f32[2,64,256]{2,1,0:T(8,128)} %param.18) | copy-start | bytes 393220
  31.5 373.7 %all-reduce.3.cloned.1.call-start = ((), (), s32[]{:S(2)}) async-start(), calls=%async_computation.1 | async-start | bytes 4194304 | tf_op jit(solution)/shard_map/psum | solution.py:42
  288.3 3.7 copy-start.3
  288.3 3.7 copy-start.5
  288.3 3.7 copy-start.13
  288.4 3.7 copy-start.14
  288.4 3.7 copy-start.16
  288.4 3.7 copy-start.28
  292.0 7.2 %copy-start = (f32[2,2,32,64,128]{4,3,2,1,0:T(8,128)S(1)}, f32[2,2,32,64,128]{4,3,2,1,0:T(8,128)}, u32[]{:S(2)}) copy-start(f32[2,2,32,64,128]{4,3,2,1,0:T(8,128)} %get-tuple-element.46) | copy-start | bytes 12582916
  303.0 4.3 copy-start.2
  303.0 4.3 copy-start.15
  316.8 4.3 copy-start.4
  405.1 4.0 copy-start.20
  405.1 4.0 copy-start.27
  405.1 4.0 copy-start.29
  412.0 3.7 copy-start.17
  412.0 3.7 copy-start.32
  412.0 3.7 copy-start.35
  415.7 4.3 copy-start.18
  415.7 4.3 copy-start.31
  415.7 4.3 copy-start.36
  (7 other events, 14.6 us)
Sparse Core Ops, SparseCore 0:
  31.6 227.8 all-gather.3
  288.4 116.6 all-reduce.2
where the time goes:
time: 476 us; the launch traced here: 469 us
  waiting for transfers between devices  271 us (57%)
  matrix products  55.1 us (12%)
  blocking collectives  46 us (10%)
  other arithmetic  41.1 us (9%)
  local copies, waits for them, and re-layouts  40.3 us (8%)
  between operations  15.3 us (3%)
    all_gather x1, waiting for transfers between devices, entering_2(): lax.all_gather(a.astype(kind), axis)  191 us
    psum x1, waiting for transfers between devices, spread(): return lax.psum(block, axis)  80 us
    all_gather x1, blocking collectives, shards(): lax.all_gather(new_output, 'ctx', axis=0, tiled=True)  26.6 us
    add x4, other arithmetic, combine(): jnp.exp(later[0])[:, :, :, None, None] * earlier[1] + later[1]  21.5 us
    dot_general x2, matrix products, block_terms(): jnp.einsum('gkts,sgkp->tgkp', mixing, inputs_head, preferred_element_type...  16.7 us
    dot_general x4, matrix products, decode_step(): jnp.einsum('gkpn,gn->gkp', carry_state, c_groups, precision=lax.Precision...  16.3 us
    all_gather x1, blocking collectives, entering_2(): lax.all_gather(a.astype(kind), axis)  15.6 us
    slice x3, local copies, waits for them, and re-layouts, shards(): ssm_input[request]  10.6 us
  transfers between devices with their start and end apart: 2, of which 2 were waited for; matrix products, arithmetic and copies ran while one was open for 12% of the time, Pallas kernels for 0%

commit v1 on v0

v1 whole, which is shorter than its diff:
```python
import jax
import jax.numpy as jnp
from jax import lax
from jax.sharding import PartitionSpec as P

HEADS = 128
HEAD_DIM = 64
STATE = 128
GROUPS = 4

HIGH = lax.Precision.HIGHEST


def block_terms(block_input, block_b, block_c, block_step, block_logd):
    block_size = block_input.shape[0]
    head_count = block_step.shape[0]
    per_group = HEADS // GROUPS
    group_count = head_count // per_group
    cumulative = jnp.cumsum(block_logd, axis=1)
    block_total = cumulative[:, -1]
    inputs_head = block_input.reshape(block_size, group_count, per_group, HEAD_DIM)
    b_groups = block_b.reshape(block_size, group_count, STATE)
    c_groups = block_c.reshape(block_size, group_count, STATE)
    scores = jnp.einsum("tgn,sgn->gts", c_groups, b_groups, preferred_element_type=jnp.float32)
    row_index = lax.broadcasted_iota(jnp.int32, (block_size, block_size), 0)
    col_index = lax.broadcasted_iota(jnp.int32, (block_size, block_size), 1)
    causal = row_index >= col_index
    log_gap = cumulative[:, :, None] - cumulative[:, None, :]
    decay_rate = (
        jnp.where(causal, jnp.exp(jnp.where(causal, log_gap, 0.0)), 0.0) * block_step[:, None, :]
    )
    mixing = (
        scores[:, None, :, :] * decay_rate.reshape(group_count, per_group, block_size, block_size)
    ).astype(jnp.bfloat16)
    local_out = jnp.einsum(
        "gkts,sgkp->tgkp", mixing, inputs_head, preferred_element_type=jnp.float32
    )
    weighting = jnp.exp(block_total[:, None] - cumulative) * block_step
    weighted = (weighting.T.reshape(block_size, group_count, per_group, 1) * inputs_head).astype(
        jnp.bfloat16
    )
    block_state = jnp.einsum(
        "sgkp,sgn->gkpn", weighted, b_groups, preferred_element_type=jnp.float32
    )
    return (cumulative, block_total.reshape(group_count, per_group), local_out, block_state)


def finish(local_out, cumulative, block_c, entering, block_input, skip_gain):
    block_size = block_input.shape[0]
    group_count, per_group = (entering.shape[0], entering.shape[1])
    c_groups = block_c.reshape(block_size, group_count, STATE).astype(jnp.float32)
    carried = jnp.einsum("tgn,gkpn->tgkp", c_groups, entering, precision=HIGH)
    carried = carried * jnp.exp(cumulative).T.reshape(block_size, group_count, per_group, 1)
    inputs_head = block_input.reshape(block_size, group_count, per_group, HEAD_DIM)
    skipped = skip_gain.reshape(group_count, per_group, 1) * inputs_head
    return (
        (local_out + carried + skipped)
        .reshape(block_size, group_count * per_group * HEAD_DIM)
        .astype(jnp.bfloat16)
    )


def range_decay(all_totals, low, high):
    place = lax.broadcasted_iota(jnp.int32, all_totals.shape, 0)
    keep = (place >= low) & (place <= high)
    return jnp.exp(jnp.sum(jnp.where(keep, all_totals, 0.0), axis=0))


def scale(factor, state):
    return factor[..., None, None] * state


def send(value, pairs):
    return lax.ppermute(value.astype(jnp.bfloat16), "ctx", pairs).astype(jnp.float32)


def prefix_states(states, all_totals):
    count = lax.axis_size("ctx")
    columns = count // 2
    place = lax.axis_index("ctx")
    row = place % 2
    column = place // 2
    half = states.shape[-2] // 2
    first = states[..., :half, :]
    second = states[..., half:, :]
    row_zero = row == 0
    mine = jnp.where(row_zero, first, second)
    other = jnp.where(row_zero, second, first)
    across = [(2 * m, 2 * m + 1) for m in range(columns)] + [
        (2 * m + 1, 2 * m) for m in range(columns)
    ]
    received = send(other, across)
    even_state = jnp.where(row_zero, mine, received)
    odd_state = jnp.where(row_zero, received, mine)
    odd_decay = range_decay(all_totals, 2 * column + 1, 2 * column + 1)
    window = scale(odd_decay, even_state) + odd_state
    before = jnp.zeros_like(window)
    step = 1
    while step < columns:
        pairs = [(y + 2 * m, y + 2 * (m + step)) for y in range(2) for m in range(columns - step)]
        got = send(window, pairs)
        low = 2 * (column - step) + 2
        before = scale(range_decay(all_totals, low, 2 * column - 1), got) + before
        if 2 * step < columns:
            window = scale(range_decay(all_totals, low, 2 * column + 1), got) + window
        step *= 2
    even_decay = range_decay(all_totals, 2 * column, 2 * column)
    odd_entering = scale(even_decay, before) + even_state
    outgoing = jnp.where(row_zero, odd_entering, before)
    partner = send(outgoing, across)
    own_half = jnp.where(row_zero, before, odd_entering)
    first_half = jnp.where(row_zero, own_half, partner)
    second_half = jnp.where(row_zero, partner, own_half)
    return jnp.concatenate([first_half, second_half], axis=-2)


def shards(
    ssm_input,
    b_proj,
    c_proj,
    step_size,
    log_decay,
    skip_gain,
    request_of_slot,
    new_input,
    new_b,
    new_c,
    new_step,
    new_log_decay,
    out_weight,
):
    request_count = ssm_input.shape[0]
    count = lax.axis_size("ctx")
    place = lax.axis_index("ctx")
    terms = []
    for request in range(request_count):
        terms.append(
            block_terms(
                ssm_input[request],
                b_proj[request],
                c_proj[request],
                step_size[request],
                log_decay[request],
            )
        )
    totals = jnp.stack([term[1] for term in terms])
    states = jnp.stack([term[3] for term in terms])
    group_count, per_group = totals.shape[1], totals.shape[2]

    slots, steps = new_input.shape[0], new_input.shape[1]
    pieces = [
        totals,
        request_of_slot.astype(jnp.float32),
        new_input.astype(jnp.float32),
        new_b.astype(jnp.float32),
        new_c.astype(jnp.float32),
        new_step,
        new_log_decay,
    ]
    packed = jnp.concatenate([piece.reshape(-1) for piece in pieces])
    gathered = lax.all_gather(packed, "ctx")
    unpacked = []
    offset = 0
    for piece in pieces:
        size = piece.size
        unpacked.append(
            gathered[:, offset : offset + size].reshape((count,) + piece.shape)
        )
        offset += size
    all_totals, all_request, all_input, all_b, all_c, all_step, all_logd = unpacked
    all_slots = count * slots
    all_request = all_request.reshape(all_slots)
    all_input = all_input.reshape(all_slots, steps, group_count, per_group, HEAD_DIM)
    all_b = all_b.reshape(all_slots, steps, group_count, STATE)
    all_c = all_c.reshape(all_slots, steps, group_count, STATE)
    all_step = all_step.reshape(all_slots, steps, group_count, per_group)
    all_logd = all_logd.reshape(all_slots, steps, group_count, per_group)

    later = range_decay(all_totals, place + 1, count - 1)
    weighted_states = scale(later, states)
    projected = jnp.einsum("rgkpn,jugn->rjugkp", weighted_states, all_c, precision=HIGH)
    request_numbers = lax.broadcasted_iota(jnp.int32, (request_count, 1), 0).astype(jnp.float32)
    chosen = (request_numbers == all_request[None, :]).astype(jnp.float32)
    contribution = jnp.einsum("rj,rjugkp->jugkp", chosen, projected, precision=HIGH)
    from_prompt = lax.psum(contribution, "ctx")

    cum_logd = jnp.cumsum(all_logd, axis=1)
    inner = jnp.einsum("jvgn,jugn->jvug", all_b, all_c, precision=HIGH)
    driven = all_step[..., None] * all_input
    outputs = []
    for u in range(steps):
        value = jnp.exp(cum_logd[:, u])[..., None] * from_prompt[:, u]
        for v in range(u + 1):
            gap = jnp.exp(cum_logd[:, u] - cum_logd[:, v])
            coefficient = gap * inner[:, v, u][:, :, None]
            value = value + coefficient[..., None] * driven[:, v]
        value = value + skip_gain.reshape(group_count, per_group, 1) * all_input[:, u]
        outputs.append(value.reshape(all_slots, -1).astype(jnp.bfloat16))
    new_output = jnp.stack(outputs, axis=1)
    partial_value = jnp.einsum(
        "jup,pd->jud", new_output, out_weight, preferred_element_type=jnp.float32
    )
    decoded = lax.psum(partial_value, "heads").astype(jnp.bfloat16)

    entering = prefix_states(states, all_totals)
    prefill_rows = []
    for request in range(request_count):
        prefill_rows.append(
            finish(
                terms[request][2],
                terms[request][0],
                c_proj[request],
                entering[request],
                ssm_input[request],
                skip_gain,
            )
        )
    prefill_out = jnp.stack(prefill_rows)
    return (prefill_out, decoded)


def solution(mesh):
    in_specs = (
        P("groups", "ctx", "heads"),
        P("groups", "ctx", "heads"),
        P("groups", "ctx", "heads"),
        P("groups", "heads", "ctx"),
        P("groups", "heads", "ctx"),
        P("heads"),
        P(("groups", "ctx")),
        P(("groups", "ctx"), None, "heads"),
        P(("groups", "ctx"), None, "heads"),
        P(("groups", "ctx"), None, "heads"),
        P(("groups", "ctx"), None, "heads"),
        P(("groups", "ctx"), None, "heads"),
        P("heads", "ctx"),
    )
    out_specs = (P("groups", "ctx", "heads"), P("groups", None, "ctx"))
    return jax.shard_map(shards, mesh=mesh, in_specs=in_specs, out_specs=out_specs, check_vma=False)
```

time: 476 us -> 317 us (0.67)
  waiting for transfers between devices: 271 us -> 93.1 us
  local copies, waits for them, and re-layouts: 40.3 us -> 109 us
  blocking collectives: 46 us -> 4.36 us
  other arithmetic: 41.1 us -> 31.6 us
  starting transfers between devices: 0.08 us -> 7.61 us
    all_gather x1 -> x0, waiting for transfers between devices: 191 us -> none  [entering_2(): lax.all_gather(a.astype(kind), axis)]
    all_gather x2 -> x0, blocking collectives: 42.1 us -> none  [the longest x1 26.6 us: shards(): lax.all_gather(new_output, 'ctx', axis=0, tiled=True)]
    unnamed x2 -> x3, waiting for transfers between devices: 0.03 us -> 30.2 us
    psum x1, waiting for transfers between devices: 80 us -> 50.8 us  [shards(): from_prompt = lax.psum(contribution, 'ctx')]
    mul x4 -> x41, local copies, waits for them, and re-layouts: 2.56 us -> 25.2 us  [the longest x20 15.8 us: shards(): value = value + coefficient[..., None] * driven[:, v]]
    add x4 -> x0, other arithmetic: 21.5 us -> none  [combine(): jnp.exp(later[0])[:, :, :, None, None] * earlier[1] + later[1]]
    squeeze x0 -> x12, local copies, waits for them, and re-layouts: none -> 18.1 us  [the longest x4 6.87 us: shards(): value = jnp.exp(cum_logd[:, u])[..., None] * from_prompt[:, u]]
    convert_element_type x3 -> x7, other arithmetic: 0.88 us -> 13.9 us  [the longest x4 11.5 us: send(): value.astype(jnp.bfloat16)]
  transfers between devices with their start and end apart: 2 -> 6, of which waited for: 2 -> 3; matrix products, arithmetic and copies ran while one was open for 12% -> 49% of each run, Pallas kernels for 0% -> 0%
where the time goes in v1:
time: 317 us; the launch traced here: 314 us
  local copies, waits for them, and re-layouts  109 us (34%)
  waiting for transfers between devices  93.1 us (29%)
  matrix products  52.7 us (17%)
  other arithmetic  31.6 us (10%)
  between operations  16.2 us (5%)
  starting transfers between devices  7.61 us (2%)
  blocking collectives  4.36 us (1%)
    psum x1, waiting for transfers between devices, shards(): from_prompt = lax.psum(contribution, 'ctx')  50.8 us
    unnamed x3, waiting for transfers between devices  30.2 us
    mul x20, local copies, waits for them, and re-layouts, shards(): value = value + coefficient[..., None] * driven[:, v]  15.8 us
    dot_general x2, matrix products, block_terms(): jnp.einsum('gkts,sgkp->tgkp', mixing, inputs_head, preferred_element_type...  14.6 us
    dot_general x1, matrix products, shards(): jnp.einsum('rgkpn,jugn->rjugkp', weighted_states, all_c, precision=HIGH)  12.9 us
    ppermute x4, waiting for transfers between devices, send(): lax.ppermute(value.astype(jnp.bfloat16), 'ctx', pairs).astype(jnp.float32)  12.1 us
    convert_element_type x4, other arithmetic, send(): value.astype(jnp.bfloat16)  11.5 us
    slice x3, local copies, waits for them, and re-layouts, shards(): ssm_input[request]  10.6 us
  transfers between devices with their start and end apart: 6, of which 3 were waited for; matrix products, arithmetic and copies ran while one was open for 49% of the time, Pallas kernels for 0%

profile of v1, /device:TPU:18, one launch (start us, length us, event | category | flops | bytes accessed | tf_op | source)
XLA Modules:
  0.0 314.2 jit_solution(35564834466314363)
XLA Ops:
  19.5 3.9 %fusion.76 = (bf16[1,256,4096]{2,1,0:T(8,128)(2,1)}, bf16[1,256,4096]{2,1,0:T(8,128)(2,1)S(1)}) fusion(bf16[2,256,4096]{2,1,0:T(8,128)(2,1)} %param.13), kind=kLoop, calls=%fused_computation.144 | loop fusion | bytes 8388608 | tf_op jit(solution)/shard_map/slice | solution.py:139
  23.4 4.2 %copy.105 = bf16[1,256,4096]{1,2,0:T(8,128)(2,1)} copy(bf16[1,256,4096]{2,1,0:T(8,128)(2,1)} %get-tuple-element.18) | data formatting | bytes 4194304 | tf_op jit(solution)/shard_map/slice | solution.py:139
  27.8 2.5 copy.110
  30.4 2.4 fusion.52
  45.5 8.0 %fusion = f32[2,32,256,64]{2,3,1,0:T(8,128)} fusion(bf16[256,2,32,64]{0,3,2,1:T(8,128)(2,1)} %bitcast.245, f32[2,32,256]{2,1,0:T(8,128)} %bitcast.270, f32[2,32,256]{2,1,0:T(8,128)} %reduce_window_sum.59, f32[2,256,256]{2,1,0:T(8,128)S(1)} %fusion.88, pred[256,256]{1,0:T(8,128)(4,1)} %iota_compare_fusion), kind=kOutput, calls=%fused_computation.2 | convolution fusion | flops 562036736 | bytes 7012352 | tf_op jit(solution)/shard_map/gkts,sgkp->tgkp/dot_general | solution.py:35
  53.5 6.6 %fusion.1 = f32[2,32,256,64]{2,3,1,0:T(8,128)} fusion(bf16[256,2,32,64]{0,3,2,1:T(8,128)(2,1)S(1)} %bitcast.248, f32[2,32,256]{2,1,0:T(8,128)S(1)} %bitcast.269, f32[2,32,256]{2,1,0:T(8,128)S(1)} %copy-done.32, f32[2,256,256]{2,1,0:T(8,128)S(1)} %fusion.89, pred[256,256]{1,0:T(8,128)(4,1)S(1)} %copy-done.31), kind=kOutput, calls=%fused_computation.3 | convolution fusion | flops 562036736 | bytes 7012352 | tf_op jit(solution)/shard_map/gkts,sgkp->tgkp/dot_general | solution.py:35
  62.6 30.2 %all-reduce.7.cloned.1.call-done = f32[152584]{0:T(1024)} async-done(((f32[152584]{0:T(1024)}), f32[152584]{0:T(1024)}) %all-reduce.7.cloned.1.call-update) | async-done | bytes 610352
  92.8 2.3 reshape.861
  100.5 2.0 slice.261
  106.0 1.7 mul.693
  113.4 12.9 %fusion.49 = f32[2,8,4,2,32,64]{5,1,4,0,2,3:T(8,128)S(1)} fusion(f32[8,4,2,128,1,1]{3,0,2,1,5,4:T(8,128)S(1)} %bitcast.262, f32[1,2,32,64,128]{4,3,2,1,0:T(8,128)} %copy-done, f32[1,2,32,64,128]{4,3,2,1,0:T(8,128)S(1)} %fusion.52, f32[2,2,32]{2,1,0:T(2,128)S(1)} %exp.239), kind=kOutput, calls=%fused_computation.71 | convolution fusion | flops 404750336 | bytes 5276160 | tf_op jit(solution)/shard_map/rgkpn,jugn->rjugkp/dot_general | solution.py:181
  126.3 4.9 %fusion.47 = f32[8,1,4,2,32,64]{5,1,4,3,2,0:T(1,128)S(1)} fusion(pred[2,8,1,1,1,1]{0,2,5,4,3,1:T(4,128)(4,1)S(1)} %copy.162, f32[2,8,4,2,32,64]{5,1,4,0,2,3:T(8,128)S(1)} %fusion.49), kind=kOutput, calls=%fused_computation.69 | convolution fusion | flops 3145728 | bytes 1572880 | tf_op jit(solution)/shard_map/rj,rjugkp->jugkp/dot_general | solution.py:184
  132.3 2.5 reshape_reshape.15
  135.0 3.9 %fusion.58 = (bf16[2,2,32,32,128]{4,3,2,1,0:T(8,128)(2,1)}, f32[2,2,32,32,128]{4,3,2,1,0:T(8,128)}) fusion(bf16[2,2,32,32,128]{4,3,2,1,0:T(8,128)(2,1)S(1)} %collective-permute-done, pred[]{:T(512)S(6)} %eq.20, f32[2,2,32]{2,1,0:T(2,128)S(1)} %exp.226, f32[1,2,32,64,128]{4,3,2,1,0:T(8,128)} %copy-done, f32[1,2,32,64,128]{4,3,2,1,0:T(8,128)S(1)} %fusion.52), kind=kLoop, calls=%fused_computation.77 | loop fusion | flops 4718592 | bytes 8389121 | tf_op jit(solution)/shard_map/convert_element_type | solution.py:74
  138.8 3.2 %collective-permute-start.1 = (bf16[2,2,32,32,128]{4,3,2,1,0:T(8,128)(2,1)}, bf16[2,2,32,32,128]{4,3,2,1,0:T(8,128)(2,1)}, u32[]{:S(2)}, u32[]{:S(2)}) collective-permute-start(bf16[2,2,32,32,128]{4,3,2,1,0:T(8,128)(2,1)} %get-tuple-element.14), channel_id=1, source_target_pairs={{0,4},{4,8},{8,12},{2,6},{6,10},{10,14},{1,5},{5,9},{9,13},{3,7},{... | collective-permute-start | bytes 3145736 | tf_op jit(solution)/shard_map/ppermute | solution.py:74
  158.9 1.9 mul.749
  162.5 1.7 squeeze.46
  172.4 1.7 squeeze.44
  187.3 3.0 fusion.30
  191.6 50.8 %all-reduce.5.cloned.1.call-done = f32[8,4,2,32,64]{4,3,2,0,1:T(8,128)} async-done(((f32[8,4,2,32,64]{4,3,2,0,1:T(8,128)}), f32[8,4,2,32,64]{4,3,2,0,1:T(8,128)}) %all-reduce.5.cloned.1.call-update) | async-done | bytes 524304 | tf_op jit(solution)/shard_map/psum | solution.py:185
  242.4 2.2 fusion.77
  244.6 1.7 squeeze.36
  253.4 3.1 select_convert_fusion
  258.1 4.9 %fusion.2 = f32[8,4,1024]{2,0,1:T(8,128)S(1)} fusion(bf16[4096,1024]{1,0:T(8,128)(2,1)} %param.25, bf16[8,1,4096]{2,0,1:T(8,128)(2,1)S(1)} %get-tuple-element.37, bf16[8,1,4096]{2,0,1:T(8,128)(2,1)S(1)} %get-tuple-element.36, bf16[8,1,4096]{2,0,1:T(8,128)(2,1)S(1)} %get-tuple-element.43, bf16[8,1,4096]{2,0,1:T(8,128)(2,1)S(1)} %get-tuple-element.42), kind=kOutput, calls=%fused_computation.4 | convolution fusion | flops 268828672 | bytes 8781824 | tf_op jit(solution)/shard_map/jup,pd->jud/dot_general | solution.py:200
  263.0 4.4 %all-reduce.8 = bf16[8,4,1024]{2,0,1:T(8,128)(2,1)} all-reduce(f32[8,4,1024]{2,0,1:T(8,128)S(1)} %fusion.2), channel_id=1, replica_groups=mesh['groups'=2,'ctx'=8,'heads'=2] {'heads'}, use_global_device_ids=true, to_apply=%region_12.13 | all-reduce | flops 32768 | bytes 196608 | tf_op jit(solution)/shard_map/psum | solution.py:203
  268.9 12.1 %collective-permute-done.3 = bf16[2,2,32,32,128]{4,3,2,1,0:T(8,128)(2,1)} collective-permute-done((bf16[2,2,32,32,128]{4,3,2,1,0:T(8,128)(2,1)}, bf16[2,2,32,32,128]{4,3,2,1,0:T(8,128)(2,1)}, u32[]{:S(2)}, u32[]{:S(2)}) %collective-permute-start.3) | collective-permute-done | bytes 1048608 | tf_op jit(solution)/shard_map/ppermute | solution.py:74
  281.0 2.8 convert_select_fusion.1
  284.2 4.0 %fusion.18 = bf16[256,2,32,64]{0,3,2,1:T(8,128)(2,1)} fusion(bf16[256,2,32,64]{0,3,2,1:T(8,128)(2,1)S(1)} %bitcast.246, f32[2,32,256,64]{2,3,1,0:T(8,128)S(1)} %copy-done.11, bf16[256,2,128,1]{0,2,3,1:T(8,128)(2,1)S(1)} %bitcast.256, f32[2,2,32,32,128]{4,3,2,1,0:T(8,128)S(1)} %get-tuple-element.16, f32[2,2,32,32,128]{4,3,2,1,0:T(8,128)S(1)} %get-tuple-element.17, ...), kind=kOutput, calls=%fused_computation.29 | convolution fusion | flops 1617428480 | bytes 12779776 | tf_op jit(solution)/shard_map/tgn,gkpn->tgkp/dot_general | solution.py:52
  288.2 4.4 %copy.119 = bf16[1,256,4096]{2,1,0:T(8,128)(2,1)} copy(bf16[1,256,4096]{1,2,0:T(8,128)(2,1)} %bitcast.251) | data formatting | bytes 4194304 | tf_op jit(solution)/shard_map/convert_element_type | solution.py:59
  292.5 6.6 %fusion.21 = bf16[256,2,32,64]{0,3,2,1:T(8,128)(2,1)} fusion(bf16[256,2,32,64]{0,3,2,1:T(8,128)(2,1)S(1)} %bitcast.249, f32[2,32,256,64]{2,3,1,0:T(8,128)} %fusion.1, bf16[256,2,128,1]{0,2,3,1:T(8,128)(2,1)S(1)} %bitcast.254, f32[2,2,32,32,128]{4,3,2,1,0:T(8,128)} %copy-done.7, f32[2,2,32,32,128]{4,3,2,1,0:T(8,128)} %copy-done.6, ...), kind=kOutput, calls=%fused_computation.32 | convolution fusion | flops 1617428480 | bytes 12779776 | tf_op jit(solution)/shard_map/tgn,gkpn->tgkp/dot_general | solution.py:52
  299.1 4.3 %copy.120 = bf16[1,256,4096]{2,1,0:T(8,128)(2,1)} copy(bf16[1,256,4096]{1,2,0:T(8,128)(2,1)} %bitcast.250) | data formatting | bytes 4194304 | tf_op jit(solution)/shard_map/convert_element_type | solution.py:59
  303.3 4.0 %pad_maximum_fusion.1 = bf16[2,256,4096]{2,1,0:T(8,128)(2,1)} fusion(bf16[1,256,4096]{2,1,0:T(8,128)(2,1)} %copy.120, bf16[1,256,4096]{2,1,0:T(8,128)(2,1)S(1)} %copy-done.10), kind=kLoop, calls=%fused_computation.37 | loop fusion | flops 2097152 | bytes 8388608 | tf_op jit(solution)/shard_map/stack | solution.py:218
  (262 shorter events, 93.3 us)
Async XLA Ops:
  7.2 11.5 %copy-start.24 = (f32[2,64,256]{2,1,0:T(8,128)S(1)}, f32[2,64,256]{2,1,0:T(8,128)}, u32[]{:S(2)}) copy-start(f32[2,64,256]{2,1,0:T(8,128)} %param.16) | copy-start | bytes 393220
  7.2 85.6 %all-reduce.7.cloned.1.call-start = ((), (), s32[]{:S(2)}) async-start(), calls=%async_computation.1 | async-start | bytes 1228800
  18.6 223.8 %all-reduce.5.cloned.1.call-start = ((), (), s32[]{:S(2)}) async-start(), calls=%async_computation | async-start | bytes 2097152 | tf_op jit(solution)/shard_map/psum | solution.py:185
  35.3 99.7 %collective-permute-start = (bf16[2,2,32,32,128]{4,3,2,1,0:T(8,128)(2,1)}, bf16[2,2,32,32,128]{4,3,2,1,0:T(8,128)(2,1)S(1)}, u32[]{:S(2)}, u32[]{:S(2)}) collective-permute-start(bf16[2,2,32,32,128]{4,3,2,1,0:T(8,128)(2,1)} %select_convert_fusion.1), channel_id=1, source_target_pairs={{0,2},{4,6},{8,10},{12,14},{2,0},{6,4},{10,8},{14,12},{1,3},{5,7},... | collective-permute-start | bytes 3145736 | tf_op jit(solution)/shard_map/ppermute | solution.py:74
  45.4 8.0 %copy-start.4 = (bf16[1,256,4096]{1,2,0:T(8,128)(2,1)S(1)}, bf16[1,256,4096]{1,2,0:T(8,128)(2,1)}, u32[]{:S(2)}) copy-start(bf16[1,256,4096]{1,2,0:T(8,128)(2,1)} %copy.110) | copy-start | bytes 6291460
  45.4 8.0 %copy-start.31 = (pred[256,256]{1,0:T(8,128)(4,1)S(1)}, pred[256,256]{1,0:T(8,128)(4,1)}, u32[]{:S(2)}) copy-start(pred[256,256]{1,0:T(8,128)(4,1)} %iota_compare_fusion) | copy-start | bytes 196612
  45.5 8.0 %copy-start.32 = (f32[2,32,256]{2,1,0:T(8,128)S(1)}, f32[2,32,256]{2,1,0:T(8,128)}, u32[]{:S(2)}) copy-start(f32[2,32,256]{2,1,0:T(8,128)} %reduce_window_sum.63) | copy-start | bytes 196612
  45.5 8.0 %copy-start.33 = (f32[1,64,256]{2,1,0:T(8,128)S(1)}, f32[1,64,256]{2,1,0:T(8,128)}, u32[]{:S(2)}) copy-start(f32[1,64,256]{2,1,0:T(8,128)} %get-tuple-element.45) | copy-start | bytes 196612
  53.5 6.6 %copy-start.50 = (f32[64]{0:T(128)S(1)}, f32[64]{0:T(128)}, u32[]{:S(2)}) copy-start(f32[64]{0:T(128)} %param.18) | copy-start | bytes 772
  60.2 32.6 %copy-start.48 = (f32[2,32]{1,0:T(2,128)}, f32[2,32]{1,0:T(2,128)S(1)}, u32[]{:S(2)}) copy-start(f32[2,32]{1,0:T(2,128)S(1)} %mul.656) | copy-start | bytes 772
  135.0 7.1 %copy-start.8 = (f32[8,4,2,32,64]{4,3,2,1,0:T(8,128)S(1)}, f32[8,4,2,32,64]{4,3,2,1,0:T(8,128)}, u32[]{:S(2)}) copy-start(f32[8,4,2,32,64]{4,3,2,1,0:T(8,128)} %reshape_reshape.15) | copy-start | bytes 1572868
  138.8 48.5 %collective-permute-start.1 = (bf16[2,2,32,32,128]{4,3,2,1,0:T(8,128)(2,1)}, bf16[2,2,32,32,128]{4,3,2,1,0:T(8,128)(2,1)}, u32[]{:S(2)}, u32[]{:S(2)}) collective-permute-start(bf16[2,2,32,32,128]{4,3,2,1,0:T(8,128)(2,1)} %get-tuple-element.14), channel_id=1, source_target_pairs={{0,4},{4,8},{8,12},{2,6},{6,10},{10,14},{1,5},{5,9},{9,13},{3,7},{... | collective-permute-start | bytes 3145736 | tf_op jit(solution)/shard_map/ppermute | solution.py:74
  142.4 7.0 %copy-start.9 = (f32[8,4,2,32,64]{4,3,2,1,0:T(8,128)S(1)}, f32[8,4,2,32,64]{4,3,2,1,0:T(8,128)}, u32[]{:S(2)}) copy-start(f32[8,4,2,32,64]{4,3,2,1,0:T(8,128)} %reshape_reshape.15) | copy-start | bytes 1572868
  150.4 5.2 %copy-start.36 = (f32[8,1,1,2]{1,2,3,0:T(1,128)S(1)}, f32[8,1,1,2]{1,2,3,0:T(1,128)}, u32[]{:S(2)}) copy-start(f32[8,1,1,2]{1,2,3,0:T(1,128)} %get-tuple-element.66) | copy-start | bytes 196
  150.4 5.4 %copy-start.35 = (f32[8,1,1,2]{1,2,3,0:T(1,128)S(1)}, f32[8,1,1,2]{1,2,3,0:T(1,128)}, u32[]{:S(2)}) copy-start(f32[8,1,1,2]{1,2,3,0:T(1,128)} %get-tuple-element.65) | copy-start | bytes 196
  150.4 5.6 %copy-start.34 = (f32[8,1,1,2]{1,2,3,0:T(1,128)S(1)}, f32[8,1,1,2]{1,2,3,0:T(1,128)}, u32[]{:S(2)}) copy-start(f32[8,1,1,2]{1,2,3,0:T(1,128)} %get-tuple-element.64) | copy-start | bytes 196
  150.4 5.7 %copy-start.27 = (f32[8,4,2,32]{3,2,1,0:T(2,128)S(1)}, f32[8,4,2,32]{3,2,1,0:T(2,128)}, u32[]{:S(2)}) copy-start(f32[8,4,2,32]{3,2,1,0:T(2,128)} %copy-done.26) | copy-start | bytes 24580
  158.9 28.4 %copy-start.1 = (f32[2,2,32,32,128]{4,3,2,1,0:T(8,128)S(1)}, f32[2,2,32,32,128]{4,3,2,1,0:T(8,128)}, u32[]{:S(2)}) copy-start(f32[2,2,32,32,128]{4,3,2,1,0:T(8,128)} %get-tuple-element.15) | copy-start | bytes 6291460
  190.3 63.0 %collective-permute-start.2 = (bf16[2,2,32,32,128]{4,3,2,1,0:T(8,128)(2,1)}, bf16[2,2,32,32,128]{4,3,2,1,0:T(8,128)(2,1)}, u32[]{:S(2)}, u32[]{:S(2)}) collective-permute-start(bf16[2,2,32,32,128]{4,3,2,1,0:T(8,128)(2,1)} %fusion.30), channel_id=1, source_target_pairs={{0,8},{4,12},{2,10},{6,14},{1,9},{5,13},{3,11},{7,15},{16,24},{20,... | collective-permute-start | bytes 3145736 | tf_op jit(solution)/shard_map/ppermute | solution.py:74
  253.2 4.7 %copy-start.13 = (f32[8,1,4096]{2,0,1:T(8,128)S(1)}, f32[8,1,4096]{2,0,1:T(8,128)}, u32[]{:S(2)}) copy-start(f32[8,1,4096]{2,0,1:T(8,128)} %squeeze.40) | copy-start | bytes 393220
  253.2 4.7 %copy-start.15 = (f32[8,1,4096]{2,0,1:T(8,128)S(1)}, f32[8,1,4096]{2,0,1:T(8,128)}, u32[]{:S(2)}) copy-start(f32[8,1,4096]{2,0,1:T(8,128)} %mul.677) | copy-start | bytes 393220
  253.2 4.7 %copy-start.16 = (f32[8,1,4096]{2,0,1:T(8,128)S(1)}, f32[8,1,4096]{2,0,1:T(8,128)}, u32[]{:S(2)}) copy-start(f32[8,1,4096]{2,0,1:T(8,128)} %mul.693) | copy-start | bytes 393220
  253.3 4.7 %copy-start.17 = (f32[8,1,4096]{2,0,1:T(8,128)S(1)}, f32[8,1,4096]{2,0,1:T(8,128)}, u32[]{:S(2)}) copy-start(f32[8,1,4096]{2,0,1:T(8,128)} %mul.699) | copy-start | bytes 393220
  253.3 4.7 %copy-start.18 = (f32[8,1,4096]{2,0,1:T(8,128)S(1)}, f32[8,1,4096]{2,0,1:T(8,128)}, u32[]{:S(2)}) copy-start(f32[8,1,4096]{2,0,1:T(8,128)} %mul.669) | copy-start | bytes 393220
  253.3 4.7 %copy-start.19 = (f32[8,1,4096]{2,0,1:T(8,128)S(1)}, f32[8,1,4096]{2,0,1:T(8,128)}, u32[]{:S(2)}) copy-start(f32[8,1,4096]{2,0,1:T(8,128)} %mul.687) | copy-start | bytes 393220
  256.4 24.6 %collective-permute-start.3 = (bf16[2,2,32,32,128]{4,3,2,1,0:T(8,128)(2,1)}, bf16[2,2,32,32,128]{4,3,2,1,0:T(8,128)(2,1)}, u32[]{:S(2)}, u32[]{:S(2)}) collective-permute-start(bf16[2,2,32,32,128]{4,3,2,1,0:T(8,128)(2,1)} %select_convert_fusion), channel_id=1, source_target_pairs={{0,2},{4,6},{8,10},{12,14},{2,0},{6,4},{10,8},{14,12},{1,3},{5,7},... | collective-permute-start | bytes 3145736 | tf_op jit(solution)/shard_map/ppermute | solution.py:74
  258.1 22.9 %copy-start.43 = (f32[2,2,32]{2,1,0:T(2,128)S(1)}, f32[2,2,32]{2,1,0:T(2,128)}, u32[]{:S(2)}) copy-start(f32[2,2,32]{2,1,0:T(2,128)} %exp.222) | copy-start | bytes 1540
  258.1 22.9 %copy-start.45 = (f32[2,2,32]{2,1,0:T(2,128)S(1)}, f32[2,2,32]{2,1,0:T(2,128)}, u32[]{:S(2)}) copy-start(f32[2,2,32]{2,1,0:T(2,128)} %exp.230) | copy-start | bytes 1540
  258.1 22.9 %copy-start.47 = (f32[2,2,32]{2,1,0:T(2,128)S(1)}, f32[2,2,32]{2,1,0:T(2,128)}, u32[]{:S(2)}) copy-start(f32[2,2,32]{2,1,0:T(2,128)} %exp.232) | copy-start | bytes 1540
  268.9 15.0 %copy-start.2 = (bf16[1,256,4096]{1,2,0:T(8,128)(2,1)S(1)}, bf16[1,256,4096]{1,2,0:T(8,128)(2,1)}, u32[]{:S(2)}) copy-start(bf16[1,256,4096]{1,2,0:T(8,128)(2,1)} %copy.105) | copy-start | bytes 6291460
  268.9 15.0 %copy-start.29 = (f32[64,256]{1,0:T(8,128)S(1)}, f32[64,256]{1,0:T(8,128)}, u32[]{:S(2)}) copy-start(f32[64,256]{1,0:T(8,128)} %get-tuple-element.51) | copy-start | bytes 196612
  268.9 15.0 %copy-start.49 = (f32[2,32]{1,0:T(2,128)S(1)}, f32[2,32]{1,0:T(2,128)}, u32[]{:S(2)}) copy-start(f32[2,32]{1,0:T(2,128)} %copy-done.48) | copy-start | bytes 772
  (25 other events, 83.0 us)
Sparse Core Ops, SparseCore 0:
  18.8 73.9 all-reduce.6
  132.4 109.9 all-reduce.4

commit v2 on v1

--- a/solution.py
+++ b/solution.py
@@ -148,15 +148,7 @@
     group_count, per_group = totals.shape[1], totals.shape[2]
 
     slots, steps = new_input.shape[0], new_input.shape[1]
-    pieces = [
-        totals,
-        request_of_slot.astype(jnp.float32),
-        new_input.astype(jnp.float32),
-        new_b.astype(jnp.float32),
-        new_c.astype(jnp.float32),
-        new_step,
-        new_log_decay,
-    ]
+    pieces = [totals, request_of_slot.astype(jnp.float32), new_c.astype(jnp.float32)]
     packed = jnp.concatenate([piece.reshape(-1) for piece in pieces])
     gathered = lax.all_gather(packed, "ctx")
     unpacked = []
@@ -167,38 +159,53 @@
             gathered[:, offset : offset + size].reshape((count,) + piece.shape)
         )
         offset += size
-    all_totals, all_request, all_input, all_b, all_c, all_step, all_logd = unpacked
+    all_totals, all_request, all_c = unpacked
     all_slots = count * slots
     all_request = all_request.reshape(all_slots)
-    all_input = all_input.reshape(all_slots, steps, group_count, per_group, HEAD_DIM)
-    all_b = all_b.reshape(all_slots, steps, group_count, STATE)
     all_c = all_c.reshape(all_slots, steps, group_count, STATE)
-    all_step = all_step.reshape(all_slots, steps, group_count, per_group)
-    all_logd = all_logd.reshape(all_slots, steps, group_count, per_group)
 
     later = range_decay(all_totals, place + 1, count - 1)
     weighted_states = scale(later, states)
-    projected = jnp.einsum("rgkpn,jugn->rjugkp", weighted_states, all_c, precision=HIGH)
-    request_numbers = lax.broadcasted_iota(jnp.int32, (request_count, 1), 0).astype(jnp.float32)
-    chosen = (request_numbers == all_request[None, :]).astype(jnp.float32)
-    contribution = jnp.einsum("rj,rjugkp->jugkp", chosen, projected, precision=HIGH)
-    from_prompt = lax.psum(contribution, "ctx")
-
-    cum_logd = jnp.cumsum(all_logd, axis=1)
-    inner = jnp.einsum("jvgn,jugn->jvug", all_b, all_c, precision=HIGH)
-    driven = all_step[..., None] * all_input
-    outputs = []
-    for u in range(steps):
-        value = jnp.exp(cum_logd[:, u])[..., None] * from_prompt[:, u]
-        for v in range(u + 1):
-            gap = jnp.exp(cum_logd[:, u] - cum_logd[:, v])
-            coefficient = gap * inner[:, v, u][:, :, None]
-            value = value + coefficient[..., None] * driven[:, v]
-        value = value + skip_gain.reshape(group_count, per_group, 1) * all_input[:, u]
-        outputs.append(value.reshape(all_slots, -1).astype(jnp.bfloat16))
-    new_output = jnp.stack(outputs, axis=1)
+    high = weighted_states.astype(jnp.bfloat16)
+    low = (weighted_states - high.astype(jnp.float32)).astype(jnp.bfloat16)
+    c_rows = all_c.astype(jnp.bfloat16)
+    projected = jnp.einsum(
+        "rgkpn,jugn->rjugkp", high, c_rows, preferred_element_type=jnp.float32
+    ) + jnp.einsum("rgkpn,jugn->rjugkp", low, c_rows, preferred_element_type=jnp.float32)
+    contribution = projected[0]
+    for request in range(1, request_count):
+        pick = (all_request == request)[:, None, None, None, None]
+        contribution = jnp.where(pick, projected[request], contribution)
+    from_prompt = lax.psum_scatter(contribution, "ctx", scatter_dimension=0, tiled=True)
+
+    row_input = new_input.reshape(slots, steps, group_count, per_group, HEAD_DIM).astype(
+        jnp.float32
+    )
+    row_b = new_b.reshape(slots, steps, group_count, STATE).astype(jnp.float32)
+    row_c = new_c.reshape(slots, steps, group_count, STATE).astype(jnp.float32)
+    row_step = new_step.reshape(slots, steps, group_count, per_group)
+    row_logd = new_log_decay.reshape(slots, steps, group_count, per_group)
+    cum_logd = jnp.cumsum(row_logd, axis=1)
+    inner = jnp.einsum("jvgn,jugn->jvug", row_b, row_c, precision=HIGH)
+    order_v = lax.broadcasted_iota(jnp.int32, (steps, steps), 0)
+    order_u = lax.broadcasted_iota(jnp.int32, (steps, steps), 1)
+    causal = (order_v <= order_u)[None, :, :, None, None]
+    gap = cum_logd[:, None, :, :, :] - cum_logd[:, :, None, :, :]
+    coefficient = jnp.where(
+        causal, jnp.exp(jnp.where(causal, gap, 0.0)) * inner[..., None], 0.0
+    ) * row_step[:, :, None, :, :]
+    local_part = jnp.sum(coefficient[..., None] * row_input[:, :, None], axis=1)
+    value = (
+        jnp.exp(cum_logd)[..., None] * from_prompt
+        + local_part
+        + skip_gain.reshape(group_count, per_group, 1) * row_input
+    )
+    new_output = value.reshape(slots, steps, -1).astype(jnp.bfloat16)
     partial_value = jnp.einsum(
-        "jup,pd->jud", new_output, out_weight, preferred_element_type=jnp.float32
+        "jup,pd->jud",
+        lax.all_gather(new_output, "ctx", axis=0, tiled=True),
+        out_weight,
+        preferred_element_type=jnp.float32,
     )
     decoded = lax.psum(partial_value, "heads").astype(jnp.bfloat16)
 

time: 317 us -> 267 us (0.84)
  the two profiles are of different devices: /device:TPU:18 before, /device:TPU:0 now
where the time goes in v2:
time: 267 us
  blocking collectives  110 us (41%)
  matrix products  38.9 us (15%)
  local copies, waits for them, and re-layouts  36.1 us (14%)
  waiting for transfers between devices  33.8 us (13%)
  other arithmetic  25.3 us (9%)
  between operations  15.9 us (6%)
  starting transfers between devices  6.43 us (2%)
    all_gather x1, blocking collectives, shards(): lax.all_gather(new_output, 'ctx', axis=0, tiled=True)  66.3 us
    unnamed x1, blocking collectives  39.2 us
    ppermute x4, waiting for transfers between devices, send(): lax.ppermute(value.astype(jnp.bfloat16), 'ctx', pairs).astype(jnp.float32)  33.8 us
    dot_general x2, matrix products, block_terms(): jnp.einsum('gkts,sgkp->tgkp', mixing, inputs_head, preferred_element_type...  13.3 us
    slice x3, local copies, waits for them, and re-layouts, shards(): ssm_input[request]  10.5 us
    dot_general x2, matrix products, finish(): carried = jnp.einsum('tgn,gkpn->tgkp', c_groups, entering, precision=HIGH)  10.5 us
    convert_element_type x4, other arithmetic, send(): value.astype(jnp.bfloat16)  9.62 us
    convert_element_type x2, local copies, waits for them, and re-layouts, finish(): return (local_out + carried + skipped).reshape(block_size, group_count *...  8.55 us
  transfers between devices with their start and end apart: 5, of which 3 were waited for; matrix products, arithmetic and copies ran while one was open for 17% of the time, Pallas kernels for 0%

profile of v2, /device:TPU:0, one launch (start us, length us, event | category | flops | bytes accessed | tf_op | source)
XLA Modules:
  0.0 266.5 jit_solution(17520741777906803276)
XLA Ops:
  11.9 1.2 dynamic-slice
  14.2 39.2 %all-reduce = f32[9224]{0:T(1024)S(1)} all-reduce(f32[9224]{0:T(1024)S(1)} %dynamic-update-slice), channel_id=2, replica_groups=mesh['groups'=2,'ctx'=8,'heads'=2] {'ctx'}, use_global_device_ids=true, to_apply=%add | all-reduce | flops 9224 | bytes 73792
  54.5 1.6 bitcast_multiply_fusion.3
  56.1 3.9 %fusion.75 = (bf16[1,256,4096]{2,1,0:T(8,128)(2,1)}, bf16[1,256,4096]{2,1,0:T(8,128)(2,1)S(1)}) fusion(bf16[2,256,4096]{2,1,0:T(8,128)(2,1)} %param.13), kind=kLoop, calls=%fused_computation.128 | loop fusion | bytes 8388608 | tf_op jit(solution)/shard_map/slice | solution.py:139
  60.0 4.1 %copy.144 = bf16[1,256,4096]{1,2,0:T(8,128)(2,1)} copy(bf16[1,256,4096]{2,1,0:T(8,128)(2,1)} %get-tuple-element.24) | data formatting | bytes 4194304 | tf_op jit(solution)/shard_map/slice | solution.py:139
  64.3 2.5 copy.149
  66.9 2.5 fusion.53
  71.4 2.0 fusion.43
  73.4 2.1 add_bitcast_fusion
  76.9 3.0 %select_convert_fusion.1 = bf16[2,2,32,32,128]{4,3,2,1,0:T(8,128)(2,1)} fusion(pred[]{:T(512)S(6)} %eq.15, f32[1,2,32,64,128]{4,3,2,1,0:T(8,128)} %copy-done.1, f32[1,2,32,64,128]{4,3,2,1,0:T(8,128)S(1)} %fusion.53), kind=kLoop, calls=%fused_computation.71 | loop fusion | flops 1572864 | bytes 5242881 | tf_op jit(solution)/shard_map/convert_element_type | solution.py:74
  80.9 1.6 fusion.76
  85.4 1.2 fusion.81
  87.8 12.8 %collective-permute-done = bf16[2,2,32,32,128]{4,3,2,1,0:T(8,128)(2,1)S(1)} collective-permute-done((bf16[2,2,32,32,128]{4,3,2,1,0:T(8,128)(2,1)}, bf16[2,2,32,32,128]{4,3,2,1,0:T(8,128)(2,1)S(1)}, u32[]{:S(2)}, u32[]{:S(2)}) %collective-permute-start) | collective-permute-done | bytes 1048608 | tf_op jit(solution)/shard_map/ppermute | solution.py:74
  100.6 2.1 fusion.60
  102.7 1.4 collective-permute-start.1
  104.1 6.6 %fusion = f32[2,32,256,64]{2,3,1,0:T(8,128)} fusion(bf16[256,2,32,64]{0,3,2,1:T(8,128)(2,1)S(1)} %bitcast.147, f32[2,32,256]{2,1,0:T(8,128)S(1)} %bitcast.169, f32[2,32,256]{2,1,0:T(8,128)S(1)} %copy-done.21, f32[2,256,256]{2,1,0:T(8,128)S(1)} %fusion.81, pred[256,256]{1,0:T(8,128)(4,1)S(1)} %iota_compare_fusion), kind=kOutput, calls=%fused_computation.2 | convolution fusion | flops 562036736 | bytes 7012352 | tf_op jit(solution)/shard_map/gkts,sgkp->tgkp/dot_general | solution.py:35
  110.7 10.2 %collective-permute-done.1 = bf16[2,2,32,32,128]{4,3,2,1,0:T(8,128)(2,1)S(1)} collective-permute-done((bf16[2,2,32,32,128]{4,3,2,1,0:T(8,128)(2,1)S(1)}, bf16[2,2,32,32,128]{4,3,2,1,0:T(8,128)(2,1)S(1)}, u32[]{:S(2)}, u32[]{:S(2)}) %collective-permute-start.1) | collective-permute-done | bytes 1048608 | tf_op jit(solution)/shard_map/ppermute | solution.py:74
  120.9 1.7 fusion.29
  122.6 4.4 %collective-permute-start.2 = (bf16[2,2,32,32,128]{4,3,2,1,0:T(8,128)(2,1)}, bf16[2,2,32,32,128]{4,3,2,1,0:T(8,128)(2,1)}, u32[]{:S(2)}, u32[]{:S(2)}) collective-permute-start(bf16[2,2,32,32,128]{4,3,2,1,0:T(8,128)(2,1)} %fusion.29), channel_id=1, source_target_pairs={{0,8},{4,12},{2,10},{6,14},{1,9},{5,13},{3,11},{7,15},{16,24},{20,... | collective-permute-start | bytes 3145736 | tf_op jit(solution)/shard_map/ppermute | solution.py:74
  127.1 6.6 %fusion.1 = f32[2,32,256,64]{2,3,1,0:T(8,128)} fusion(bf16[256,2,32,64]{0,3,2,1:T(8,128)(2,1)S(1)} %bitcast.150, f32[2,32,256]{2,1,0:T(8,128)S(1)} %bitcast.168, f32[2,32,256]{2,1,0:T(8,128)S(1)} %copy-done.20, f32[2,256,256]{2,1,0:T(8,128)S(1)} %fusion.82, pred[256,256]{1,0:T(8,128)(4,1)S(1)} %iota_compare_fusion), kind=kOutput, calls=%fused_computation.3 | convolution fusion | flops 562036736 | bytes 7012352 | tf_op jit(solution)/shard_map/gkts,sgkp->tgkp/dot_general | solution.py:35
  136.5 10.7 %collective-permute-done.2 = bf16[2,2,32,32,128]{4,3,2,1,0:T(8,128)(2,1)} collective-permute-done((bf16[2,2,32,32,128]{4,3,2,1,0:T(8,128)(2,1)}, bf16[2,2,32,32,128]{4,3,2,1,0:T(8,128)(2,1)}, u32[]{:S(2)}, u32[]{:S(2)}) %collective-permute-start.2) | collective-permute-done | bytes 1048608 | tf_op jit(solution)/shard_map/ppermute | solution.py:74
  147.2 2.9 %select_convert_fusion = bf16[2,2,32,32,128]{4,3,2,1,0:T(8,128)(2,1)} fusion(bf16[2,2,32,32,128]{4,3,2,1,0:T(8,128)(2,1)} %copy-done.11, bf16[2,2,32,32,128]{4,3,2,1,0:T(8,128)(2,1)} %collective-permute-done.2, f32[2,2,32]{2,1,0:T(2,128)S(1)} %exp.110, f32[2,2,32]{2,1,0:T(2,128)S(1)} %exp.108, f32[2,2,32]{2,1,0:T(2,128)S(1)} %exp.100, pred[]{:T(512)S(6)} %eq.15, ...), kind=kLoop, calls=%fused_computation.68 | loop fusion | flops 5767168 | bytes 6292993 | tf_op jit(solution)/shard_map/convert_element_type | solution.py:74
  155.5 66.3 %all_gather.11 = bf16[8,4,4096]{2,1,0:T(4,128)(2,1)S(1)} all-gather(bf16[1,4,4096]{2,1,0:T(4,128)(2,1)} %convert_element_type.160), channel_id=1, replica_groups=mesh['groups'=2,'ctx'=8,'heads'=2] {'ctx'}, dimensions={0}, use_global_device_ids=true | all-gather | bytes 294912 | tf_op jit(solution)/shard_map/all_gather | solution.py:206
  221.8 5.5 %fusion.2 = f32[8,4,1024]{2,0,1:T(8,128)} fusion(bf16[4096,1024]{1,0:T(8,128)(2,1)} %param.25, bf16[8,4,4096]{2,1,0:T(4,128)(2,1)S(1)} %all_gather.11), kind=kOutput, calls=%fused_computation.4 | convolution fusion | flops 268435456 | bytes 8781824 | tf_op jit(solution)/shard_map/jup,pd->jud/dot_general | solution.py:204
  227.3 4.5 %all-reduce.2 = bf16[8,4,1024]{2,0,1:T(8,128)(2,1)S(1)} all-reduce(f32[8,4,1024]{2,0,1:T(8,128)} %fusion.2), channel_id=1, replica_groups=mesh['groups'=2,'ctx'=8,'heads'=2] {'heads'}, use_global_device_ids=true, to_apply=%region_13.14 | all-reduce | flops 32768 | bytes 196608 | tf_op jit(solution)/shard_map/psum | solution.py:210
  232.6 2.6 convert_select_fusion.1
  235.3 1.4 copy-done.13
  236.6 3.8 %fusion.18 = bf16[256,2,32,64]{0,3,2,1:T(8,128)(2,1)} fusion(bf16[256,2,32,64]{0,3,2,1:T(8,128)(2,1)S(1)} %bitcast.148, f32[2,32,256,64]{2,3,1,0:T(8,128)S(1)} %copy-done.13, bf16[256,2,128,1]{0,2,3,1:T(8,128)(2,1)S(1)} %bitcast.155, f32[2,2,32,32,128]{4,3,2,1,0:T(8,128)S(1)} %get-tuple-element.20, f32[2,2,32,32,128]{4,3,2,1,0:T(8,128)S(1)} %get-tuple-element.21, ...), kind=kOutput, calls=%fused_computation.29 | convolution fusion | flops 1617428480 | bytes 12779776 | tf_op jit(solution)/shard_map/tgn,gkpn->tgkp/dot_general | solution.py:52
  240.4 4.3 %copy.158 = bf16[1,256,4096]{2,1,0:T(8,128)(2,1)} copy(bf16[1,256,4096]{1,2,0:T(8,128)(2,1)} %bitcast.153) | data formatting | bytes 4194304 | tf_op jit(solution)/shard_map/convert_element_type | solution.py:59
  244.7 6.7 %fusion.21 = bf16[256,2,32,64]{0,3,2,1:T(8,128)(2,1)} fusion(bf16[256,2,32,64]{0,3,2,1:T(8,128)(2,1)S(1)} %bitcast.151, f32[2,32,256,64]{2,3,1,0:T(8,128)} %fusion.1, bf16[256,2,128,1]{0,2,3,1:T(8,128)(2,1)S(1)} %bitcast.157, f32[2,2,32,32,128]{4,3,2,1,0:T(8,128)} %copy-done.10, f32[2,2,32,32,128]{4,3,2,1,0:T(8,128)} %copy-done.9, ...), kind=kOutput, calls=%fused_computation.32 | convolution fusion | flops 1617428480 | bytes 12779776 | tf_op jit(solution)/shard_map/tgn,gkpn->tgkp/dot_general | solution.py:52
  251.4 4.3 %copy.159 = bf16[1,256,4096]{2,1,0:T(8,128)(2,1)} copy(bf16[1,256,4096]{1,2,0:T(8,128)(2,1)} %bitcast.152) | data formatting | bytes 4194304 | tf_op jit(solution)/shard_map/convert_element_type | solution.py:59
  255.7 4.0 %pad_maximum_fusion.1 = bf16[2,256,4096]{2,1,0:T(8,128)(2,1)} fusion(bf16[1,256,4096]{2,1,0:T(8,128)(2,1)} %copy.159, bf16[1,256,4096]{2,1,0:T(8,128)(2,1)S(1)} %copy-done.12), kind=kLoop, calls=%fused_computation.36 | loop fusion | flops 2097152 | bytes 8388608 | tf_op jit(solution)/shard_map/stack | solution.py:225
  (144 shorter events, 22.9 us)
Async XLA Ops:
  7.2 126.5 %copy-start = (bf16[1,4,256]{2,1,0:T(4,128)(2,1)S(1)}, bf16[1,4,256]{2,1,0:T(4,128)(2,1)}, u32[]{:S(2)}) copy-start(bf16[1,4,256]{2,1,0:T(4,128)(2,1)} %param.21) | copy-start | bytes 6148
  7.2 146.5 %reduce-scatter.2.cloned.1.call-start = ((), (), s32[]{:S(2)}) async-start(), calls=%async_computation.1 | async-start | bytes 1179648 | tf_op jit(solution)/shard_map/reduce_scatter | solution.py:179
  60.0 4.1 %copy-start.18 = (bf16[2,256,256]{2,1,0:T(8,128)(2,1)S(1)}, bf16[2,256,256]{2,1,0:T(8,128)(2,1)}, u32[]{:S(2)}) copy-start(bf16[2,256,256]{2,1,0:T(8,128)(2,1)} %param.14) | copy-start | bytes 786436
  64.3 2.6 copy-start.14
  79.9 20.7 %collective-permute-start = (bf16[2,2,32,32,128]{4,3,2,1,0:T(8,128)(2,1)}, bf16[2,2,32,32,128]{4,3,2,1,0:T(8,128)(2,1)S(1)}, u32[]{:S(2)}, u32[]{:S(2)}) collective-permute-start(bf16[2,2,32,32,128]{4,3,2,1,0:T(8,128)(2,1)} %select_convert_fusion.1), channel_id=1, source_target_pairs={{0,2},{4,6},{8,10},{12,14},{2,0},{6,4},{10,8},{14,12},{1,3},{5,7},... | collective-permute-start | bytes 3145736 | tf_op jit(solution)/shard_map/ppermute | solution.py:74
  87.7 16.3 %copy-start.4 = (bf16[1,256,4096]{1,2,0:T(8,128)(2,1)S(1)}, bf16[1,256,4096]{1,2,0:T(8,128)(2,1)}, u32[]{:S(2)}) copy-start(bf16[1,256,4096]{1,2,0:T(8,128)(2,1)} %copy.144) | copy-start | bytes 6291460
  87.7 16.3 %copy-start.21 = (f32[2,32,256]{2,1,0:T(8,128)S(1)}, f32[2,32,256]{2,1,0:T(8,128)}, u32[]{:S(2)}) copy-start(f32[2,32,256]{2,1,0:T(8,128)} %reduce_window_sum.61) | copy-start | bytes 196612
  102.7 18.2 %copy-start.2 = (f32[2,2,32,32,128]{4,3,2,1,0:T(8,128)}, f32[2,2,32,32,128]{4,3,2,1,0:T(8,128)S(1)}, u32[]{:S(2)}) copy-start(f32[2,2,32,32,128]{4,3,2,1,0:T(8,128)S(1)} %get-tuple-element.19) | copy-start | bytes 6291460
  102.7 18.2 %collective-permute-start.1 = (bf16[2,2,32,32,128]{4,3,2,1,0:T(8,128)(2,1)S(1)}, bf16[2,2,32,32,128]{4,3,2,1,0:T(8,128)(2,1)S(1)}, u32[]{:S(2)}, u32[]{:S(2)}) collective-permute-start(bf16[2,2,32,32,128]{4,3,2,1,0:T(8,128)(2,1)S(1)} %get-tuple-element.18), channel_id=1, source_target_pairs={{0,4},{4,8},{8,12},{2,6},{6,10},{10,14},{1,5},{5,9},{9,13},{3,7},{... | collective-permute-start | bytes 3145736 | tf_op jit(solution)/shard_map/ppermute | solution.py:74
  120.9 6.1 %copy-start.7 = (bf16[1,256,4096]{1,2,0:T(8,128)(2,1)S(1)}, bf16[1,256,4096]{1,2,0:T(8,128)(2,1)}, u32[]{:S(2)}) copy-start(bf16[1,256,4096]{1,2,0:T(8,128)(2,1)} %copy.149) | copy-start | bytes 6291460
  120.9 6.1 %copy-start.20 = (f32[2,32,256]{2,1,0:T(8,128)S(1)}, f32[2,32,256]{2,1,0:T(8,128)}, u32[]{:S(2)}) copy-start(f32[2,32,256]{2,1,0:T(8,128)} %reduce_window_sum.65) | copy-start | bytes 196612
  122.6 24.6 %collective-permute-start.2 = (bf16[2,2,32,32,128]{4,3,2,1,0:T(8,128)(2,1)}, bf16[2,2,32,32,128]{4,3,2,1,0:T(8,128)(2,1)}, u32[]{:S(2)}, u32[]{:S(2)}) collective-permute-start(bf16[2,2,32,32,128]{4,3,2,1,0:T(8,128)(2,1)} %fusion.29), channel_id=1, source_target_pairs={{0,8},{4,12},{2,10},{6,14},{1,9},{5,13},{3,11},{7,15},{16,24},{20,... | collective-permute-start | bytes 3145736 | tf_op jit(solution)/shard_map/ppermute | solution.py:74
  127.0 6.7 %copy-start.24 = (bf16[1,4,256]{2,1,0:T(4,128)(2,1)S(1)}, bf16[1,4,256]{2,1,0:T(4,128)(2,1)}, u32[]{:S(2)}) copy-start(bf16[1,4,256]{2,1,0:T(4,128)(2,1)} %param.22) | copy-start | bytes 6148
  127.0 7.3 %copy-start.25 = (f32[1,4,64]{2,1,0:T(4,128)S(1)}, f32[1,4,64]{2,1,0:T(4,128)}, u32[]{:S(2)}) copy-start(f32[1,4,64]{2,1,0:T(4,128)} %param.24) | copy-start | bytes 3076
  127.0 7.5 %copy-start.26 = (f32[1,4,64]{2,1,0:T(4,128)S(1)}, f32[1,4,64]{2,1,0:T(4,128)}, u32[]{:S(2)}) copy-start(f32[1,4,64]{2,1,0:T(4,128)} %param.23) | copy-start | bytes 3076
  127.0 7.6 %copy-start.19 = (bf16[1,4,4096]{2,1,0:T(4,128)(2,1)S(1)}, bf16[1,4,4096]{2,1,0:T(4,128)(2,1)}, u32[]{:S(2)}) copy-start(bf16[1,4,4096]{2,1,0:T(4,128)(2,1)} %param.20) | copy-start | bytes 98308
  127.0 8.4 %copy-start.29 = (f32[128]{0:T(128)S(1)}, f32[128]{0:T(128)}, u32[]{:S(2)}) copy-start(f32[128]{0:T(128)} %get-tuple-element.17) | copy-start | bytes 1540
  127.0 8.4 %copy-start.28 = (f32[128]{0:T(128)S(1)}, f32[128]{0:T(128)}, u32[]{:S(2)}) copy-start(f32[128]{0:T(128)} %get-tuple-element.15) | copy-start | bytes 1540
  127.0 8.5 %copy-start.27 = (f32[128]{0:T(128)S(1)}, f32[128]{0:T(128)}, u32[]{:S(2)}) copy-start(f32[128]{0:T(128)} %get-tuple-element.16) | copy-start | bytes 1540
  127.1 20.2 %copy-start.3 = (f32[2,2,32,32,128]{4,3,2,1,0:T(8,128)S(1)}, f32[2,2,32,32,128]{4,3,2,1,0:T(8,128)}, u32[]{:S(2)}) copy-start(f32[2,2,32,32,128]{4,3,2,1,0:T(8,128)} %copy-done.2) | copy-start | bytes 6291460
  136.4 14.3 %copy-start.16 = (f32[4,2,32,64]{3,2,1,0:T(8,128)S(1)}, f32[4,2,32,64]{3,2,1,0:T(8,128)}, u32[]{:S(2)}) copy-start(f32[4,2,32,64]{3,2,1,0:T(8,128)} %reshape.314) | copy-start | bytes 196612
  136.5 16.5 %copy-start.30 = (f32[64]{0:T(128)S(1)}, f32[64]{0:T(128)}, u32[]{:S(2)}) copy-start(f32[64]{0:T(128)} %param.18) | copy-start | bytes 772
  150.1 82.4 %collective-permute-start.3 = (bf16[2,2,32,32,128]{4,3,2,1,0:T(8,128)(2,1)}, bf16[2,2,32,32,128]{4,3,2,1,0:T(8,128)(2,1)}, u32[]{:S(2)}, u32[]{:S(2)}) collective-permute-start(bf16[2,2,32,32,128]{4,3,2,1,0:T(8,128)(2,1)} %select_convert_fusion), channel_id=1, source_target_pairs={{0,2},{4,6},{8,10},{12,14},{2,0},{6,4},{10,8},{14,12},{1,3},{5,7},... | collective-permute-start | bytes 3145736 | tf_op jit(solution)/shard_map/ppermute | solution.py:74
  232.5 2.7 %copy-start.5 = (bf16[1,256,4096]{1,2,0:T(8,128)(2,1)S(1)}, bf16[1,256,4096]{1,2,0:T(8,128)(2,1)}, u32[]{:S(2)}) copy-start(bf16[1,256,4096]{1,2,0:T(8,128)(2,1)} %copy.144) | copy-start | bytes 6291460
  232.5 2.7 %copy-start.17 = (f32[64,256]{1,0:T(8,128)S(1)}, f32[64,256]{1,0:T(8,128)}, u32[]{:S(2)}) copy-start(f32[64,256]{1,0:T(8,128)} %get-tuple-element.37) | copy-start | bytes 196612
  232.5 2.7 %copy-start.22 = (f32[2,32]{1,0:T(2,128)S(1)}, f32[2,32]{1,0:T(2,128)}, u32[]{:S(2)}) copy-start(f32[2,32]{1,0:T(2,128)} %mul.269) | copy-start | bytes 772
  232.6 4.1 %copy-start.13 = (f32[2,32,256,64]{2,3,1,0:T(8,128)S(1)}, f32[2,32,256,64]{2,3,1,0:T(8,128)}, u32[]{:S(2)}) copy-start(f32[2,32,256,64]{2,3,1,0:T(8,128)} %fusion) | copy-start | bytes 12582916
  235.2 5.2 %copy-start.9 = (f32[2,2,32,32,128]{4,3,2,1,0:T(8,128)}, f32[2,2,32,32,128]{4,3,2,1,0:T(8,128)S(1)}, u32[]{:S(2)}) copy-start(f32[2,2,32,32,128]{4,3,2,1,0:T(8,128)S(1)} %get-tuple-element.20) | copy-start | bytes 6291460
  235.2 5.2 %copy-start.10 = (f32[2,2,32,32,128]{4,3,2,1,0:T(8,128)}, f32[2,2,32,32,128]{4,3,2,1,0:T(8,128)S(1)}, u32[]{:S(2)}) copy-start(f32[2,2,32,32,128]{4,3,2,1,0:T(8,128)S(1)} %get-tuple-element.21) | copy-start | bytes 6291460
  240.4 4.3 %copy-start.8 = (bf16[1,256,4096]{1,2,0:T(8,128)(2,1)S(1)}, bf16[1,256,4096]{1,2,0:T(8,128)(2,1)}, u32[]{:S(2)}) copy-start(bf16[1,256,4096]{1,2,0:T(8,128)(2,1)} %copy.149) | copy-start | bytes 6291460
  240.4 4.3 %copy-start.23 = (f32[2,32]{1,0:T(2,128)S(1)}, f32[2,32]{1,0:T(2,128)}, u32[]{:S(2)}) copy-start(f32[2,32]{1,0:T(2,128)} %mul.269) | copy-start | bytes 772
  251.4 4.3 %copy-start.12 = (bf16[1,256,4096]{2,1,0:T(8,128)(2,1)S(1)}, bf16[1,256,4096]{2,1,0:T(8,128)(2,1)}, u32[]{:S(2)}) copy-start(bf16[1,256,4096]{2,1,0:T(8,128)(2,1)} %copy.158) | copy-start | bytes 6291460
  (4 other events, 8.0 us)
Sparse Core Ops, SparseCore 0:
  77.0 75.1 reduce-scatter.1

commit v3 on v2

--- a/solution.py
+++ b/solution.py
@@ -70,44 +70,63 @@
     return factor[..., None, None] * state
 
 
-def send(value, pairs):
-    return lax.ppermute(value.astype(jnp.bfloat16), "ctx", pairs).astype(jnp.float32)
-
-
-def prefix_states(states, all_totals):
+def send(value, total, pairs):
+    state, total = lax.ppermute((value.astype(jnp.bfloat16), total), "ctx", pairs)
+    return state.astype(jnp.float32), total
+
+
+def gather_ctx(value):
+    count = lax.axis_size("ctx")
+    if count & (count - 1):
+        return lax.all_gather(value, "ctx", axis=0, tiled=True)
+    place = lax.axis_index("ctx")
+    reach = 1
+    while reach < count:
+        got = lax.ppermute(value, "ctx", [(i, i ^ reach) for i in range(count)])
+        upper = (place & reach) != 0
+        value = jnp.where(
+            upper, jnp.concatenate([got, value], axis=0), jnp.concatenate([value, got], axis=0)
+        )
+        reach *= 2
+    return value
+
+
+def prefix_states(states, totals):
     count = lax.axis_size("ctx")
     columns = count // 2
     place = lax.axis_index("ctx")
-    row = place % 2
-    column = place // 2
+    row_zero = place % 2 == 0
     half = states.shape[-2] // 2
     first = states[..., :half, :]
     second = states[..., half:, :]
-    row_zero = row == 0
     mine = jnp.where(row_zero, first, second)
     other = jnp.where(row_zero, second, first)
     across = [(2 * m, 2 * m + 1) for m in range(columns)] + [
         (2 * m + 1, 2 * m) for m in range(columns)
     ]
-    received = send(other, across)
+    received, partner_total = send(other, totals, across)
     even_state = jnp.where(row_zero, mine, received)
     odd_state = jnp.where(row_zero, received, mine)
-    odd_decay = range_decay(all_totals, 2 * column + 1, 2 * column + 1)
-    window = scale(odd_decay, even_state) + odd_state
+    even_total = jnp.where(row_zero, totals, partner_total)
+    odd_total = jnp.where(row_zero, partner_total, totals)
+    window = scale(jnp.exp(odd_total), even_state) + odd_state
+    window_total = even_total + odd_total
     before = jnp.zeros_like(window)
+    before_total = jnp.zeros_like(totals)
     step = 1
     while step < columns:
         pairs = [(y + 2 * m, y + 2 * (m + step)) for y in range(2) for m in range(columns - step)]
-        got = send(window, pairs)
-        low = 2 * (column - step) + 2
-        before = scale(range_decay(all_totals, low, 2 * column - 1), got) + before
+        got, got_total = send(window, window_total, pairs)
+        new_before = scale(jnp.exp(before_total), got) + before
         if 2 * step < columns:
-            window = scale(range_decay(all_totals, low, 2 * column + 1), got) + window
+            window = scale(jnp.exp(window_total), got) + window
+            window_total = got_total + window_total
+        before = new_before
+        before_total = got_total + before_total
         step *= 2
-    even_decay = range_decay(all_totals, 2 * column, 2 * column)
-    odd_entering = scale(even_decay, before) + even_state
+    odd_entering = scale(jnp.exp(even_total), before) + even_state
     outgoing = jnp.where(row_zero, odd_entering, before)
-    partner = send(outgoing, across)
+    partner, _ = send(outgoing, totals, across)
     own_half = jnp.where(row_zero, before, odd_entering)
     first_half = jnp.where(row_zero, own_half, partner)
     second_half = jnp.where(row_zero, partner, own_half)
@@ -150,7 +169,7 @@
     slots, steps = new_input.shape[0], new_input.shape[1]
     pieces = [totals, request_of_slot.astype(jnp.float32), new_c.astype(jnp.float32)]
     packed = jnp.concatenate([piece.reshape(-1) for piece in pieces])
-    gathered = lax.all_gather(packed, "ctx")
+    gathered = gather_ctx(packed[None])
     unpacked = []
     offset = 0
     for piece in pieces:
@@ -203,13 +222,13 @@
     new_output = value.reshape(slots, steps, -1).astype(jnp.bfloat16)
     partial_value = jnp.einsum(
         "jup,pd->jud",
-        lax.all_gather(new_output, "ctx", axis=0, tiled=True),
+        gather_ctx(new_output),
         out_weight,
         preferred_element_type=jnp.float32,
     )
     decoded = lax.psum(partial_value, "heads").astype(jnp.bfloat16)
 
-    entering = prefix_states(states, all_totals)
+    entering = prefix_states(states, totals)
     prefill_rows = []
     for request in range(request_count):
         prefill_rows.append(

time: 267 us -> 261 us (0.978)
  the two profiles are of different devices: /device:TPU:0 before, /device:TPU:24 now
where the time goes in v3:
time: 261 us; the launch traced here: 260 us
  waiting for transfers between devices  111 us (43%)
  matrix products  40.2 us (15%)
  local copies, waits for them, and re-layouts  39.3 us (15%)
  other arithmetic  33.6 us (13%)
  starting transfers between devices  16.4 us (6%)
  between operations  15.3 us (6%)
  blocking collectives  4.52 us (2%)
    ppermute x6, waiting for transfers between devices, send(): lax.ppermute((value.astype(jnp.bfloat16), total), 'ctx', pairs)  53.5 us
    reduce_scatter x1, waiting for transfers between devices, shards(): lax.psum_scatter(contribution, 'ctx', scatter_dimension=0, tiled=True)  51.6 us
    dot_general x2, matrix products, block_terms(): jnp.einsum('gkts,sgkp->tgkp', mixing, inputs_head, preferred_element_type...  15.6 us
    dot_general x2, matrix products, finish(): carried = jnp.einsum('tgn,gkpn->tgkp', c_groups, entering, precision=HIGH)  10.7 us
    slice x3, local copies, waits for them, and re-layouts, shards(): ssm_input[request]  10.6 us
    convert_element_type x4, other arithmetic, send(): value.astype(jnp.bfloat16)  9.95 us
    ppermute x6, starting transfers between devices, send(): lax.ppermute((value.astype(jnp.bfloat16), total), 'ctx', pairs)  8.66 us
    convert_element_type x2, local copies, waits for them, and re-layouts, finish(): return (local_out + carried + skipped).reshape(block_size, group_count *...  8.57 us
  transfers between devices with their start and end apart: 13, of which 6 were waited for; matrix products, arithmetic and copies ran while one was open for 32% of the time, Pallas kernels for 0%

profile of v3, /device:TPU:24, one launch (start us, length us, event | category | flops | bytes accessed | tf_op | source)
XLA Modules:
  0.0 260.0 jit_solution(7195355639967988058)
XLA Ops:
  15.8 1.6 bitcast_multiply_fusion.3
  17.4 3.9 %fusion.80 = (bf16[1,256,4096]{2,1,0:T(8,128)(2,1)}, bf16[1,256,4096]{2,1,0:T(8,128)(2,1)S(1)}) fusion(bf16[2,256,4096]{2,1,0:T(8,128)(2,1)} %param.13), kind=kLoop, calls=%fused_computation.131 | loop fusion | bytes 8388608 | tf_op jit(solution)/shard_map/slice | solution.py:158
  21.4 4.2 %copy.144 = bf16[1,256,4096]{1,2,0:T(8,128)(2,1)} copy(bf16[1,256,4096]{2,1,0:T(8,128)(2,1)} %get-tuple-element.20) | data formatting | bytes 4194304 | tf_op jit(solution)/shard_map/slice | solution.py:158
  25.7 2.5 copy.149
  28.3 2.5 fusion.52
  31.6 1.7 select_convert_fusion.1
  33.3 1.5 collective-permute-start.2
  37.6 1.6 fusion.81
  41.5 2.0 fusion.87
  43.5 7.8 %fusion = f32[2,32,256,64]{2,3,1,0:T(8,128)} fusion(bf16[256,2,32,64]{0,3,2,1:T(8,128)(2,1)} %bitcast.146, f32[2,32,256]{2,1,0:T(8,128)} %bitcast.170, f32[2,32,256]{2,1,0:T(8,128)} %reduce_window_sum.61, f32[2,256,256]{2,1,0:T(8,128)S(1)} %fusion.86, pred[256,256]{1,0:T(8,128)(4,1)} %iota_compare_fusion), kind=kOutput, calls=%fused_computation.2 | convolution fusion | flops 562036736 | bytes 7012352 | tf_op jit(solution)/shard_map/gkts,sgkp->tgkp/dot_general | solution.py:35
  54.6 2.2 collective-permute-done.7
  60.6 2.6 %collective-permute-done.8 = f32[4,1153]{1,0:T(4,128)} collective-permute-done((f32[4,1153]{1,0:T(4,128)}, f32[4,1153]{1,0:T(4,128)}, u32[]{:S(2)}, u32[]{:S(2)}) %collective-permute-start.8) | collective-permute-done | bytes 18480 | tf_op jit(solution)/shard_map/ppermute | solution.py:85
  67.5 2.3 fusion.26
  69.9 2.0 fusion.42
  71.9 2.1 add_bitcast_fusion
  82.4 3.8 %fusion.59 = (bf16[2,2,32,32,128]{4,3,2,1,0:T(8,128)(2,1)}, f32[2,2,32,32,128]{4,3,2,1,0:T(8,128)}) fusion(bf16[2,2,32,32,128]{4,3,2,1,0:T(8,128)(2,1)S(1)} %collective-permute-done.2, pred[]{:T(512)S(6)} %eq.15, f32[2,2,32]{2,1,0:T(2,128)S(1)} %get-tuple-element.35, f32[1,2,32,64,128]{4,3,2,1,0:T(8,128)} %copy-done.2, f32[1,2,32,64,128]{4,3,2,1,0:T(8,128)S(1)} %fusion.52), kind=kLoop, calls=%fused_computation.81 | loop fusion | flops 4718592 | bytes 8389121 | tf_op jit(solution)/shard_map/convert_element_type | solution.py:74
  87.8 51.6 %reduce-scatter.2.cloned.1.call-done = f32[1,4,2,32,64]{4,3,2,1,0:T(8,128)} async-done(((f32[8,4,2,32,64]{4,3,2,1,0:T(8,128)}), f32[1,4,2,32,64]{4,3,2,1,0:T(8,128)}) %reduce-scatter.2.cloned.1.call-update) | async-done | bytes 65552 | tf_op jit(solution)/shard_map/reduce_scatter | solution.py:198
  144.6 1.9 collective-permute-start.10
  146.5 2.7 %fusion.29 = bf16[2,2,32,32,128]{4,3,2,1,0:T(8,128)(2,1)S(1)} fusion(bf16[2,2,32,32,128]{4,3,2,1,0:T(8,128)(2,1)S(1)} %collective-permute-done.3, f32[2,2,32]{2,1,0:T(2,128)} %get-tuple-element.36, f32[2,2,32,32,128]{4,3,2,1,0:T(8,128)} %get-tuple-element.15, bf16[2,2,32,32,128]{4,3,2,1,0:T(8,128)(2,1)S(1)} %collective-permute-done.2, pred[]{:T(512)S(6)} %eq.15, ...), kind=kLoop, calls=%fused_computation.52 | loop fusion | flops 4718592 | bytes 5243905 | tf_op jit(solution)/shard_map/convert_element_type | solution.py:74
  150.7 7.8 %fusion.1 = f32[2,32,256,64]{2,3,1,0:T(8,128)} fusion(bf16[256,2,32,64]{0,3,2,1:T(8,128)(2,1)S(1)} %bitcast.150, f32[2,32,256]{2,1,0:T(8,128)} %bitcast.169, f32[2,32,256]{2,1,0:T(8,128)S(1)} %copy-done.24, f32[2,256,256]{2,1,0:T(8,128)} %fusion.87, pred[256,256]{1,0:T(8,128)(4,1)} %iota_compare_fusion), kind=kOutput, calls=%fused_computation.3 | convolution fusion | flops 562036736 | bytes 7012352 | tf_op jit(solution)/shard_map/gkts,sgkp->tgkp/dot_general | solution.py:35
  158.7 3.7 %collective-permute-start.11 = (bf16[4,4,4096]{2,1,0:T(4,128)(2,1)S(1)}, bf16[4,4,4096]{2,1,0:T(4,128)(2,1)S(1)}, u32[]{:S(2)}, u32[]{:S(2)}) collective-permute-start(bf16[4,4,4096]{2,1,0:T(4,128)(2,1)S(1)} %maximum_select_fusion.1), channel_id=1, source_target_pairs={{0,8},{2,10},{4,12},{6,14},{8,0},{10,2},{12,4},{14,6},{1,9},{3,11}... | collective-permute-start | bytes 393224 | tf_op jit(solution)/shard_map/ppermute | solution.py:85
  162.4 37.3 %collective-permute-done.4 = bf16[2,2,32,32,128]{4,3,2,1,0:T(8,128)(2,1)S(1)} collective-permute-done((bf16[2,2,32,32,128]{4,3,2,1,0:T(8,128)(2,1)S(1)}, bf16[2,2,32,32,128]{4,3,2,1,0:T(8,128)(2,1)S(1)}, u32[]{:S(2)}, u32[]{:S(2)}) %collective-permute-start.4) | collective-permute-done | bytes 1048608 | tf_op jit(solution)/shard_map/ppermute | solution.py:74
  199.7 1.8 select_convert_fusion
  203.2 2.1 fusion.2
  205.3 4.5 %all-reduce.1 = bf16[8,4,1024]{2,0,1:T(8,128)(2,1)S(1)} all-reduce(f32[8,4,1024]{2,0,1:T(8,128)} %fusion.2), channel_id=1, replica_groups=mesh['groups'=2,'ctx'=8,'heads'=2] {'heads'}, use_global_device_ids=true, to_apply=%region_8.9 | all-reduce | flops 32768 | bytes 196608 | tf_op jit(solution)/shard_map/psum | solution.py:229
  210.5 16.2 %collective-permute-done.5 = bf16[2,2,32,32,128]{4,3,2,1,0:T(8,128)(2,1)} collective-permute-done((bf16[2,2,32,32,128]{4,3,2,1,0:T(8,128)(2,1)}, bf16[2,2,32,32,128]{4,3,2,1,0:T(8,128)(2,1)}, u32[]{:S(2)}, u32[]{:S(2)}) %collective-permute-start.5) | collective-permute-done | bytes 1048608 | tf_op jit(solution)/shard_map/ppermute | solution.py:74
  226.7 3.0 %convert_select_fusion.1 = (f32[2,2,32,32,128]{4,3,2,1,0:T(8,128)S(1)}, f32[2,2,32,32,128]{4,3,2,1,0:T(8,128)S(1)}) fusion(bf16[2,2,32,32,128]{4,3,2,1,0:T(8,128)(2,1)} %collective-permute-done.5, pred[]{:T(512)S(6)} %eq.15, f32[2,2,32,32,128]{4,3,2,1,0:T(8,128)S(1)} %copy-done.3, bf16[2,2,32,32,128]{4,3,2,1,0:T(8,128)(2,1)S(1)} %collective-permute-done.2, ...), kind=kLoop, calls=%fused_computation.44 | loop fusion | flops 6291456 | bytes 10486785 | tf_op jit(solution)/shard_map/jit(_where)/select_n | solution.py:131
  229.9 3.8 %fusion.18 = bf16[256,2,32,64]{0,3,2,1:T(8,128)(2,1)} fusion(bf16[256,2,32,64]{0,3,2,1:T(8,128)(2,1)S(1)} %bitcast.147, f32[2,32,256,64]{2,3,1,0:T(8,128)S(1)} %copy-done.13, bf16[256,2,128,1]{0,2,3,1:T(8,128)(2,1)S(1)} %bitcast.158, f32[2,2,32,32,128]{4,3,2,1,0:T(8,128)S(1)} %get-tuple-element.16, f32[2,2,32,32,128]{4,3,2,1,0:T(8,128)S(1)} %get-tuple-element.17, ...), kind=kOutput, calls=%fused_computation.29 | convolution fusion | flops 1617428480 | bytes 12779776 | tf_op jit(solution)/shard_map/tgn,gkpn->tgkp/dot_general | solution.py:52
  233.6 4.3 %copy.158 = bf16[1,256,4096]{2,1,0:T(8,128)(2,1)} copy(bf16[1,256,4096]{1,2,0:T(8,128)(2,1)} %bitcast.152) | data formatting | bytes 4194304 | tf_op jit(solution)/shard_map/convert_element_type | solution.py:59
  238.0 6.9 %fusion.21 = bf16[256,2,32,64]{0,3,2,1:T(8,128)(2,1)} fusion(bf16[256,2,32,64]{0,3,2,1:T(8,128)(2,1)} %bitcast.148, f32[2,32,256,64]{2,3,1,0:T(8,128)} %fusion.1, bf16[256,2,128,1]{0,2,3,1:T(8,128)(2,1)S(1)} %bitcast.156, f32[2,2,32,32,128]{4,3,2,1,0:T(8,128)} %copy-done.6, f32[2,2,32,32,128]{4,3,2,1,0:T(8,128)S(1)} %copy-done.5, ...), kind=kOutput, calls=%fused_computation.32 | convolution fusion | flops 1617428480 | bytes 12779776 | tf_op jit(solution)/shard_map/tgn,gkpn->tgkp/dot_general | solution.py:52
  244.9 4.3 %copy.159 = bf16[1,256,4096]{2,1,0:T(8,128)(2,1)} copy(bf16[1,256,4096]{1,2,0:T(8,128)(2,1)} %bitcast.151) | data formatting | bytes 4194304 | tf_op jit(solution)/shard_map/convert_element_type | solution.py:59
  249.1 4.0 %pad_maximum_fusion.1 = bf16[2,256,4096]{2,1,0:T(8,128)(2,1)} fusion(bf16[1,256,4096]{2,1,0:T(8,128)(2,1)} %copy.159, bf16[1,256,4096]{2,1,0:T(8,128)(2,1)S(1)} %copy-done.12), kind=kLoop, calls=%fused_computation.36 | loop fusion | flops 2097152 | bytes 8388608 | tf_op jit(solution)/shard_map/stack | solution.py:244
  (155 shorter events, 44.6 us)
Async XLA Ops:
  7.2 46.1 %copy-start = (bf16[1,4,256]{2,1,0:T(4,128)(2,1)S(1)}, bf16[1,4,256]{2,1,0:T(4,128)(2,1)}, u32[]{:S(2)}) copy-start(bf16[1,4,256]{2,1,0:T(4,128)(2,1)} %param.21) | copy-start | bytes 6148
  7.2 132.2 %reduce-scatter.2.cloned.1.call-start = ((), (), s32[]{:S(2)}) async-start(), calls=%async_computation.1 | async-start | bytes 1179648 | tf_op jit(solution)/shard_map/reduce_scatter | solution.py:198
  9.0 12.4 %copy-start.25 = (f32[64,2]{0,1:T(2,128)}, f32[64,2]{0,1:T(2,128)S(1)}, u32[]{:S(2)}) copy-start(f32[64,2]{0,1:T(2,128)S(1)} %slice.90) | copy-start | bytes 1540
  11.6 69.6 %collective-permute-start = (f32[2,2,32]{2,1,0:T(2,128)}, f32[2,2,32]{2,1,0:T(2,128)}, u32[]{:S(2)}, u32[]{:S(2)}) collective-permute-start(f32[2,2,32]{2,1,0:T(2,128)} %constant_dynamic-update-slice_fusion), channel_id=1, source_target_pairs={{0,2},{4,6},{8,10},{12,14},{2,0},{6,4},{10,8},{14,12},{1,3},{5,7},... | collective-permute-start | bytes 1544 | tf_op jit(solution)/shard_map/ppermute | solution.py:74
  15.3 36.1 %collective-permute-start.6 = (f32[1,1153]{1,0:T(1,128)S(1)}, f32[1,1153]{1,0:T(1,128)}, u32[]{:S(2)}, u32[]{:S(2)}) collective-permute-start(f32[1,1153]{1,0:T(1,128)S(1)} %broadcast_in_dim.74), channel_id=1, source_target_pairs={{0,2},{2,0},{4,6},{6,4},{8,10},{10,8},{12,14},{14,12},{1,3},{3,1},... | collective-permute-start | bytes 13844 | tf_op jit(solution)/shard_map/ppermute | solution.py:85
  21.4 4.2 %copy-start.20 = (bf16[2,256,256]{2,1,0:T(8,128)(2,1)S(1)}, bf16[2,256,256]{2,1,0:T(8,128)(2,1)}, u32[]{:S(2)}) copy-start(bf16[2,256,256]{2,1,0:T(8,128)(2,1)} %param.14) | copy-start | bytes 786436
  31.6 4.6 %copy-start.29 = (f32[1,4,64]{2,1,0:T(4,128)S(1)}, f32[1,4,64]{2,1,0:T(4,128)}, u32[]{:S(2)}) copy-start(f32[1,4,64]{2,1,0:T(4,128)} %param.24) | copy-start | bytes 3076
  33.3 49.2 %collective-permute-start.2 = (bf16[2,2,32,32,128]{4,3,2,1,0:T(8,128)(2,1)}, bf16[2,2,32,32,128]{4,3,2,1,0:T(8,128)(2,1)S(1)}, u32[]{:S(2)}, u32[]{:S(2)}) collective-permute-start(bf16[2,2,32,32,128]{4,3,2,1,0:T(8,128)(2,1)} %select_convert_fusion.1), channel_id=1, source_target_pairs={{0,2},{4,6},{8,10},{12,14},{2,0},{6,4},{10,8},{14,12},{1,3},{5,7},... | collective-permute-start | bytes 3145736 | tf_op jit(solution)/shard_map/ppermute | solution.py:74
  43.5 7.8 %copy-start.27 = (f32[4,2,32]{2,1,0:T(2,128)S(1)}, f32[4,2,32]{2,1,0:T(2,128)}, u32[]{:S(2)}) copy-start(f32[4,2,32]{2,1,0:T(2,128)} %reduce_window_sum.66) | copy-start | bytes 3076
  52.8 4.0 %collective-permute-start.7 = (f32[2,1153]{1,0:T(2,128)}, f32[2,1153]{1,0:T(2,128)}, u32[]{:S(2)}, u32[]{:S(2)}) collective-permute-start(f32[2,1153]{1,0:T(2,128)} %maximum_select_fusion.5), channel_id=1, source_target_pairs={{0,4},{2,6},{4,0},{6,2},{8,12},{10,14},{12,8},{14,10},{1,5},{3,7},... | collective-permute-start | bytes 27680 | tf_op jit(solution)/shard_map/ppermute | solution.py:85
  58.2 5.1 %collective-permute-start.8 = (f32[4,1153]{1,0:T(4,128)}, f32[4,1153]{1,0:T(4,128)}, u32[]{:S(2)}, u32[]{:S(2)}) collective-permute-start(f32[4,1153]{1,0:T(4,128)} %maximum_select_fusion.4), channel_id=1, source_target_pairs={{0,8},{2,10},{4,12},{6,14},{8,0},{10,2},{12,4},{14,6},{1,9},{3,11}... | collective-permute-start | bytes 55352 | tf_op jit(solution)/shard_map/ppermute | solution.py:85
  82.4 5.1 %copy-start.17 = (f32[4,2,32,64]{3,2,1,0:T(8,128)S(1)}, f32[4,2,32,64]{3,2,1,0:T(8,128)}, u32[]{:S(2)}) copy-start(f32[4,2,32,64]{3,2,1,0:T(8,128)} %reshape.278) | copy-start | bytes 196612
  82.4 5.1 %copy-start.23 = (f32[4,4,2,32]{3,2,1,0:T(2,128)S(1)}, f32[4,4,2,32]{3,2,1,0:T(2,128)}, u32[]{:S(2)}) copy-start(f32[4,4,2,32]{3,2,1,0:T(2,128)} %select_multiply_fusion) | copy-start | bytes 12292
  82.4 59.0 %copy-start.26 = (f32[64,2]{0,1:T(2,128)S(1)}, f32[64,2]{0,1:T(2,128)}, u32[]{:S(2)}) copy-start(f32[64,2]{0,1:T(2,128)} %copy-done.25) | copy-start | bytes 1540
  86.3 60.3 %collective-permute-start.3 = (bf16[2,2,32,32,128]{4,3,2,1,0:T(8,128)(2,1)}, bf16[2,2,32,32,128]{4,3,2,1,0:T(8,128)(2,1)S(1)}, u32[]{:S(2)}, u32[]{:S(2)}) collective-permute-start(bf16[2,2,32,32,128]{4,3,2,1,0:T(8,128)(2,1)} %get-tuple-element.14), channel_id=1, source_target_pairs={{0,4},{4,8},{8,12},{2,6},{6,10},{10,14},{1,5},{5,9},{9,13},{3,7},{... | collective-permute-start | bytes 3145736 | tf_op jit(solution)/shard_map/ppermute | solution.py:74
  140.6 4.0 %collective-permute-start.9 = (bf16[1,4,4096]{2,1,0:T(4,128)(2,1)S(1)}, bf16[1,4,4096]{2,1,0:T(4,128)(2,1)S(1)}, u32[]{:S(2)}, u32[]{:S(2)}) collective-permute-start(bf16[1,4,4096]{2,1,0:T(4,128)(2,1)S(1)} %convert_element_type.160), channel_id=1, source_target_pairs={{0,2},{2,0},{4,6},{6,4},{8,10},{10,8},{12,14},{14,12},{1,3},{3,1},... | collective-permute-start | bytes 98312 | tf_op jit(solution)/shard_map/ppermute | solution.py:85
  142.3 16.2 %collective-permute-start.1 = (f32[2,2,32]{2,1,0:T(2,128)}, f32[2,2,32]{2,1,0:T(2,128)S(1)}, u32[]{:S(2)}, u32[]{:S(2)}) collective-permute-start(f32[2,2,32]{2,1,0:T(2,128)} %get-tuple-element.37), channel_id=1, source_target_pairs={{0,4},{4,8},{8,12},{2,6},{6,10},{10,14},{1,5},{5,9},{9,13},{3,7},{... | collective-permute-start | bytes 1544 | tf_op jit(solution)/shard_map/ppermute | solution.py:74
  144.6 6.1 %copy-start.24 = (f32[2,32,256]{2,1,0:T(8,128)S(1)}, f32[2,32,256]{2,1,0:T(8,128)}, u32[]{:S(2)}) copy-start(f32[2,32,256]{2,1,0:T(8,128)} %reduce_window_sum.65) | copy-start | bytes 196612
  144.6 13.9 %collective-permute-start.10 = (bf16[2,4,4096]{2,1,0:T(4,128)(2,1)S(1)}, bf16[2,4,4096]{2,1,0:T(4,128)(2,1)S(1)}, u32[]{:S(2)}, u32[]{:S(2)}) collective-permute-start(bf16[2,4,4096]{2,1,0:T(4,128)(2,1)S(1)} %maximum_select_fusion.2), channel_id=1, source_target_pairs={{0,4},{2,6},{4,0},{6,2},{8,12},{10,14},{12,8},{14,10},{1,5},{3,7},... | collective-permute-start | bytes 196616 | tf_op jit(solution)/shard_map/ppermute | solution.py:85
  146.5 4.2 %copy-start.9 = (bf16[1,256,4096]{1,2,0:T(8,128)(2,1)S(1)}, bf16[1,256,4096]{1,2,0:T(8,128)(2,1)}, u32[]{:S(2)}) copy-start(bf16[1,256,4096]{1,2,0:T(8,128)(2,1)} %copy.149) | copy-start | bytes 6291460
  146.5 56.6 %slice-start = ((s8[8388608]{0:T(1024)(128)(4,1)}), s8[4194304]{0:T(1024)(128)(4,1)S(1)}, s32[]{:S(2)}) async-start(s8[8388608]{0:T(1024)(128)(4,1)} %bitcast.153), calls=%async_computation.2 | async-start | bytes 8388608
  149.3 50.4 %collective-permute-start.4 = (bf16[2,2,32,32,128]{4,3,2,1,0:T(8,128)(2,1)S(1)}, bf16[2,2,32,32,128]{4,3,2,1,0:T(8,128)(2,1)S(1)}, u32[]{:S(2)}, u32[]{:S(2)}) collective-permute-start(bf16[2,2,32,32,128]{4,3,2,1,0:T(8,128)(2,1)S(1)} %fusion.29), channel_id=1, source_target_pairs={{0,8},{4,12},{2,10},{6,14},{1,9},{5,13},{3,11},{7,15},{16,24},{20,... | collective-permute-start | bytes 3145736 | tf_op jit(solution)/shard_map/ppermute | solution.py:74
  150.7 49.0 %copy-start.3 = (f32[2,2,32,32,128]{4,3,2,1,0:T(8,128)S(1)}, f32[2,2,32,32,128]{4,3,2,1,0:T(8,128)}, u32[]{:S(2)}) copy-start(f32[2,2,32,32,128]{4,3,2,1,0:T(8,128)} %get-tuple-element.15) | copy-start | bytes 6291460
  150.7 49.0 %copy-start.11 = (bf16[2,2,32,32,128]{4,3,2,1,0:T(8,128)(2,1)S(1)}, bf16[2,2,32,32,128]{4,3,2,1,0:T(8,128)(2,1)}, u32[]{:S(2)}) copy-start(bf16[2,2,32,32,128]{4,3,2,1,0:T(8,128)(2,1)} %copy-done.10) | copy-start | bytes 3145732
  150.7 52.5 %slice-start.1 = ((s8[8388608]{0:T(1024)(128)(4,1)}), s8[4194304]{0:T(1024)(128)(4,1)S(1)}, s32[]{:S(2)}) async-start(s8[8388608]{0:T(1024)(128)(4,1)} %bitcast.153), calls=%async_computation.3 | async-start | bytes 8388608
  158.7 44.2 %collective-permute-start.11 = (bf16[4,4,4096]{2,1,0:T(4,128)(2,1)S(1)}, bf16[4,4,4096]{2,1,0:T(4,128)(2,1)S(1)}, u32[]{:S(2)}, u32[]{:S(2)}) collective-permute-start(bf16[4,4,4096]{2,1,0:T(4,128)(2,1)S(1)} %maximum_select_fusion.1), channel_id=1, source_target_pairs={{0,8},{2,10},{4,12},{6,14},{8,0},{10,2},{12,4},{14,6},{1,9},{3,11}... | collective-permute-start | bytes 393224 | tf_op jit(solution)/shard_map/ppermute | solution.py:85
  201.4 25.3 %collective-permute-start.5 = (bf16[2,2,32,32,128]{4,3,2,1,0:T(8,128)(2,1)}, bf16[2,2,32,32,128]{4,3,2,1,0:T(8,128)(2,1)}, u32[]{:S(2)}, u32[]{:S(2)}) collective-permute-start(bf16[2,2,32,32,128]{4,3,2,1,0:T(8,128)(2,1)} %select_convert_fusion), channel_id=1, source_target_pairs={{0,2},{4,6},{8,10},{12,14},{2,0},{6,4},{10,8},{14,12},{1,3},{5,7},... | collective-permute-start | bytes 3145736 | tf_op jit(solution)/shard_map/ppermute | solution.py:74
  210.5 19.2 %copy-start.7 = (bf16[1,256,4096]{1,2,0:T(8,128)(2,1)S(1)}, bf16[1,256,4096]{1,2,0:T(8,128)(2,1)}, u32[]{:S(2)}) copy-start(bf16[1,256,4096]{1,2,0:T(8,128)(2,1)} %copy.144) | copy-start | bytes 6291460
  210.5 19.2 %copy-start.19 = (f32[64,256]{1,0:T(8,128)S(1)}, f32[64,256]{1,0:T(8,128)}, u32[]{:S(2)}) copy-start(f32[64,256]{1,0:T(8,128)} %get-tuple-element.33) | copy-start | bytes 196612
  210.5 19.2 %copy-start.28 = (f32[2,32]{1,0:T(2,128)S(1)}, f32[2,32]{1,0:T(2,128)}, u32[]{:S(2)}) copy-start(f32[2,32]{1,0:T(2,128)} %mul.241) | copy-start | bytes 772
  233.6 4.3 %copy-start.5 = (f32[2,2,32,32,128]{4,3,2,1,0:T(8,128)S(1)}, f32[2,2,32,32,128]{4,3,2,1,0:T(8,128)}, u32[]{:S(2)}) copy-start(f32[2,2,32,32,128]{4,3,2,1,0:T(8,128)} %copy-done.4) | copy-start | bytes 6291460
  244.9 4.3 %copy-start.12 = (bf16[1,256,4096]{2,1,0:T(8,128)(2,1)S(1)}, bf16[1,256,4096]{2,1,0:T(8,128)(2,1)}, u32[]{:S(2)}) copy-start(bf16[1,256,4096]{2,1,0:T(8,128)(2,1)} %copy.158) | copy-start | bytes 6291460
  (13 other events, 35.2 us)
Sparse Core Ops, SparseCore 0:
  76.2 63.1 reduce-scatter.1

commit v4 on v3

--- a/solution.py
+++ b/solution.py
@@ -87,6 +87,22 @@
         value = jnp.where(
             upper, jnp.concatenate([got, value], axis=0), jnp.concatenate([value, got], axis=0)
         )
+        reach *= 2
+    return value
+
+
+def reduce_scatter_ctx(value):
+    count = lax.axis_size("ctx")
+    if count & (count - 1):
+        return lax.psum_scatter(value, "ctx", scatter_dimension=0, tiled=True)
+    place = lax.axis_index("ctx")
+    reach = 1
+    while reach < count:
+        pairs = value.reshape((value.shape[0] // 2, 2) + value.shape[1:])
+        upper = (place & reach) != 0
+        keep = jnp.where(upper, pairs[:, 1], pairs[:, 0])
+        give = jnp.where(upper, pairs[:, 0], pairs[:, 1])
+        value = keep + lax.ppermute(give, "ctx", [(i, i ^ reach) for i in range(count)])
         reach *= 2
     return value
 
@@ -195,7 +211,7 @@
     for request in range(1, request_count):
         pick = (all_request == request)[:, None, None, None, None]
         contribution = jnp.where(pick, projected[request], contribution)
-    from_prompt = lax.psum_scatter(contribution, "ctx", scatter_dimension=0, tiled=True)
+    from_prompt = reduce_scatter_ctx(contribution)
 
     row_input = new_input.reshape(slots, steps, group_count, per_group, HEAD_DIM).astype(
         jnp.float32

time: 261 us -> 213 us (0.82)
  waiting for transfers between devices: 111 us -> 83.7 us
  between operations: 15.3 us -> 1.91 us
    reduce_scatter x1 -> x0, waiting for transfers between devices: 51.6 us -> none  [shards(): lax.psum_scatter(contribution, 'ctx', scatter_dimension=0, tiled=True)]
    ppermute x0 -> x3, waiting for transfers between devices: none -> 15.4 us  [reduce_scatter_ctx(): lax.ppermute(give, 'ctx', [(i, i ^ reach) for i in range(count)])]
    ppermute x6, waiting for transfers between devices: 53.5 us -> 60.5 us  [send(): lax.ppermute((value.astype(jnp.bfloat16), total), 'ctx', pairs)]
    select_n x6, other arithmetic: 4.12 us -> 1.33 us  [gather_ctx(): jnp.where(upper, jnp.concatenate([got, value], axis=0), jnp.concatenate([...]
  transfers between devices with their start and end apart: 13 -> 15, of which waited for: 6 -> 9; matrix products, arithmetic and copies ran while one was open for 32% -> 35% of each run, Pallas kernels for 0% -> 0%
where the time goes in v4:
time: 213 us; the launch traced here: 212 us
  waiting for transfers between devices  83.7 us (39%)
  matrix products  37.9 us (18%)
  local copies, waits for them, and re-layouts  36.8 us (17%)
  other arithmetic  32.1 us (15%)
  starting transfers between devices  16.1 us (8%)
  blocking collectives  3.85 us (2%)
    ppermute x6, waiting for transfers between devices, send(): lax.ppermute((value.astype(jnp.bfloat16), total), 'ctx', pairs)  60.5 us
    dot_general x2, matrix products, block_terms(): jnp.einsum('gkts,sgkp->tgkp', mixing, inputs_head, preferred_element_type...  15.6 us
    ppermute x3, waiting for transfers between devices, reduce_scatter_ctx(): lax.ppermute(give, 'ctx', [(i, i ^ reach) for i in range(count)])  15.4 us
    dot_general x2, matrix products, finish(): carried = jnp.einsum('tgn,gkpn->tgkp', c_groups, entering, precision=HIGH)  10.7 us
    slice x3, local copies, waits for them, and re-layouts, shards(): ssm_input[request]  10.6 us
    convert_element_type x2, local copies, waits for them, and re-layouts, finish(): return (local_out + carried + skipped).reshape(block_size, group_count *...  8.58 us
    convert_element_type x4, other arithmetic, send(): value.astype(jnp.bfloat16)  8.35 us
    ppermute x6, waiting for transfers between devices, gather_ctx(): got = lax.ppermute(value, 'ctx', [(i, i ^ reach) for i in range(count)])  7.82 us
  transfers between devices with their start and end apart: 15, of which 9 were waited for; matrix products, arithmetic and copies ran while one was open for 35% of the time, Pallas kernels for 0%

profile of v4, /device:TPU:24, one launch (start us, length us, event | category | flops | bytes accessed | tf_op | source)
XLA Modules:
  0.0 212.4 jit_solution(8581995645019510488)
XLA Ops:
  10.8 3.9 %fusion.81 = (bf16[1,256,4096]{2,1,0:T(8,128)(2,1)}, bf16[1,256,4096]{2,1,0:T(8,128)(2,1)S(1)}) fusion(bf16[2,256,4096]{2,1,0:T(8,128)(2,1)} %param.13), kind=kLoop, calls=%fused_computation.139 | loop fusion | bytes 8388608 | tf_op jit(solution)/shard_map/slice | solution.py:174
  14.7 4.2 %copy.111 = bf16[1,256,4096]{1,2,0:T(8,128)(2,1)} copy(bf16[1,256,4096]{2,1,0:T(8,128)(2,1)} %get-tuple-element.18) | data formatting | bytes 4194304 | tf_op jit(solution)/shard_map/slice | solution.py:174
  19.0 2.5 %copy.116 = bf16[1,256,4096]{1,2,0:T(8,128)(2,1)} copy(bf16[1,256,4096]{2,1,0:T(8,128)(2,1)S(1)} %get-tuple-element.19) | data formatting | bytes 4194304 | tf_op jit(solution)/shard_map/slice | solution.py:174
  21.6 2.5 %fusion.52 = f32[1,2,32,64,128]{4,3,2,1,0:T(8,128)S(1)} fusion(bf16[256,2,128,1]{0,2,3,1:T(8,128)(2,1)S(1)} %bitcast.190, bf16[256,2,32,64]{0,3,2,1:T(8,128)(2,1)} %bitcast.170, f32[256,2,32]{0,2,1:T(8,128)S(1)} %bitcast.195), kind=kOutput, calls=%fused_computation.74 | convolution fusion | flops 271581184 | bytes 4390912 | tf_op jit(solution)/shard_map/sgkp,sgn->gkpn/dot_general | solution.py:42
  24.9 1.7 select_convert_fusion.1
  31.1 1.7 fusion.83
  35.0 7.8 %fusion = f32[2,32,256,64]{2,3,1,0:T(8,128)} fusion(bf16[256,2,32,64]{0,3,2,1:T(8,128)(2,1)} %bitcast.171, f32[2,32,256]{2,1,0:T(8,128)} %bitcast.199, f32[2,32,256]{2,1,0:T(8,128)} %reduce_window_sum.61, f32[2,256,256]{2,1,0:T(8,128)S(1)} %fusion.88, pred[256,256]{1,0:T(8,128)(4,1)} %iota_compare_fusion), kind=kOutput, calls=%fused_computation.2 | convolution fusion | flops 562036736 | bytes 7012352 | tf_op jit(solution)/shard_map/gkts,sgkp->tgkp/dot_general | solution.py:35
  44.9 3.2 %collective-permute-done.7 = f32[2,1153]{1,0:T(2,128)S(1)} collective-permute-done((f32[2,1153]{1,0:T(2,128)S(1)}, f32[2,1153]{1,0:T(2,128)S(1)}, u32[]{:S(2)}, u32[]{:S(2)}) %collective-permute-start.7) | collective-permute-done | bytes 9256 | tf_op jit(solution)/shard_map/ppermute | solution.py:85
  50.1 2.9 %collective-permute-done.8 = f32[4,1153]{1,0:T(4,128)S(1)} collective-permute-done((f32[4,1153]{1,0:T(4,128)S(1)}, f32[4,1153]{1,0:T(4,128)S(1)}, u32[]{:S(2)}, u32[]{:S(2)}) %collective-permute-start.8) | collective-permute-done | bytes 18480 | tf_op jit(solution)/shard_map/ppermute | solution.py:85
  53.4 2.3 %fusion.26 = (bf16[2,2,32,64,128,1]{4,3,2,1,0,5:T(8,128)(2,1)S(1)}, bf16[2,2,32,64,128,1]{4,3,2,1,0,5:T(8,128)(2,1)S(1)}) fusion(f32[1,2,32,64,128]{4,3,2,1,0:T(8,128)} %copy-done.2, f32[1,2,32,64,128]{4,3,2,1,0:T(8,128)S(1)} %fusion.52, f32[2,2,32]{2,1,0:T(2,128)S(1)} %exp.72), kind=kLoop, calls=%fused_computation.49 | loop fusion | flops 6291456 | bytes 8389120 | tf_op jit(solution)/shard_map/convert_element_type | solution.py:204
  55.7 2.0 fusion.42
  57.7 2.1 add_bitcast_fusion
  61.4 2.0 copy_select_fusion
  69.4 7.1 %collective-permute-done.9 = f32[4,4,2,32,64]{4,3,2,1,0:T(8,128)} collective-permute-done((f32[4,4,2,32,64]{4,3,2,1,0:T(8,128)}, f32[4,4,2,32,64]{4,3,2,1,0:T(8,128)}, u32[]{:S(2)}, u32[]{:S(2)}) %collective-permute-start.9) | collective-permute-done | bytes 262176 | tf_op jit(solution)/shard_map/ppermute | solution.py:105
  79.7 5.4 %collective-permute-done.10 = f32[2,4,2,32,64]{4,3,2,1,0:T(8,128)S(1)} collective-permute-done((f32[2,4,2,32,64]{4,3,2,1,0:T(8,128)S(1)}, f32[2,4,2,32,64]{4,3,2,1,0:T(8,128)S(1)}, u32[]{:S(2)}, u32[]{:S(2)}) %collective-permute-start.10) | collective-permute-done | bytes 131104 | tf_op jit(solution)/shard_map/ppermute | solution.py:105
  86.6 2.2 %fusion.58 = (bf16[2,2,32,32,128]{4,3,2,1,0:T(8,128)(2,1)}, f32[2,2,32,32,128]{4,3,2,1,0:T(8,128)}) fusion(bf16[2,2,32,32,128]{4,3,2,1,0:T(8,128)(2,1)S(1)} %collective-permute-done.2, pred[]{:T(512)S(6)} %eq.15, f32[2,2,32]{2,1,0:T(2,128)S(1)} %get-tuple-element.35, f32[1,2,32,64,128]{4,3,2,1,0:T(8,128)S(1)} %copy-done.3, f32[1,2,32,64,128]{4,3,2,1,0:T(8,128)S(1)} %fusion.52), kind=kLoop, calls=%fused_computation.79 | loop fusion | flops 4718592 | bytes 8389121 | tf_op jit(solution)/shard_map/convert_element_type | solution.py:74
  91.9 3.0 %collective-permute-done.11 = f32[1,4,2,32,64]{4,3,2,1,0:T(8,128)} collective-permute-done((f32[1,4,2,32,64]{4,3,2,1,0:T(8,128)}, f32[1,4,2,32,64]{4,3,2,1,0:T(8,128)}, u32[]{:S(2)}, u32[]{:S(2)}) %collective-permute-start.11) | collective-permute-done | bytes 65568 | tf_op jit(solution)/shard_map/ppermute | solution.py:105
  98.3 1.7 collective-permute-done.12
  101.1 11.2 %collective-permute-done.3 = bf16[2,2,32,32,128]{4,3,2,1,0:T(8,128)(2,1)S(1)} collective-permute-done((bf16[2,2,32,32,128]{4,3,2,1,0:T(8,128)(2,1)}, bf16[2,2,32,32,128]{4,3,2,1,0:T(8,128)(2,1)S(1)}, u32[]{:S(2)}, u32[]{:S(2)}) %collective-permute-start.3) | collective-permute-done | bytes 1048608 | tf_op jit(solution)/shard_map/ppermute | solution.py:74
  112.2 2.7 %fusion.29 = bf16[2,2,32,32,128]{4,3,2,1,0:T(8,128)(2,1)S(1)} fusion(bf16[2,2,32,32,128]{4,3,2,1,0:T(8,128)(2,1)S(1)} %collective-permute-done.3, f32[2,2,32]{2,1,0:T(2,128)} %get-tuple-element.36, f32[2,2,32,32,128]{4,3,2,1,0:T(8,128)} %get-tuple-element.13, bf16[2,2,32,32,128]{4,3,2,1,0:T(8,128)(2,1)S(1)} %collective-permute-done.2, pred[]{:T(512)S(6)} %eq.15, ...), kind=kLoop, calls=%fused_computation.52 | loop fusion | flops 4718592 | bytes 5243905 | tf_op jit(solution)/shard_map/convert_element_type | solution.py:74
  116.4 7.8 %fusion.1 = f32[2,32,256,64]{2,3,1,0:T(8,128)} fusion(bf16[256,2,32,64]{0,3,2,1:T(8,128)(2,1)S(1)} %bitcast.175, f32[2,32,256]{2,1,0:T(8,128)} %bitcast.198, f32[2,32,256]{2,1,0:T(8,128)S(1)} %reduce_window_sum.65, f32[2,256,256]{2,1,0:T(8,128)} %fusion.89, pred[256,256]{1,0:T(8,128)(4,1)S(1)} %copy-done.28), kind=kOutput, calls=%fused_computation.3 | convolution fusion | flops 562036736 | bytes 7012352 | tf_op jit(solution)/shard_map/gkts,sgkp->tgkp/dot_general | solution.py:35
  124.4 3.7 %collective-permute-start.14 = (bf16[4,4,4096]{2,1,0:T(4,128)(2,1)S(1)}, bf16[4,4,4096]{2,1,0:T(4,128)(2,1)S(1)}, u32[]{:S(2)}, u32[]{:S(2)}) collective-permute-start(bf16[4,4,4096]{2,1,0:T(4,128)(2,1)S(1)} %maximum_select_fusion.1), channel_id=1, source_target_pairs={{0,8},{2,10},{4,12},{6,14},{8,0},{10,2},{12,4},{14,6},{1,9},{3,11}... | collective-permute-start | bytes 393224 | tf_op jit(solution)/shard_map/ppermute | solution.py:85
  128.1 35.3 %collective-permute-done.4 = bf16[2,2,32,32,128]{4,3,2,1,0:T(8,128)(2,1)S(1)} collective-permute-done((bf16[2,2,32,32,128]{4,3,2,1,0:T(8,128)(2,1)S(1)}, bf16[2,2,32,32,128]{4,3,2,1,0:T(8,128)(2,1)S(1)}, u32[]{:S(2)}, u32[]{:S(2)}) %collective-permute-start.4) | collective-permute-done | bytes 1048608 | tf_op jit(solution)/shard_map/ppermute | solution.py:74
  163.4 1.8 select_convert_fusion
  167.5 3.9 %all-reduce.1 = bf16[8,4,1024]{2,0,1:T(8,128)(2,1)S(1)} all-reduce(f32[8,4,1024]{2,0,1:T(8,128)S(1)} %fusion.2), channel_id=1, replica_groups=mesh['groups'=2,'ctx'=8,'heads'=2] {'heads'}, use_global_device_ids=true, to_apply=%region_7.8 | all-reduce | flops 32768 | bytes 196608 | tf_op jit(solution)/shard_map/psum | solution.py:245
  172.0 14.0 %collective-permute-done.5 = bf16[2,2,32,32,128]{4,3,2,1,0:T(8,128)(2,1)} collective-permute-done((bf16[2,2,32,32,128]{4,3,2,1,0:T(8,128)(2,1)}, bf16[2,2,32,32,128]{4,3,2,1,0:T(8,128)(2,1)}, u32[]{:S(2)}, u32[]{:S(2)}) %collective-permute-start.5) | collective-permute-done | bytes 1048608 | tf_op jit(solution)/shard_map/ppermute | solution.py:74
  186.0 3.0 %convert_select_fusion.1 = (f32[2,2,32,32,128]{4,3,2,1,0:T(8,128)S(1)}, f32[2,2,32,32,128]{4,3,2,1,0:T(8,128)S(1)}) fusion(bf16[2,2,32,32,128]{4,3,2,1,0:T(8,128)(2,1)} %collective-permute-done.5, pred[]{:T(512)S(6)} %eq.15, f32[2,2,32,32,128]{4,3,2,1,0:T(8,128)S(1)} %copy-done.4, bf16[2,2,32,32,128]{4,3,2,1,0:T(8,128)(2,1)S(1)} %collective-permute-done.2, ...), kind=kLoop, calls=%fused_computation.44 | loop fusion | flops 6291456 | bytes 10486785 | tf_op jit(solution)/shard_map/jit(_where)/select_n | solution.py:147
  189.1 3.8 %fusion.18 = bf16[256,2,32,64]{0,3,2,1:T(8,128)(2,1)} fusion(bf16[256,2,32,64]{0,3,2,1:T(8,128)(2,1)S(1)} %bitcast.172, f32[2,32,256,64]{2,3,1,0:T(8,128)S(1)} %copy-done.15, bf16[256,2,128,1]{0,2,3,1:T(8,128)(2,1)S(1)} %bitcast.185, f32[2,2,32,32,128]{4,3,2,1,0:T(8,128)S(1)} %get-tuple-element.14, f32[2,2,32,32,128]{4,3,2,1,0:T(8,128)S(1)} %get-tuple-element.15, ...), kind=kOutput, calls=%fused_computation.29 | convolution fusion | flops 1617428480 | bytes 12779776 | tf_op jit(solution)/shard_map/tgn,gkpn->tgkp/dot_general | solution.py:52
  192.9 4.3 %copy.125 = bf16[1,256,4096]{2,1,0:T(8,128)(2,1)} copy(bf16[1,256,4096]{1,2,0:T(8,128)(2,1)} %bitcast.177) | data formatting | bytes 4194304 | tf_op jit(solution)/shard_map/convert_element_type | solution.py:59
  197.2 6.9 %fusion.21 = bf16[256,2,32,64]{0,3,2,1:T(8,128)(2,1)} fusion(bf16[256,2,32,64]{0,3,2,1:T(8,128)(2,1)} %bitcast.173, f32[2,32,256,64]{2,3,1,0:T(8,128)} %fusion.1, bf16[256,2,128,1]{0,2,3,1:T(8,128)(2,1)S(1)} %bitcast.187, f32[2,2,32,32,128]{4,3,2,1,0:T(8,128)} %copy-done.7, f32[2,2,32,32,128]{4,3,2,1,0:T(8,128)S(1)} %copy-done.6, ...), kind=kOutput, calls=%fused_computation.32 | convolution fusion | flops 1617428480 | bytes 12779776 | tf_op jit(solution)/shard_map/tgn,gkpn->tgkp/dot_general | solution.py:52
  204.1 4.2 %copy.126 = bf16[1,256,4096]{2,1,0:T(8,128)(2,1)} copy(bf16[1,256,4096]{1,2,0:T(8,128)(2,1)} %bitcast.176) | data formatting | bytes 4194304 | tf_op jit(solution)/shard_map/convert_element_type | solution.py:59
  208.4 4.0 %pad_maximum_fusion.1 = bf16[2,256,4096]{2,1,0:T(8,128)(2,1)} fusion(bf16[1,256,4096]{2,1,0:T(8,128)(2,1)} %copy.126, bf16[1,256,4096]{2,1,0:T(8,128)(2,1)S(1)} %copy-done.14), kind=kLoop, calls=%fused_computation.36 | loop fusion | flops 2097152 | bytes 8388608 | tf_op jit(solution)/shard_map/stack | solution.py:260
  (173 shorter events, 46.1 us)
Async XLA Ops:
  0.6 42.2 %copy-start = (bf16[1,4,256]{2,1,0:T(4,128)(2,1)S(1)}, bf16[1,4,256]{2,1,0:T(4,128)(2,1)}, u32[]{:S(2)}) copy-start(bf16[1,4,256]{2,1,0:T(4,128)(2,1)} %param.21) | copy-start | bytes 6148
  2.4 12.3 %copy-start.29 = (f32[64,2]{0,1:T(2,128)}, f32[64,2]{0,1:T(2,128)S(1)}, u32[]{:S(2)}) copy-start(f32[64,2]{0,1:T(2,128)S(1)} %slice.114) | copy-start | bytes 1540
  3.4 5.8 %copy-start.31 = (f32[64,2]{0,1:T(2,128)}, f32[64,2]{0,1:T(2,128)S(1)}, u32[]{:S(2)}) copy-start(f32[64,2]{0,1:T(2,128)S(1)} %slice.108) | copy-start | bytes 1540
  4.9 73.5 %collective-permute-start = (f32[2,2,32]{2,1,0:T(2,128)}, f32[2,2,32]{2,1,0:T(2,128)}, u32[]{:S(2)}, u32[]{:S(2)}) collective-permute-start(f32[2,2,32]{2,1,0:T(2,128)} %constant_dynamic-update-slice_fusion), channel_id=1, source_target_pairs={{0,2},{4,6},{8,10},{12,14},{2,0},{6,4},{10,8},{14,12},{1,3},{5,7},... | collective-permute-start | bytes 1544 | tf_op jit(solution)/shard_map/ppermute | solution.py:74
  8.6 34.9 %collective-permute-start.6 = (f32[1,1153]{1,0:T(1,128)S(1)}, f32[1,1153]{1,0:T(1,128)}, u32[]{:S(2)}, u32[]{:S(2)}) collective-permute-start(f32[1,1153]{1,0:T(1,128)S(1)} %broadcast_in_dim.74), channel_id=1, source_target_pairs={{0,2},{2,0},{4,6},{6,4},{8,10},{10,8},{12,14},{14,12},{1,3},{3,1},... | collective-permute-start | bytes 13844 | tf_op jit(solution)/shard_map/ppermute | solution.py:85
  26.6 60.0 %collective-permute-start.2 = (bf16[2,2,32,32,128]{4,3,2,1,0:T(8,128)(2,1)}, bf16[2,2,32,32,128]{4,3,2,1,0:T(8,128)(2,1)S(1)}, u32[]{:S(2)}, u32[]{:S(2)}) collective-permute-start(bf16[2,2,32,32,128]{4,3,2,1,0:T(8,128)(2,1)} %select_convert_fusion.1), channel_id=1, source_target_pairs={{0,2},{4,6},{8,10},{12,14},{2,0},{6,4},{10,8},{14,12},{1,3},{5,7},... | collective-permute-start | bytes 3145736 | tf_op jit(solution)/shard_map/ppermute | solution.py:74
  33.8 9.1 %copy-start.17 = (bf16[1,256,256]{1,2,0:T(8,128)(2,1)}, bf16[1,256,256]{1,2,0:T(8,128)(2,1)S(1)}, u32[]{:S(2)}) copy-start(bf16[1,256,256]{1,2,0:T(8,128)(2,1)S(1)} %copy.172) | copy-start | bytes 393220
  35.0 7.8 %copy-start.33 = (bf16[1,4,256]{2,1,0:T(4,128)(2,1)S(1)}, bf16[1,4,256]{2,1,0:T(4,128)(2,1)}, u32[]{:S(2)}) copy-start(bf16[1,4,256]{2,1,0:T(4,128)(2,1)} %param.22) | copy-start | bytes 6148
  44.3 3.7 %collective-permute-start.7 = (f32[2,1153]{1,0:T(2,128)S(1)}, f32[2,1153]{1,0:T(2,128)S(1)}, u32[]{:S(2)}, u32[]{:S(2)}) collective-permute-start(f32[2,1153]{1,0:T(2,128)S(1)} %maximum_select_fusion.5), channel_id=1, source_target_pairs={{0,4},{2,6},{4,0},{6,2},{8,12},{10,14},{12,8},{14,10},{1,5},{3,7},... | collective-permute-start | bytes 27680 | tf_op jit(solution)/shard_map/ppermute | solution.py:85
  48.1 4.8 %collective-permute-start.8 = (f32[4,1153]{1,0:T(4,128)S(1)}, f32[4,1153]{1,0:T(4,128)S(1)}, u32[]{:S(2)}, u32[]{:S(2)}) collective-permute-start(f32[4,1153]{1,0:T(4,128)S(1)} %maximum_select_fusion.4), channel_id=1, source_target_pairs={{0,8},{2,10},{4,12},{6,14},{8,0},{10,2},{12,4},{14,6},{1,9},{3,11}... | collective-permute-start | bytes 55352 | tf_op jit(solution)/shard_map/ppermute | solution.py:85
  61.4 5.1 %copy-start.26 = (bf16[1,4,4096]{2,1,0:T(4,128)(2,1)S(1)}, bf16[1,4,4096]{2,1,0:T(4,128)(2,1)}, u32[]{:S(2)}) copy-start(bf16[1,4,4096]{2,1,0:T(4,128)(2,1)} %param.20) | copy-start | bytes 98308
  65.3 11.1 %collective-permute-start.9 = (f32[4,4,2,32,64]{4,3,2,1,0:T(8,128)}, f32[4,4,2,32,64]{4,3,2,1,0:T(8,128)}, u32[]{:S(2)}, u32[]{:S(2)}) collective-permute-start(f32[4,4,2,32,64]{4,3,2,1,0:T(8,128)} %select_bitcast_fusion), channel_id=1, source_target_pairs={{0,2},{2,0},{4,6},{6,4},{8,10},{10,8},{12,14},{14,12},{1,3},{3,1},... | collective-permute-start | bytes 786440 | tf_op jit(solution)/shard_map/ppermute | solution.py:105
  68.3 11.4 %copy-start.19 = (bf16[1,256,256]{1,2,0:T(8,128)(2,1)}, bf16[1,256,256]{1,2,0:T(8,128)(2,1)S(1)}, u32[]{:S(2)}) copy-start(bf16[1,256,256]{1,2,0:T(8,128)(2,1)S(1)} %copy.175) | copy-start | bytes 393220
  69.4 17.2 %copy-start.3 = (f32[1,2,32,64,128]{4,3,2,1,0:T(8,128)S(1)}, f32[1,2,32,64,128]{4,3,2,1,0:T(8,128)}, u32[]{:S(2)}) copy-start(f32[1,2,32,64,128]{4,3,2,1,0:T(8,128)} %copy-done.2) | copy-start | bytes 6291460
  78.0 7.1 %collective-permute-start.10 = (f32[2,4,2,32,64]{4,3,2,1,0:T(8,128)S(1)}, f32[2,4,2,32,64]{4,3,2,1,0:T(8,128)S(1)}, u32[]{:S(2)}, u32[]{:S(2)}) collective-permute-start(f32[2,4,2,32,64]{4,3,2,1,0:T(8,128)S(1)} %select_bitcast_fusion.1), channel_id=1, source_target_pairs={{0,4},{2,6},{4,0},{6,2},{8,12},{10,14},{12,8},{14,10},{1,5},{3,7},... | collective-permute-start | bytes 393224 | tf_op jit(solution)/shard_map/ppermute | solution.py:105
  85.8 9.1 %collective-permute-start.11 = (f32[1,4,2,32,64]{4,3,2,1,0:T(8,128)}, f32[1,4,2,32,64]{4,3,2,1,0:T(8,128)}, u32[]{:S(2)}, u32[]{:S(2)}) collective-permute-start(f32[1,4,2,32,64]{4,3,2,1,0:T(8,128)} %select_bitcast_fusion.2), channel_id=1, source_target_pairs={{0,8},{2,10},{4,12},{6,14},{8,0},{10,2},{12,4},{14,6},{1,9},{3,11}... | collective-permute-start | bytes 196616 | tf_op jit(solution)/shard_map/ppermute | solution.py:105
  86.6 10.0 %copy-start.30 = (f32[64,2]{0,1:T(2,128)S(1)}, f32[64,2]{0,1:T(2,128)}, u32[]{:S(2)}) copy-start(f32[64,2]{0,1:T(2,128)} %copy-done.29) | copy-start | bytes 1540
  88.8 23.5 %collective-permute-start.3 = (bf16[2,2,32,32,128]{4,3,2,1,0:T(8,128)(2,1)}, bf16[2,2,32,32,128]{4,3,2,1,0:T(8,128)(2,1)S(1)}, u32[]{:S(2)}, u32[]{:S(2)}) collective-permute-start(bf16[2,2,32,32,128]{4,3,2,1,0:T(8,128)(2,1)} %get-tuple-element.12), channel_id=1, source_target_pairs={{0,4},{4,8},{8,12},{2,6},{6,10},{10,14},{1,5},{5,9},{9,13},{3,7},{... | collective-permute-start | bytes 3145736 | tf_op jit(solution)/shard_map/ppermute | solution.py:74
  96.0 4.0 %collective-permute-start.12 = (bf16[1,4,4096]{2,1,0:T(4,128)(2,1)S(1)}, bf16[1,4,4096]{2,1,0:T(4,128)(2,1)S(1)}, u32[]{:S(2)}, u32[]{:S(2)}) collective-permute-start(bf16[1,4,4096]{2,1,0:T(4,128)(2,1)S(1)} %convert_element_type.160), channel_id=1, source_target_pairs={{0,2},{2,0},{4,6},{6,4},{8,10},{10,8},{12,14},{14,12},{1,3},{3,1},... | collective-permute-start | bytes 98312 | tf_op jit(solution)/shard_map/ppermute | solution.py:85
  96.7 19.6 %copy-start.28 = (pred[256,256]{1,0:T(8,128)(4,1)S(1)}, pred[256,256]{1,0:T(8,128)(4,1)}, u32[]{:S(2)}) copy-start(pred[256,256]{1,0:T(8,128)(4,1)} %iota_compare_fusion) | copy-start | bytes 196612
  96.8 27.4 %collective-permute-start.1 = (f32[2,2,32]{2,1,0:T(2,128)}, f32[2,2,32]{2,1,0:T(2,128)S(1)}, u32[]{:S(2)}, u32[]{:S(2)}) collective-permute-start(f32[2,2,32]{2,1,0:T(2,128)} %get-tuple-element.37), channel_id=1, source_target_pairs={{0,4},{4,8},{8,12},{2,6},{6,10},{10,14},{1,5},{5,9},{9,13},{3,7},{... | collective-permute-start | bytes 1544 | tf_op jit(solution)/shard_map/ppermute | solution.py:74
  100.1 24.2 %collective-permute-start.13 = (bf16[2,4,4096]{2,1,0:T(4,128)(2,1)S(1)}, bf16[2,4,4096]{2,1,0:T(4,128)(2,1)S(1)}, u32[]{:S(2)}, u32[]{:S(2)}) collective-permute-start(bf16[2,4,4096]{2,1,0:T(4,128)(2,1)S(1)} %maximum_select_fusion.2), channel_id=1, source_target_pairs={{0,4},{2,6},{4,0},{6,2},{8,12},{10,14},{12,8},{14,10},{1,5},{3,7},... | collective-permute-start | bytes 196616 | tf_op jit(solution)/shard_map/ppermute | solution.py:85
  112.2 53.8 %slice-start = ((s8[8388608]{0:T(1024)(128)(4,1)}), s8[4194304]{0:T(1024)(128)(4,1)S(1)}, s32[]{:S(2)}) async-start(s8[8388608]{0:T(1024)(128)(4,1)} %bitcast.178), calls=%async_computation | async-start | bytes 8388608
  115.0 48.4 %collective-permute-start.4 = (bf16[2,2,32,32,128]{4,3,2,1,0:T(8,128)(2,1)S(1)}, bf16[2,2,32,32,128]{4,3,2,1,0:T(8,128)(2,1)S(1)}, u32[]{:S(2)}, u32[]{:S(2)}) collective-permute-start(bf16[2,2,32,32,128]{4,3,2,1,0:T(8,128)(2,1)S(1)} %fusion.29), channel_id=1, source_target_pairs={{0,8},{4,12},{2,10},{6,14},{1,9},{5,13},{3,11},{7,15},{16,24},{20,... | collective-permute-start | bytes 3145736 | tf_op jit(solution)/shard_map/ppermute | solution.py:74
  116.4 47.0 %copy-start.4 = (f32[2,2,32,32,128]{4,3,2,1,0:T(8,128)S(1)}, f32[2,2,32,32,128]{4,3,2,1,0:T(8,128)}, u32[]{:S(2)}) copy-start(f32[2,2,32,32,128]{4,3,2,1,0:T(8,128)} %get-tuple-element.13) | copy-start | bytes 6291460
  116.4 47.0 %copy-start.13 = (bf16[2,2,32,32,128]{4,3,2,1,0:T(8,128)(2,1)S(1)}, bf16[2,2,32,32,128]{4,3,2,1,0:T(8,128)(2,1)}, u32[]{:S(2)}) copy-start(bf16[2,2,32,32,128]{4,3,2,1,0:T(8,128)(2,1)} %copy-done.12) | copy-start | bytes 3145732
  116.4 49.6 %slice-start.1 = ((s8[8388608]{0:T(1024)(128)(4,1)}), s8[4194304]{0:T(1024)(128)(4,1)S(1)}, s32[]{:S(2)}) async-start(s8[8388608]{0:T(1024)(128)(4,1)} %bitcast.178), calls=%async_computation.1 | async-start | bytes 8388608
  124.4 41.3 %collective-permute-start.14 = (bf16[4,4,4096]{2,1,0:T(4,128)(2,1)S(1)}, bf16[4,4,4096]{2,1,0:T(4,128)(2,1)S(1)}, u32[]{:S(2)}, u32[]{:S(2)}) collective-permute-start(bf16[4,4,4096]{2,1,0:T(4,128)(2,1)S(1)} %maximum_select_fusion.1), channel_id=1, source_target_pairs={{0,8},{2,10},{4,12},{6,14},{8,0},{10,2},{12,4},{14,6},{1,9},{3,11}... | collective-permute-start | bytes 393224 | tf_op jit(solution)/shard_map/ppermute | solution.py:85
  165.2 20.8 %collective-permute-start.5 = (bf16[2,2,32,32,128]{4,3,2,1,0:T(8,128)(2,1)}, bf16[2,2,32,32,128]{4,3,2,1,0:T(8,128)(2,1)}, u32[]{:S(2)}, u32[]{:S(2)}) collective-permute-start(bf16[2,2,32,32,128]{4,3,2,1,0:T(8,128)(2,1)} %select_convert_fusion), channel_id=1, source_target_pairs={{0,2},{4,6},{8,10},{12,14},{2,0},{6,4},{10,8},{14,12},{1,3},{5,7},... | collective-permute-start | bytes 3145736 | tf_op jit(solution)/shard_map/ppermute | solution.py:74
  172.0 16.9 %copy-start.8 = (bf16[1,256,4096]{1,2,0:T(8,128)(2,1)S(1)}, bf16[1,256,4096]{1,2,0:T(8,128)(2,1)}, u32[]{:S(2)}) copy-start(bf16[1,256,4096]{1,2,0:T(8,128)(2,1)} %copy.111) | copy-start | bytes 6291460
  172.0 17.0 %copy-start.18 = (bf16[1,256,256]{1,2,0:T(8,128)(2,1)S(1)}, bf16[1,256,256]{1,2,0:T(8,128)(2,1)}, u32[]{:S(2)}) copy-start(bf16[1,256,256]{1,2,0:T(8,128)(2,1)} %copy-done.17) | copy-start | bytes 393220
  172.0 17.0 %copy-start.24 = (f32[64,256]{1,0:T(8,128)S(1)}, f32[64,256]{1,0:T(8,128)}, u32[]{:S(2)}) copy-start(f32[64,256]{1,0:T(8,128)} %get-tuple-element.33) | copy-start | bytes 196612
  (19 other events, 62.2 us)

commit v5 on v4

--- a/solution.py
+++ b/solution.py
@@ -107,7 +107,7 @@
     return value
 
 
-def prefix_states(states, totals):
+def prefix_states(states, totals, rider):
     count = lax.axis_size("ctx")
     columns = count // 2
     place = lax.axis_index("ctx")
@@ -133,6 +133,8 @@
     while step < columns:
         pairs = [(y + 2 * m, y + 2 * (m + step)) for y in range(2) for m in range(columns - step)]
         got, got_total = send(window, window_total, pairs)
+        if step == 1:
+            got, rider = lax.optimization_barrier((got, rider))
         new_before = scale(jnp.exp(before_total), got) + before
         if 2 * step < columns:
             window = scale(jnp.exp(window_total), got) + window
@@ -146,7 +148,7 @@
     own_half = jnp.where(row_zero, before, odd_entering)
     first_half = jnp.where(row_zero, own_half, partner)
     second_half = jnp.where(row_zero, partner, own_half)
-    return jnp.concatenate([first_half, second_half], axis=-2)
+    return jnp.concatenate([first_half, second_half], axis=-2), rider
 
 
 def shards(
@@ -211,6 +213,7 @@
     for request in range(1, request_count):
         pick = (all_request == request)[:, None, None, None, None]
         contribution = jnp.where(pick, projected[request], contribution)
+    entering, contribution = prefix_states(states, totals, contribution)
     from_prompt = reduce_scatter_ctx(contribution)
 
     row_input = new_input.reshape(slots, steps, group_count, per_group, HEAD_DIM).astype(
@@ -244,7 +247,6 @@
     )
     decoded = lax.psum(partial_value, "heads").astype(jnp.bfloat16)
 
-    entering = prefix_states(states, totals)
     prefill_rows = []
     for request in range(request_count):
         prefill_rows.append(

time: 213 us -> 216 us (1.014)
  the two profiles are of different devices: /device:TPU:24 before, /device:TPU:26 now
where the time goes in v5:
time: 216 us; the launch traced here: 215 us
  waiting for transfers between devices  71 us (33%)
  matrix products  38.2 us (18%)
  local copies, waits for them, and re-layouts  38 us (18%)
  other arithmetic  33.9 us (16%)
  starting transfers between devices  27.5 us (13%)
  blocking collectives  4.74 us (2%)
    ppermute x6, waiting for transfers between devices, send(): lax.ppermute((value.astype(jnp.bfloat16), total), 'ctx', pairs)  52.1 us
    ppermute x6, starting transfers between devices, gather_ctx(): got = lax.ppermute(value, 'ctx', [(i, i ^ reach) for i in range(count)])  17.5 us
    dot_general x2, matrix products, block_terms(): jnp.einsum('gkts,sgkp->tgkp', mixing, inputs_head, preferred_element_type...  15.6 us
    ppermute x3, waiting for transfers between devices, reduce_scatter_ctx(): lax.ppermute(give, 'ctx', [(i, i ^ reach) for i in range(count)])  12.4 us
    dot_general x2, matrix products, finish(): carried = jnp.einsum('tgn,gkpn->tgkp', c_groups, entering, precision=HIGH)  10.9 us
    slice x3, local copies, waits for them, and re-layouts, shards(): ssm_input[request]  10.6 us
    ppermute x6, starting transfers between devices, send(): lax.ppermute((value.astype(jnp.bfloat16), total), 'ctx', pairs)  8.67 us
    convert_element_type x2, local copies, waits for them, and re-layouts, finish(): return (local_out + carried + skipped).reshape(block_size, group_count *...  8.47 us
  transfers between devices with their start and end apart: 15, of which 7 were waited for; matrix products, arithmetic and copies ran while one was open for 33% of the time, Pallas kernels for 0%

profile of v5, /device:TPU:26, one launch (start us, length us, event | category | flops | bytes accessed | tf_op | source)
XLA Modules:
  0.0 215.1 jit_solution(15434426008315784837)
XLA Ops:
  10.9 3.9 %fusion.81 = (bf16[1,256,4096]{2,1,0:T(8,128)(2,1)}, bf16[1,256,4096]{2,1,0:T(8,128)(2,1)S(1)}) fusion(bf16[2,256,4096]{2,1,0:T(8,128)(2,1)} %param.13), kind=kLoop, calls=%fused_computation.139 | loop fusion | bytes 8388608 | tf_op jit(solution)/shard_map/slice | solution.py:176
  14.8 4.2 %copy.113 = bf16[1,256,4096]{1,2,0:T(8,128)(2,1)} copy(bf16[1,256,4096]{2,1,0:T(8,128)(2,1)} %get-tuple-element.22) | data formatting | bytes 4194304 | tf_op jit(solution)/shard_map/slice | solution.py:176
  19.1 2.5 %copy.118 = bf16[1,256,4096]{1,2,0:T(8,128)(2,1)} copy(bf16[1,256,4096]{2,1,0:T(8,128)(2,1)S(1)} %get-tuple-element.23) | data formatting | bytes 4194304 | tf_op jit(solution)/shard_map/slice | solution.py:176
  21.8 2.5 %fusion.50 = f32[1,2,32,64,128]{4,3,2,1,0:T(8,128)S(1)} fusion(bf16[256,2,128,1]{0,2,3,1:T(8,128)(2,1)S(1)} %bitcast.198, bf16[256,2,32,64]{0,3,2,1:T(8,128)(2,1)} %bitcast.179, f32[256,2,32]{0,2,1:T(8,128)S(1)} %bitcast.203), kind=kOutput, calls=%fused_computation.72 | convolution fusion | flops 271581184 | bytes 4390912 | tf_op jit(solution)/shard_map/sgkp,sgn->gkpn/dot_general | solution.py:42
  25.0 1.7 select_convert_fusion.1
  34.1 7.8 %fusion = f32[2,32,256,64]{2,3,1,0:T(8,128)} fusion(bf16[256,2,32,64]{0,3,2,1:T(8,128)(2,1)} %bitcast.180, f32[2,32,256]{2,1,0:T(8,128)} %bitcast.207, f32[2,32,256]{2,1,0:T(8,128)} %reduce_window_sum.61, f32[2,256,256]{2,1,0:T(8,128)S(1)} %fusion.88, pred[256,256]{1,0:T(8,128)(4,1)} %iota_compare_fusion), kind=kOutput, calls=%fused_computation.2 | convolution fusion | flops 562036736 | bytes 7012352 | tf_op jit(solution)/shard_map/gkts,sgkp->tgkp/dot_general | solution.py:35
  43.4 3.2 %collective-permute-done.5 = f32[2,1153]{1,0:T(2,128)S(1)} collective-permute-done((f32[2,1153]{1,0:T(2,128)S(1)}, f32[2,1153]{1,0:T(2,128)S(1)}, u32[]{:S(2)}, u32[]{:S(2)}) %collective-permute-start.5) | collective-permute-done | bytes 9256 | tf_op jit(solution)/shard_map/ppermute | solution.py:85
  48.3 3.2 %collective-permute-done.6 = f32[4,1153]{1,0:T(4,128)S(1)} collective-permute-done((f32[4,1153]{1,0:T(4,128)S(1)}, f32[4,1153]{1,0:T(4,128)S(1)}, u32[]{:S(2)}, u32[]{:S(2)}) %collective-permute-start.6) | collective-permute-done | bytes 18480 | tf_op jit(solution)/shard_map/ppermute | solution.py:85
  51.8 2.5 %fusion.26 = (bf16[2,2,32,64,128,1]{4,3,2,1,0,5:T(8,128)(2,1)S(1)}, bf16[2,2,32,64,128,1]{4,3,2,1,0,5:T(8,128)(2,1)S(1)}) fusion(f32[1,2,32,64,128]{4,3,2,1,0:T(8,128)} %copy-done.2, f32[1,2,32,64,128]{4,3,2,1,0:T(8,128)S(1)} %fusion.50, f32[2,2,32]{2,1,0:T(2,128)S(1)} %exp.67), kind=kLoop, calls=%fused_computation.47 | loop fusion | flops 6291456 | bytes 8389120 | tf_op jit(solution)/shard_map/convert_element_type | solution.py:206
  54.3 1.9 fusion.57
  57.7 2.0 fusion.40
  59.8 2.1 add_bitcast_fusion
  62.0 18.1 %collective-permute-done.3 = bf16[2,2,32,32,128]{4,3,2,1,0:T(8,128)(2,1)S(1)} collective-permute-done((bf16[2,2,32,32,128]{4,3,2,1,0:T(8,128)(2,1)S(1)}, bf16[2,2,32,32,128]{4,3,2,1,0:T(8,128)(2,1)S(1)}, u32[]{:S(2)}, u32[]{:S(2)}) %collective-permute-start.3) | collective-permute-done | bytes 1048608 | tf_op jit(solution)/shard_map/ppermute | solution.py:74
  87.7 5.1 %collective-permute-done.9 = f32[4,4,2,32,64]{4,3,2,1,0:T(8,128)S(1)} collective-permute-done((f32[4,4,2,32,64]{4,3,2,1,0:T(8,128)S(1)}, f32[4,4,2,32,64]{4,3,2,1,0:T(8,128)S(1)}, u32[]{:S(2)}, u32[]{:S(2)}) %collective-permute-start.9) | collective-permute-done | bytes 262176 | tf_op jit(solution)/shard_map/ppermute | solution.py:105
  93.5 7.3 %collective-permute-done.10 = f32[2,4,2,32,64]{4,3,2,1,0:T(8,128)S(1)} collective-permute-done((f32[2,4,2,32,64]{4,3,2,1,0:T(8,128)S(1)}, f32[2,4,2,32,64]{4,3,2,1,0:T(8,128)S(1)}, u32[]{:S(2)}, u32[]{:S(2)}) %collective-permute-start.10) | collective-permute-done | bytes 131104 | tf_op jit(solution)/shard_map/ppermute | solution.py:105
  109.4 1.8 fusion.61
  112.8 2.3 %add_convert_fusion = bf16[2,2,32,32,128]{4,3,2,1,0:T(8,128)(2,1)S(1)} fusion(f32[2,2,32,32,128]{4,3,2,1,0:T(8,128)} %convert_element_type.140, f32[2,2,32]{2,1,0:T(2,128)} %get-tuple-element.40, f32[2,2,32,32,128]{4,3,2,1,0:T(8,128)S(1)} %copy-done.4, bf16[2,2,32,32,128]{4,3,2,1,0:T(8,128)(2,1)S(1)} %collective-permute-done.2, pred[]{:T(512)S(6)} %eq.15, ...), kind=kLoop, calls=%fused_computation.66 | loop fusion | flops 4194304 | bytes 6292481 | tf_op jit(solution)/shard_map/convert_element_type | solution.py:74
  116.7 2.7 %collective-permute-start.13 = (bf16[2,4,4096]{2,1,0:T(4,128)(2,1)S(1)}, bf16[2,4,4096]{2,1,0:T(4,128)(2,1)S(1)}, u32[]{:S(2)}, u32[]{:S(2)}) collective-permute-start(bf16[2,4,4096]{2,1,0:T(4,128)(2,1)S(1)} %maximum_select_fusion.2), channel_id=1, source_target_pairs={{0,4},{2,6},{4,0},{6,2},{8,12},{10,14},{12,8},{14,10},{1,5},{3,7},... | collective-permute-start | bytes 196616 | tf_op jit(solution)/shard_map/ppermute | solution.py:85
  119.4 7.8 %fusion.1 = f32[2,32,256,64]{2,3,1,0:T(8,128)} fusion(bf16[256,2,32,64]{0,3,2,1:T(8,128)(2,1)S(1)} %bitcast.184, f32[2,32,256]{2,1,0:T(8,128)} %bitcast.206, f32[2,32,256]{2,1,0:T(8,128)S(1)} %copy-done.23, f32[2,256,256]{2,1,0:T(8,128)} %fusion.89, pred[256,256]{1,0:T(8,128)(4,1)S(1)} %copy-done.22), kind=kOutput, calls=%fused_computation.3 | convolution fusion | flops 562036736 | bytes 7012352 | tf_op jit(solution)/shard_map/gkts,sgkp->tgkp/dot_general | solution.py:35
  128.0 12.7 %collective-permute-start.14 = (bf16[4,4,4096]{2,1,0:T(4,128)(2,1)S(1)}, bf16[4,4,4096]{2,1,0:T(4,128)(2,1)S(1)}, u32[]{:S(2)}, u32[]{:S(2)}) collective-permute-start(bf16[4,4,4096]{2,1,0:T(4,128)(2,1)S(1)} %maximum_select_fusion.1), channel_id=1, source_target_pairs={{0,8},{2,10},{4,12},{6,14},{8,0},{10,2},{12,4},{14,6},{1,9},{3,11}... | collective-permute-start | bytes 393224 | tf_op jit(solution)/shard_map/ppermute | solution.py:85
  140.7 21.2 %collective-permute-done.7 = bf16[2,2,32,32,128]{4,3,2,1,0:T(8,128)(2,1)S(1)} collective-permute-done((bf16[2,2,32,32,128]{4,3,2,1,0:T(8,128)(2,1)S(1)}, bf16[2,2,32,32,128]{4,3,2,1,0:T(8,128)(2,1)S(1)}, u32[]{:S(2)}, u32[]{:S(2)}) %collective-permute-start.7) | collective-permute-done | bytes 1048608 | tf_op jit(solution)/shard_map/ppermute | solution.py:74
  162.0 1.7 select_convert_fusion
  165.5 2.1 fusion.2
  167.6 4.7 %all-reduce.1 = bf16[8,4,1024]{2,0,1:T(8,128)(2,1)S(1)} all-reduce(f32[8,4,1024]{2,0,1:T(8,128)} %fusion.2), channel_id=1, replica_groups=mesh['groups'=2,'ctx'=8,'heads'=2] {'heads'}, use_global_device_ids=true, to_apply=%region_7.8 | all-reduce | flops 32768 | bytes 196608 | tf_op jit(solution)/shard_map/psum | solution.py:248
  173.0 12.8 %collective-permute-done.8 = bf16[2,2,32,32,128]{4,3,2,1,0:T(8,128)(2,1)} collective-permute-done((bf16[2,2,32,32,128]{4,3,2,1,0:T(8,128)(2,1)}, bf16[2,2,32,32,128]{4,3,2,1,0:T(8,128)(2,1)}, u32[]{:S(2)}, u32[]{:S(2)}) %collective-permute-start.8) | collective-permute-done | bytes 1048608 | tf_op jit(solution)/shard_map/ppermute | solution.py:74
  185.8 3.1 %convert_select_fusion.1 = (f32[2,2,32,32,128]{4,3,2,1,0:T(8,128)S(1)}, f32[2,2,32,32,128]{4,3,2,1,0:T(8,128)S(1)}) fusion(bf16[2,2,32,32,128]{4,3,2,1,0:T(8,128)(2,1)} %collective-permute-done.8, pred[]{:T(512)S(6)} %eq.15, f32[2,2,32,32,128]{4,3,2,1,0:T(8,128)S(1)} %copy-done.4, bf16[2,2,32,32,128]{4,3,2,1,0:T(8,128)(2,1)S(1)} %collective-permute-done.2, ...), kind=kLoop, calls=%fused_computation.44 | loop fusion | flops 5242880 | bytes 11535361 | tf_op jit(solution)/shard_map/jit(_where)/select_n | solution.py:149
  189.0 2.4 %convert_select_fusion = f32[2,2,32,32,128]{4,3,2,1,0:T(8,128)S(1)} fusion(f32[2,2,32,32,128]{4,3,2,1,0:T(8,128)S(1)} %get-tuple-element.15, bf16[2,2,32,32,128]{4,3,2,1,0:T(8,128)(2,1)} %collective-permute-done.8, pred[]{:T(512)S(6)} %eq.15), kind=kLoop, calls=%fused_computation.43 | loop fusion | flops 1048576 | bytes 5242881 | tf_op jit(solution)/shard_map/jit(_where)/select_n | solution.py:150
  191.7 3.9 %fusion.18 = bf16[256,2,32,64]{0,3,2,1:T(8,128)(2,1)} fusion(bf16[256,2,32,64]{0,3,2,1:T(8,128)(2,1)S(1)} %bitcast.181, f32[2,32,256,64]{2,3,1,0:T(8,128)S(1)} %copy-done.11, bf16[256,2,128,1]{0,2,3,1:T(8,128)(2,1)S(1)} %bitcast.193, f32[2,2,32,32,128]{4,3,2,1,0:T(8,128)S(1)} %get-tuple-element.14, f32[2,2,32,32,128]{4,3,2,1,0:T(8,128)S(1)} %convert_select_fusion, ...), kind=kOutput, calls=%fused_computation.29 | convolution fusion | flops 1617428480 | bytes 12779776 | tf_op jit(solution)/shard_map/tgn,gkpn->tgkp/dot_general | solution.py:52
  195.7 4.2 %copy.132 = bf16[1,256,4096]{2,1,0:T(8,128)(2,1)} copy(bf16[1,256,4096]{1,2,0:T(8,128)(2,1)} %bitcast.186) | data formatting | bytes 4194304 | tf_op jit(solution)/shard_map/convert_element_type | solution.py:59
  199.9 6.9 %fusion.21 = bf16[256,2,32,64]{0,3,2,1:T(8,128)(2,1)} fusion(bf16[256,2,32,64]{0,3,2,1:T(8,128)(2,1)} %bitcast.182, f32[2,32,256,64]{2,3,1,0:T(8,128)} %fusion.1, bf16[256,2,128,1]{0,2,3,1:T(8,128)(2,1)S(1)} %bitcast.195, f32[2,2,32,32,128]{4,3,2,1,0:T(8,128)S(1)} %convert_select_fusion, f32[2,2,32,32,128]{4,3,2,1,0:T(8,128)} %copy-done.9, ...), kind=kOutput, calls=%fused_computation.32 | convolution fusion | flops 1617428480 | bytes 12779776 | tf_op jit(solution)/shard_map/tgn,gkpn->tgkp/dot_general | solution.py:52
  206.8 4.2 %copy.133 = bf16[1,256,4096]{2,1,0:T(8,128)(2,1)} copy(bf16[1,256,4096]{1,2,0:T(8,128)(2,1)} %bitcast.185) | data formatting | bytes 4194304 | tf_op jit(solution)/shard_map/convert_element_type | solution.py:59
  211.1 4.0 %pad_maximum_fusion.1 = bf16[2,256,4096]{2,1,0:T(8,128)(2,1)} fusion(bf16[1,256,4096]{2,1,0:T(8,128)(2,1)} %copy.133, bf16[1,256,4096]{2,1,0:T(8,128)(2,1)S(1)} %copy-done.10), kind=kLoop, calls=%fused_computation.36 | loop fusion | flops 2097152 | bytes 8388608 | tf_op jit(solution)/shard_map/stack | solution.py:262
  (165 shorter events, 46.6 us)
Async XLA Ops:
  0.6 41.3 %copy-start = (bf16[1,4,256]{2,1,0:T(4,128)(2,1)S(1)}, bf16[1,4,256]{2,1,0:T(4,128)(2,1)}, u32[]{:S(2)}) copy-start(bf16[1,4,256]{2,1,0:T(4,128)(2,1)} %param.21) | copy-start | bytes 6148
  5.0 42.0 %collective-permute-start = (f32[2,2,32]{2,1,0:T(2,128)}, f32[2,2,32]{2,1,0:T(2,128)}, u32[]{:S(2)}, u32[]{:S(2)}) collective-permute-start(f32[2,2,32]{2,1,0:T(2,128)} %constant_dynamic-update-slice_fusion), channel_id=1, source_target_pairs={{0,2},{4,6},{8,10},{12,14},{2,0},{6,4},{10,8},{14,12},{1,3},{5,7},... | collective-permute-start | bytes 1544 | tf_op jit(solution)/shard_map/ppermute | solution.py:74
  8.8 33.3 %collective-permute-start.4 = (f32[1,1153]{1,0:T(1,128)S(1)}, f32[1,1153]{1,0:T(1,128)}, u32[]{:S(2)}, u32[]{:S(2)}) collective-permute-start(f32[1,1153]{1,0:T(1,128)S(1)} %broadcast_in_dim.74), channel_id=1, source_target_pairs={{0,2},{2,0},{4,6},{6,4},{8,10},{10,8},{12,14},{14,12},{1,3},{3,1},... | collective-permute-start | bytes 13844 | tf_op jit(solution)/shard_map/ppermute | solution.py:85
  25.0 5.4 %copy-start.27 = (f32[1,4,64]{2,1,0:T(4,128)S(1)}, f32[1,4,64]{2,1,0:T(4,128)}, u32[]{:S(2)}) copy-start(f32[1,4,64]{2,1,0:T(4,128)} %param.24) | copy-start | bytes 3076
  26.7 27.6 %collective-permute-start.2 = (bf16[2,2,32,32,128]{4,3,2,1,0:T(8,128)(2,1)}, bf16[2,2,32,32,128]{4,3,2,1,0:T(8,128)(2,1)S(1)}, u32[]{:S(2)}, u32[]{:S(2)}) collective-permute-start(bf16[2,2,32,32,128]{4,3,2,1,0:T(8,128)(2,1)} %select_convert_fusion.1), channel_id=1, source_target_pairs={{0,2},{4,6},{8,10},{12,14},{2,0},{6,4},{10,8},{14,12},{1,3},{5,7},... | collective-permute-start | bytes 3145736 | tf_op jit(solution)/shard_map/ppermute | solution.py:74
  34.1 7.9 %copy-start.26 = (bf16[1,4,256]{2,1,0:T(4,128)(2,1)S(1)}, bf16[1,4,256]{2,1,0:T(4,128)(2,1)}, u32[]{:S(2)}) copy-start(bf16[1,4,256]{2,1,0:T(4,128)(2,1)} %param.22) | copy-start | bytes 6148
  42.9 3.7 %collective-permute-start.5 = (f32[2,1153]{1,0:T(2,128)S(1)}, f32[2,1153]{1,0:T(2,128)S(1)}, u32[]{:S(2)}, u32[]{:S(2)}) collective-permute-start(f32[2,1153]{1,0:T(2,128)S(1)} %maximum_select_fusion.5), channel_id=1, source_target_pairs={{0,4},{2,6},{4,0},{6,2},{8,12},{10,14},{12,8},{14,10},{1,5},{3,7},... | collective-permute-start | bytes 27680 | tf_op jit(solution)/shard_map/ppermute | solution.py:85
  46.6 4.9 %collective-permute-start.6 = (f32[4,1153]{1,0:T(4,128)S(1)}, f32[4,1153]{1,0:T(4,128)S(1)}, u32[]{:S(2)}, u32[]{:S(2)}) collective-permute-start(f32[4,1153]{1,0:T(4,128)S(1)} %maximum_select_fusion.4), channel_id=1, source_target_pairs={{0,8},{2,10},{4,12},{6,14},{8,0},{10,2},{12,4},{14,6},{1,9},{3,11}... | collective-permute-start | bytes 55352 | tf_op jit(solution)/shard_map/ppermute | solution.py:85
  56.2 23.9 %collective-permute-start.3 = (bf16[2,2,32,32,128]{4,3,2,1,0:T(8,128)(2,1)S(1)}, bf16[2,2,32,32,128]{4,3,2,1,0:T(8,128)(2,1)S(1)}, u32[]{:S(2)}, u32[]{:S(2)}) collective-permute-start(bf16[2,2,32,32,128]{4,3,2,1,0:T(8,128)(2,1)S(1)} %get-tuple-element.18), channel_id=1, source_target_pairs={{0,4},{4,8},{8,12},{2,6},{6,10},{10,14},{1,5},{5,9},{9,13},{3,7},{... | collective-permute-start | bytes 3145736 | tf_op jit(solution)/shard_map/ppermute | solution.py:74
  82.9 9.9 %collective-permute-start.9 = (f32[4,4,2,32,64]{4,3,2,1,0:T(8,128)S(1)}, f32[4,4,2,32,64]{4,3,2,1,0:T(8,128)S(1)}, u32[]{:S(2)}, u32[]{:S(2)}) collective-permute-start(f32[4,4,2,32,64]{4,3,2,1,0:T(8,128)S(1)} %select_bitcast_fusion), channel_id=1, source_target_pairs={{0,2},{2,0},{4,6},{6,4},{8,10},{10,8},{12,14},{14,12},{1,3},{3,1},... | collective-permute-start | bytes 786440 | tf_op jit(solution)/shard_map/ppermute | solution.py:105
  86.6 6.9 %copy-start.13 = (bf16[1,256,256]{1,2,0:T(8,128)(2,1)}, bf16[1,256,256]{1,2,0:T(8,128)(2,1)S(1)}, u32[]{:S(2)}) copy-start(bf16[1,256,256]{1,2,0:T(8,128)(2,1)S(1)} %copy.178) | copy-start | bytes 393220
  86.6 6.8 %copy-start.25 = (f32[4,2,32]{2,1,0:T(2,128)S(1)}, f32[4,2,32]{2,1,0:T(2,128)}, u32[]{:S(2)}) copy-start(f32[4,2,32]{2,1,0:T(2,128)} %mul.260) | copy-start | bytes 3076
  86.6 6.8 %copy-start.29 = (pred[4,4]{1,0:T(4,128)(4,1)S(1)}, pred[4,4]{1,0:T(4,128)(4,1)}, u32[]{:S(2)}) copy-start(pred[4,4]{1,0:T(4,128)(4,1)} %iota_compare_fusion.1) | copy-start | bytes 52
  87.7 14.3 %copy-start.16 = (f32[4,2,32,64]{3,2,1,0:T(8,128)S(1)}, f32[4,2,32,64]{3,2,1,0:T(8,128)}, u32[]{:S(2)}) copy-start(f32[4,2,32,64]{3,2,1,0:T(8,128)} %reshape.342) | copy-start | bytes 196612
  92.9 19.8 %copy-start.4 = (f32[2,2,32,32,128]{4,3,2,1,0:T(8,128)S(1)}, f32[2,2,32,32,128]{4,3,2,1,0:T(8,128)}, u32[]{:S(2)}) copy-start(f32[2,2,32,32,128]{4,3,2,1,0:T(8,128)} %get-tuple-element.19) | copy-start | bytes 6291460
  93.0 7.8 %collective-permute-start.10 = (f32[2,4,2,32,64]{4,3,2,1,0:T(8,128)S(1)}, f32[2,4,2,32,64]{4,3,2,1,0:T(8,128)S(1)}, u32[]{:S(2)}, u32[]{:S(2)}) collective-permute-start(f32[2,4,2,32,64]{4,3,2,1,0:T(8,128)S(1)} %select_bitcast_fusion.1), channel_id=1, source_target_pairs={{0,4},{2,6},{4,0},{6,2},{8,12},{10,14},{12,8},{14,10},{1,5},{3,7},... | collective-permute-start | bytes 393224 | tf_op jit(solution)/shard_map/ppermute | solution.py:105
  101.6 7.9 %collective-permute-start.11 = (f32[1,4,2,32,64]{4,3,2,1,0:T(8,128)}, f32[1,4,2,32,64]{4,3,2,1,0:T(8,128)}, u32[]{:S(2)}, u32[]{:S(2)}) collective-permute-start(f32[1,4,2,32,64]{4,3,2,1,0:T(8,128)} %select_bitcast_fusion.2), channel_id=1, source_target_pairs={{0,8},{2,10},{4,12},{6,14},{8,0},{10,2},{12,4},{14,6},{1,9},{3,11}... | collective-permute-start | bytes 196616 | tf_op jit(solution)/shard_map/ppermute | solution.py:105
  108.1 19.1 %collective-permute-start.1 = (f32[2,2,32]{2,1,0:T(2,128)}, f32[2,2,32]{2,1,0:T(2,128)}, u32[]{:S(2)}, u32[]{:S(2)}) collective-permute-start(f32[2,2,32]{2,1,0:T(2,128)} %get-tuple-element.41), channel_id=1, source_target_pairs={{0,4},{4,8},{8,12},{2,6},{6,10},{10,14},{1,5},{5,9},{9,13},{3,7},{... | collective-permute-start | bytes 1544 | tf_op jit(solution)/shard_map/ppermute | solution.py:74
  112.2 4.4 %collective-permute-start.12 = (bf16[1,4,4096]{2,1,0:T(4,128)(2,1)S(1)}, bf16[1,4,4096]{2,1,0:T(4,128)(2,1)S(1)}, u32[]{:S(2)}, u32[]{:S(2)}) collective-permute-start(bf16[1,4,4096]{2,1,0:T(4,128)(2,1)S(1)} %convert_element_type.160), channel_id=1, source_target_pairs={{0,2},{2,0},{4,6},{6,4},{8,10},{10,8},{12,14},{14,12},{1,3},{3,1},... | collective-permute-start | bytes 98312 | tf_op jit(solution)/shard_map/ppermute | solution.py:85
  112.8 6.6 %copy-start.8 = (bf16[1,256,4096]{1,2,0:T(8,128)(2,1)S(1)}, bf16[1,256,4096]{1,2,0:T(8,128)(2,1)}, u32[]{:S(2)}) copy-start(bf16[1,256,4096]{1,2,0:T(8,128)(2,1)} %copy.118) | copy-start | bytes 6291460
  112.8 6.6 %copy-start.22 = (pred[256,256]{1,0:T(8,128)(4,1)S(1)}, pred[256,256]{1,0:T(8,128)(4,1)}, u32[]{:S(2)}) copy-start(pred[256,256]{1,0:T(8,128)(4,1)} %iota_compare_fusion) | copy-start | bytes 196612
  112.8 6.6 %copy-start.23 = (f32[2,32,256]{2,1,0:T(8,128)S(1)}, f32[2,32,256]{2,1,0:T(8,128)}, u32[]{:S(2)}) copy-start(f32[2,32,256]{2,1,0:T(8,128)} %reduce_window_sum.65) | copy-start | bytes 196612
  112.8 52.7 %slice-start = ((s8[8388608]{0:T(1024)(128)(4,1)}), s8[4194304]{0:T(1024)(128)(4,1)S(1)}, s32[]{:S(2)}) async-start(s8[8388608]{0:T(1024)(128)(4,1)} %bitcast.187), calls=%async_computation | async-start | bytes 8388608
  115.2 46.8 %collective-permute-start.7 = (bf16[2,2,32,32,128]{4,3,2,1,0:T(8,128)(2,1)S(1)}, bf16[2,2,32,32,128]{4,3,2,1,0:T(8,128)(2,1)S(1)}, u32[]{:S(2)}, u32[]{:S(2)}) collective-permute-start(bf16[2,2,32,32,128]{4,3,2,1,0:T(8,128)(2,1)S(1)} %add_convert_fusion), channel_id=1, source_target_pairs={{0,8},{4,12},{2,10},{6,14},{1,9},{5,13},{3,11},{7,15},{16,24},{20,... | collective-permute-start | bytes 3145736 | tf_op jit(solution)/shard_map/ppermute | solution.py:74
  116.7 11.2 %collective-permute-start.13 = (bf16[2,4,4096]{2,1,0:T(4,128)(2,1)S(1)}, bf16[2,4,4096]{2,1,0:T(4,128)(2,1)S(1)}, u32[]{:S(2)}, u32[]{:S(2)}) collective-permute-start(bf16[2,4,4096]{2,1,0:T(4,128)(2,1)S(1)} %maximum_select_fusion.2), channel_id=1, source_target_pairs={{0,4},{2,6},{4,0},{6,2},{8,12},{10,14},{12,8},{14,10},{1,5},{3,7},... | collective-permute-start | bytes 196616 | tf_op jit(solution)/shard_map/ppermute | solution.py:85
  119.4 42.6 %copy-start.5 = (f32[2,2,32,32,128]{4,3,2,1,0:T(8,128)S(1)}, f32[2,2,32,32,128]{4,3,2,1,0:T(8,128)}, u32[]{:S(2)}) copy-start(f32[2,2,32,32,128]{4,3,2,1,0:T(8,128)} %convert_element_type.140) | copy-start | bytes 6291460
  119.4 42.6 %copy-start.24 = (f32[2,2,32]{2,1,0:T(2,128)S(1)}, f32[2,2,32]{2,1,0:T(2,128)}, u32[]{:S(2)}) copy-start(f32[2,2,32]{2,1,0:T(2,128)} %get-tuple-element.38) | copy-start | bytes 1540
  119.4 46.1 %slice-start.1 = ((s8[8388608]{0:T(1024)(128)(4,1)}), s8[4194304]{0:T(1024)(128)(4,1)S(1)}, s32[]{:S(2)}) async-start(s8[8388608]{0:T(1024)(128)(4,1)} %bitcast.187), calls=%async_computation.1 | async-start | bytes 8388608
  128.0 37.1 %collective-permute-start.14 = (bf16[4,4,4096]{2,1,0:T(4,128)(2,1)S(1)}, bf16[4,4,4096]{2,1,0:T(4,128)(2,1)S(1)}, u32[]{:S(2)}, u32[]{:S(2)}) collective-permute-start(bf16[4,4,4096]{2,1,0:T(4,128)(2,1)S(1)} %maximum_select_fusion.1), channel_id=1, source_target_pairs={{0,8},{2,10},{4,12},{6,14},{8,0},{10,2},{12,4},{14,6},{1,9},{3,11}... | collective-permute-start | bytes 393224 | tf_op jit(solution)/shard_map/ppermute | solution.py:85
  163.7 22.1 %collective-permute-start.8 = (bf16[2,2,32,32,128]{4,3,2,1,0:T(8,128)(2,1)}, bf16[2,2,32,32,128]{4,3,2,1,0:T(8,128)(2,1)}, u32[]{:S(2)}, u32[]{:S(2)}) collective-permute-start(bf16[2,2,32,32,128]{4,3,2,1,0:T(8,128)(2,1)} %select_convert_fusion), channel_id=1, source_target_pairs={{0,2},{4,6},{8,10},{12,14},{2,0},{6,4},{10,8},{14,12},{1,3},{5,7},... | collective-permute-start | bytes 3145736 | tf_op jit(solution)/shard_map/ppermute | solution.py:74
  185.8 5.6 %copy-start.11 = (f32[2,32,256,64]{2,3,1,0:T(8,128)S(1)}, f32[2,32,256,64]{2,3,1,0:T(8,128)}, u32[]{:S(2)}) copy-start(f32[2,32,256,64]{2,3,1,0:T(8,128)} %fusion) | copy-start | bytes 12582916
  206.8 4.2 %copy-start.10 = (bf16[1,256,4096]{2,1,0:T(8,128)(2,1)S(1)}, bf16[1,256,4096]{2,1,0:T(8,128)(2,1)}, u32[]{:S(2)}) copy-start(bf16[1,256,4096]{2,1,0:T(8,128)(2,1)} %copy.132) | copy-start | bytes 6291460
  (15 other events, 44.3 us)

commit v6 on v5

--- a/solution.py
+++ b/solution.py
@@ -133,8 +133,6 @@
     while step < columns:
         pairs = [(y + 2 * m, y + 2 * (m + step)) for y in range(2) for m in range(columns - step)]
         got, got_total = send(window, window_total, pairs)
-        if step == 1:
-            got, rider = lax.optimization_barrier((got, rider))
         new_before = scale(jnp.exp(before_total), got) + before
         if 2 * step < columns:
             window = scale(jnp.exp(window_total), got) + window
@@ -148,6 +146,7 @@
     own_half = jnp.where(row_zero, before, odd_entering)
     first_half = jnp.where(row_zero, own_half, partner)
     second_half = jnp.where(row_zero, partner, own_half)
+    first_half, second_half, rider = lax.optimization_barrier((first_half, second_half, rider))
     return jnp.concatenate([first_half, second_half], axis=-2), rider
 
 

time: 216 us -> 242 us (1.12)
  the two profiles are of different devices: /device:TPU:26 before, /device:TPU:0 now
where the time goes in v6:
time: 242 us; the launch traced here: 240 us
  starting transfers between devices  61.9 us (26%)
  waiting for transfers between devices  60.7 us (25%)
  local copies, waits for them, and re-layouts  43 us (18%)
  matrix products  34.7 us (14%)
  other arithmetic  34.5 us (14%)
  blocking collectives  3.85 us (2%)
    ppermute x6, waiting for transfers between devices, send(): lax.ppermute((value.astype(jnp.bfloat16), total), 'ctx', pairs)  47.3 us
    ppermute x3, starting transfers between devices, reduce_scatter_ctx(): lax.ppermute(give, 'ctx', [(i, i ^ reach) for i in range(count)])  36.8 us
    ppermute x6, starting transfers between devices, send(): lax.ppermute((value.astype(jnp.bfloat16), total), 'ctx', pairs)  21.7 us
    dot_general x2, matrix products, block_terms(): jnp.einsum('gkts,sgkp->tgkp', mixing, inputs_head, preferred_element_type...  14.3 us
    convert_element_type x4, other arithmetic, send(): value.astype(jnp.bfloat16)  11.4 us
    slice x3, local copies, waits for them, and re-layouts, shards(): ssm_input[request]  10.5 us
    ppermute x3, waiting for transfers between devices, reduce_scatter_ctx(): lax.ppermute(give, 'ctx', [(i, i ^ reach) for i in range(count)])  10.3 us
    convert_element_type x2, local copies, waits for them, and re-layouts, finish(): return (local_out + carried + skipped).reshape(block_size, group_count *...  7.05 us
  transfers between devices with their start and end apart: 15, of which 7 were waited for; matrix products, arithmetic and copies ran while one was open for 40% of the time, Pallas kernels for 0%

profile of v6, /device:TPU:0, one launch (start us, length us, event | category | flops | bytes accessed | tf_op | source)
XLA Modules:
  0.0 240.4 jit_solution(12222772678798044019)
XLA Ops:
  4.9 3.0 %collective-permute-start = (f32[2,2,32]{2,1,0:T(2,128)}, f32[2,2,32]{2,1,0:T(2,128)}, u32[]{:S(2)}, u32[]{:S(2)}) collective-permute-start(f32[2,2,32]{2,1,0:T(2,128)} %constant_dynamic-update-slice_fusion), channel_id=1, source_target_pairs={{0,2},{4,6},{8,10},{12,14},{2,0},{6,4},{10,8},{14,12},{1,3},{5,7},... | collective-permute-start | bytes 1544 | tf_op jit(solution)/shard_map/ppermute | solution.py:74
  12.3 3.9 %fusion.76 = (bf16[1,256,4096]{2,1,0:T(8,128)(2,1)}, bf16[1,256,4096]{2,1,0:T(8,128)(2,1)S(1)}) fusion(bf16[2,256,4096]{2,1,0:T(8,128)(2,1)} %param.13), kind=kLoop, calls=%fused_computation.138 | loop fusion | bytes 8388608 | tf_op jit(solution)/shard_map/slice | solution.py:175
  16.3 4.1 %copy.113 = bf16[1,256,4096]{1,2,0:T(8,128)(2,1)} copy(bf16[1,256,4096]{2,1,0:T(8,128)(2,1)} %get-tuple-element.24) | data formatting | bytes 4194304 | tf_op jit(solution)/shard_map/slice | solution.py:175
  20.5 2.5 %copy.118 = bf16[1,256,4096]{1,2,0:T(8,128)(2,1)} copy(bf16[1,256,4096]{2,1,0:T(8,128)(2,1)S(1)} %get-tuple-element.25) | data formatting | bytes 4194304 | tf_op jit(solution)/shard_map/slice | solution.py:175
  23.2 2.5 %fusion.48 = f32[1,2,32,64,128]{4,3,2,1,0:T(8,128)S(1)} fusion(bf16[256,2,128,1]{0,2,3,1:T(8,128)(2,1)S(1)} %bitcast.192, bf16[256,2,32,64]{0,3,2,1:T(8,128)(2,1)} %bitcast.181, f32[256,2,32]{0,2,1:T(8,128)} %bitcast.197), kind=kOutput, calls=%fused_computation.71 | convolution fusion | flops 271581184 | bytes 4390912 | tf_op jit(solution)/shard_map/sgkp,sgn->gkpn/dot_general | solution.py:42
  28.0 2.0 collective-permute-start.2
  41.9 11.0 %collective-permute-done.2 = bf16[2,2,32,32,128]{4,3,2,1,0:T(8,128)(2,1)S(1)} collective-permute-done((bf16[2,2,32,32,128]{4,3,2,1,0:T(8,128)(2,1)}, bf16[2,2,32,32,128]{4,3,2,1,0:T(8,128)(2,1)S(1)}, u32[]{:S(2)}, u32[]{:S(2)}) %collective-permute-start.2) | collective-permute-done | bytes 1048608 | tf_op jit(solution)/shard_map/ppermute | solution.py:74
  52.9 3.8 %fusion.55 = (bf16[2,2,32,32,128]{4,3,2,1,0:T(8,128)(2,1)}, f32[2,2,32,32,128]{4,3,2,1,0:T(8,128)}) fusion(bf16[2,2,32,32,128]{4,3,2,1,0:T(8,128)(2,1)S(1)} %collective-permute-done.2, pred[]{:T(512)S(6)} %eq.15, f32[2,2,32]{2,1,0:T(2,128)S(1)} %get-tuple-element.41, f32[1,2,32,64,128]{4,3,2,1,0:T(8,128)} %copy-done.2, f32[1,2,32,64,128]{4,3,2,1,0:T(8,128)S(1)} %fusion.48), kind=kLoop, calls=%fused_computation.78 | loop fusion | flops 4718592 | bytes 8389121 | tf_op jit(solution)/shard_map/convert_element_type | solution.py:74
  56.7 4.7 %collective-permute-start.3 = (bf16[2,2,32,32,128]{4,3,2,1,0:T(8,128)(2,1)}, bf16[2,2,32,32,128]{4,3,2,1,0:T(8,128)(2,1)}, u32[]{:S(2)}, u32[]{:S(2)}) collective-permute-start(bf16[2,2,32,32,128]{4,3,2,1,0:T(8,128)(2,1)} %get-tuple-element.18), channel_id=1, source_target_pairs={{0,4},{4,8},{8,12},{2,6},{6,10},{10,14},{1,5},{5,9},{9,13},{3,7},{... | collective-permute-start | bytes 3145736 | tf_op jit(solution)/shard_map/ppermute | solution.py:74
  66.0 15.7 %collective-permute-done.3 = bf16[2,2,32,32,128]{4,3,2,1,0:T(8,128)(2,1)} collective-permute-done((bf16[2,2,32,32,128]{4,3,2,1,0:T(8,128)(2,1)}, bf16[2,2,32,32,128]{4,3,2,1,0:T(8,128)(2,1)}, u32[]{:S(2)}, u32[]{:S(2)}) %collective-permute-start.3) | collective-permute-done | bytes 1048608 | tf_op jit(solution)/shard_map/ppermute | solution.py:74
  81.7 3.7 %fusion.29 = bf16[2,2,32,32,128]{4,3,2,1,0:T(8,128)(2,1)} fusion(bf16[2,2,32,32,128]{4,3,2,1,0:T(8,128)(2,1)} %collective-permute-done.3, f32[2,2,32]{2,1,0:T(2,128)} %get-tuple-element.42, f32[2,2,32,32,128]{4,3,2,1,0:T(8,128)} %get-tuple-element.19, bf16[2,2,32,32,128]{4,3,2,1,0:T(8,128)(2,1)S(1)} %collective-permute-done.2, pred[]{:T(512)S(6)} %eq.15, ...), kind=kLoop, calls=%fused_computation.50 | loop fusion | flops 4718592 | bytes 5243905 | tf_op jit(solution)/shard_map/convert_element_type | solution.py:74
  85.4 6.3 %collective-permute-start.4 = (bf16[2,2,32,32,128]{4,3,2,1,0:T(8,128)(2,1)}, bf16[2,2,32,32,128]{4,3,2,1,0:T(8,128)(2,1)}, u32[]{:S(2)}, u32[]{:S(2)}) collective-permute-start(bf16[2,2,32,32,128]{4,3,2,1,0:T(8,128)(2,1)} %fusion.29), channel_id=1, source_target_pairs={{0,8},{4,12},{2,10},{6,14},{1,9},{5,13},{3,11},{7,15},{16,24},{20,... | collective-permute-start | bytes 3145736 | tf_op jit(solution)/shard_map/ppermute | solution.py:74
  93.6 4.2 %collective-permute-start.1 = (f32[2,2,32]{2,1,0:T(2,128)S(1)}, f32[2,2,32]{2,1,0:T(2,128)}, u32[]{:S(2)}, u32[]{:S(2)}) collective-permute-start(f32[2,2,32]{2,1,0:T(2,128)S(1)} %copy-done.29), channel_id=1, source_target_pairs={{0,4},{4,8},{8,12},{2,6},{6,10},{10,14},{1,5},{5,9},{9,13},{3,7},{... | collective-permute-start | bytes 1544 | tf_op jit(solution)/shard_map/ppermute | solution.py:74
  105.9 5.5 %collective-permute-done.1 = f32[2,2,32]{2,1,0:T(2,128)} collective-permute-done((f32[2,2,32]{2,1,0:T(2,128)S(1)}, f32[2,2,32]{2,1,0:T(2,128)}, u32[]{:S(2)}, u32[]{:S(2)}) %collective-permute-start.1) | collective-permute-done | bytes 544 | tf_op jit(solution)/shard_map/ppermute | solution.py:74
  115.6 2.5 %fusion.26 = (bf16[2,2,32,64,128,1]{4,3,2,1,0,5:T(8,128)(2,1)S(1)}, bf16[2,2,32,64,128,1]{4,3,2,1,0,5:T(8,128)(2,1)S(1)}) fusion(f32[1,2,32,64,128]{4,3,2,1,0:T(8,128)} %copy-done.2, f32[1,2,32,64,128]{4,3,2,1,0:T(8,128)S(1)} %fusion.48, f32[2,2,32]{2,1,0:T(2,128)S(1)} %exp.68), kind=kLoop, calls=%fused_computation.47 | loop fusion | flops 6291456 | bytes 8389120 | tf_op jit(solution)/shard_map/convert_element_type | solution.py:205
  118.2 2.3 select_convert_fusion
  124.9 2.1 add_bitcast_fusion
  127.1 15.1 %collective-permute-done.5 = bf16[2,2,32,32,128]{4,3,2,1,0:T(8,128)(2,1)S(1)} collective-permute-done((bf16[2,2,32,32,128]{4,3,2,1,0:T(8,128)(2,1)S(1)}, bf16[2,2,32,32,128]{4,3,2,1,0:T(8,128)(2,1)S(1)}, u32[]{:S(2)}, u32[]{:S(2)}) %collective-permute-start.5) | collective-permute-done | bytes 1048608 | tf_op jit(solution)/shard_map/ppermute | solution.py:74
  142.1 2.5 %convert_select_fusion = (f32[2,2,32,32,128]{4,3,2,1,0:T(8,128)S(1)}, f32[2,2,32,32,128]{4,3,2,1,0:T(8,128)S(1)}) fusion(bf16[2,2,32,32,128]{4,3,2,1,0:T(8,128)(2,1)S(1)} %collective-permute-done.5, pred[]{:T(512)S(6)} %eq.15, f32[2,2,32,32,128]{4,3,2,1,0:T(8,128)S(1)} %copy-done.3, bf16[2,2,32,32,128]{4,3,2,1,0:T(8,128)(2,1)S(1)} %collective-permute-done.2, ...), kind=kLoop, calls=%fused_computation.41 | loop fusion | flops 6291456 | bytes 10486785 | tf_op jit(solution)/shard_map/jit(_where)/select_n | solution.py:148
  147.8 7.5 %collective-permute-done.9 = f32[4,4,2,32,64]{4,3,2,1,0:T(8,128)S(1)} collective-permute-done((f32[4,4,2,32,64]{4,3,2,1,0:T(8,128)S(1)}, f32[4,4,2,32,64]{4,3,2,1,0:T(8,128)S(1)}, u32[]{:S(2)}, u32[]{:S(2)}) %collective-permute-start.9) | collective-permute-done | bytes 262176 | tf_op jit(solution)/shard_map/ppermute | solution.py:105
  155.4 31.4 %collective-permute-start.10 = (f32[2,4,2,32,64]{4,3,2,1,0:T(8,128)S(1)}, f32[2,4,2,32,64]{4,3,2,1,0:T(8,128)S(1)}, u32[]{:S(2)}, u32[]{:S(2)}) collective-permute-start(f32[2,4,2,32,64]{4,3,2,1,0:T(8,128)S(1)} %select_bitcast_fusion.1), channel_id=1, source_target_pairs={{0,4},{2,6},{4,0},{6,2},{8,12},{10,14},{12,8},{14,10},{1,5},{3,7},... | collective-permute-start | bytes 393224 | tf_op jit(solution)/shard_map/ppermute | solution.py:105
  188.8 2.8 %collective-permute-done.10 = f32[2,4,2,32,64]{4,3,2,1,0:T(8,128)S(1)} collective-permute-done((f32[2,4,2,32,64]{4,3,2,1,0:T(8,128)S(1)}, f32[2,4,2,32,64]{4,3,2,1,0:T(8,128)S(1)}, u32[]{:S(2)}, u32[]{:S(2)}) %collective-permute-start.10) | collective-permute-done | bytes 131104 | tf_op jit(solution)/shard_map/ppermute | solution.py:105
  191.6 3.8 %collective-permute-start.11 = (f32[1,4,2,32,64]{4,3,2,1,0:T(8,128)S(1)}, f32[1,4,2,32,64]{4,3,2,1,0:T(8,128)S(1)}, u32[]{:S(2)}, u32[]{:S(2)}) collective-permute-start(f32[1,4,2,32,64]{4,3,2,1,0:T(8,128)S(1)} %select_bitcast_fusion.2), channel_id=1, source_target_pairs={{0,8},{2,10},{4,12},{6,14},{8,0},{10,2},{12,4},{14,6},{1,9},{3,11}... | collective-permute-start | bytes 196616 | tf_op jit(solution)/shard_map/ppermute | solution.py:105
  195.4 7.3 %fusion.18 = bf16[256,2,32,64]{0,3,2,1:T(8,128)(2,1)} fusion(bf16[256,2,32,64]{0,3,2,1:T(8,128)(2,1)S(1)} %bitcast.182, f32[2,32,64,256]{3,2,1,0:T(8,128)S(1)} %fusion.37, f32[2,32,256]{2,1,0:T(8,128)S(1)} %bitcast.201, f32[2,32,256]{2,1,0:T(8,128)S(1)} %copy-done.21, f32[2,256,256]{2,1,0:T(8,128)S(1)} %copy-done.12, pred[256,256]{1,0:T(8,128)(4,1)S(1)} %copy-done.19, ...), kind=kOutput, calls=%fused_computation.29 | convolution fusion | flops 568328192 | bytes 9175296 | tf_op jit(solution)/shard_map/gkts,sgkp->tgkp/dot_general | solution.py:35
  204.6 3.6 %fusion.36 = f32[2,32,64,256]{3,2,1,0:T(8,128)S(1)} fusion(bf16[256,2,128,1]{0,2,3,1:T(8,128)(2,1)S(1)} %bitcast.189, f32[2,2,32,64,128]{4,3,2,1,0:T(8,128)} %copy-done.4), kind=kOutput, calls=%fused_computation.56 | convolution fusion | flops 1610612736 | bytes 6422528 | tf_op jit(solution)/shard_map/tgn,gkpn->tgkp/dot_general | solution.py:52
  209.1 7.1 %fusion.21 = bf16[256,2,32,64]{0,3,2,1:T(8,128)(2,1)} fusion(bf16[256,2,32,64]{0,3,2,1:T(8,128)(2,1)S(1)} %bitcast.180, f32[2,32,64,256]{3,2,1,0:T(8,128)S(1)} %fusion.36, f32[2,32,256]{2,1,0:T(8,128)S(1)} %bitcast.200, f32[2,32,256]{2,1,0:T(8,128)S(1)} %copy-done.20, f32[2,256,256]{2,1,0:T(8,128)S(1)} %copy-done.11, pred[256,256]{1,0:T(8,128)(4,1)S(1)} %copy-done.19, ...), kind=kOutput, calls=%fused_computation.32 | convolution fusion | flops 568328192 | bytes 9175296 | tf_op jit(solution)/shard_map/gkts,sgkp->tgkp/dot_general | solution.py:35
  216.1 2.9 %copy.132 = bf16[1,256,4096]{2,1,0:T(8,128)(2,1)S(1)} copy(bf16[1,256,4096]{1,2,0:T(8,128)(2,1)} %bitcast.186) | data formatting | bytes 4194304 | tf_op jit(solution)/shard_map/convert_element_type | solution.py:59
  219.0 4.1 %copy.133 = bf16[1,256,4096]{2,1,0:T(8,128)(2,1)} copy(bf16[1,256,4096]{1,2,0:T(8,128)(2,1)} %bitcast.187) | data formatting | bytes 4194304 | tf_op jit(solution)/shard_map/convert_element_type | solution.py:59
  223.6 4.0 %pad_maximum_fusion.1 = bf16[2,256,4096]{2,1,0:T(8,128)(2,1)} fusion(bf16[1,256,4096]{2,1,0:T(8,128)(2,1)} %copy.133, bf16[1,256,4096]{2,1,0:T(8,128)(2,1)S(1)} %copy.132), kind=kLoop, calls=%fused_computation.34 | loop fusion | flops 2097152 | bytes 8388608 | tf_op jit(solution)/shard_map/stack | solution.py:261
  227.6 3.1 %collective-permute-done.14 = bf16[4,4,4096]{2,1,0:T(4,128)(2,1)S(1)} collective-permute-done((bf16[4,4,4096]{2,1,0:T(4,128)(2,1)S(1)}, bf16[4,4,4096]{2,1,0:T(4,128)(2,1)S(1)}, u32[]{:S(2)}, u32[]{:S(2)}) %collective-permute-start.14) | collective-permute-done | bytes 131104 | tf_op jit(solution)/shard_map/ppermute | solution.py:85
  231.0 4.8 %fusion.2 = f32[8,4,1024]{2,0,1:T(8,128)S(1)} fusion(bf16[4096,1024]{1,0:T(8,128)(2,1)} %param.25, bf16[8,4,4096]{2,1,0:T(4,128)(2,1)S(1)} %maximum_select_fusion), kind=kOutput, calls=%fused_computation.4 | convolution fusion | flops 268435456 | bytes 8781824 | tf_op jit(solution)/shard_map/jup,pd->jud/dot_general | solution.py:241
  235.8 3.8 %all-reduce.1 = bf16[8,4,1024]{2,0,1:T(8,128)(2,1)S(1)} all-reduce(f32[8,4,1024]{2,0,1:T(8,128)S(1)} %fusion.2), channel_id=1, replica_groups=mesh['groups'=2,'ctx'=8,'heads'=2] {'heads'}, use_global_device_ids=true, to_apply=%region_7.8 | all-reduce | flops 32768 | bytes 196608 | tf_op jit(solution)/shard_map/psum | solution.py:247
  (164 shorter events, 55.1 us)
Async XLA Ops:
  0.6 30.9 %copy-start = (bf16[1,4,256]{2,1,0:T(4,128)(2,1)S(1)}, bf16[1,4,256]{2,1,0:T(4,128)(2,1)}, u32[]{:S(2)}) copy-start(bf16[1,4,256]{2,1,0:T(4,128)(2,1)} %param.21) | copy-start | bytes 6148
  4.9 35.7 %collective-permute-start = (f32[2,2,32]{2,1,0:T(2,128)}, f32[2,2,32]{2,1,0:T(2,128)}, u32[]{:S(2)}, u32[]{:S(2)}) collective-permute-start(f32[2,2,32]{2,1,0:T(2,128)} %constant_dynamic-update-slice_fusion), channel_id=1, source_target_pairs={{0,2},{4,6},{8,10},{12,14},{2,0},{6,4},{10,8},{14,12},{1,3},{5,7},... | collective-permute-start | bytes 1544 | tf_op jit(solution)/shard_map/ppermute | solution.py:74
  10.6 53.9 %collective-permute-start.6 = (f32[1,1153]{1,0:T(1,128)}, f32[1,1153]{1,0:T(1,128)}, u32[]{:S(2)}, u32[]{:S(2)}) collective-permute-start(f32[1,1153]{1,0:T(1,128)} %broadcast_in_dim.74), channel_id=1, source_target_pairs={{0,2},{2,0},{4,6},{6,4},{8,10},{10,8},{12,14},{14,12},{1,3},{3,1},... | collective-permute-start | bytes 13844 | tf_op jit(solution)/shard_map/ppermute | solution.py:85
  28.0 24.8 %collective-permute-start.2 = (bf16[2,2,32,32,128]{4,3,2,1,0:T(8,128)(2,1)}, bf16[2,2,32,32,128]{4,3,2,1,0:T(8,128)(2,1)S(1)}, u32[]{:S(2)}, u32[]{:S(2)}) collective-permute-start(bf16[2,2,32,32,128]{4,3,2,1,0:T(8,128)(2,1)} %select_convert_fusion.1), channel_id=1, source_target_pairs={{0,2},{4,6},{8,10},{12,14},{2,0},{6,4},{10,8},{14,12},{1,3},{5,7},... | collective-permute-start | bytes 3145736 | tf_op jit(solution)/shard_map/ppermute | solution.py:74
  41.9 14.8 %copy-start.26 = (f32[2,2,32]{2,1,0:T(2,128)}, f32[2,2,32]{2,1,0:T(2,128)S(1)}, u32[]{:S(2)}) copy-start(f32[2,2,32]{2,1,0:T(2,128)S(1)} %get-tuple-element.41) | copy-start | bytes 1540
  52.9 8.5 %copy-start.27 = (f32[4,2,32]{2,1,0:T(2,128)S(1)}, f32[4,2,32]{2,1,0:T(2,128)}, u32[]{:S(2)}) copy-start(f32[4,2,32]{2,1,0:T(2,128)} %mul.260) | copy-start | bytes 3076
  52.9 8.5 %copy-start.31 = (pred[4,4]{1,0:T(4,128)(4,1)S(1)}, pred[4,4]{1,0:T(4,128)(4,1)}, u32[]{:S(2)}) copy-start(pred[4,4]{1,0:T(4,128)(4,1)} %iota_compare_fusion.1) | copy-start | bytes 52
  52.9 9.7 %copy-start.9 = (bf16[1,256,256]{1,2,0:T(8,128)(2,1)S(1)}, bf16[1,256,256]{1,2,0:T(8,128)(2,1)}, u32[]{:S(2)}) copy-start(bf16[1,256,256]{1,2,0:T(8,128)(2,1)} %copy-done.8) | copy-start | bytes 393220
  52.9 10.8 %copy-start.13 = (f32[4,2,32,64]{3,2,1,0:T(8,128)S(1)}, f32[4,2,32,64]{3,2,1,0:T(8,128)}, u32[]{:S(2)}) copy-start(f32[4,2,32,64]{3,2,1,0:T(8,128)} %reshape.342) | copy-start | bytes 196612
  56.7 25.0 %collective-permute-start.3 = (bf16[2,2,32,32,128]{4,3,2,1,0:T(8,128)(2,1)}, bf16[2,2,32,32,128]{4,3,2,1,0:T(8,128)(2,1)}, u32[]{:S(2)}, u32[]{:S(2)}) collective-permute-start(bf16[2,2,32,32,128]{4,3,2,1,0:T(8,128)(2,1)} %get-tuple-element.18), channel_id=1, source_target_pairs={{0,4},{4,8},{8,12},{2,6},{6,10},{10,14},{1,5},{5,9},{9,13},{3,7},{... | collective-permute-start | bytes 3145736 | tf_op jit(solution)/shard_map/ppermute | solution.py:74
  65.3 27.1 %collective-permute-start.7 = (f32[2,1153]{1,0:T(2,128)S(1)}, f32[2,1153]{1,0:T(2,128)S(1)}, u32[]{:S(2)}, u32[]{:S(2)}) collective-permute-start(f32[2,1153]{1,0:T(2,128)S(1)} %maximum_select_fusion.5), channel_id=1, source_target_pairs={{0,4},{2,6},{4,0},{6,2},{8,12},{10,14},{12,8},{14,10},{1,5},{3,7},... | collective-permute-start | bytes 27680 | tf_op jit(solution)/shard_map/ppermute | solution.py:85
  81.7 11.8 %copy-start.29 = (f32[2,2,32]{2,1,0:T(2,128)S(1)}, f32[2,2,32]{2,1,0:T(2,128)}, u32[]{:S(2)}) copy-start(f32[2,2,32]{2,1,0:T(2,128)} %get-tuple-element.43) | copy-start | bytes 1540
  85.4 32.7 %collective-permute-start.4 = (bf16[2,2,32,32,128]{4,3,2,1,0:T(8,128)(2,1)}, bf16[2,2,32,32,128]{4,3,2,1,0:T(8,128)(2,1)}, u32[]{:S(2)}, u32[]{:S(2)}) collective-permute-start(bf16[2,2,32,32,128]{4,3,2,1,0:T(8,128)(2,1)} %fusion.29), channel_id=1, source_target_pairs={{0,8},{4,12},{2,10},{6,14},{1,9},{5,13},{3,11},{7,15},{16,24},{20,... | collective-permute-start | bytes 3145736 | tf_op jit(solution)/shard_map/ppermute | solution.py:74
  93.0 19.1 %collective-permute-start.8 = (f32[4,1153]{1,0:T(4,128)}, f32[4,1153]{1,0:T(4,128)}, u32[]{:S(2)}, u32[]{:S(2)}) collective-permute-start(f32[4,1153]{1,0:T(4,128)} %maximum_select_fusion.4), channel_id=1, source_target_pairs={{0,8},{2,10},{4,12},{6,14},{8,0},{10,2},{12,4},{14,6},{1,9},{3,11}... | collective-permute-start | bytes 55352 | tf_op jit(solution)/shard_map/ppermute | solution.py:85
  93.6 17.9 %collective-permute-start.1 = (f32[2,2,32]{2,1,0:T(2,128)S(1)}, f32[2,2,32]{2,1,0:T(2,128)}, u32[]{:S(2)}, u32[]{:S(2)}) collective-permute-start(f32[2,2,32]{2,1,0:T(2,128)S(1)} %copy-done.29), channel_id=1, source_target_pairs={{0,4},{4,8},{8,12},{2,6},{6,10},{10,14},{1,5},{5,9},{9,13},{3,7},{... | collective-permute-start | bytes 1544 | tf_op jit(solution)/shard_map/ppermute | solution.py:74
  120.5 21.7 %collective-permute-start.5 = (bf16[2,2,32,32,128]{4,3,2,1,0:T(8,128)(2,1)S(1)}, bf16[2,2,32,32,128]{4,3,2,1,0:T(8,128)(2,1)S(1)}, u32[]{:S(2)}, u32[]{:S(2)}) collective-permute-start(bf16[2,2,32,32,128]{4,3,2,1,0:T(8,128)(2,1)S(1)} %select_convert_fusion), channel_id=1, source_target_pairs={{0,2},{4,6},{8,10},{12,14},{2,0},{6,4},{10,8},{14,12},{1,3},{5,7},... | collective-permute-start | bytes 3145736 | tf_op jit(solution)/shard_map/ppermute | solution.py:74
  145.7 9.5 %collective-permute-start.9 = (f32[4,4,2,32,64]{4,3,2,1,0:T(8,128)S(1)}, f32[4,4,2,32,64]{4,3,2,1,0:T(8,128)S(1)}, u32[]{:S(2)}, u32[]{:S(2)}) collective-permute-start(f32[4,4,2,32,64]{4,3,2,1,0:T(8,128)S(1)} %select_bitcast_fusion), channel_id=1, source_target_pairs={{0,2},{2,0},{4,6},{6,4},{8,10},{10,8},{12,14},{14,12},{1,3},{3,1},... | collective-permute-start | bytes 786440 | tf_op jit(solution)/shard_map/ppermute | solution.py:105
  147.7 41.0 %copy-start.4 = (f32[2,2,32,64,128]{4,3,2,1,0:T(8,128)}, f32[2,2,32,64,128]{4,3,2,1,0:T(8,128)S(1)}, u32[]{:S(2)}) copy-start(f32[2,2,32,64,128]{4,3,2,1,0:T(8,128)S(1)} %constant_dynamic-update-slice_fusion.2) | copy-start | bytes 12582916
  155.4 36.1 %collective-permute-start.10 = (f32[2,4,2,32,64]{4,3,2,1,0:T(8,128)S(1)}, f32[2,4,2,32,64]{4,3,2,1,0:T(8,128)S(1)}, u32[]{:S(2)}, u32[]{:S(2)}) collective-permute-start(f32[2,4,2,32,64]{4,3,2,1,0:T(8,128)S(1)} %select_bitcast_fusion.1), channel_id=1, source_target_pairs={{0,4},{2,6},{4,0},{6,2},{8,12},{10,14},{12,8},{14,10},{1,5},{3,7},... | collective-permute-start | bytes 393224 | tf_op jit(solution)/shard_map/ppermute | solution.py:105
  186.8 8.6 %copy-start.7 = (bf16[1,256,4096]{1,2,0:T(8,128)(2,1)S(1)}, bf16[1,256,4096]{1,2,0:T(8,128)(2,1)}, u32[]{:S(2)}) copy-start(bf16[1,256,4096]{1,2,0:T(8,128)(2,1)} %copy.113) | copy-start | bytes 6291460
  186.8 8.6 %copy-start.12 = (f32[2,256,256]{2,1,0:T(8,128)S(1)}, f32[2,256,256]{2,1,0:T(8,128)}, u32[]{:S(2)}) copy-start(f32[2,256,256]{2,1,0:T(8,128)} %fusion.83) | copy-start | bytes 1572868
  186.8 8.6 %copy-start.19 = (pred[256,256]{1,0:T(8,128)(4,1)S(1)}, pred[256,256]{1,0:T(8,128)(4,1)}, u32[]{:S(2)}) copy-start(pred[256,256]{1,0:T(8,128)(4,1)} %iota_compare_fusion) | copy-start | bytes 196612
  186.8 8.6 %copy-start.21 = (f32[2,32,256]{2,1,0:T(8,128)S(1)}, f32[2,32,256]{2,1,0:T(8,128)}, u32[]{:S(2)}) copy-start(f32[2,32,256]{2,1,0:T(8,128)} %reduce_window_sum.61) | copy-start | bytes 196612
  186.8 8.6 %copy-start.23 = (f32[1,64,256]{2,1,0:T(8,128)S(1)}, f32[1,64,256]{2,1,0:T(8,128)}, u32[]{:S(2)}) copy-start(f32[1,64,256]{2,1,0:T(8,128)} %get-tuple-element.32) | copy-start | bytes 196612
  186.8 8.6 %copy-start.25 = (f32[64,256]{1,0:T(8,128)S(1)}, f32[64,256]{1,0:T(8,128)}, u32[]{:S(2)}) copy-start(f32[64,256]{1,0:T(8,128)} %get-tuple-element.39) | copy-start | bytes 196612
  186.8 8.6 %copy-start.30 = (f32[2,32]{1,0:T(2,128)S(1)}, f32[2,32]{1,0:T(2,128)}, u32[]{:S(2)}) copy-start(f32[2,32]{1,0:T(2,128)} %mul.243) | copy-start | bytes 772
  191.6 11.1 %collective-permute-start.11 = (f32[1,4,2,32,64]{4,3,2,1,0:T(8,128)S(1)}, f32[1,4,2,32,64]{4,3,2,1,0:T(8,128)S(1)}, u32[]{:S(2)}, u32[]{:S(2)}) collective-permute-start(f32[1,4,2,32,64]{4,3,2,1,0:T(8,128)S(1)} %select_bitcast_fusion.2), channel_id=1, source_target_pairs={{0,8},{2,10},{4,12},{6,14},{8,0},{10,2},{12,4},{14,6},{1,9},{3,11}... | collective-permute-start | bytes 196616 | tf_op jit(solution)/shard_map/ppermute | solution.py:105
  195.4 7.3 %copy-start.10 = (f32[4,2,32,64]{3,2,1,0:T(8,128)S(1)}, f32[4,2,32,64]{3,2,1,0:T(8,128)}, u32[]{:S(2)}) copy-start(f32[4,2,32,64]{3,2,1,0:T(8,128)} %multiply_reduce_fusion) | copy-start | bytes 196612
  203.0 5.2 %collective-permute-start.12 = (bf16[1,4,4096]{2,1,0:T(4,128)(2,1)S(1)}, bf16[1,4,4096]{2,1,0:T(4,128)(2,1)S(1)}, u32[]{:S(2)}, u32[]{:S(2)}) collective-permute-start(bf16[1,4,4096]{2,1,0:T(4,128)(2,1)S(1)} %convert_element_type.160), channel_id=1, source_target_pairs={{0,2},{2,0},{4,6},{6,4},{8,10},{10,8},{12,14},{14,12},{1,3},{3,1},... | collective-permute-start | bytes 98312 | tf_op jit(solution)/shard_map/ppermute | solution.py:85
  208.2 15.0 %collective-permute-start.13 = (bf16[2,4,4096]{2,1,0:T(4,128)(2,1)S(1)}, bf16[2,4,4096]{2,1,0:T(4,128)(2,1)S(1)}, u32[]{:S(2)}, u32[]{:S(2)}) collective-permute-start(bf16[2,4,4096]{2,1,0:T(4,128)(2,1)S(1)} %maximum_select_fusion.2), channel_id=1, source_target_pairs={{0,4},{2,6},{4,0},{6,2},{8,12},{10,14},{12,8},{14,10},{1,5},{3,7},... | collective-permute-start | bytes 196616 | tf_op jit(solution)/shard_map/ppermute | solution.py:85
  223.3 7.3 %collective-permute-start.14 = (bf16[4,4,4096]{2,1,0:T(4,128)(2,1)S(1)}, bf16[4,4,4096]{2,1,0:T(4,128)(2,1)S(1)}, u32[]{:S(2)}, u32[]{:S(2)}) collective-permute-start(bf16[4,4,4096]{2,1,0:T(4,128)(2,1)S(1)} %maximum_select_fusion.1), channel_id=1, source_target_pairs={{0,8},{2,10},{4,12},{6,14},{8,0},{10,2},{12,4},{14,6},{1,9},{3,11}... | collective-permute-start | bytes 393224 | tf_op jit(solution)/shard_map/ppermute | solution.py:85
  231.0 9.4 %copy-start.1 = (bf16[1,4,256]{2,1,0:T(4,128)(2,1)S(1)}, bf16[1,4,256]{2,1,0:T(4,128)(2,1)}, u32[]{:S(2)}) copy-start(bf16[1,4,256]{2,1,0:T(4,128)(2,1)} %param.21) | copy-start | bytes 6148
  (15 other events, 55.4 us)

commit v7 on v4

--- a/solution.py
+++ b/solution.py
@@ -33,7 +33,7 @@
         scores[:, None, :, :] * decay_rate.reshape(group_count, per_group, block_size, block_size)
     ).astype(jnp.bfloat16)
     local_out = jnp.einsum(
-        "gkts,sgkp->tgkp", mixing, inputs_head, preferred_element_type=jnp.float32
+        "gkts,sgkp->gktp", mixing, inputs_head, preferred_element_type=jnp.float32
     )
     weighting = jnp.exp(block_total[:, None] - cumulative) * block_step
     weighted = (weighting.T.reshape(block_size, group_count, per_group, 1) * inputs_head).astype(
@@ -45,19 +45,25 @@
     return (cumulative, block_total.reshape(group_count, per_group), local_out, block_state)
 
 
-def finish(local_out, cumulative, block_c, entering, block_input, skip_gain):
-    block_size = block_input.shape[0]
-    group_count, per_group = (entering.shape[0], entering.shape[1])
-    c_groups = block_c.reshape(block_size, group_count, STATE).astype(jnp.float32)
-    carried = jnp.einsum("tgn,gkpn->tgkp", c_groups, entering, precision=HIGH)
-    carried = carried * jnp.exp(cumulative).T.reshape(block_size, group_count, per_group, 1)
-    inputs_head = block_input.reshape(block_size, group_count, per_group, HEAD_DIM)
+def finish(local_out, cumulative, c_proj, entering, ssm_input, skip_gain):
+    request_count, group_count, per_group, block_size = local_out.shape[:4]
+    c_groups = c_proj.reshape(request_count, block_size, group_count, STATE)
+    flat = entering.reshape(request_count, group_count, per_group * HEAD_DIM, STATE)
+    high = flat.astype(jnp.bfloat16)
+    low = (flat - high.astype(jnp.float32)).astype(jnp.bfloat16)
+    numbers = (((3,), (3,)), ((0, 2), (0, 1)))
+    carried = lax.dot_general(
+        c_groups, high, numbers, preferred_element_type=jnp.float32
+    ) + lax.dot_general(c_groups, low, numbers, preferred_element_type=jnp.float32)
+    carried = carried.reshape(request_count, group_count, block_size, per_group, HEAD_DIM)
+    growth = jnp.exp(cumulative).reshape(request_count, group_count, per_group, block_size)
+    carried = carried * growth.transpose(0, 1, 3, 2)[..., None]
+    inputs_head = ssm_input.reshape(
+        request_count, block_size, group_count, per_group, HEAD_DIM
+    ).astype(jnp.float32)
     skipped = skip_gain.reshape(group_count, per_group, 1) * inputs_head
-    return (
-        (local_out + carried + skipped)
-        .reshape(block_size, group_count * per_group * HEAD_DIM)
-        .astype(jnp.bfloat16)
-    )
+    total = carried.transpose(0, 2, 1, 3, 4) + local_out.transpose(0, 3, 1, 2, 4) + skipped
+    return total.reshape(request_count, block_size, -1).astype(jnp.bfloat16)
 
 
 def range_decay(all_totals, low, high):
@@ -245,19 +251,14 @@
     decoded = lax.psum(partial_value, "heads").astype(jnp.bfloat16)
 
     entering = prefix_states(states, totals)
-    prefill_rows = []
-    for request in range(request_count):
-        prefill_rows.append(
-            finish(
-                terms[request][2],
-                terms[request][0],
-                c_proj[request],
-                entering[request],
-                ssm_input[request],
-                skip_gain,
-            )
-        )
-    prefill_out = jnp.stack(prefill_rows)
+    prefill_out = finish(
+        jnp.stack([term[2] for term in terms]),
+        jnp.stack([term[0] for term in terms]),
+        c_proj,
+        entering,
+        ssm_input,
+        skip_gain,
+    )
     return (prefill_out, decoded)
 
 

time: 213 us -> 212 us (level)
  the two profiles are of different devices: /device:TPU:24 before, /device:TPU:0 now
where the time goes in v7:
time: 212 us; the launch traced here: 210 us
  starting transfers between devices  51.2 us (24%)
  local copies, waits for them, and re-layouts  47.2 us (22%)
  other arithmetic  39.3 us (19%)
  matrix products  33.1 us (16%)
  waiting for transfers between devices  32.8 us (15%)
  blocking collectives  5.04 us (2%)
    ppermute x6, starting transfers between devices, gather_ctx(): got = lax.ppermute(value, 'ctx', [(i, i ^ reach) for i in range(count)])  26.1 us
    ppermute x3, waiting for transfers between devices, reduce_scatter_ctx(): lax.ppermute(give, 'ctx', [(i, i ^ reach) for i in range(count)])  24.4 us
    ppermute x6, starting transfers between devices, send(): lax.ppermute((value.astype(jnp.bfloat16), total), 'ctx', pairs)  20.7 us
    unnamed x74, local copies, waits for them, and re-layouts  17.4 us
    dot_general x2, matrix products, block_terms(): jnp.einsum('gkts,sgkp->gktp', mixing, inputs_head, preferred_element_type...  14.5 us
    slice x3, local copies, waits for them, and re-layouts, shards(): ssm_input[request]  10.5 us
    convert_element_type x4, other arithmetic, send(): value.astype(jnp.bfloat16)  9.85 us
    convert_element_type x1, local copies, waits for them, and re-layouts, finish(): inputs_head = ssm_input.reshape(request_count, block_size, group_count, p...  7.1 us
  transfers between devices with their start and end apart: 15, of which 6 were waited for; matrix products, arithmetic and copies ran while one was open for 43% of the time, Pallas kernels for 0%

profile of v7, /device:TPU:0, one launch (start us, length us, event | category | flops | bytes accessed | tf_op | source)
XLA Modules:
  0.0 210.5 jit_solution(11793994809875237968)
XLA Ops:
  5.0 3.0 %collective-permute-start = (f32[2,2,32]{2,1,0:T(2,128)}, f32[2,2,32]{2,1,0:T(2,128)}, u32[]{:S(2)}, u32[]{:S(2)}) collective-permute-start(f32[2,2,32]{2,1,0:T(2,128)} %constant_dynamic-update-slice_fusion), channel_id=1, source_target_pairs={{0,2},{4,6},{8,10},{12,14},{2,0},{6,4},{10,8},{14,12},{1,3},{5,7},... | collective-permute-start | bytes 1544 | tf_op jit(solution)/shard_map/ppermute | solution.py:80
  11.5 4.0 %fusion.69 = (bf16[1,256,4096]{2,1,0:T(8,128)(2,1)}, bf16[1,256,4096]{2,1,0:T(8,128)(2,1)S(1)}) fusion(bf16[2,256,4096]{2,1,0:T(8,128)(2,1)} %param.13), kind=kLoop, calls=%fused_computation.133 | loop fusion | bytes 8388608 | tf_op jit(solution)/shard_map/slice | solution.py:180
  15.5 4.1 %copy.150 = bf16[1,256,4096]{1,2,0:T(8,128)(2,1)} copy(bf16[1,256,4096]{2,1,0:T(8,128)(2,1)} %get-tuple-element.22) | data formatting | bytes 4194304 | tf_op jit(solution)/shard_map/slice | solution.py:180
  19.5 2.4 %copy.153 = bf16[1,256,4096]{1,2,0:T(8,128)(2,1)} copy(bf16[1,256,4096]{2,1,0:T(8,128)(2,1)S(1)} %get-tuple-element.23) | data formatting | bytes 4194304 | tf_op jit(solution)/shard_map/slice | solution.py:180
  22.0 2.5 %fusion.43 = f32[1,2,32,64,128]{4,3,2,1,0:T(8,128)S(1)} fusion(bf16[256,2,128,1]{0,2,3,1:T(8,128)(2,1)S(1)} %bitcast.180, bf16[256,2,32,64]{0,3,2,1:T(8,128)(2,1)} %bitcast.174, f32[256,2,32]{0,2,1:T(8,128)S(1)} %bitcast.187), kind=kOutput, calls=%fused_computation.66 | convolution fusion | flops 271581184 | bytes 4390912 | tf_op jit(solution)/shard_map/sgkp,sgn->gkpn/dot_general | solution.py:42
  26.9 2.0 collective-permute-start.2
  35.8 2.0 fusion.77
  39.1 7.9 %fusion.23 = f32[1,2,32,256,64]{3,4,2,1,0:T(8,128)} fusion(bf16[256,2,32,64]{0,3,2,1:T(8,128)(2,1)} %bitcast.175, f32[2,32,256]{2,1,0:T(8,128)} %bitcast.191, f32[2,32,256]{2,1,0:T(8,128)} %reduce_window_sum.88, f32[2,256,256]{2,1,0:T(8,128)S(1)} %fusion.76, pred[256,256]{1,0:T(8,128)(4,1)S(1)} %copy-done.18), kind=kOutput, calls=%fused_computation.44 | convolution fusion | flops 562036736 | bytes 7012352 | tf_op jit(solution)/shard_map/gkts,sgkp->gktp/dot_general | solution.py:35
  49.6 2.1 collective-permute-done.7
  51.7 2.7 %collective-permute-start.8 = (f32[4,1153]{1,0:T(4,128)S(1)}, f32[4,1153]{1,0:T(4,128)S(1)}, u32[]{:S(2)}, u32[]{:S(2)}) collective-permute-start(f32[4,1153]{1,0:T(4,128)S(1)} %maximum_select_fusion.4), channel_id=1, source_target_pairs={{0,8},{2,10},{4,12},{6,14},{8,0},{10,2},{12,4},{14,6},{1,9},{3,11}... | collective-permute-start | bytes 55352 | tf_op jit(solution)/shard_map/ppermute | solution.py:91
  54.4 2.1 collective-permute-done.8
  57.1 2.3 %fusion.24 = (bf16[2,2,32,64,128,1]{4,3,2,1,0,5:T(8,128)(2,1)S(1)}, bf16[2,2,32,64,128,1]{4,3,2,1,0,5:T(8,128)(2,1)S(1)}) fusion(f32[1,2,32,64,128]{4,3,2,1,0:T(8,128)} %copy-done.2, f32[1,2,32,64,128]{4,3,2,1,0:T(8,128)S(1)} %fusion.43, f32[2,2,32]{2,1,0:T(2,128)S(1)} %exp.69), kind=kLoop, calls=%fused_computation.45 | loop fusion | flops 6291456 | bytes 8389120 | tf_op jit(solution)/shard_map/convert_element_type | solution.py:210
  59.4 2.0 fusion.32
  61.4 2.1 add_bitcast_fusion
  68.5 8.6 %collective-permute-done.9 = f32[4,4,2,32,64]{4,3,2,1,0:T(8,128)} collective-permute-done((f32[4,4,2,32,64]{4,3,2,1,0:T(8,128)}, f32[4,4,2,32,64]{4,3,2,1,0:T(8,128)}, u32[]{:S(2)}, u32[]{:S(2)}) %collective-permute-start.9) | collective-permute-done | bytes 262176 | tf_op jit(solution)/shard_map/ppermute | solution.py:111
  80.3 2.1 %fusion.44 = (bf16[2,2,32,32,128]{4,3,2,1,0:T(8,128)(2,1)}, f32[2,2,32,32,128]{4,3,2,1,0:T(8,128)}) fusion(bf16[2,2,32,32,128]{4,3,2,1,0:T(8,128)(2,1)S(1)} %collective-permute-done.2, pred[]{:T(512)S(6)} %eq.15, f32[2,2,32]{2,1,0:T(2,128)S(1)} %get-tuple-element.37, f32[1,2,32,64,128]{4,3,2,1,0:T(8,128)S(1)} %copy-done.3, f32[1,2,32,64,128]{4,3,2,1,0:T(8,128)S(1)} %fusion.43), kind=kLoop, calls=%fused_computation.70 | loop fusion | flops 4718592 | bytes 8389121 | tf_op jit(solution)/shard_map/convert_element_type | solution.py:80
  82.5 3.5 %collective-permute-start.3 = (bf16[2,2,32,32,128]{4,3,2,1,0:T(8,128)(2,1)}, bf16[2,2,32,32,128]{4,3,2,1,0:T(8,128)(2,1)}, u32[]{:S(2)}, u32[]{:S(2)}) collective-permute-start(bf16[2,2,32,32,128]{4,3,2,1,0:T(8,128)(2,1)} %get-tuple-element.16), channel_id=1, source_target_pairs={{0,4},{4,8},{8,12},{2,6},{6,10},{10,14},{1,5},{5,9},{9,13},{3,7},{... | collective-permute-start | bytes 3145736 | tf_op jit(solution)/shard_map/ppermute | solution.py:80
  88.4 2.6 %collective-permute-start.11 = (f32[1,4,2,32,64]{4,3,2,1,0:T(8,128)}, f32[1,4,2,32,64]{4,3,2,1,0:T(8,128)}, u32[]{:S(2)}, u32[]{:S(2)}) collective-permute-start(f32[1,4,2,32,64]{4,3,2,1,0:T(8,128)} %select_bitcast_fusion.2), channel_id=1, source_target_pairs={{0,8},{2,10},{4,12},{6,14},{8,0},{10,2},{12,4},{14,6},{1,9},{3,11}... | collective-permute-start | bytes 196616 | tf_op jit(solution)/shard_map/ppermute | solution.py:111
  94.3 14.9 %collective-permute-done.11 = f32[1,4,2,32,64]{4,3,2,1,0:T(8,128)} collective-permute-done((f32[1,4,2,32,64]{4,3,2,1,0:T(8,128)}, f32[1,4,2,32,64]{4,3,2,1,0:T(8,128)}, u32[]{:S(2)}, u32[]{:S(2)}) %collective-permute-start.11) | collective-permute-done | bytes 65568 | tf_op jit(solution)/shard_map/ppermute | solution.py:111
  113.5 3.0 %fusion.27 = bf16[2,2,32,32,128]{4,3,2,1,0:T(8,128)(2,1)} fusion(bf16[2,2,32,32,128]{4,3,2,1,0:T(8,128)(2,1)} %collective-permute-done.3, f32[2,2,32]{2,1,0:T(2,128)} %get-tuple-element.38, f32[2,2,32,32,128]{4,3,2,1,0:T(8,128)S(1)} %copy-done.4, bf16[2,2,32,32,128]{4,3,2,1,0:T(8,128)(2,1)S(1)} %collective-permute-done.2, pred[]{:T(512)S(6)} %eq.15, ...), kind=kLoop, calls=%fused_computation.48 | loop fusion | flops 4718592 | bytes 5243905 | tf_op jit(solution)/shard_map/convert_element_type | solution.py:80
  116.6 6.3 %collective-permute-start.4 = (bf16[2,2,32,32,128]{4,3,2,1,0:T(8,128)(2,1)}, bf16[2,2,32,32,128]{4,3,2,1,0:T(8,128)(2,1)}, u32[]{:S(2)}, u32[]{:S(2)}) collective-permute-start(bf16[2,2,32,32,128]{4,3,2,1,0:T(8,128)(2,1)} %fusion.27), channel_id=1, source_target_pairs={{0,8},{4,12},{2,10},{6,14},{1,9},{5,13},{3,11},{7,15},{16,24},{20,... | collective-permute-start | bytes 3145736 | tf_op jit(solution)/shard_map/ppermute | solution.py:80
  122.9 6.6 %fusion.22 = f32[1,2,32,256,64]{3,4,2,1,0:T(8,128)} fusion(bf16[256,2,32,64]{0,3,2,1:T(8,128)(2,1)S(1)} %bitcast.173, f32[2,32,256]{2,1,0:T(8,128)S(1)} %bitcast.190, f32[2,32,256]{2,1,0:T(8,128)S(1)} %copy-done.20, f32[2,256,256]{2,1,0:T(8,128)S(1)} %copy-done.14, pred[256,256]{1,0:T(8,128)(4,1)S(1)} %copy-done.19), kind=kOutput, calls=%fused_computation.43 | convolution fusion | flops 562036736 | bytes 7012352 | tf_op jit(solution)/shard_map/gkts,sgkp->gktp/dot_general | solution.py:35
  130.9 4.4 %collective-permute-start.1 = (f32[2,2,32]{2,1,0:T(2,128)S(1)}, f32[2,2,32]{2,1,0:T(2,128)S(1)}, u32[]{:S(2)}, u32[]{:S(2)}) collective-permute-start(f32[2,2,32]{2,1,0:T(2,128)S(1)} %copy-done.29), channel_id=1, source_target_pairs={{0,4},{4,8},{8,12},{2,6},{6,10},{10,14},{1,5},{5,9},{9,13},{3,7},{... | collective-permute-start | bytes 1544 | tf_op jit(solution)/shard_map/ppermute | solution.py:80
  137.8 7.1 %copy.168 = f32[2,256,4096]{1,2,0:T(8,128)} copy(bf16[2,256,4096]{2,1,0:T(8,128)(2,1)} %param.13) | data formatting | bytes 12582912 | tf_op jit(solution)/shard_map/convert_element_type | solution.py:63
  146.0 21.1 %collective-permute-start.14 = (bf16[4,4,4096]{2,1,0:T(4,128)(2,1)S(1)}, bf16[4,4,4096]{2,1,0:T(4,128)(2,1)S(1)}, u32[]{:S(2)}, u32[]{:S(2)}) collective-permute-start(bf16[4,4,4096]{2,1,0:T(4,128)(2,1)S(1)} %maximum_select_fusion.1), channel_id=1, source_target_pairs={{0,8},{2,10},{4,12},{6,14},{8,0},{10,2},{12,4},{14,6},{1,9},{3,11}... | collective-permute-start | bytes 393224 | tf_op jit(solution)/shard_map/ppermute | solution.py:91
  167.1 3.3 %select_convert_fusion = bf16[2,2,32,32,128]{4,3,2,1,0:T(8,128)(2,1)} fusion(bf16[2,2,32,32,128]{4,3,2,1,0:T(8,128)(2,1)} %collective-permute-done.3, bf16[2,2,32,32,128]{4,3,2,1,0:T(8,128)(2,1)} %collective-permute-done.4, f32[2,2,32]{2,1,0:T(2,128)S(1)} %get-tuple-element.36, f32[2,2,32]{2,1,0:T(2,128)S(1)} %exp.58, pred[]{:T(512)S(6)} %eq.15, ...), kind=kLoop, calls=%fused_computation.58 | loop fusion | flops 5242880 | bytes 6292481 | tf_op jit(solution)/shard_map/convert_element_type | solution.py:80
  172.2 5.5 %fusion.5 = f32[8,4,1024]{2,0,1:T(8,128)} fusion(bf16[4096,1024]{1,0:T(8,128)(2,1)} %param.25, bf16[8,4,4096]{2,1,0:T(4,128)(2,1)S(1)} %maximum_select_fusion), kind=kOutput, calls=%fused_computation.8 | convolution fusion | flops 268435456 | bytes 8781824 | tf_op jit(solution)/shard_map/jup,pd->jud/dot_general | solution.py:245
  177.6 5.0 %all-reduce.1 = bf16[8,4,1024]{2,0,1:T(8,128)(2,1)} all-reduce(f32[8,4,1024]{2,0,1:T(8,128)} %fusion.5), channel_id=1, replica_groups=mesh['groups'=2,'ctx'=8,'heads'=2] {'heads'}, use_global_device_ids=true, to_apply=%region_7.8 | all-reduce | flops 32768 | bytes 196608 | tf_op jit(solution)/shard_map/psum | solution.py:251
  184.2 4.3 %collective-permute-done.5 = bf16[2,2,32,32,128]{4,3,2,1,0:T(8,128)(2,1)} collective-permute-done((bf16[2,2,32,32,128]{4,3,2,1,0:T(8,128)(2,1)}, bf16[2,2,32,32,128]{4,3,2,1,0:T(8,128)(2,1)}, u32[]{:S(2)}, u32[]{:S(2)}) %collective-permute-start.5) | collective-permute-done | bytes 1048608 | tf_op jit(solution)/shard_map/ppermute | solution.py:80
  188.5 2.8 %convert_select_fusion.1 = (f32[2,2,32,32,128]{4,3,2,1,0:T(8,128)S(1)}, f32[2,2,32,32,128]{4,3,2,1,0:T(8,128)S(1)}) fusion(bf16[2,2,32,32,128]{4,3,2,1,0:T(8,128)(2,1)} %collective-permute-done.5, pred[]{:T(512)S(6)} %eq.15, f32[2,2,32,32,128]{4,3,2,1,0:T(8,128)S(1)} %copy-done.4, bf16[2,2,32,32,128]{4,3,2,1,0:T(8,128)(2,1)S(1)} %collective-permute-done.2, ...), kind=kLoop, calls=%fused_computation.38 | loop fusion | flops 6291456 | bytes 10486785 | tf_op jit(solution)/shard_map/jit(_where)/select_n | solution.py:153
  198.2 6.0 %fusion.4 = bf16[2,256,2,32,64]{1,4,3,2,0:T(8,128)(2,1)} fusion(f32[1,2,32,256,64]{3,4,2,1,0:T(8,128)} %fusion.22, f32[1,2,32,256,64]{3,4,2,1,0:T(8,128)S(1)} %copy-done.8, f32[2,256,2,32,64]{1,4,3,2,0:T(8,128)S(1)} %bitcast.170, f32[2,2,256,32,64]{2,4,3,1,0:T(8,128)S(1)} %bitcast.167, f32[2,32]{1,0:T(2,128)S(1)} %copy-done.26, f32[2,2,256,32]{2,3,1,0:T(8,128)S(1)} %fusion.52), kind=kLoop, calls=%fused_computation.7 | loop fusion | flops 12582912 | bytes 29491456 | tf_op jit(solution)/shard_map/convert_element_type | solution.py:66
  204.2 6.3 %copy.183 = bf16[2,256,4096]{2,1,0:T(8,128)(2,1)} copy(bf16[2,256,4096]{1,2,0:T(8,128)(2,1)} %bitcast.171) | data formatting | bytes 8388608
  (172 shorter events, 54.1 us)
Async XLA Ops:
  0.6 46.3 %copy-start = (bf16[1,4,256]{2,1,0:T(4,128)(2,1)S(1)}, bf16[1,4,256]{2,1,0:T(4,128)(2,1)}, u32[]{:S(2)}) copy-start(bf16[1,4,256]{2,1,0:T(4,128)(2,1)} %param.21) | copy-start | bytes 6148
  0.6 10.6 %copy-start.16 = (bf16[2,256,256]{2,1,0:T(8,128)(2,1)S(1)}, bf16[2,256,256]{2,1,0:T(8,128)(2,1)}, u32[]{:S(2)}) copy-start(bf16[2,256,256]{2,1,0:T(8,128)(2,1)} %param.14) | copy-start | bytes 786436
  5.0 62.1 %collective-permute-start = (f32[2,2,32]{2,1,0:T(2,128)}, f32[2,2,32]{2,1,0:T(2,128)}, u32[]{:S(2)}, u32[]{:S(2)}) collective-permute-start(f32[2,2,32]{2,1,0:T(2,128)} %constant_dynamic-update-slice_fusion), channel_id=1, source_target_pairs={{0,2},{4,6},{8,10},{12,14},{2,0},{6,4},{10,8},{14,12},{1,3},{5,7},... | collective-permute-start | bytes 1544 | tf_op jit(solution)/shard_map/ppermute | solution.py:80
  10.2 37.0 %collective-permute-start.6 = (f32[1,1153]{1,0:T(1,128)S(1)}, f32[1,1153]{1,0:T(1,128)}, u32[]{:S(2)}, u32[]{:S(2)}) collective-permute-start(f32[1,1153]{1,0:T(1,128)S(1)} %broadcast_in_dim.75), channel_id=1, source_target_pairs={{0,2},{2,0},{4,6},{6,4},{8,10},{10,8},{12,14},{14,12},{1,3},{3,1},... | collective-permute-start | bytes 13844 | tf_op jit(solution)/shard_map/ppermute | solution.py:91
  11.4 10.6 %copy-start.11 = (bf16[1,256,256]{1,2,0:T(8,128)(2,1)}, bf16[1,256,256]{1,2,0:T(8,128)(2,1)S(1)}, u32[]{:S(2)}) copy-start(bf16[1,256,256]{1,2,0:T(8,128)(2,1)S(1)} %copy.209) | copy-start | bytes 393220
  11.5 12.9 %copy-start.12 = (bf16[1,256,256]{1,2,0:T(8,128)(2,1)}, bf16[1,256,256]{1,2,0:T(8,128)(2,1)S(1)}, u32[]{:S(2)}) copy-start(bf16[1,256,256]{1,2,0:T(8,128)(2,1)S(1)} %copy.210) | copy-start | bytes 393220
  26.9 53.4 %collective-permute-start.2 = (bf16[2,2,32,32,128]{4,3,2,1,0:T(8,128)(2,1)}, bf16[2,2,32,32,128]{4,3,2,1,0:T(8,128)(2,1)S(1)}, u32[]{:S(2)}, u32[]{:S(2)}) collective-permute-start(bf16[2,2,32,32,128]{4,3,2,1,0:T(8,128)(2,1)} %select_convert_fusion.1), channel_id=1, source_target_pairs={{0,2},{4,6},{8,10},{12,14},{2,0},{6,4},{10,8},{14,12},{1,3},{5,7},... | collective-permute-start | bytes 3145736 | tf_op jit(solution)/shard_map/ppermute | solution.py:80
  30.3 8.7 %copy-start.18 = (pred[256,256]{1,0:T(8,128)(4,1)S(1)}, pred[256,256]{1,0:T(8,128)(4,1)}, u32[]{:S(2)}) copy-start(pred[256,256]{1,0:T(8,128)(4,1)} %iota_compare_fusion) | copy-start | bytes 196612
  39.1 8.0 %copy-start.27 = (f32[1,4,64]{2,1,0:T(4,128)S(1)}, f32[1,4,64]{2,1,0:T(4,128)}, u32[]{:S(2)}) copy-start(f32[1,4,64]{2,1,0:T(4,128)} %param.24) | copy-start | bytes 3076
  48.0 3.7 %collective-permute-start.7 = (f32[2,1153]{1,0:T(2,128)S(1)}, f32[2,1153]{1,0:T(2,128)S(1)}, u32[]{:S(2)}, u32[]{:S(2)}) collective-permute-start(f32[2,1153]{1,0:T(2,128)S(1)} %maximum_select_fusion.5), channel_id=1, source_target_pairs={{0,4},{2,6},{4,0},{6,2},{8,12},{10,14},{12,8},{14,10},{1,5},{3,7},... | collective-permute-start | bytes 27680 | tf_op jit(solution)/shard_map/ppermute | solution.py:91
  51.7 4.7 %collective-permute-start.8 = (f32[4,1153]{1,0:T(4,128)S(1)}, f32[4,1153]{1,0:T(4,128)S(1)}, u32[]{:S(2)}, u32[]{:S(2)}) collective-permute-start(f32[4,1153]{1,0:T(4,128)S(1)} %maximum_select_fusion.4), channel_id=1, source_target_pairs={{0,8},{2,10},{4,12},{6,14},{8,0},{10,2},{12,4},{14,6},{1,9},{3,11}... | collective-permute-start | bytes 55352 | tf_op jit(solution)/shard_map/ppermute | solution.py:91
  66.0 11.1 %collective-permute-start.9 = (f32[4,4,2,32,64]{4,3,2,1,0:T(8,128)}, f32[4,4,2,32,64]{4,3,2,1,0:T(8,128)}, u32[]{:S(2)}, u32[]{:S(2)}) collective-permute-start(f32[4,4,2,32,64]{4,3,2,1,0:T(8,128)} %select_bitcast_fusion), channel_id=1, source_target_pairs={{0,2},{2,0},{4,6},{6,4},{8,10},{10,8},{12,14},{14,12},{1,3},{3,1},... | collective-permute-start | bytes 786440 | tf_op jit(solution)/shard_map/ppermute | solution.py:111
  67.1 13.2 %copy-start.3 = (f32[1,2,32,64,128]{4,3,2,1,0:T(8,128)S(1)}, f32[1,2,32,64,128]{4,3,2,1,0:T(8,128)}, u32[]{:S(2)}) copy-start(f32[1,2,32,64,128]{4,3,2,1,0:T(8,128)} %copy-done.2) | copy-start | bytes 6291460
  78.7 8.3 %collective-permute-start.10 = (f32[2,4,2,32,64]{4,3,2,1,0:T(8,128)S(1)}, f32[2,4,2,32,64]{4,3,2,1,0:T(8,128)S(1)}, u32[]{:S(2)}, u32[]{:S(2)}) collective-permute-start(f32[2,4,2,32,64]{4,3,2,1,0:T(8,128)S(1)} %select_bitcast_fusion.1), channel_id=1, source_target_pairs={{0,4},{2,6},{4,0},{6,2},{8,12},{10,14},{12,8},{14,10},{1,5},{3,7},... | collective-permute-start | bytes 393224 | tf_op jit(solution)/shard_map/ppermute | solution.py:111
  80.3 10.8 %copy-start.15 = (f32[4,2,32,64]{3,2,1,0:T(8,128)S(1)}, f32[4,2,32,64]{3,2,1,0:T(8,128)}, u32[]{:S(2)}) copy-start(f32[4,2,32,64]{3,2,1,0:T(8,128)} %reshape.383) | copy-start | bytes 196612
  80.3 12.4 %copy-start.30 = (f32[64]{0:T(128)S(1)}, f32[64]{0:T(128)}, u32[]{:S(2)}) copy-start(f32[64]{0:T(128)} %param.18) | copy-start | bytes 772
  82.5 31.0 %copy-start.4 = (f32[2,2,32,32,128]{4,3,2,1,0:T(8,128)S(1)}, f32[2,2,32,32,128]{4,3,2,1,0:T(8,128)}, u32[]{:S(2)}) copy-start(f32[2,2,32,32,128]{4,3,2,1,0:T(8,128)} %get-tuple-element.17) | copy-start | bytes 6291460
  82.5 31.0 %collective-permute-start.3 = (bf16[2,2,32,32,128]{4,3,2,1,0:T(8,128)(2,1)}, bf16[2,2,32,32,128]{4,3,2,1,0:T(8,128)(2,1)}, u32[]{:S(2)}, u32[]{:S(2)}) collective-permute-start(bf16[2,2,32,32,128]{4,3,2,1,0:T(8,128)(2,1)} %get-tuple-element.16), channel_id=1, source_target_pairs={{0,4},{4,8},{8,12},{2,6},{6,10},{10,14},{1,5},{5,9},{9,13},{3,7},{... | collective-permute-start | bytes 3145736 | tf_op jit(solution)/shard_map/ppermute | solution.py:80
  88.4 20.9 %collective-permute-start.11 = (f32[1,4,2,32,64]{4,3,2,1,0:T(8,128)}, f32[1,4,2,32,64]{4,3,2,1,0:T(8,128)}, u32[]{:S(2)}, u32[]{:S(2)}) collective-permute-start(f32[1,4,2,32,64]{4,3,2,1,0:T(8,128)} %select_bitcast_fusion.2), channel_id=1, source_target_pairs={{0,8},{2,10},{4,12},{6,14},{8,0},{10,2},{12,4},{14,6},{1,9},{3,11}... | collective-permute-start | bytes 196616 | tf_op jit(solution)/shard_map/ppermute | solution.py:111
  92.8 23.8 %copy-start.25 = (f32[2,32]{1,0:T(2,128)}, f32[2,32]{1,0:T(2,128)S(1)}, u32[]{:S(2)}) copy-start(f32[2,32]{1,0:T(2,128)S(1)} %mul.227) | copy-start | bytes 772
  112.8 22.5 %collective-permute-start.12 = (bf16[1,4,4096]{2,1,0:T(4,128)(2,1)}, bf16[1,4,4096]{2,1,0:T(4,128)(2,1)}, u32[]{:S(2)}, u32[]{:S(2)}) collective-permute-start(bf16[1,4,4096]{2,1,0:T(4,128)(2,1)} %convert_element_type.154), channel_id=1, source_target_pairs={{0,2},{2,0},{4,6},{6,4},{8,10},{10,8},{12,14},{14,12},{1,3},{3,1},... | collective-permute-start | bytes 98312 | tf_op jit(solution)/shard_map/ppermute | solution.py:91
  113.5 9.4 %copy-start.7 = (bf16[1,256,4096]{1,2,0:T(8,128)(2,1)S(1)}, bf16[1,256,4096]{1,2,0:T(8,128)(2,1)}, u32[]{:S(2)}) copy-start(bf16[1,256,4096]{1,2,0:T(8,128)(2,1)} %copy.153) | copy-start | bytes 6291460
  113.5 9.4 %copy-start.14 = (f32[2,256,256]{2,1,0:T(8,128)S(1)}, f32[2,256,256]{2,1,0:T(8,128)}, u32[]{:S(2)}) copy-start(f32[2,256,256]{2,1,0:T(8,128)} %fusion.77) | copy-start | bytes 1572868
  113.5 9.4 %copy-start.19 = (pred[256,256]{1,0:T(8,128)(4,1)S(1)}, pred[256,256]{1,0:T(8,128)(4,1)}, u32[]{:S(2)}) copy-start(pred[256,256]{1,0:T(8,128)(4,1)} %iota_compare_fusion) | copy-start | bytes 196612
  113.5 9.4 %copy-start.20 = (f32[2,32,256]{2,1,0:T(8,128)S(1)}, f32[2,32,256]{2,1,0:T(8,128)}, u32[]{:S(2)}) copy-start(f32[2,32,256]{2,1,0:T(8,128)} %reduce_window_sum.89) | copy-start | bytes 196612
  113.5 9.4 %copy-start.21 = (f32[1,64,256]{2,1,0:T(8,128)S(1)}, f32[1,64,256]{2,1,0:T(8,128)}, u32[]{:S(2)}) copy-start(f32[1,64,256]{2,1,0:T(8,128)} %get-tuple-element.35) | copy-start | bytes 196612
  116.6 50.5 %collective-permute-start.4 = (bf16[2,2,32,32,128]{4,3,2,1,0:T(8,128)(2,1)}, bf16[2,2,32,32,128]{4,3,2,1,0:T(8,128)(2,1)}, u32[]{:S(2)}, u32[]{:S(2)}) collective-permute-start(bf16[2,2,32,32,128]{4,3,2,1,0:T(8,128)(2,1)} %fusion.27), channel_id=1, source_target_pairs={{0,8},{4,12},{2,10},{6,14},{1,9},{5,13},{3,11},{7,15},{16,24},{20,... | collective-permute-start | bytes 3145736 | tf_op jit(solution)/shard_map/ppermute | solution.py:80
  122.9 8.0 %copy-start.29 = (f32[2,2,32]{2,1,0:T(2,128)S(1)}, f32[2,2,32]{2,1,0:T(2,128)}, u32[]{:S(2)}) copy-start(f32[2,2,32]{2,1,0:T(2,128)} %get-tuple-element.39) | copy-start | bytes 1540
  130.9 14.0 %collective-permute-start.1 = (f32[2,2,32]{2,1,0:T(2,128)S(1)}, f32[2,2,32]{2,1,0:T(2,128)S(1)}, u32[]{:S(2)}, u32[]{:S(2)}) collective-permute-start(f32[2,2,32]{2,1,0:T(2,128)S(1)} %copy-done.29), channel_id=1, source_target_pairs={{0,4},{4,8},{8,12},{2,6},{6,10},{10,14},{1,5},{5,9},{9,13},{3,7},{... | collective-permute-start | bytes 1544 | tf_op jit(solution)/shard_map/ppermute | solution.py:80
  136.9 8.0 %collective-permute-start.13 = (bf16[2,4,4096]{2,1,0:T(4,128)(2,1)}, bf16[2,4,4096]{2,1,0:T(4,128)(2,1)}, u32[]{:S(2)}, u32[]{:S(2)}) collective-permute-start(bf16[2,4,4096]{2,1,0:T(4,128)(2,1)} %maximum_select_fusion.2), channel_id=1, source_target_pairs={{0,4},{2,6},{4,0},{6,2},{8,12},{10,14},{12,8},{14,10},{1,5},{3,7},... | collective-permute-start | bytes 196616 | tf_op jit(solution)/shard_map/ppermute | solution.py:91
  146.0 25.9 %collective-permute-start.14 = (bf16[4,4,4096]{2,1,0:T(4,128)(2,1)S(1)}, bf16[4,4,4096]{2,1,0:T(4,128)(2,1)S(1)}, u32[]{:S(2)}, u32[]{:S(2)}) collective-permute-start(bf16[4,4,4096]{2,1,0:T(4,128)(2,1)S(1)} %maximum_select_fusion.1), channel_id=1, source_target_pairs={{0,8},{2,10},{4,12},{6,14},{8,0},{10,2},{12,4},{14,6},{1,9},{3,11}... | collective-permute-start | bytes 393224 | tf_op jit(solution)/shard_map/ppermute | solution.py:91
  170.4 18.1 %collective-permute-start.5 = (bf16[2,2,32,32,128]{4,3,2,1,0:T(8,128)(2,1)}, bf16[2,2,32,32,128]{4,3,2,1,0:T(8,128)(2,1)}, u32[]{:S(2)}, u32[]{:S(2)}) collective-permute-start(bf16[2,2,32,32,128]{4,3,2,1,0:T(8,128)(2,1)} %select_convert_fusion), channel_id=1, source_target_pairs={{0,2},{4,6},{8,10},{12,14},{2,0},{6,4},{10,8},{14,12},{1,3},{5,7},... | collective-permute-start | bytes 3145736 | tf_op jit(solution)/shard_map/ppermute | solution.py:80
  (16 other events, 63.1 us)

commit v8 on v7

--- a/solution.py
+++ b/solution.py
@@ -111,6 +111,13 @@
         value = keep + lax.ppermute(give, "ctx", [(i, i ^ reach) for i in range(count)])
         reach *= 2
     return value
+
+
+def exchange_ctx(value, total):
+    count = lax.axis_size("ctx")
+    got = lax.all_to_all(value, "ctx", 0, 0, tiled=True)
+    got = got.reshape((count, value.shape[0] // count) + value.shape[1:])
+    return jnp.sum(got, axis=0) if total else got.reshape(value.shape)
 
 
 def prefix_states(states, totals):
@@ -217,7 +224,7 @@
     for request in range(1, request_count):
         pick = (all_request == request)[:, None, None, None, None]
         contribution = jnp.where(pick, projected[request], contribution)
-    from_prompt = reduce_scatter_ctx(contribution)
+    from_prompt = exchange_ctx(contribution, True)
 
     row_input = new_input.reshape(slots, steps, group_count, per_group, HEAD_DIM).astype(
         jnp.float32
@@ -244,7 +251,7 @@
     new_output = value.reshape(slots, steps, -1).astype(jnp.bfloat16)
     partial_value = jnp.einsum(
         "jup,pd->jud",
-        gather_ctx(new_output),
+        exchange_ctx(jnp.concatenate([new_output] * count, axis=0), False),
         out_weight,
         preferred_element_type=jnp.float32,
     )

time: 212 us -> 222 us (1.047)
  the two profiles are of different devices: /device:TPU:0 before, /device:TPU:27 now
where the time goes in v8:
time: 222 us; the launch traced here: 221 us
  local copies, waits for them, and re-layouts  59.5 us (27%)
  waiting for transfers between devices  50 us (23%)
  other arithmetic  41.9 us (19%)
  matrix products  32.7 us (15%)
  starting transfers between devices  24 us (11%)
  blocking collectives  10.5 us (5%)
    ppermute x6, waiting for transfers between devices, send(): lax.ppermute((value.astype(jnp.bfloat16), total), 'ctx', pairs)  47.8 us
    unnamed x74, local copies, waits for them, and re-layouts  20.3 us
    all_to_all x2, starting transfers between devices, exchange_ctx(): got = lax.all_to_all(value, 'ctx', 0, 0, tiled=True)  16.2 us
    dot_general x2, matrix products, block_terms(): jnp.einsum('gkts,sgkp->gktp', mixing, inputs_head, preferred_element_type...  13.3 us
    convert_element_type x4, other arithmetic, send(): value.astype(jnp.bfloat16)  11.6 us
    psum x1, blocking collectives, shards(): decoded = lax.psum(partial_value, 'heads').astype(jnp.bfloat16)  10.5 us
    slice x3, local copies, waits for them, and re-layouts, shards(): ssm_input[request]  10.5 us
    ppermute x6, starting transfers between devices, send(): lax.ppermute((value.astype(jnp.bfloat16), total), 'ctx', pairs)  7.23 us
  transfers between devices with their start and end apart: 11, of which 3 were waited for; matrix products, arithmetic and copies ran while one was open for 47% of the time, Pallas kernels for 0%

profile of v8, /device:TPU:27, one launch (start us, length us, event | category | flops | bytes accessed | tf_op | source)
XLA Modules:
  0.0 220.5 jit_solution(2266539888242575711)
XLA Ops:
  10.6 4.0 %fusion.67 = (bf16[1,256,4096]{2,1,0:T(8,128)(2,1)}, bf16[1,256,4096]{2,1,0:T(8,128)(2,1)S(1)}) fusion(bf16[2,256,4096]{2,1,0:T(8,128)(2,1)} %param.13), kind=kLoop, calls=%fused_computation.122 | loop fusion | bytes 8388608 | tf_op jit(solution)/shard_map/slice | solution.py:187
  14.6 4.1 %copy.208 = bf16[1,256,4096]{1,2,0:T(8,128)(2,1)} copy(bf16[1,256,4096]{2,1,0:T(8,128)(2,1)} %get-tuple-element.26) | data formatting | bytes 4194304 | tf_op jit(solution)/shard_map/slice | solution.py:187
  18.7 2.4 %copy.211 = bf16[1,256,4096]{1,2,0:T(8,128)(2,1)} copy(bf16[1,256,4096]{2,1,0:T(8,128)(2,1)S(1)} %get-tuple-element.27) | data formatting | bytes 4194304 | tf_op jit(solution)/shard_map/slice | solution.py:187
  21.1 2.5 %fusion.43 = f32[1,2,32,64,128]{4,3,2,1,0:T(8,128)S(1)} fusion(bf16[256,2,128,1]{0,2,3,1:T(8,128)(2,1)S(1)} %bitcast.152, bf16[256,2,32,64]{0,3,2,1:T(8,128)(2,1)} %bitcast.149, f32[256,2,32]{0,2,1:T(8,128)S(1)} %bitcast.159), kind=kOutput, calls=%fused_computation.66 | convolution fusion | flops 271581184 | bytes 4390912 | tf_op jit(solution)/shard_map/sgkp,sgn->gkpn/dot_general | solution.py:42
  34.0 1.6 copy.275
  35.6 2.0 fusion.73
  37.6 2.0 fusion.72
  42.7 1.5 reshape.343
  47.2 2.2 collective-permute-done.8
  52.0 2.3 %fusion.24 = (bf16[2,2,32,64,128,1]{4,3,2,1,0,5:T(8,128)(2,1)S(1)}, bf16[2,2,32,64,128,1]{4,3,2,1,0,5:T(8,128)(2,1)S(1)}) fusion(f32[1,2,32,64,128]{4,3,2,1,0:T(8,128)} %copy-done.2, f32[1,2,32,64,128]{4,3,2,1,0:T(8,128)S(1)} %fusion.43, f32[2,2,32]{2,1,0:T(2,128)} %exp.69), kind=kLoop, calls=%fused_computation.45 | loop fusion | flops 6291456 | bytes 8389120 | tf_op jit(solution)/shard_map/convert_element_type | solution.py:217
  54.5 2.0 fusion.32
  56.5 2.1 add_bitcast_fusion
  60.0 2.7 %reshape.359 = f32[8,1,16384]{2,1,0:T(1,128)} reshape(f32[8,2,4,32,64]{4,3,2,1,0:T(8,128)} %bitcast.151) | data formatting | bytes 1048576
  62.7 5.2 %all-to-all-start = ((f32[8,1,16384]{2,1,0:T(1,128)}), f32[8,1,16384]{2,1,0:T(1,128)}, u32[]{:S(2)}, u32[]{:S(2)}) async-start(f32[8,1,16384]{2,1,0:T(1,128)} %reshape.359), calls=%async_computation | async-start | bytes 1048576 | tf_op jit(solution)/shard_map/all_to_all | solution.py:118
  68.0 3.9 %fusion.45 = (bf16[2,2,32,32,128]{4,3,2,1,0:T(8,128)(2,1)}, f32[2,2,32,32,128]{4,3,2,1,0:T(8,128)}) fusion(bf16[2,2,32,32,128]{4,3,2,1,0:T(8,128)(2,1)S(1)} %collective-permute-done.2, pred[]{:T(512)S(6)} %eq.15, f32[2,2,32]{2,1,0:T(2,128)S(1)} %copy-done.23, f32[1,2,32,64,128]{4,3,2,1,0:T(8,128)} %copy-done.2, f32[1,2,32,64,128]{4,3,2,1,0:T(8,128)S(1)} %fusion.43), kind=kLoop, calls=%fused_computation.72 | loop fusion | flops 4718592 | bytes 8389121 | tf_op jit(solution)/shard_map/convert_element_type | solution.py:80
  73.3 6.7 %fusion.23 = f32[1,2,32,256,64]{3,4,2,1,0:T(8,128)} fusion(bf16[256,2,32,64]{0,3,2,1:T(8,128)(2,1)S(1)} %bitcast.150, f32[2,32,256]{2,1,0:T(8,128)S(1)} %bitcast.163, f32[2,32,256]{2,1,0:T(8,128)S(1)} %copy-done.19, f32[2,256,256]{2,1,0:T(8,128)S(1)} %copy-done.14, pred[256,256]{1,0:T(8,128)(4,1)S(1)} %copy-done.17), kind=kOutput, calls=%fused_computation.44 | convolution fusion | flops 562036736 | bytes 7012352 | tf_op jit(solution)/shard_map/gkts,sgkp->gktp/dot_general | solution.py:35
  84.7 13.9 %collective-permute-done.1 = f32[2,2,32]{2,1,0:T(2,128)} collective-permute-done((f32[2,2,32]{2,1,0:T(2,128)}, f32[2,2,32]{2,1,0:T(2,128)}, u32[]{:S(2)}, u32[]{:S(2)}) %collective-permute-start.1) | collective-permute-done | bytes 544 | tf_op jit(solution)/shard_map/ppermute | solution.py:80
  99.8 3.8 %reduce.16 = f32[8,16384]{1,0:T(8,128)} reduce(f32[8,1,16384]{2,1,0:T(1,128)} %all-to-all-done, f32[]{:T(128)} %broadcast.165), dimensions={1}, to_apply=%all_to_all.6.reduce_sub_computation | reduce | bytes 1048580 | tf_op jit(solution)/shard_map/all_to_all | solution.py:118
  103.6 2.5 %reshape.360 = f32[8,2,4,32,64]{4,3,2,1,0:T(8,128)} reshape(f32[8,16384]{1,0:T(8,128)} %reduce.16) | data formatting | bytes 1048576
  107.5 2.9 %fusion.27 = bf16[2,2,32,32,128]{4,3,2,1,0:T(8,128)(2,1)} fusion(bf16[2,2,32,32,128]{4,3,2,1,0:T(8,128)(2,1)} %collective-permute-done.3, f32[2,2,32]{2,1,0:T(2,128)} %get-tuple-element.40, f32[2,2,32,32,128]{4,3,2,1,0:T(8,128)S(1)} %copy-done.3, bf16[2,2,32,32,128]{4,3,2,1,0:T(8,128)(2,1)S(1)} %collective-permute-done.2, pred[]{:T(512)S(6)} %eq.15, ...), kind=kLoop, calls=%fused_computation.48 | loop fusion | flops 4718592 | bytes 5243905 | tf_op jit(solution)/shard_map/convert_element_type | solution.py:80
  112.5 1.6 add.79
  115.8 11.0 %all-to-all-start.1 = ((bf16[8,4,4096]{2,1,0:T(4,128)(2,1)}), bf16[8,4,4096]{2,1,0:T(4,128)(2,1)}, u32[]{:S(2)}, u32[]{:S(2)}) async-start(bf16[8,4,4096]{2,1,0:T(4,128)(2,1)} %concatenate.36), calls=%async_computation.1 | async-start | bytes 524288 | tf_op jit(solution)/shard_map/all_to_all | solution.py:118
  126.8 33.9 %collective-permute-done.4 = bf16[2,2,32,32,128]{4,3,2,1,0:T(8,128)(2,1)} collective-permute-done((bf16[2,2,32,32,128]{4,3,2,1,0:T(8,128)(2,1)}, bf16[2,2,32,32,128]{4,3,2,1,0:T(8,128)(2,1)}, u32[]{:S(2)}, u32[]{:S(2)}) %collective-permute-start.4) | collective-permute-done | bytes 1048608 | tf_op jit(solution)/shard_map/ppermute | solution.py:80
  160.7 3.4 %select_convert_fusion = bf16[2,2,32,32,128]{4,3,2,1,0:T(8,128)(2,1)} fusion(bf16[2,2,32,32,128]{4,3,2,1,0:T(8,128)(2,1)} %collective-permute-done.3, bf16[2,2,32,32,128]{4,3,2,1,0:T(8,128)(2,1)} %collective-permute-done.4, f32[2,2,32]{2,1,0:T(2,128)S(1)} %get-tuple-element.38, f32[2,2,32]{2,1,0:T(2,128)S(1)} %exp.58, pred[]{:T(512)S(6)} %eq.15, ...), kind=kLoop, calls=%fused_computation.58 | loop fusion | flops 5242880 | bytes 6292481 | tf_op jit(solution)/shard_map/convert_element_type | solution.py:80
  164.9 6.6 %fusion.22 = f32[1,2,32,256,64]{3,4,2,1,0:T(8,128)} fusion(bf16[256,2,32,64]{0,3,2,1:T(8,128)(2,1)S(1)} %bitcast.148, f32[2,32,256]{2,1,0:T(8,128)S(1)} %bitcast.162, f32[2,32,256]{2,1,0:T(8,128)S(1)} %copy-done.20, f32[2,256,256]{2,1,0:T(8,128)S(1)} %copy-done.13, pred[256,256]{1,0:T(8,128)(4,1)S(1)} %copy-done.18), kind=kOutput, calls=%fused_computation.43 | convolution fusion | flops 562036736 | bytes 7012352 | tf_op jit(solution)/shard_map/gkts,sgkp->gktp/dot_general | solution.py:35
  172.9 7.1 %copy.226 = f32[2,256,4096]{1,2,0:T(8,128)} copy(bf16[2,256,4096]{2,1,0:T(8,128)(2,1)} %param.13) | data formatting | bytes 12582912 | tf_op jit(solution)/shard_map/convert_element_type | solution.py:63
  180.9 5.6 %fusion.5 = f32[8,4,1024]{2,0,1:T(8,128)} fusion(bf16[4096,1024]{1,0:T(8,128)(2,1)} %param.25, bf16[8,4,4096]{2,1,0:T(4,128)(2,1)} %all-to-all-done.1), kind=kOutput, calls=%fused_computation.8 | convolution fusion | flops 268435456 | bytes 8781824 | tf_op jit(solution)/shard_map/jup,pd->jud/dot_general | solution.py:252
  186.4 10.5 %all-reduce.1 = bf16[8,4,1024]{2,0,1:T(8,128)(2,1)} all-reduce(f32[8,4,1024]{2,0,1:T(8,128)} %fusion.5), channel_id=1, replica_groups=mesh['groups'=2,'ctx'=8,'heads'=2] {'heads'}, use_global_device_ids=true, to_apply=%region_8.9 | all-reduce | flops 32768 | bytes 196608 | tf_op jit(solution)/shard_map/psum | solution.py:258
  197.0 1.5 copy.245
  198.5 2.8 %convert_select_fusion.1 = (f32[2,2,32,32,128]{4,3,2,1,0:T(8,128)S(1)}, f32[2,2,32,32,128]{4,3,2,1,0:T(8,128)S(1)}) fusion(bf16[2,2,32,32,128]{4,3,2,1,0:T(8,128)(2,1)} %collective-permute-done.5, pred[]{:T(512)S(6)} %eq.15, f32[2,2,32,32,128]{4,3,2,1,0:T(8,128)S(1)} %copy-done.3, bf16[2,2,32,32,128]{4,3,2,1,0:T(8,128)(2,1)S(1)} %collective-permute-done.2, ...), kind=kLoop, calls=%fused_computation.38 | loop fusion | flops 6291456 | bytes 10486785 | tf_op jit(solution)/shard_map/jit(_where)/select_n | solution.py:160
  208.2 6.0 %fusion.4 = bf16[2,256,2,32,64]{1,4,3,2,0:T(8,128)(2,1)} fusion(f32[1,2,32,256,64]{3,4,2,1,0:T(8,128)} %fusion.22, f32[1,2,32,256,64]{3,4,2,1,0:T(8,128)S(1)} %copy-done.7, f32[2,256,2,32,64]{1,4,3,2,0:T(8,128)S(1)} %bitcast.145, f32[2,2,256,32,64]{2,4,3,1,0:T(8,128)S(1)} %bitcast.142, f32[2,32]{1,0:T(2,128)S(1)} %copy-done.27, f32[2,2,256,32]{2,3,1,0:T(8,128)S(1)} %fusion.52), kind=kLoop, calls=%fused_computation.7 | loop fusion | flops 12582912 | bytes 29491456 | tf_op jit(solution)/shard_map/convert_element_type | solution.py:66
  214.2 6.3 %copy.244 = bf16[2,256,4096]{2,1,0:T(8,128)(2,1)} copy(bf16[2,256,4096]{1,2,0:T(8,128)(2,1)} %bitcast.146) | data formatting | bytes 8388608
  (163 shorter events, 52.0 us)
Async XLA Ops:
  0.6 29.3 %copy-start = (bf16[1,4,256]{2,1,0:T(4,128)(2,1)S(1)}, bf16[1,4,256]{2,1,0:T(4,128)(2,1)}, u32[]{:S(2)}) copy-start(bf16[1,4,256]{2,1,0:T(4,128)(2,1)} %param.21) | copy-start | bytes 6148
  0.6 9.7 %copy-start.16 = (bf16[2,256,256]{2,1,0:T(8,128)(2,1)S(1)}, bf16[2,256,256]{2,1,0:T(8,128)(2,1)}, u32[]{:S(2)}) copy-start(bf16[2,256,256]{2,1,0:T(8,128)(2,1)} %param.14) | copy-start | bytes 786436
  5.1 40.8 %collective-permute-start = (f32[2,2,32]{2,1,0:T(2,128)}, f32[2,2,32]{2,1,0:T(2,128)}, u32[]{:S(2)}, u32[]{:S(2)}) collective-permute-start(f32[2,2,32]{2,1,0:T(2,128)} %constant_dynamic-update-slice_fusion), channel_id=1, source_target_pairs={{0,2},{4,6},{8,10},{12,14},{2,0},{6,4},{10,8},{14,12},{1,3},{5,7},... | collective-permute-start | bytes 1544 | tf_op jit(solution)/shard_map/ppermute | solution.py:80
  9.1 32.0 %collective-permute-start.6 = (f32[1,1153]{1,0:T(1,128)}, f32[1,1153]{1,0:T(1,128)}, u32[]{:S(2)}, u32[]{:S(2)}) collective-permute-start(f32[1,1153]{1,0:T(1,128)} %broadcast_in_dim.75), channel_id=1, source_target_pairs={{0,2},{2,0},{4,6},{6,4},{8,10},{10,8},{12,14},{14,12},{1,3},{3,1},... | collective-permute-start | bytes 13844 | tf_op jit(solution)/shard_map/ppermute | solution.py:91
  10.5 10.6 %copy-start.9 = (bf16[1,256,256]{1,2,0:T(8,128)(2,1)}, bf16[1,256,256]{1,2,0:T(8,128)(2,1)S(1)}, u32[]{:S(2)}) copy-start(bf16[1,256,256]{1,2,0:T(8,128)(2,1)S(1)} %copy.271) | copy-start | bytes 393220
  10.6 13.0 %copy-start.10 = (bf16[1,256,256]{1,2,0:T(8,128)(2,1)}, bf16[1,256,256]{1,2,0:T(8,128)(2,1)S(1)}, u32[]{:S(2)}) copy-start(bf16[1,256,256]{1,2,0:T(8,128)(2,1)S(1)} %copy.272) | copy-start | bytes 393220
  24.3 4.9 %copy-start.11 = (f32[2,64,256]{2,1,0:T(8,128)S(1)}, f32[2,64,256]{2,1,0:T(8,128)}, u32[]{:S(2)}) copy-start(f32[2,64,256]{2,1,0:T(8,128)} %param.16) | copy-start | bytes 393220
  24.4 5.6 %copy-start.25 = (bf16[1,4,256]{2,1,0:T(4,128)(2,1)S(1)}, bf16[1,4,256]{2,1,0:T(4,128)(2,1)}, u32[]{:S(2)}) copy-start(bf16[1,4,256]{2,1,0:T(4,128)(2,1)} %param.22) | copy-start | bytes 6148
  24.4 6.4 %copy-start.28 = (f32[1,4,64]{2,1,0:T(4,128)S(1)}, f32[1,4,64]{2,1,0:T(4,128)}, u32[]{:S(2)}) copy-start(f32[1,4,64]{2,1,0:T(4,128)} %param.23) | copy-start | bytes 3076
  24.4 7.8 %copy-start.8 = (bf16[2,256,256]{2,1,0:T(8,128)(2,1)S(1)}, bf16[2,256,256]{2,1,0:T(8,128)(2,1)}, u32[]{:S(2)}) copy-start(bf16[2,256,256]{2,1,0:T(8,128)(2,1)} %param.15) | copy-start | bytes 786436
  26.0 41.9 %collective-permute-start.2 = (bf16[2,2,32,32,128]{4,3,2,1,0:T(8,128)(2,1)}, bf16[2,2,32,32,128]{4,3,2,1,0:T(8,128)(2,1)S(1)}, u32[]{:S(2)}, u32[]{:S(2)}) collective-permute-start(bf16[2,2,32,32,128]{4,3,2,1,0:T(8,128)(2,1)} %select_convert_fusion.1), channel_id=1, source_target_pairs={{0,2},{4,6},{8,10},{12,14},{2,0},{6,4},{10,8},{14,12},{1,3},{5,7},... | collective-permute-start | bytes 3145736 | tf_op jit(solution)/shard_map/ppermute | solution.py:80
  41.9 3.9 %collective-permute-start.7 = (f32[2,1153]{1,0:T(2,128)S(1)}, f32[2,1153]{1,0:T(2,128)S(1)}, u32[]{:S(2)}, u32[]{:S(2)}) collective-permute-start(f32[2,1153]{1,0:T(2,128)S(1)} %maximum_select_fusion.2), channel_id=1, source_target_pairs={{0,4},{2,6},{4,0},{6,2},{8,12},{10,14},{12,8},{14,10},{1,5},{3,7},... | collective-permute-start | bytes 27680 | tf_op jit(solution)/shard_map/ppermute | solution.py:91
  45.8 3.6 %collective-permute-start.8 = (f32[4,1153]{1,0:T(4,128)S(1)}, f32[4,1153]{1,0:T(4,128)S(1)}, u32[]{:S(2)}, u32[]{:S(2)}) collective-permute-start(f32[4,1153]{1,0:T(4,128)S(1)} %maximum_select_fusion.1), channel_id=1, source_target_pairs={{0,8},{2,10},{4,12},{6,14},{8,0},{10,2},{12,4},{14,6},{1,9},{3,11}... | collective-permute-start | bytes 55352 | tf_op jit(solution)/shard_map/ppermute | solution.py:91
  58.8 9.2 %copy-start.23 = (f32[2,2,32]{2,1,0:T(2,128)S(1)}, f32[2,2,32]{2,1,0:T(2,128)}, u32[]{:S(2)}) copy-start(f32[2,2,32]{2,1,0:T(2,128)} %get-tuple-element.39) | copy-start | bytes 1540
  62.7 36.6 %all-to-all-start = ((f32[8,1,16384]{2,1,0:T(1,128)}), f32[8,1,16384]{2,1,0:T(1,128)}, u32[]{:S(2)}, u32[]{:S(2)}) async-start(f32[8,1,16384]{2,1,0:T(1,128)} %reshape.359), calls=%async_computation | async-start | bytes 1048576 | tf_op jit(solution)/shard_map/all_to_all | solution.py:118
  67.9 5.3 %copy-start.6 = (bf16[1,256,4096]{1,2,0:T(8,128)(2,1)S(1)}, bf16[1,256,4096]{1,2,0:T(8,128)(2,1)}, u32[]{:S(2)}) copy-start(bf16[1,256,4096]{1,2,0:T(8,128)(2,1)} %copy.208) | copy-start | bytes 6291460
  67.9 5.3 %copy-start.14 = (f32[2,256,256]{2,1,0:T(8,128)S(1)}, f32[2,256,256]{2,1,0:T(8,128)}, u32[]{:S(2)}) copy-start(f32[2,256,256]{2,1,0:T(8,128)} %fusion.72) | copy-start | bytes 1572868
  67.9 5.3 %copy-start.17 = (pred[256,256]{1,0:T(8,128)(4,1)S(1)}, pred[256,256]{1,0:T(8,128)(4,1)}, u32[]{:S(2)}) copy-start(pred[256,256]{1,0:T(8,128)(4,1)} %iota_compare_fusion) | copy-start | bytes 196612
  67.9 5.3 %copy-start.19 = (f32[2,32,256]{2,1,0:T(8,128)S(1)}, f32[2,32,256]{2,1,0:T(8,128)}, u32[]{:S(2)}) copy-start(f32[2,32,256]{2,1,0:T(8,128)} %reduce_window_sum.88) | copy-start | bytes 196612
  68.0 5.3 %copy-start.22 = (f32[1,64,256]{2,1,0:T(8,128)S(1)}, f32[1,64,256]{2,1,0:T(8,128)}, u32[]{:S(2)}) copy-start(f32[1,64,256]{2,1,0:T(8,128)} %get-tuple-element.36) | copy-start | bytes 196612
  71.9 35.6 %collective-permute-start.3 = (bf16[2,2,32,32,128]{4,3,2,1,0:T(8,128)(2,1)}, bf16[2,2,32,32,128]{4,3,2,1,0:T(8,128)(2,1)}, u32[]{:S(2)}, u32[]{:S(2)}) collective-permute-start(bf16[2,2,32,32,128]{4,3,2,1,0:T(8,128)(2,1)} %get-tuple-element.20), channel_id=1, source_target_pairs={{0,4},{4,8},{8,12},{2,6},{6,10},{10,14},{1,5},{5,9},{9,13},{3,7},{... | collective-permute-start | bytes 3145736 | tf_op jit(solution)/shard_map/ppermute | solution.py:80
  73.2 8.1 %copy-start.15 = (f32[4,2,32,64]{3,2,1,0:T(8,128)S(1)}, f32[4,2,32,64]{3,2,1,0:T(8,128)}, u32[]{:S(2)}) copy-start(f32[4,2,32,64]{3,2,1,0:T(8,128)} %reshape.343) | copy-start | bytes 196612
  73.2 9.0 %copy-start.29 = (f32[64]{0:T(128)S(1)}, f32[64]{0:T(128)}, u32[]{:S(2)}) copy-start(f32[64]{0:T(128)} %param.18) | copy-start | bytes 772
  79.9 18.7 %collective-permute-start.1 = (f32[2,2,32]{2,1,0:T(2,128)}, f32[2,2,32]{2,1,0:T(2,128)}, u32[]{:S(2)}, u32[]{:S(2)}) collective-permute-start(f32[2,2,32]{2,1,0:T(2,128)} %get-tuple-element.41), channel_id=1, source_target_pairs={{0,4},{4,8},{8,12},{2,6},{6,10},{10,14},{1,5},{5,9},{9,13},{3,7},{... | collective-permute-start | bytes 1544 | tf_op jit(solution)/shard_map/ppermute | solution.py:80
  82.3 25.2 %copy-start.3 = (f32[2,2,32,32,128]{4,3,2,1,0:T(8,128)S(1)}, f32[2,2,32,32,128]{4,3,2,1,0:T(8,128)}, u32[]{:S(2)}) copy-start(f32[2,2,32,32,128]{4,3,2,1,0:T(8,128)} %get-tuple-element.21) | copy-start | bytes 6291460
  82.3 25.2 %copy-start.24 = (f32[2,2,32]{2,1,0:T(2,128)S(1)}, f32[2,2,32]{2,1,0:T(2,128)}, u32[]{:S(2)}) copy-start(f32[2,2,32]{2,1,0:T(2,128)} %get-tuple-element.39) | copy-start | bytes 1540
  110.4 50.3 %collective-permute-start.4 = (bf16[2,2,32,32,128]{4,3,2,1,0:T(8,128)(2,1)}, bf16[2,2,32,32,128]{4,3,2,1,0:T(8,128)(2,1)}, u32[]{:S(2)}, u32[]{:S(2)}) collective-permute-start(bf16[2,2,32,32,128]{4,3,2,1,0:T(8,128)(2,1)} %fusion.27), channel_id=1, source_target_pairs={{0,8},{4,12},{2,10},{6,14},{1,9},{5,13},{3,11},{7,15},{16,24},{20,... | collective-permute-start | bytes 3145736 | tf_op jit(solution)/shard_map/ppermute | solution.py:80
  115.8 65.1 %all-to-all-start.1 = ((bf16[8,4,4096]{2,1,0:T(4,128)(2,1)}), bf16[8,4,4096]{2,1,0:T(4,128)(2,1)}, u32[]{:S(2)}, u32[]{:S(2)}) async-start(bf16[8,4,4096]{2,1,0:T(4,128)(2,1)} %concatenate.36), calls=%async_computation.1 | async-start | bytes 524288 | tf_op jit(solution)/shard_map/all_to_all | solution.py:118
  164.2 34.3 %collective-permute-start.5 = (bf16[2,2,32,32,128]{4,3,2,1,0:T(8,128)(2,1)}, bf16[2,2,32,32,128]{4,3,2,1,0:T(8,128)(2,1)}, u32[]{:S(2)}, u32[]{:S(2)}) collective-permute-start(bf16[2,2,32,32,128]{4,3,2,1,0:T(8,128)(2,1)} %select_convert_fusion), channel_id=1, source_target_pairs={{0,2},{4,6},{8,10},{12,14},{2,0},{6,4},{10,8},{14,12},{1,3},{5,7},... | collective-permute-start | bytes 3145736 | tf_op jit(solution)/shard_map/ppermute | solution.py:80
  203.6 4.6 %copy-start.7 = (f32[1,2,32,256,64]{3,4,2,1,0:T(8,128)S(1)}, f32[1,2,32,256,64]{3,4,2,1,0:T(8,128)}, u32[]{:S(2)}) copy-start(f32[1,2,32,256,64]{3,4,2,1,0:T(8,128)} %fusion.23) | copy-start | bytes 12582916
  203.6 4.6 %copy-start.27 = (f32[2,32]{1,0:T(2,128)S(1)}, f32[2,32]{1,0:T(2,128)}, u32[]{:S(2)}) copy-start(f32[2,32]{1,0:T(2,128)} %copy-done.26) | copy-start | bytes 772
  214.2 6.3 %copy-start.1 = (bf16[1,4,256]{2,1,0:T(4,128)(2,1)S(1)}, bf16[1,4,256]{2,1,0:T(4,128)(2,1)}, u32[]{:S(2)}) copy-start(bf16[1,4,256]{2,1,0:T(4,128)(2,1)} %param.21) | copy-start | bytes 6148
  (11 other events, 37.3 us)

commit v9 on v7

--- a/solution.py
+++ b/solution.py
@@ -113,11 +113,29 @@
     return value
 
 
+def chain_columns(window, window_total, column, columns):
+    chunks = window.shape[0]
+    growth = jnp.exp(window_total)
+    entering = [jnp.zeros_like(window[k]) for k in range(chunks)]
+    for stage in range(columns - 1 + chunks - 1):
+        senders = [m for m in range(columns - 1) if 0 <= stage - m < chunks]
+        pairs = [(y + 2 * m, y + 2 * (m + 1)) for y in range(2) for m in senders]
+        outgoing = jnp.zeros_like(window[0])
+        for k in range(chunks):
+            leaving = scale(growth[k], entering[k]) + window[k]
+            outgoing = jnp.where(stage - column == k, leaving, outgoing)
+        got = lax.ppermute(outgoing.astype(jnp.bfloat16), "ctx", pairs).astype(jnp.float32)
+        for k in range(chunks):
+            entering[k] = jnp.where(stage - column + 1 == k, got, entering[k])
+    return jnp.stack(entering)
+
+
 def prefix_states(states, totals):
     count = lax.axis_size("ctx")
     columns = count // 2
     place = lax.axis_index("ctx")
     row_zero = place % 2 == 0
+    column = place // 2
     half = states.shape[-2] // 2
     first = states[..., :half, :]
     second = states[..., half:, :]
@@ -133,19 +151,24 @@
     odd_total = jnp.where(row_zero, partner_total, totals)
     window = scale(jnp.exp(odd_total), even_state) + odd_state
     window_total = even_total + odd_total
-    before = jnp.zeros_like(window)
-    before_total = jnp.zeros_like(totals)
-    step = 1
-    while step < columns:
-        pairs = [(y + 2 * m, y + 2 * (m + step)) for y in range(2) for m in range(columns - step)]
-        got, got_total = send(window, window_total, pairs)
-        new_before = scale(jnp.exp(before_total), got) + before
-        if 2 * step < columns:
-            window = scale(jnp.exp(window_total), got) + window
-            window_total = got_total + window_total
-        before = new_before
-        before_total = got_total + before_total
-        step *= 2
+    if columns <= 4:
+        before = chain_columns(window, window_total, column, columns)
+    else:
+        before = jnp.zeros_like(window)
+        before_total = jnp.zeros_like(totals)
+        step = 1
+        while step < columns:
+            pairs = [
+                (y + 2 * m, y + 2 * (m + step)) for y in range(2) for m in range(columns - step)
+            ]
+            got, got_total = send(window, window_total, pairs)
+            new_before = scale(jnp.exp(before_total), got) + before
+            if 2 * step < columns:
+                window = scale(jnp.exp(window_total), got) + window
+                window_total = got_total + window_total
+            before = new_before
+            before_total = got_total + before_total
+            step *= 2
     odd_entering = scale(jnp.exp(even_total), before) + even_state
     outgoing = jnp.where(row_zero, odd_entering, before)
     partner, _ = send(outgoing, totals, across)

time: 212 us -> 198 us (0.934)
  the two profiles are of different devices: /device:TPU:0 before, /device:TPU:18 now
where the time goes in v9:
time: 198 us; the launch traced here: 195 us
  local copies, waits for them, and re-layouts  47.1 us (24%)
  other arithmetic  38.3 us (19%)
  waiting for transfers between devices  36.3 us (18%)
  starting transfers between devices  33.6 us (17%)
  matrix products  33.1 us (17%)
  blocking collectives  5.02 us (3%)
  between operations  2.05 us (1%)
    ppermute x3, waiting for transfers between devices, reduce_scatter_ctx(): lax.ppermute(give, 'ctx', [(i, i ^ reach) for i in range(count)])  19.5 us
    unnamed x92, local copies, waits for them, and re-layouts  15.8 us
    ppermute x3, starting transfers between devices, reduce_scatter_ctx(): lax.ppermute(give, 'ctx', [(i, i ^ reach) for i in range(count)])  14.8 us
    dot_general x2, matrix products, block_terms(): jnp.einsum('gkts,sgkp->gktp', mixing, inputs_head, preferred_element_type...  14.5 us
    ppermute x4, starting transfers between devices, chain_columns(): lax.ppermute(outgoing.astype(jnp.bfloat16), 'ctx', pairs)  11 us
    slice x3, local copies, waits for them, and re-layouts, shards(): ssm_input[request]  10.5 us
    ppermute x4, waiting for transfers between devices, chain_columns(): lax.ppermute(outgoing.astype(jnp.bfloat16), 'ctx', pairs)  7.74 us
    convert_element_type x1, local copies, waits for them, and re-layouts, finish(): inputs_head = ssm_input.reshape(request_count, block_size, group_count, p...  7.13 us
  transfers between devices with their start and end apart: 16, of which 7 were waited for; matrix products, arithmetic and copies ran while one was open for 45% of the time, Pallas kernels for 0%

profile of v9, /device:TPU:18, one launch (start us, length us, event | category | flops | bytes accessed | tf_op | source)
XLA Modules:
  0.0 195.4 jit_solution(13767626427118383942)
XLA Ops:
  10.6 4.0 %fusion.72 = (bf16[1,256,4096]{2,1,0:T(8,128)(2,1)}, bf16[1,256,4096]{2,1,0:T(8,128)(2,1)S(1)}) fusion(bf16[2,256,4096]{2,1,0:T(8,128)(2,1)} %param.13), kind=kLoop, calls=%fused_computation.154 | loop fusion | bytes 8388608 | tf_op jit(solution)/shard_map/slice | solution.py:203
  14.5 4.1 %copy.150 = bf16[1,256,4096]{1,2,0:T(8,128)(2,1)} copy(bf16[1,256,4096]{2,1,0:T(8,128)(2,1)} %get-tuple-element.20) | data formatting | bytes 4194304 | tf_op jit(solution)/shard_map/slice | solution.py:203
  18.6 2.4 %copy.153 = bf16[1,256,4096]{1,2,0:T(8,128)(2,1)} copy(bf16[1,256,4096]{2,1,0:T(8,128)(2,1)S(1)} %get-tuple-element.21) | data formatting | bytes 4194304 | tf_op jit(solution)/shard_map/slice | solution.py:203
  21.1 2.5 %fusion.41 = f32[1,2,32,64,128]{4,3,2,1,0:T(8,128)S(1)} fusion(bf16[256,2,128,1]{0,2,3,1:T(8,128)(2,1)S(1)} %bitcast.212, bf16[256,2,32,64]{0,3,2,1:T(8,128)(2,1)} %bitcast.206, f32[256,2,32]{0,2,1:T(8,128)S(1)} %bitcast.219), kind=kOutput, calls=%fused_computation.63 | convolution fusion | flops 271581184 | bytes 4390912 | tf_op jit(solution)/shard_map/sgkp,sgn->gkpn/dot_general | solution.py:42
  33.3 1.7 copy.211
  36.7 2.1 %fusion.80 = f32[2,256,256]{2,1,0:T(8,128)} fusion(bf16[256,2,128]{0,2,1:T(8,128)(2,1)} %bitcast.217, bf16[256,2,128]{0,2,1:T(8,128)(2,1)} %bitcast.215), kind=kOutput, calls=%fused_computation.162 | convolution fusion | flops 33554432 | bytes 786432 | tf_op jit(solution)/shard_map/tgn,sgn->gts/dot_general | solution.py:24
  40.0 7.9 %fusion.23 = f32[1,2,32,256,64]{3,4,2,1,0:T(8,128)} fusion(bf16[256,2,32,64]{0,3,2,1:T(8,128)(2,1)} %bitcast.207, f32[2,32,256]{2,1,0:T(8,128)} %bitcast.223, f32[2,32,256]{2,1,0:T(8,128)} %reduce_window_sum.88, f32[2,256,256]{2,1,0:T(8,128)S(1)} %fusion.79, pred[256,256]{1,0:T(8,128)(4,1)} %iota_compare_fusion), kind=kOutput, calls=%fused_computation.42 | convolution fusion | flops 562036736 | bytes 7012352 | tf_op jit(solution)/shard_map/gkts,sgkp->gktp/dot_general | solution.py:35
  54.7 3.7 %collective-permute-done.9 = f32[4,1153]{1,0:T(4,128)} collective-permute-done((f32[4,1153]{1,0:T(4,128)S(1)}, f32[4,1153]{1,0:T(4,128)}, u32[]{:S(2)}, u32[]{:S(2)}) %collective-permute-start.9) | collective-permute-done | bytes 18480 | tf_op jit(solution)/shard_map/ppermute | solution.py:91
  59.8 2.3 %fusion.24 = (bf16[2,2,32,64,128,1]{4,3,2,1,0,5:T(8,128)(2,1)S(1)}, bf16[2,2,32,64,128,1]{4,3,2,1,0,5:T(8,128)(2,1)S(1)}) fusion(f32[1,2,32,64,128]{4,3,2,1,0:T(8,128)} %copy-done.4, f32[1,2,32,64,128]{4,3,2,1,0:T(8,128)S(1)} %fusion.41, f32[2,2,32]{2,1,0:T(2,128)S(1)} %exp.65), kind=kLoop, calls=%fused_computation.43 | loop fusion | flops 6291456 | bytes 8389120 | tf_op jit(solution)/shard_map/convert_element_type | solution.py:233
  62.1 2.0 %fusion.30 = f32[2,8,4,2,32,64]{5,1,4,3,2,0:T(8,128)S(1)} fusion(bf16[2,2,32,64,128,1]{4,3,2,1,0,5:T(8,128)(2,1)S(1)} %get-tuple-element.19, bf16[8,4,2,128,1,1]{3,0,2,1,5,4:T(8,128)(2,1)S(1)} %bitcast.220), kind=kOutput, calls=%fused_computation.50 | convolution fusion | flops 67108864 | bytes 3162112 | tf_op jit(solution)/shard_map/rgkpn,jugn->rjugkp/dot_general | solution.py:238
  64.1 2.1 %add_bitcast_fusion = f32[2,8,4,2,32,64]{5,1,4,0,2,3:T(8,128)S(1)} fusion(f32[2,8,4,2,32,64]{5,1,4,3,2,0:T(8,128)S(1)} %fusion.30, bf16[2,2,32,64,128,1]{4,3,2,1,0,5:T(8,128)(2,1)S(1)} %get-tuple-element.18, bf16[8,4,2,128,1,1]{3,0,2,1,5,4:T(8,128)(2,1)S(1)} %bitcast.221), kind=kOutput, calls=%fused_computation.54 | convolution fusion | flops 67371008 | bytes 4210688 | tf_op jit(solution)/shard_map/rgkpn,jugn->rjugkp/dot_general | solution.py:236
  68.3 9.2 %collective-permute-done.10 = f32[4,4,2,32,64]{4,3,2,1,0:T(8,128)S(1)} collective-permute-done((f32[4,4,2,32,64]{4,3,2,1,0:T(8,128)S(1)}, f32[4,4,2,32,64]{4,3,2,1,0:T(8,128)S(1)}, u32[]{:S(2)}, u32[]{:S(2)}) %collective-permute-start.10) | collective-permute-done | bytes 262176 | tf_op jit(solution)/shard_map/ppermute | solution.py:111
  77.7 1.8 fusion.25
  80.5 1.7 collective-permute-start.11
  82.3 4.7 %collective-permute-done.11 = f32[2,4,2,32,64]{4,3,2,1,0:T(8,128)S(1)} collective-permute-done((f32[2,4,2,32,64]{4,3,2,1,0:T(8,128)S(1)}, f32[2,4,2,32,64]{4,3,2,1,0:T(8,128)S(1)}, u32[]{:S(2)}, u32[]{:S(2)}) %collective-permute-start.11) | collective-permute-done | bytes 131104 | tf_op jit(solution)/shard_map/ppermute | solution.py:111
  90.5 12.5 %collective-permute-start.12 = (f32[1,4,2,32,64]{4,3,2,1,0:T(8,128)}, f32[1,4,2,32,64]{4,3,2,1,0:T(8,128)}, u32[]{:S(2)}, u32[]{:S(2)}) collective-permute-start(f32[1,4,2,32,64]{4,3,2,1,0:T(8,128)} %select_bitcast_fusion.2), channel_id=1, source_target_pairs={{0,8},{2,10},{4,12},{6,14},{8,0},{10,2},{12,4},{14,6},{1,9},{3,11}... | collective-permute-start | bytes 196616 | tf_op jit(solution)/shard_map/ppermute | solution.py:111
  106.3 5.7 %collective-permute-done.12 = f32[1,4,2,32,64]{4,3,2,1,0:T(8,128)} collective-permute-done((f32[1,4,2,32,64]{4,3,2,1,0:T(8,128)}, f32[1,4,2,32,64]{4,3,2,1,0:T(8,128)}, u32[]{:S(2)}, u32[]{:S(2)}) %collective-permute-start.12) | collective-permute-done | bytes 65568 | tf_op jit(solution)/shard_map/ppermute | solution.py:111
  111.9 1.9 fusion.60
  116.5 2.0 %select_convert_fusion.3 = bf16[2,32,32,128]{3,2,1,0:T(8,128)(2,1)} fusion(bf16[2,32,32,128]{3,2,1,0:T(8,128)(2,1)S(1)} %collective-permute-done.2, bf16[2,32,32,128]{3,2,1,0:T(8,128)(2,1)S(1)} %collective-permute-done.3, f32[2,2,32,32,128]{4,3,2,1,0:T(8,128)S(1)} %get-tuple-element.14, f32[2,32]{1,0:T(2,128)} %copy-done.33, ...), kind=kLoop, calls=%fused_computation.86 | loop fusion | flops 3407872 | bytes 3670532 | tf_op jit(solution)/shard_map/convert_element_type | solution.py:127
  118.5 4.9 %collective-permute-start.4 = (bf16[2,32,32,128]{3,2,1,0:T(8,128)(2,1)}, bf16[2,32,32,128]{3,2,1,0:T(8,128)(2,1)}, u32[]{:S(2)}, u32[]{:S(2)}) collective-permute-start(bf16[2,32,32,128]{3,2,1,0:T(8,128)(2,1)} %select_convert_fusion.3), channel_id=1, source_target_pairs={{4,8},{8,12},{6,10},{10,14},{5,9},{9,13},{7,11},{11,15},{20,24},{2... | collective-permute-start | bytes 1572872 | tf_op jit(solution)/shard_map/ppermute | solution.py:127
  123.5 6.6 %fusion.22 = f32[1,2,32,256,64]{3,4,2,1,0:T(8,128)} fusion(bf16[256,2,32,64]{0,3,2,1:T(8,128)(2,1)S(1)} %bitcast.205, f32[2,32,256]{2,1,0:T(8,128)S(1)} %bitcast.222, f32[2,32,256]{2,1,0:T(8,128)S(1)} %copy-done.29, f32[2,256,256]{2,1,0:T(8,128)S(1)} %copy-done.20, pred[256,256]{1,0:T(8,128)(4,1)S(1)} %copy-done.28), kind=kOutput, calls=%fused_computation.41 | convolution fusion | flops 562036736 | bytes 7012352 | tf_op jit(solution)/shard_map/gkts,sgkp->gktp/dot_general | solution.py:35
  131.4 7.1 %copy.168 = f32[2,256,4096]{1,2,0:T(8,128)} copy(bf16[2,256,4096]{2,1,0:T(8,128)(2,1)} %param.13) | data formatting | bytes 12582912 | tf_op jit(solution)/shard_map/convert_element_type | solution.py:63
  139.6 1.7 select_convert_fusion.2
  141.3 3.9 %collective-permute-start.5 = (bf16[2,32,32,128]{3,2,1,0:T(8,128)(2,1)S(1)}, bf16[2,32,32,128]{3,2,1,0:T(8,128)(2,1)S(1)}, u32[]{:S(2)}, u32[]{:S(2)}) collective-permute-start(bf16[2,32,32,128]{3,2,1,0:T(8,128)(2,1)S(1)} %select_convert_fusion.2), channel_id=1, source_target_pairs={{8,12},{10,14},{9,13},{11,15},{24,28},{26,30},{25,29},{27,31}} | collective-permute-start | bytes 1572872 | tf_op jit(solution)/shard_map/ppermute | solution.py:127
  145.6 7.7 %collective-permute-done.5 = bf16[2,32,32,128]{3,2,1,0:T(8,128)(2,1)S(1)} collective-permute-done((bf16[2,32,32,128]{3,2,1,0:T(8,128)(2,1)S(1)}, bf16[2,32,32,128]{3,2,1,0:T(8,128)(2,1)S(1)}, u32[]{:S(2)}, u32[]{:S(2)}) %collective-permute-start.5) | collective-permute-done | bytes 524320 | tf_op jit(solution)/shard_map/ppermute | solution.py:127
  153.3 1.8 fusion.49
  157.9 5.5 %fusion.5 = f32[8,4,1024]{2,0,1:T(8,128)} fusion(bf16[4096,1024]{1,0:T(8,128)(2,1)} %param.25, bf16[8,4,4096]{2,1,0:T(4,128)(2,1)S(1)} %maximum_select_fusion), kind=kOutput, calls=%fused_computation.8 | convolution fusion | flops 268435456 | bytes 8781824 | tf_op jit(solution)/shard_map/jup,pd->jud/dot_general | solution.py:268
  163.4 5.0 %all-reduce.1 = bf16[8,4,1024]{2,0,1:T(8,128)(2,1)} all-reduce(f32[8,4,1024]{2,0,1:T(8,128)} %fusion.5), channel_id=1, replica_groups=mesh['groups'=2,'ctx'=8,'heads'=2] {'heads'}, use_global_device_ids=true, to_apply=%region_7.8 | all-reduce | flops 32768 | bytes 196608 | tf_op jit(solution)/shard_map/psum | solution.py:274
  169.9 3.8 %collective-permute-done.6 = bf16[2,2,32,32,128]{4,3,2,1,0:T(8,128)(2,1)} collective-permute-done((bf16[2,2,32,32,128]{4,3,2,1,0:T(8,128)(2,1)}, bf16[2,2,32,32,128]{4,3,2,1,0:T(8,128)(2,1)}, u32[]{:S(2)}, u32[]{:S(2)}) %collective-permute-start.6) | collective-permute-done | bytes 1048608 | tf_op jit(solution)/shard_map/ppermute | solution.py:80
  173.7 2.5 %convert_select_fusion.1 = (f32[2,2,32,32,128]{4,3,2,1,0:T(8,128)S(1)}, f32[2,2,32,32,128]{4,3,2,1,0:T(8,128)S(1)}) fusion(bf16[2,2,32,32,128]{4,3,2,1,0:T(8,128)(2,1)} %collective-permute-done.6, pred[]{:T(512)S(6)} %eq.51, f32[2,2,32,32,128]{4,3,2,1,0:T(8,128)S(1)} %copy-done.6, bf16[2,2,32,32,128]{4,3,2,1,0:T(8,128)(2,1)} %copy-done.8, ...), kind=kLoop, calls=%fused_computation.38 | loop fusion | flops 4718592 | bytes 10486273 | tf_op jit(solution)/shard_map/jit(_where)/select_n | solution.py:176
  183.2 6.0 %fusion.4 = bf16[2,256,2,32,64]{1,4,3,2,0:T(8,128)(2,1)} fusion(f32[1,2,32,256,64]{3,4,2,1,0:T(8,128)} %fusion.22, f32[1,2,32,256,64]{3,4,2,1,0:T(8,128)S(1)} %copy-done.14, f32[2,256,2,32,64]{1,4,3,2,0:T(8,128)S(1)} %bitcast.202, f32[2,2,256,32,64]{2,4,3,1,0:T(8,128)S(1)} %bitcast.199, f32[2,32]{1,0:T(2,128)S(1)} %copy-done.37, f32[2,2,256,32]{2,3,1,0:T(8,128)S(1)} %fusion.58), kind=kLoop, calls=%fused_computation.7 | loop fusion | flops 12582912 | bytes 29491456 | tf_op jit(solution)/shard_map/convert_element_type | solution.py:66
  189.1 6.3 %copy.183 = bf16[2,256,4096]{2,1,0:T(8,128)(2,1)} copy(bf16[2,256,4096]{1,2,0:T(8,128)(2,1)} %bitcast.203) | data formatting | bytes 8388608
  (197 shorter events, 56.4 us)
Async XLA Ops:
  0.6 29.5 %copy-start = (bf16[1,4,256]{2,1,0:T(4,128)(2,1)S(1)}, bf16[1,4,256]{2,1,0:T(4,128)(2,1)}, u32[]{:S(2)}) copy-start(bf16[1,4,256]{2,1,0:T(4,128)(2,1)} %param.21) | copy-start | bytes 6148
  0.6 9.7 %copy-start.22 = (bf16[2,256,256]{2,1,0:T(8,128)(2,1)S(1)}, bf16[2,256,256]{2,1,0:T(8,128)(2,1)}, u32[]{:S(2)}) copy-start(bf16[2,256,256]{2,1,0:T(8,128)(2,1)} %param.14) | copy-start | bytes 786436
  3.4 11.1 %copy-start.31 = (f32[64,2]{0,1:T(2,128)}, f32[64,2]{0,1:T(2,128)S(1)}, u32[]{:S(2)}) copy-start(f32[64,2]{0,1:T(2,128)S(1)} %slice.124) | copy-start | bytes 1540
  5.0 62.4 %collective-permute-start = (f32[2,2,32]{2,1,0:T(2,128)}, f32[2,2,32]{2,1,0:T(2,128)}, u32[]{:S(2)}, u32[]{:S(2)}) collective-permute-start(f32[2,2,32]{2,1,0:T(2,128)} %constant_dynamic-update-slice_fusion), channel_id=1, source_target_pairs={{0,2},{4,6},{8,10},{12,14},{2,0},{6,4},{10,8},{14,12},{1,3},{5,7},... | collective-permute-start | bytes 1544 | tf_op jit(solution)/shard_map/ppermute | solution.py:80
  8.8 39.3 %collective-permute-start.7 = (f32[1,1153]{1,0:T(1,128)S(1)}, f32[1,1153]{1,0:T(1,128)}, u32[]{:S(2)}, u32[]{:S(2)}) collective-permute-start(f32[1,1153]{1,0:T(1,128)S(1)} %broadcast_in_dim.73), channel_id=1, source_target_pairs={{0,2},{2,0},{4,6},{6,4},{8,10},{10,8},{12,14},{14,12},{1,3},{3,1},... | collective-permute-start | bytes 13844 | tf_op jit(solution)/shard_map/ppermute | solution.py:91
  10.4 10.6 %copy-start.17 = (bf16[1,256,256]{1,2,0:T(8,128)(2,1)}, bf16[1,256,256]{1,2,0:T(8,128)(2,1)S(1)}, u32[]{:S(2)}) copy-start(bf16[1,256,256]{1,2,0:T(8,128)(2,1)S(1)} %copy.209) | copy-start | bytes 393220
  10.6 13.0 %copy-start.18 = (bf16[1,256,256]{1,2,0:T(8,128)(2,1)}, bf16[1,256,256]{1,2,0:T(8,128)(2,1)S(1)}, u32[]{:S(2)}) copy-start(bf16[1,256,256]{1,2,0:T(8,128)(2,1)S(1)} %copy.210) | copy-start | bytes 393220
  23.5 36.3 %copy-start.2 = (f32[1,2,32,64,128]{4,3,2,1,0:T(8,128)}, f32[1,2,32,64,128]{4,3,2,1,0:T(8,128)S(1)}, u32[]{:S(2)}) copy-start(f32[1,2,32,64,128]{4,3,2,1,0:T(8,128)S(1)} %fusion.41) | copy-start | bytes 6291460
  25.9 51.7 %collective-permute-start.1 = (bf16[2,2,32,32,128]{4,3,2,1,0:T(8,128)(2,1)}, bf16[2,2,32,32,128]{4,3,2,1,0:T(8,128)(2,1)S(1)}, u32[]{:S(2)}, u32[]{:S(2)}) collective-permute-start(bf16[2,2,32,32,128]{4,3,2,1,0:T(8,128)(2,1)} %select_convert_fusion.1), channel_id=1, source_target_pairs={{0,2},{4,6},{8,10},{12,14},{2,0},{6,4},{10,8},{14,12},{1,3},{5,7},... | collective-permute-start | bytes 3145736 | tf_op jit(solution)/shard_map/ppermute | solution.py:80
  40.0 14.0 %copy-start.25 = (bf16[1,4,4096]{2,1,0:T(4,128)(2,1)S(1)}, bf16[1,4,4096]{2,1,0:T(4,128)(2,1)}, u32[]{:S(2)}) copy-start(bf16[1,4,4096]{2,1,0:T(4,128)(2,1)} %param.20) | copy-start | bytes 98308
  48.9 3.8 %collective-permute-start.8 = (f32[2,1153]{1,0:T(2,128)S(1)}, f32[2,1153]{1,0:T(2,128)}, u32[]{:S(2)}, u32[]{:S(2)}) collective-permute-start(f32[2,1153]{1,0:T(2,128)S(1)} %maximum_select_fusion.5), channel_id=1, source_target_pairs={{0,4},{2,6},{4,0},{6,2},{8,12},{10,14},{12,8},{14,10},{1,5},{3,7},... | collective-permute-start | bytes 27680 | tf_op jit(solution)/shard_map/ppermute | solution.py:91
  53.5 4.9 %collective-permute-start.9 = (f32[4,1153]{1,0:T(4,128)S(1)}, f32[4,1153]{1,0:T(4,128)}, u32[]{:S(2)}, u32[]{:S(2)}) collective-permute-start(f32[4,1153]{1,0:T(4,128)S(1)} %maximum_select_fusion.4), channel_id=1, source_target_pairs={{0,8},{2,10},{4,12},{6,14},{8,0},{10,2},{12,4},{14,6},{1,9},{3,11}... | collective-permute-start | bytes 55352 | tf_op jit(solution)/shard_map/ppermute | solution.py:91
  66.4 11.3 %copy-start.5 = (f32[1,2,32,64,128]{4,3,2,1,0:T(8,128)S(1)}, f32[1,2,32,64,128]{4,3,2,1,0:T(8,128)}, u32[]{:S(2)}) copy-start(f32[1,2,32,64,128]{4,3,2,1,0:T(8,128)} %copy-done.4) | copy-start | bytes 6291460
  66.8 10.9 %copy-start.3 = (f32[1,2,32,64,128]{4,3,2,1,0:T(8,128)S(1)}, f32[1,2,32,64,128]{4,3,2,1,0:T(8,128)}, u32[]{:S(2)}) copy-start(f32[1,2,32,64,128]{4,3,2,1,0:T(8,128)} %copy-done.2) | copy-start | bytes 6291460
  66.9 10.6 %collective-permute-start.10 = (f32[4,4,2,32,64]{4,3,2,1,0:T(8,128)S(1)}, f32[4,4,2,32,64]{4,3,2,1,0:T(8,128)S(1)}, u32[]{:S(2)}, u32[]{:S(2)}) collective-permute-start(f32[4,4,2,32,64]{4,3,2,1,0:T(8,128)S(1)} %select_bitcast_fusion), channel_id=1, source_target_pairs={{0,2},{2,0},{4,6},{6,4},{8,10},{10,8},{12,14},{14,12},{1,3},{3,1},... | collective-permute-start | bytes 786440 | tf_op jit(solution)/shard_map/ppermute | solution.py:111
  79.8 7.3 %collective-permute-start.2 = (bf16[2,32,32,128]{3,2,1,0:T(8,128)(2,1)S(1)}, bf16[2,32,32,128]{3,2,1,0:T(8,128)(2,1)S(1)}, u32[]{:S(2)}, u32[]{:S(2)}) collective-permute-start(bf16[2,32,32,128]{3,2,1,0:T(8,128)(2,1)S(1)} %select_convert_fusion.4), channel_id=1, source_target_pairs={{0,4},{2,6},{1,5},{3,7},{16,20},{18,22},{17,21},{19,23}} | collective-permute-start | bytes 1572872 | tf_op jit(solution)/shard_map/ppermute | solution.py:127
  80.5 6.4 %collective-permute-start.11 = (f32[2,4,2,32,64]{4,3,2,1,0:T(8,128)S(1)}, f32[2,4,2,32,64]{4,3,2,1,0:T(8,128)S(1)}, u32[]{:S(2)}, u32[]{:S(2)}) collective-permute-start(f32[2,4,2,32,64]{4,3,2,1,0:T(8,128)S(1)} %select_bitcast_fusion.1), channel_id=1, source_target_pairs={{0,4},{2,6},{4,0},{6,2},{8,12},{10,14},{12,8},{14,10},{1,5},{3,7},... | collective-permute-start | bytes 393224 | tf_op jit(solution)/shard_map/ppermute | solution.py:111
  82.3 20.7 %copy-start.21 = (f32[4,2,32,64]{3,2,1,0:T(8,128)S(1)}, f32[4,2,32,64]{3,2,1,0:T(8,128)}, u32[]{:S(2)}) copy-start(f32[4,2,32,64]{3,2,1,0:T(8,128)} %reshape.383) | copy-start | bytes 196612
  82.3 20.7 %copy-start.27 = (f32[4,4,2,32]{3,2,1,0:T(2,128)S(1)}, f32[4,4,2,32]{3,2,1,0:T(2,128)}, u32[]{:S(2)}) copy-start(f32[4,4,2,32]{3,2,1,0:T(2,128)} %select_multiply_fusion) | copy-start | bytes 12292
  87.0 17.6 %copy-start.39 = (f32[64]{0:T(128)S(1)}, f32[64]{0:T(128)}, u32[]{:S(2)}) copy-start(f32[64]{0:T(128)} %param.18) | copy-start | bytes 772
  87.1 52.5 %copy-start.12 = (bf16[2,32,32,128]{3,2,1,0:T(8,128)(2,1)}, bf16[2,32,32,128]{3,2,1,0:T(8,128)(2,1)S(1)}, u32[]{:S(2)}) copy-start(bf16[2,32,32,128]{3,2,1,0:T(8,128)(2,1)S(1)} %collective-permute-done.2) | copy-start | bytes 1572868
  88.3 28.2 %collective-permute-start.3 = (bf16[2,32,32,128]{3,2,1,0:T(8,128)(2,1)}, bf16[2,32,32,128]{3,2,1,0:T(8,128)(2,1)S(1)}, u32[]{:S(2)}, u32[]{:S(2)}) collective-permute-start(bf16[2,32,32,128]{3,2,1,0:T(8,128)(2,1)} %fusion.47), channel_id=1, source_target_pairs={{0,4},{4,8},{2,6},{6,10},{1,5},{5,9},{3,7},{7,11},{16,20},{20,24},... | collective-permute-start | bytes 1572872 | tf_op jit(solution)/shard_map/ppermute | solution.py:127
  90.5 21.5 %collective-permute-start.12 = (f32[1,4,2,32,64]{4,3,2,1,0:T(8,128)}, f32[1,4,2,32,64]{4,3,2,1,0:T(8,128)}, u32[]{:S(2)}, u32[]{:S(2)}) collective-permute-start(f32[1,4,2,32,64]{4,3,2,1,0:T(8,128)} %select_bitcast_fusion.2), channel_id=1, source_target_pairs={{0,8},{2,10},{4,12},{6,14},{8,0},{10,2},{12,4},{14,6},{1,9},{3,11}... | collective-permute-start | bytes 196616 | tf_op jit(solution)/shard_map/ppermute | solution.py:111
  104.7 13.8 %copy-start.36 = (f32[2,32]{1,0:T(2,128)}, f32[2,32]{1,0:T(2,128)S(1)}, u32[]{:S(2)}) copy-start(f32[2,32]{1,0:T(2,128)S(1)} %mul.283) | copy-start | bytes 772
  115.4 23.1 %collective-permute-start.13 = (bf16[1,4,4096]{2,1,0:T(4,128)(2,1)}, bf16[1,4,4096]{2,1,0:T(4,128)(2,1)}, u32[]{:S(2)}, u32[]{:S(2)}) collective-permute-start(bf16[1,4,4096]{2,1,0:T(4,128)(2,1)} %convert_element_type.170), channel_id=1, source_target_pairs={{0,2},{2,0},{4,6},{6,4},{8,10},{10,8},{12,14},{14,12},{1,3},{3,1},... | collective-permute-start | bytes 98312 | tf_op jit(solution)/shard_map/ppermute | solution.py:91
  116.5 23.1 %copy-start.13 = (bf16[2,32,32,128]{3,2,1,0:T(8,128)(2,1)}, bf16[2,32,32,128]{3,2,1,0:T(8,128)(2,1)S(1)}, u32[]{:S(2)}) copy-start(bf16[2,32,32,128]{3,2,1,0:T(8,128)(2,1)S(1)} %collective-permute-done.3) | copy-start | bytes 1572868
  118.5 21.1 %collective-permute-start.4 = (bf16[2,32,32,128]{3,2,1,0:T(8,128)(2,1)}, bf16[2,32,32,128]{3,2,1,0:T(8,128)(2,1)}, u32[]{:S(2)}, u32[]{:S(2)}) collective-permute-start(bf16[2,32,32,128]{3,2,1,0:T(8,128)(2,1)} %select_convert_fusion.3), channel_id=1, source_target_pairs={{4,8},{8,12},{6,10},{10,14},{5,9},{9,13},{7,11},{11,15},{20,24},{2... | collective-permute-start | bytes 1572872 | tf_op jit(solution)/shard_map/ppermute | solution.py:127
  139.5 5.8 %collective-permute-start.14 = (bf16[2,4,4096]{2,1,0:T(4,128)(2,1)S(1)}, bf16[2,4,4096]{2,1,0:T(4,128)(2,1)S(1)}, u32[]{:S(2)}, u32[]{:S(2)}) collective-permute-start(bf16[2,4,4096]{2,1,0:T(4,128)(2,1)S(1)} %maximum_select_fusion.2), channel_id=1, source_target_pairs={{0,4},{2,6},{4,0},{6,2},{8,12},{10,14},{12,8},{14,10},{1,5},{3,7},... | collective-permute-start | bytes 196616 | tf_op jit(solution)/shard_map/ppermute | solution.py:91
  141.3 12.0 %collective-permute-start.5 = (bf16[2,32,32,128]{3,2,1,0:T(8,128)(2,1)S(1)}, bf16[2,32,32,128]{3,2,1,0:T(8,128)(2,1)S(1)}, u32[]{:S(2)}, u32[]{:S(2)}) collective-permute-start(bf16[2,32,32,128]{3,2,1,0:T(8,128)(2,1)S(1)} %select_convert_fusion.2), channel_id=1, source_target_pairs={{8,12},{10,14},{9,13},{11,15},{24,28},{26,30},{25,29},{27,31}} | collective-permute-start | bytes 1572872 | tf_op jit(solution)/shard_map/ppermute | solution.py:127
  145.5 9.6 %copy-start.6 = (f32[2,2,32,32,128]{4,3,2,1,0:T(8,128)S(1)}, f32[2,2,32,32,128]{4,3,2,1,0:T(8,128)}, u32[]{:S(2)}) copy-start(f32[2,2,32,32,128]{4,3,2,1,0:T(8,128)} %get-tuple-element.15) | copy-start | bytes 6291460
  145.5 12.1 %collective-permute-start.15 = (bf16[4,4,4096]{2,1,0:T(4,128)(2,1)S(1)}, bf16[4,4,4096]{2,1,0:T(4,128)(2,1)S(1)}, u32[]{:S(2)}, u32[]{:S(2)}) collective-permute-start(bf16[4,4,4096]{2,1,0:T(4,128)(2,1)S(1)} %maximum_select_fusion.1), channel_id=1, source_target_pairs={{0,8},{2,10},{4,12},{6,14},{8,0},{10,2},{12,4},{14,6},{1,9},{3,11}... | collective-permute-start | bytes 393224 | tf_op jit(solution)/shard_map/ppermute | solution.py:91
  156.6 17.1 %collective-permute-start.6 = (bf16[2,2,32,32,128]{4,3,2,1,0:T(8,128)(2,1)}, bf16[2,2,32,32,128]{4,3,2,1,0:T(8,128)(2,1)}, u32[]{:S(2)}, u32[]{:S(2)}) collective-permute-start(bf16[2,2,32,32,128]{4,3,2,1,0:T(8,128)(2,1)} %select_convert_fusion), channel_id=1, source_target_pairs={{0,2},{4,6},{8,10},{12,14},{2,0},{6,4},{10,8},{14,12},{1,3},{5,7},... | collective-permute-start | bytes 3145736 | tf_op jit(solution)/shard_map/ppermute | solution.py:80
  (26 other events, 146.2 us)

commit v10 on v9

--- a/solution.py
+++ b/solution.py
@@ -102,14 +102,14 @@
     if count & (count - 1):
         return lax.psum_scatter(value, "ctx", scatter_dimension=0, tiled=True)
     place = lax.axis_index("ctx")
-    reach = 1
-    while reach < count:
-        pairs = value.reshape((value.shape[0] // 2, 2) + value.shape[1:])
+    reach = count // 2
+    while reach >= 1:
+        pairs = value.reshape((2, value.shape[0] // 2) + value.shape[1:])
         upper = (place & reach) != 0
-        keep = jnp.where(upper, pairs[:, 1], pairs[:, 0])
-        give = jnp.where(upper, pairs[:, 0], pairs[:, 1])
+        keep = jnp.where(upper, pairs[1], pairs[0])
+        give = jnp.where(upper, pairs[0], pairs[1])
         value = keep + lax.ppermute(give, "ctx", [(i, i ^ reach) for i in range(count)])
-        reach *= 2
+        reach //= 2
     return value
 
 

time: 198 us -> 217 us (1.096)
  waiting for transfers between devices: 36.3 us -> 67.1 us
  starting transfers between devices: 33.6 us -> 21.8 us
    ppermute x4, waiting for transfers between devices: 7.74 us -> 24.9 us  [chain_columns(): lax.ppermute(outgoing.astype(jnp.bfloat16), 'ctx', pairs)]
    ppermute x3, starting transfers between devices: 14.8 us -> 5.68 us  [reduce_scatter_ctx(): lax.ppermute(give, 'ctx', [(i, i ^ reach) for i in range(count)])]
    ppermute x3, waiting for transfers between devices: 3.78 us -> 11.1 us  [send(): lax.ppermute((value.astype(jnp.bfloat16), total), 'ctx', pairs)]
    ppermute x3, waiting for transfers between devices: 19.5 us -> 25.9 us  [reduce_scatter_ctx(): lax.ppermute(give, 'ctx', [(i, i ^ reach) for i in range(count)])]
    ppermute x4, starting transfers between devices: 11 us -> 8 us  [chain_columns(): lax.ppermute(outgoing.astype(jnp.bfloat16), 'ctx', pairs)]
  transfers between devices with their start and end apart: 16 -> 16, of which waited for: 7 -> 8; matrix products, arithmetic and copies ran while one was open for 45% -> 42% of each run, Pallas kernels for 0% -> 0%
where the time goes in v10:
time: 217 us; the launch traced here: 215 us
  waiting for transfers between devices  67.1 us (31%)
  local copies, waits for them, and re-layouts  46.8 us (22%)
  other arithmetic  39.1 us (18%)
  matrix products  33.1 us (15%)
  starting transfers between devices  21.8 us (10%)
  blocking collectives  5.03 us (2%)
    ppermute x3, waiting for transfers between devices, reduce_scatter_ctx(): lax.ppermute(give, 'ctx', [(i, i ^ reach) for i in range(count)])  25.9 us
    ppermute x4, waiting for transfers between devices, chain_columns(): lax.ppermute(outgoing.astype(jnp.bfloat16), 'ctx', pairs)  24.9 us
    unnamed x92, local copies, waits for them, and re-layouts  15.8 us
    dot_general x2, matrix products, block_terms(): jnp.einsum('gkts,sgkp->gktp', mixing, inputs_head, preferred_element_type...  14.5 us
    ppermute x3, waiting for transfers between devices, send(): lax.ppermute((value.astype(jnp.bfloat16), total), 'ctx', pairs)  11.1 us
    slice x3, local copies, waits for them, and re-layouts, shards(): ssm_input[request]  10.5 us
    ppermute x4, starting transfers between devices, chain_columns(): lax.ppermute(outgoing.astype(jnp.bfloat16), 'ctx', pairs)  8 us
    convert_element_type x1, local copies, waits for them, and re-layouts, finish(): inputs_head = ssm_input.reshape(request_count, block_size, group_count, p...  7.13 us
  transfers between devices with their start and end apart: 16, of which 8 were waited for; matrix products, arithmetic and copies ran while one was open for 42% of the time, Pallas kernels for 0%

profile of v10, /device:TPU:18, one launch (start us, length us, event | category | flops | bytes accessed | tf_op | source)
XLA Modules:
  0.0 214.9 jit_solution(16608659634608658704)
XLA Ops:
  10.5 4.0 %fusion.70 = (bf16[1,256,4096]{2,1,0:T(8,128)(2,1)}, bf16[1,256,4096]{2,1,0:T(8,128)(2,1)S(1)}) fusion(bf16[2,256,4096]{2,1,0:T(8,128)(2,1)} %param.13), kind=kLoop, calls=%fused_computation.152 | loop fusion | bytes 8388608 | tf_op jit(solution)/shard_map/slice | solution.py:203
  14.5 4.1 %copy.189 = bf16[1,256,4096]{1,2,0:T(8,128)(2,1)} copy(bf16[1,256,4096]{2,1,0:T(8,128)(2,1)} %get-tuple-element.22) | data formatting | bytes 4194304 | tf_op jit(solution)/shard_map/slice | solution.py:203
  18.6 2.4 %copy.192 = bf16[1,256,4096]{1,2,0:T(8,128)(2,1)} copy(bf16[1,256,4096]{2,1,0:T(8,128)(2,1)S(1)} %get-tuple-element.23) | data formatting | bytes 4194304 | tf_op jit(solution)/shard_map/slice | solution.py:203
  21.0 2.5 %fusion.40 = f32[1,2,32,64,128]{4,3,2,1,0:T(8,128)S(1)} fusion(bf16[256,2,128,1]{0,2,3,1:T(8,128)(2,1)S(1)} %bitcast.181, bf16[256,2,32,64]{0,3,2,1:T(8,128)(2,1)} %bitcast.179, f32[256,2,32]{0,2,1:T(8,128)S(1)} %bitcast.188), kind=kOutput, calls=%fused_computation.64 | convolution fusion | flops 271581184 | bytes 4390912 | tf_op jit(solution)/shard_map/sgkp,sgn->gkpn/dot_general | solution.py:42
  33.3 1.7 copy.247
  35.0 1.7 copy.248
  36.7 2.1 fusion.77
  40.0 7.9 %fusion.23 = f32[1,2,32,256,64]{3,4,2,1,0:T(8,128)} fusion(bf16[256,2,32,64]{0,3,2,1:T(8,128)(2,1)} %bitcast.180, f32[2,32,256]{2,1,0:T(8,128)} %bitcast.192, f32[2,32,256]{2,1,0:T(8,128)} %reduce_window_sum.88, f32[2,256,256]{2,1,0:T(8,128)S(1)} %fusion.76, pred[256,256]{1,0:T(8,128)(4,1)} %iota_compare_fusion), kind=kOutput, calls=%fused_computation.42 | convolution fusion | flops 562036736 | bytes 7012352 | tf_op jit(solution)/shard_map/gkts,sgkp->gktp/dot_general | solution.py:35
  54.7 3.7 %collective-permute-done.9 = f32[4,1153]{1,0:T(4,128)} collective-permute-done((f32[4,1153]{1,0:T(4,128)S(1)}, f32[4,1153]{1,0:T(4,128)}, u32[]{:S(2)}, u32[]{:S(2)}) %collective-permute-start.9) | collective-permute-done | bytes 18480 | tf_op jit(solution)/shard_map/ppermute | solution.py:91
  59.6 2.3 %fusion.24 = (bf16[2,2,32,64,128,1]{4,3,2,1,0,5:T(8,128)(2,1)S(1)}, bf16[2,2,32,64,128,1]{4,3,2,1,0,5:T(8,128)(2,1)S(1)}) fusion(f32[1,2,32,64,128]{4,3,2,1,0:T(8,128)} %copy-done.4, f32[1,2,32,64,128]{4,3,2,1,0:T(8,128)S(1)} %fusion.40, f32[2,2,32]{2,1,0:T(2,128)S(1)} %exp.65), kind=kLoop, calls=%fused_computation.43 | loop fusion | flops 6291456 | bytes 8389120 | tf_op jit(solution)/shard_map/convert_element_type | solution.py:233
  61.9 2.0 fusion.32
  64.0 2.0 fusion.30
  68.5 18.2 %collective-permute-done.10 = f32[4,4,2,32,64]{4,3,2,1,0:T(8,128)S(1)} collective-permute-done((f32[4,4,2,32,64]{4,3,2,1,0:T(8,128)S(1)}, f32[4,4,2,32,64]{4,3,2,1,0:T(8,128)S(1)}, u32[]{:S(2)}, u32[]{:S(2)}) %collective-permute-start.10) | collective-permute-done | bytes 262176 | tf_op jit(solution)/shard_map/ppermute | solution.py:111
  86.9 1.8 fusion.25
  89.9 4.6 %collective-permute-start.11 = (f32[2,4,2,32,64]{4,3,2,1,0:T(8,128)S(1)}, f32[2,4,2,32,64]{4,3,2,1,0:T(8,128)S(1)}, u32[]{:S(2)}, u32[]{:S(2)}) collective-permute-start(f32[2,4,2,32,64]{4,3,2,1,0:T(8,128)S(1)} %slice_select_fusion.1), channel_id=1, source_target_pairs={{0,4},{2,6},{4,0},{6,2},{8,12},{10,14},{12,8},{14,10},{1,5},{3,7},... | collective-permute-start | bytes 393224 | tf_op jit(solution)/shard_map/ppermute | solution.py:111
  94.5 6.5 %collective-permute-done.11 = f32[2,4,2,32,64]{4,3,2,1,0:T(8,128)S(1)} collective-permute-done((f32[2,4,2,32,64]{4,3,2,1,0:T(8,128)S(1)}, f32[2,4,2,32,64]{4,3,2,1,0:T(8,128)S(1)}, u32[]{:S(2)}, u32[]{:S(2)}) %collective-permute-start.11) | collective-permute-done | bytes 131104 | tf_op jit(solution)/shard_map/ppermute | solution.py:111
  109.6 1.9 fusion.59
  113.9 13.8 %collective-permute-done.3 = bf16[2,32,32,128]{3,2,1,0:T(8,128)(2,1)S(1)} collective-permute-done((bf16[2,32,32,128]{3,2,1,0:T(8,128)(2,1)}, bf16[2,32,32,128]{3,2,1,0:T(8,128)(2,1)S(1)}, u32[]{:S(2)}, u32[]{:S(2)}) %collective-permute-start.3) | collective-permute-done | bytes 524320 | tf_op jit(solution)/shard_map/ppermute | solution.py:127
  127.7 2.0 select_convert_fusion.3
  129.7 1.9 collective-permute-start.4
  131.6 6.6 %fusion.22 = f32[1,2,32,256,64]{3,4,2,1,0:T(8,128)} fusion(bf16[256,2,32,64]{0,3,2,1:T(8,128)(2,1)S(1)} %bitcast.178, f32[2,32,256]{2,1,0:T(8,128)S(1)} %bitcast.191, f32[2,32,256]{2,1,0:T(8,128)S(1)} %copy-done.29, f32[2,256,256]{2,1,0:T(8,128)S(1)} %copy-done.20, pred[256,256]{1,0:T(8,128)(4,1)S(1)} %copy-done.28), kind=kOutput, calls=%fused_computation.41 | convolution fusion | flops 562036736 | bytes 7012352 | tf_op jit(solution)/shard_map/gkts,sgkp->gktp/dot_general | solution.py:35
  139.6 7.1 %copy.207 = f32[2,256,4096]{1,2,0:T(8,128)} copy(bf16[2,256,4096]{2,1,0:T(8,128)(2,1)} %param.13) | data formatting | bytes 12582912 | tf_op jit(solution)/shard_map/convert_element_type | solution.py:63
  147.8 1.7 select_convert_fusion.2
  149.5 3.9 %collective-permute-start.5 = (bf16[2,32,32,128]{3,2,1,0:T(8,128)(2,1)S(1)}, bf16[2,32,32,128]{3,2,1,0:T(8,128)(2,1)S(1)}, u32[]{:S(2)}, u32[]{:S(2)}) collective-permute-start(bf16[2,32,32,128]{3,2,1,0:T(8,128)(2,1)S(1)} %select_convert_fusion.2), channel_id=1, source_target_pairs={{8,12},{10,14},{9,13},{11,15},{24,28},{26,30},{25,29},{27,31}} | collective-permute-start | bytes 1572872 | tf_op jit(solution)/shard_map/ppermute | solution.py:127
  154.7 11.1 %collective-permute-done.5 = bf16[2,32,32,128]{3,2,1,0:T(8,128)(2,1)S(1)} collective-permute-done((bf16[2,32,32,128]{3,2,1,0:T(8,128)(2,1)S(1)}, bf16[2,32,32,128]{3,2,1,0:T(8,128)(2,1)S(1)}, u32[]{:S(2)}, u32[]{:S(2)}) %collective-permute-start.5) | collective-permute-done | bytes 524320 | tf_op jit(solution)/shard_map/ppermute | solution.py:127
  165.8 1.8 fusion.48
  170.1 5.5 %fusion.5 = f32[8,4,1024]{2,0,1:T(8,128)} fusion(bf16[4096,1024]{1,0:T(8,128)(2,1)} %param.25, bf16[8,4,4096]{2,1,0:T(4,128)(2,1)S(1)} %maximum_select_fusion), kind=kOutput, calls=%fused_computation.8 | convolution fusion | flops 268435456 | bytes 8781824 | tf_op jit(solution)/shard_map/jup,pd->jud/dot_general | solution.py:268
  175.6 5.0 %all-reduce.1 = bf16[8,4,1024]{2,0,1:T(8,128)(2,1)} all-reduce(f32[8,4,1024]{2,0,1:T(8,128)} %fusion.5), channel_id=1, replica_groups=mesh['groups'=2,'ctx'=8,'heads'=2] {'heads'}, use_global_device_ids=true, to_apply=%region_7.8 | all-reduce | flops 32768 | bytes 196608 | tf_op jit(solution)/shard_map/psum | solution.py:274
  182.1 11.1 %collective-permute-done.6 = bf16[2,2,32,32,128]{4,3,2,1,0:T(8,128)(2,1)} collective-permute-done((bf16[2,2,32,32,128]{4,3,2,1,0:T(8,128)(2,1)}, bf16[2,2,32,32,128]{4,3,2,1,0:T(8,128)(2,1)}, u32[]{:S(2)}, u32[]{:S(2)}) %collective-permute-start.6) | collective-permute-done | bytes 1048608 | tf_op jit(solution)/shard_map/ppermute | solution.py:80
  193.2 2.5 %convert_select_fusion.1 = (f32[2,2,32,32,128]{4,3,2,1,0:T(8,128)S(1)}, f32[2,2,32,32,128]{4,3,2,1,0:T(8,128)S(1)}) fusion(bf16[2,2,32,32,128]{4,3,2,1,0:T(8,128)(2,1)} %collective-permute-done.6, pred[]{:T(512)S(6)} %eq.51, f32[2,2,32,32,128]{4,3,2,1,0:T(8,128)S(1)} %copy-done.6, bf16[2,2,32,32,128]{4,3,2,1,0:T(8,128)(2,1)} %copy-done.8, ...), kind=kLoop, calls=%fused_computation.38 | loop fusion | flops 4718592 | bytes 10486273 | tf_op jit(solution)/shard_map/jit(_where)/select_n | solution.py:176
  202.6 5.9 %fusion.4 = bf16[2,256,2,32,64]{1,4,3,2,0:T(8,128)(2,1)} fusion(f32[1,2,32,256,64]{3,4,2,1,0:T(8,128)} %fusion.22, f32[1,2,32,256,64]{3,4,2,1,0:T(8,128)S(1)} %copy-done.14, f32[2,256,2,32,64]{1,4,3,2,0:T(8,128)S(1)} %bitcast.175, f32[2,2,256,32,64]{2,4,3,1,0:T(8,128)S(1)} %bitcast.172, f32[2,32]{1,0:T(2,128)S(1)} %copy-done.37, f32[2,2,256,32]{2,3,1,0:T(8,128)S(1)} %fusion.57), kind=kLoop, calls=%fused_computation.7 | loop fusion | flops 12582912 | bytes 29491456 | tf_op jit(solution)/shard_map/convert_element_type | solution.py:66
  208.6 6.3 %copy.219 = bf16[2,256,4096]{2,1,0:T(8,128)(2,1)} copy(bf16[2,256,4096]{1,2,0:T(8,128)(2,1)} %bitcast.176) | data formatting | bytes 8388608
  (195 shorter events, 57.3 us)
Async XLA Ops:
  0.6 29.5 %copy-start = (bf16[1,4,256]{2,1,0:T(4,128)(2,1)S(1)}, bf16[1,4,256]{2,1,0:T(4,128)(2,1)}, u32[]{:S(2)}) copy-start(bf16[1,4,256]{2,1,0:T(4,128)(2,1)} %param.21) | copy-start | bytes 6148
  5.0 62.4 %collective-permute-start = (f32[2,2,32]{2,1,0:T(2,128)}, f32[2,2,32]{2,1,0:T(2,128)}, u32[]{:S(2)}, u32[]{:S(2)}) collective-permute-start(f32[2,2,32]{2,1,0:T(2,128)} %constant_dynamic-update-slice_fusion), channel_id=1, source_target_pairs={{0,2},{4,6},{8,10},{12,14},{2,0},{6,4},{10,8},{14,12},{1,3},{5,7},... | collective-permute-start | bytes 1544 | tf_op jit(solution)/shard_map/ppermute | solution.py:80
  8.8 39.3 %collective-permute-start.7 = (f32[1,1153]{1,0:T(1,128)S(1)}, f32[1,1153]{1,0:T(1,128)}, u32[]{:S(2)}, u32[]{:S(2)}) collective-permute-start(f32[1,1153]{1,0:T(1,128)S(1)} %broadcast_in_dim.73), channel_id=1, source_target_pairs={{0,2},{2,0},{4,6},{6,4},{8,10},{10,8},{12,14},{14,12},{1,3},{3,1},... | collective-permute-start | bytes 13844 | tf_op jit(solution)/shard_map/ppermute | solution.py:91
  10.5 13.0 %copy-start.18 = (bf16[1,256,256]{1,2,0:T(8,128)(2,1)}, bf16[1,256,256]{1,2,0:T(8,128)(2,1)S(1)}, u32[]{:S(2)}) copy-start(bf16[1,256,256]{1,2,0:T(8,128)(2,1)S(1)} %copy.246) | copy-start | bytes 393220
  23.5 36.1 %copy-start.2 = (f32[1,2,32,64,128]{4,3,2,1,0:T(8,128)}, f32[1,2,32,64,128]{4,3,2,1,0:T(8,128)S(1)}, u32[]{:S(2)}) copy-start(f32[1,2,32,64,128]{4,3,2,1,0:T(8,128)S(1)} %fusion.40) | copy-start | bytes 6291460
  25.9 61.0 %collective-permute-start.1 = (bf16[2,2,32,32,128]{4,3,2,1,0:T(8,128)(2,1)}, bf16[2,2,32,32,128]{4,3,2,1,0:T(8,128)(2,1)S(1)}, u32[]{:S(2)}, u32[]{:S(2)}) collective-permute-start(bf16[2,2,32,32,128]{4,3,2,1,0:T(8,128)(2,1)} %select_convert_fusion.1), channel_id=1, source_target_pairs={{0,2},{4,6},{8,10},{12,14},{2,0},{6,4},{10,8},{14,12},{1,3},{5,7},... | collective-permute-start | bytes 3145736 | tf_op jit(solution)/shard_map/ppermute | solution.py:80
  40.0 13.9 %copy-start.25 = (bf16[1,4,4096]{2,1,0:T(4,128)(2,1)S(1)}, bf16[1,4,4096]{2,1,0:T(4,128)(2,1)}, u32[]{:S(2)}) copy-start(bf16[1,4,4096]{2,1,0:T(4,128)(2,1)} %param.20) | copy-start | bytes 98308
  48.9 3.8 %collective-permute-start.8 = (f32[2,1153]{1,0:T(2,128)S(1)}, f32[2,1153]{1,0:T(2,128)}, u32[]{:S(2)}, u32[]{:S(2)}) collective-permute-start(f32[2,1153]{1,0:T(2,128)S(1)} %maximum_select_fusion.5), channel_id=1, source_target_pairs={{0,4},{2,6},{4,0},{6,2},{8,12},{10,14},{12,8},{14,10},{1,5},{3,7},... | collective-permute-start | bytes 27680 | tf_op jit(solution)/shard_map/ppermute | solution.py:91
  53.5 4.9 %collective-permute-start.9 = (f32[4,1153]{1,0:T(4,128)S(1)}, f32[4,1153]{1,0:T(4,128)}, u32[]{:S(2)}, u32[]{:S(2)}) collective-permute-start(f32[4,1153]{1,0:T(4,128)S(1)} %maximum_select_fusion.4), channel_id=1, source_target_pairs={{0,8},{2,10},{4,12},{6,14},{8,0},{10,2},{12,4},{14,6},{1,9},{3,11}... | collective-permute-start | bytes 55352 | tf_op jit(solution)/shard_map/ppermute | solution.py:91
  66.7 20.2 %copy-start.5 = (f32[1,2,32,64,128]{4,3,2,1,0:T(8,128)S(1)}, f32[1,2,32,64,128]{4,3,2,1,0:T(8,128)}, u32[]{:S(2)}) copy-start(f32[1,2,32,64,128]{4,3,2,1,0:T(8,128)} %copy-done.4) | copy-start | bytes 6291460
  66.9 20.0 %copy-start.3 = (f32[1,2,32,64,128]{4,3,2,1,0:T(8,128)S(1)}, f32[1,2,32,64,128]{4,3,2,1,0:T(8,128)}, u32[]{:S(2)}) copy-start(f32[1,2,32,64,128]{4,3,2,1,0:T(8,128)} %copy-done.2) | copy-start | bytes 6291460
  67.0 19.7 %collective-permute-start.10 = (f32[4,4,2,32,64]{4,3,2,1,0:T(8,128)S(1)}, f32[4,4,2,32,64]{4,3,2,1,0:T(8,128)S(1)}, u32[]{:S(2)}, u32[]{:S(2)}) collective-permute-start(f32[4,4,2,32,64]{4,3,2,1,0:T(8,128)S(1)} %slice_select_fusion), channel_id=1, source_target_pairs={{0,8},{2,10},{4,12},{6,14},{8,0},{10,2},{12,4},{14,6},{1,9},{3,11}... | collective-permute-start | bytes 786440 | tf_op jit(solution)/shard_map/ppermute | solution.py:111
  89.0 12.1 %collective-permute-start.2 = (bf16[2,32,32,128]{3,2,1,0:T(8,128)(2,1)S(1)}, bf16[2,32,32,128]{3,2,1,0:T(8,128)(2,1)S(1)}, u32[]{:S(2)}, u32[]{:S(2)}) collective-permute-start(bf16[2,32,32,128]{3,2,1,0:T(8,128)(2,1)S(1)} %select_convert_fusion.4), channel_id=1, source_target_pairs={{0,4},{2,6},{1,5},{3,7},{16,20},{18,22},{17,21},{19,23}} | collective-permute-start | bytes 1572872 | tf_op jit(solution)/shard_map/ppermute | solution.py:127
  89.9 11.1 %collective-permute-start.11 = (f32[2,4,2,32,64]{4,3,2,1,0:T(8,128)S(1)}, f32[2,4,2,32,64]{4,3,2,1,0:T(8,128)S(1)}, u32[]{:S(2)}, u32[]{:S(2)}) collective-permute-start(f32[2,4,2,32,64]{4,3,2,1,0:T(8,128)S(1)} %slice_select_fusion.1), channel_id=1, source_target_pairs={{0,4},{2,6},{4,0},{6,2},{8,12},{10,14},{12,8},{14,10},{1,5},{3,7},... | collective-permute-start | bytes 393224 | tf_op jit(solution)/shard_map/ppermute | solution.py:111
  101.1 46.7 %copy-start.12 = (bf16[2,32,32,128]{3,2,1,0:T(8,128)(2,1)}, bf16[2,32,32,128]{3,2,1,0:T(8,128)(2,1)S(1)}, u32[]{:S(2)}) copy-start(bf16[2,32,32,128]{3,2,1,0:T(8,128)(2,1)S(1)} %collective-permute-done.2) | copy-start | bytes 1572868
  102.4 25.3 %collective-permute-start.3 = (bf16[2,32,32,128]{3,2,1,0:T(8,128)(2,1)}, bf16[2,32,32,128]{3,2,1,0:T(8,128)(2,1)S(1)}, u32[]{:S(2)}, u32[]{:S(2)}) collective-permute-start(bf16[2,32,32,128]{3,2,1,0:T(8,128)(2,1)} %fusion.46), channel_id=1, source_target_pairs={{0,4},{4,8},{2,6},{6,10},{1,5},{5,9},{3,7},{7,11},{16,20},{20,24},... | collective-permute-start | bytes 1572872 | tf_op jit(solution)/shard_map/ppermute | solution.py:127
  104.3 5.3 %collective-permute-start.12 = (f32[1,4,2,32,64]{4,3,2,1,0:T(8,128)}, f32[1,4,2,32,64]{4,3,2,1,0:T(8,128)}, u32[]{:S(2)}, u32[]{:S(2)}) collective-permute-start(f32[1,4,2,32,64]{4,3,2,1,0:T(8,128)} %slice_select_fusion.2), channel_id=1, source_target_pairs={{0,2},{2,0},{4,6},{6,4},{8,10},{10,8},{12,14},{14,12},{1,3},{3,1},... | collective-permute-start | bytes 196616 | tf_op jit(solution)/shard_map/ppermute | solution.py:111
  106.8 22.9 %copy-start.36 = (f32[2,32]{1,0:T(2,128)}, f32[2,32]{1,0:T(2,128)S(1)}, u32[]{:S(2)}) copy-start(f32[2,32]{1,0:T(2,128)S(1)} %mul.283) | copy-start | bytes 772
  113.1 18.5 %copy-start.11 = (bf16[1,256,4096]{1,2,0:T(8,128)(2,1)S(1)}, bf16[1,256,4096]{1,2,0:T(8,128)(2,1)}, u32[]{:S(2)}) copy-start(bf16[1,256,4096]{1,2,0:T(8,128)(2,1)} %copy.192) | copy-start | bytes 6291460
  113.1 18.5 %copy-start.20 = (f32[2,256,256]{2,1,0:T(8,128)S(1)}, f32[2,256,256]{2,1,0:T(8,128)}, u32[]{:S(2)}) copy-start(f32[2,256,256]{2,1,0:T(8,128)} %fusion.77) | copy-start | bytes 1572868
  113.1 18.5 %copy-start.28 = (pred[256,256]{1,0:T(8,128)(4,1)S(1)}, pred[256,256]{1,0:T(8,128)(4,1)}, u32[]{:S(2)}) copy-start(pred[256,256]{1,0:T(8,128)(4,1)} %iota_compare_fusion) | copy-start | bytes 196612
  113.1 18.5 %copy-start.29 = (f32[2,32,256]{2,1,0:T(8,128)S(1)}, f32[2,32,256]{2,1,0:T(8,128)}, u32[]{:S(2)}) copy-start(f32[2,32,256]{2,1,0:T(8,128)} %reduce_window_sum.89) | copy-start | bytes 196612
  113.1 18.5 %copy-start.30 = (f32[1,64,256]{2,1,0:T(8,128)S(1)}, f32[1,64,256]{2,1,0:T(8,128)}, u32[]{:S(2)}) copy-start(f32[1,64,256]{2,1,0:T(8,128)} %get-tuple-element.35) | copy-start | bytes 196612
  113.1 33.6 %collective-permute-start.13 = (bf16[1,4,4096]{2,1,0:T(4,128)(2,1)}, bf16[1,4,4096]{2,1,0:T(4,128)(2,1)}, u32[]{:S(2)}, u32[]{:S(2)}) collective-permute-start(bf16[1,4,4096]{2,1,0:T(4,128)(2,1)} %convert_element_type.170), channel_id=1, source_target_pairs={{0,2},{2,0},{4,6},{6,4},{8,10},{10,8},{12,14},{14,12},{1,3},{3,1},... | collective-permute-start | bytes 98312 | tf_op jit(solution)/shard_map/ppermute | solution.py:91
  127.7 20.1 %copy-start.13 = (bf16[2,32,32,128]{3,2,1,0:T(8,128)(2,1)}, bf16[2,32,32,128]{3,2,1,0:T(8,128)(2,1)S(1)}, u32[]{:S(2)}) copy-start(bf16[2,32,32,128]{3,2,1,0:T(8,128)(2,1)S(1)} %collective-permute-done.3) | copy-start | bytes 1572868
  129.7 18.1 %collective-permute-start.4 = (bf16[2,32,32,128]{3,2,1,0:T(8,128)(2,1)}, bf16[2,32,32,128]{3,2,1,0:T(8,128)(2,1)}, u32[]{:S(2)}, u32[]{:S(2)}) collective-permute-start(bf16[2,32,32,128]{3,2,1,0:T(8,128)(2,1)} %select_convert_fusion.3), channel_id=1, source_target_pairs={{4,8},{8,12},{6,10},{10,14},{5,9},{9,13},{7,11},{11,15},{20,24},{2... | collective-permute-start | bytes 1572872 | tf_op jit(solution)/shard_map/ppermute | solution.py:127
  147.7 5.8 %collective-permute-start.14 = (bf16[2,4,4096]{2,1,0:T(4,128)(2,1)S(1)}, bf16[2,4,4096]{2,1,0:T(4,128)(2,1)S(1)}, u32[]{:S(2)}, u32[]{:S(2)}) collective-permute-start(bf16[2,4,4096]{2,1,0:T(4,128)(2,1)S(1)} %maximum_select_fusion.2), channel_id=1, source_target_pairs={{0,4},{2,6},{4,0},{6,2},{8,12},{10,14},{12,8},{14,10},{1,5},{3,7},... | collective-permute-start | bytes 196616 | tf_op jit(solution)/shard_map/ppermute | solution.py:91
  149.5 16.3 %collective-permute-start.5 = (bf16[2,32,32,128]{3,2,1,0:T(8,128)(2,1)S(1)}, bf16[2,32,32,128]{3,2,1,0:T(8,128)(2,1)S(1)}, u32[]{:S(2)}, u32[]{:S(2)}) collective-permute-start(bf16[2,32,32,128]{3,2,1,0:T(8,128)(2,1)S(1)} %select_convert_fusion.2), channel_id=1, source_target_pairs={{8,12},{10,14},{9,13},{11,15},{24,28},{26,30},{25,29},{27,31}} | collective-permute-start | bytes 1572872 | tf_op jit(solution)/shard_map/ppermute | solution.py:127
  153.7 13.9 %copy-start.6 = (f32[2,2,32,32,128]{4,3,2,1,0:T(8,128)S(1)}, f32[2,2,32,32,128]{4,3,2,1,0:T(8,128)}, u32[]{:S(2)}) copy-start(f32[2,2,32,32,128]{4,3,2,1,0:T(8,128)} %get-tuple-element.17) | copy-start | bytes 6291460
  153.7 13.9 %copy-start.9 = (bf16[2,2,32,32,128]{4,3,2,1,0:T(8,128)(2,1)S(1)}, bf16[2,2,32,32,128]{4,3,2,1,0:T(8,128)(2,1)}, u32[]{:S(2)}) copy-start(bf16[2,2,32,32,128]{4,3,2,1,0:T(8,128)(2,1)} %copy-done.8) | copy-start | bytes 3145732
  153.7 16.1 %collective-permute-start.15 = (bf16[4,4,4096]{2,1,0:T(4,128)(2,1)S(1)}, bf16[4,4,4096]{2,1,0:T(4,128)(2,1)S(1)}, u32[]{:S(2)}, u32[]{:S(2)}) collective-permute-start(bf16[4,4,4096]{2,1,0:T(4,128)(2,1)S(1)} %maximum_select_fusion.1), channel_id=1, source_target_pairs={{0,8},{2,10},{4,12},{6,14},{8,0},{10,2},{12,4},{14,6},{1,9},{3,11}... | collective-permute-start | bytes 393224 | tf_op jit(solution)/shard_map/ppermute | solution.py:91
  169.1 24.1 %collective-permute-start.6 = (bf16[2,2,32,32,128]{4,3,2,1,0:T(8,128)(2,1)}, bf16[2,2,32,32,128]{4,3,2,1,0:T(8,128)(2,1)}, u32[]{:S(2)}, u32[]{:S(2)}) collective-permute-start(bf16[2,2,32,32,128]{4,3,2,1,0:T(8,128)(2,1)} %select_convert_fusion), channel_id=1, source_target_pairs={{0,2},{4,6},{8,10},{12,14},{2,0},{6,4},{10,8},{14,12},{1,3},{5,7},... | collective-permute-start | bytes 3145736 | tf_op jit(solution)/shard_map/ppermute | solution.py:80
  (26 other events, 156.0 us)

commit v11 on v9

--- a/solution.py
+++ b/solution.py
@@ -128,6 +128,54 @@
         for k in range(chunks):
             entering[k] = jnp.where(stage - column + 1 == k, got, entering[k])
     return jnp.stack(entering)
+
+
+def prefix_chunked(states, totals):
+    count = lax.axis_size("ctx")
+    columns = count // 2
+    place = lax.axis_index("ctx")
+    row_zero = place % 2 == 0
+    column = place // 2
+    half = states.shape[-2] // 2
+    first = states[..., :half, :]
+    second = states[..., half:, :]
+    mine = jnp.where(row_zero, first, second)
+    other = jnp.where(row_zero, second, first)
+    across = [(2 * m, 2 * m + 1) for m in range(columns)] + [
+        (2 * m + 1, 2 * m) for m in range(columns)
+    ]
+    chunks = states.shape[0]
+    even_state, even_total, window, growth = [], [], [], []
+    for k in range(chunks):
+        received, partner_total = send(other[k], totals[k], across)
+        even_state.append(jnp.where(row_zero, mine[k], received))
+        odd_state = jnp.where(row_zero, received, mine[k])
+        even_total.append(jnp.where(row_zero, totals[k], partner_total))
+        odd_total = jnp.where(row_zero, partner_total, totals[k])
+        window.append(scale(jnp.exp(odd_total), even_state[k]) + odd_state)
+        growth.append(jnp.exp(even_total[k] + odd_total))
+    entering = [jnp.zeros_like(window[k]) for k in range(chunks)]
+    for stage in range(columns - 1 + chunks - 1):
+        senders = [m for m in range(columns - 1) if 0 <= stage - m < chunks]
+        pairs = [(y + 2 * m, y + 2 * (m + 1)) for y in range(2) for m in senders]
+        sent = sorted({stage - m for m in senders})
+        outgoing = jnp.zeros_like(window[0])
+        for k in sent:
+            leaving = scale(growth[k], entering[k]) + window[k]
+            outgoing = jnp.where(stage - column == k, leaving, outgoing)
+        got = lax.ppermute(outgoing.astype(jnp.bfloat16), "ctx", pairs).astype(jnp.float32)
+        for k in sent:
+            entering[k] = jnp.where(stage - column + 1 == k, got, entering[k])
+    results = []
+    for k in range(chunks):
+        odd_entering = scale(jnp.exp(even_total[k]), entering[k]) + even_state[k]
+        outgoing = jnp.where(row_zero, odd_entering, entering[k])
+        partner, _ = send(outgoing, totals[k], across)
+        own_half = jnp.where(row_zero, entering[k], odd_entering)
+        first_half = jnp.where(row_zero, own_half, partner)
+        second_half = jnp.where(row_zero, partner, own_half)
+        results.append(jnp.concatenate([first_half, second_half], axis=-2))
+    return jnp.stack(results)
 
 
 def prefix_states(states, totals):
@@ -273,7 +321,10 @@
     )
     decoded = lax.psum(partial_value, "heads").astype(jnp.bfloat16)
 
-    entering = prefix_states(states, totals)
+    if lax.axis_size("ctx") <= 8:
+        entering = prefix_chunked(states, totals)
+    else:
+        entering = prefix_states(states, totals)
     prefill_out = finish(
         jnp.stack([term[2] for term in terms]),
         jnp.stack([term[0] for term in terms]),

time: 198 us -> 213 us (1.076)
  other arithmetic: 38.3 us -> 50.3 us
  starting transfers between devices: 33.6 us -> 24.4 us
  matrix products: 33.1 us -> 40.4 us
  local copies, waits for them, and re-layouts: 47.1 us -> 51 us
    ppermute x3, starting transfers between devices: 14.8 us -> 2.27 us  [reduce_scatter_ctx(): lax.ppermute(give, 'ctx', [(i, i ^ reach) for i in range(count)])]
    select_n x1 -> x5, other arithmetic: 2.51 us -> 9.78 us  [the longest x2 5.7 us: prefix_chunked(): first_half = jnp.where(row_zero, own_half, partner)]
    dot_general x1, matrix products: 1.25 us -> 4.88 us  [finish(): lax.dot_general(c_groups, low, numbers, preferred_element_type=jnp.float32)]
    dot_general x1, matrix products: 1.25 us -> 4.51 us  [finish(): lax.dot_general(c_groups, high, numbers, preferred_element_type=jnp.float32)]
    ppermute x3 -> x6, starting transfers between devices: 4.02 us -> 7.19 us  [send(): lax.ppermute((value.astype(jnp.bfloat16), total), 'ctx', pairs)]
    select_n x6, other arithmetic: 3.77 us -> 5.99 us  [gather_ctx(): jnp.where(upper, jnp.concatenate([got, value], axis=0), jnp.concatenate([...]
    ppermute x3 -> x6, waiting for transfers between devices: 3.78 us -> 5.77 us  [send(): lax.ppermute((value.astype(jnp.bfloat16), total), 'ctx', pairs)]
    another operation x9 -> x10, other arithmetic: 4.65 us -> 3.23 us
  transfers between devices with their start and end apart: 16 -> 19, of which waited for: 7 -> 9; matrix products, arithmetic and copies ran while one was open for 45% -> 49% of each run, Pallas kernels for 0% -> 0%
where the time goes in v11:
time: 213 us; the launch traced here: 209 us
  local copies, waits for them, and re-layouts  51 us (24%)
  other arithmetic  50.3 us (24%)
  matrix products  40.4 us (19%)
  waiting for transfers between devices  36.4 us (17%)
  starting transfers between devices  24.4 us (11%)
  blocking collectives  5.04 us (2%)
    ppermute x3, waiting for transfers between devices, reduce_scatter_ctx(): lax.ppermute(give, 'ctx', [(i, i ^ reach) for i in range(count)])  17.6 us
    unnamed x91, local copies, waits for them, and re-layouts  16 us
    dot_general x2, matrix products, block_terms(): jnp.einsum('gkts,sgkp->gktp', mixing, inputs_head, preferred_element_type...  14.2 us
    ppermute x4, starting transfers between devices, prefix_chunked(): lax.ppermute(outgoing.astype(jnp.bfloat16), 'ctx', pairs)  10.9 us
    slice x3, local copies, waits for them, and re-layouts, shards(): ssm_input[request]  9.7 us
    ppermute x4, waiting for transfers between devices, prefix_chunked(): lax.ppermute(outgoing.astype(jnp.bfloat16), 'ctx', pairs)  7.39 us
    ppermute x6, starting transfers between devices, send(): lax.ppermute((value.astype(jnp.bfloat16), total), 'ctx', pairs)  7.19 us
    convert_element_type x1, local copies, waits for them, and re-layouts, finish(): inputs_head = ssm_input.reshape(request_count, block_size, group_count, p...  7.11 us
  transfers between devices with their start and end apart: 19, of which 9 were waited for; matrix products, arithmetic and copies ran while one was open for 49% of the time, Pallas kernels for 0%

profile of v11, /device:TPU:18, one launch (start us, length us, event | category | flops | bytes accessed | tf_op | source)
XLA Modules:
  0.0 209.4 jit_solution(9406556504453960481)
XLA Ops:
  12.1 4.0 %fusion.76 = (bf16[1,256,4096]{2,1,0:T(8,128)(2,1)S(1)}, bf16[1,256,4096]{2,1,0:T(8,128)(2,1)}) fusion(bf16[2,256,4096]{2,1,0:T(8,128)(2,1)} %param.13), kind=kLoop, calls=%fused_computation.161 | loop fusion | bytes 8388608 | tf_op jit(solution)/shard_map/slice | solution.py:251
  16.1 2.5 %copy.150 = bf16[1,256,4096]{1,2,0:T(8,128)(2,1)} copy(bf16[1,256,4096]{2,1,0:T(8,128)(2,1)S(1)} %get-tuple-element.22) | data formatting | bytes 4194304 | tf_op jit(solution)/shard_map/slice | solution.py:251
  18.6 3.3 %copy.153 = bf16[1,256,4096]{1,2,0:T(8,128)(2,1)S(1)} copy(bf16[1,256,4096]{2,1,0:T(8,128)(2,1)} %get-tuple-element.23) | data formatting | bytes 4194304 | tf_op jit(solution)/shard_map/slice | solution.py:251
  21.9 3.1 %fusion.41 = f32[1,2,32,64,128]{4,3,2,1,0:T(8,128)S(1)} fusion(bf16[256,2,128,1]{0,2,3,1:T(8,128)(2,1)S(1)} %bitcast.222, bf16[256,2,32,64]{0,3,2,1:T(8,128)(2,1)} %bitcast.214, f32[256,2,32]{0,2,1:T(8,128)S(1)} %bitcast.227), kind=kOutput, calls=%fused_computation.56 | convolution fusion | flops 271581184 | bytes 4390912 | tf_op jit(solution)/shard_map/sgkp,sgn->gkpn/dot_general | solution.py:42
  40.3 7.6 %fusion.25 = f32[1,2,32,256,64]{3,4,2,1,0:T(8,128)} fusion(bf16[256,2,32,64]{0,3,2,1:T(8,128)(2,1)S(1)} %bitcast.215, f32[2,32,256]{2,1,0:T(8,128)} %bitcast.231, f32[2,32,256]{2,1,0:T(8,128)} %reduce_window_sum.88, f32[2,256,256]{2,1,0:T(8,128)S(1)} %fusion.83, pred[256,256]{1,0:T(8,128)(4,1)} %iota_compare_fusion), kind=kOutput, calls=%fused_computation.38 | convolution fusion | flops 562036736 | bytes 7012352 | tf_op jit(solution)/shard_map/gkts,sgkp->gktp/dot_general | solution.py:35
  51.1 2.7 %broadcast_select_fusion = f32[2,2,32,32,128]{4,3,2,1,0:T(8,128)S(1)} fusion(pred[]{:T(512)S(6)} %eq.43, f32[1,2,32,64,128]{4,3,2,1,0:T(8,128)} %copy-done.3, f32[1,2,32,64,128]{4,3,2,1,0:T(8,128)} %copy-done.2), kind=kLoop, calls=%fused_computation.90 | loop fusion | flops 1572864 | bytes 6291457 | tf_op jit(solution)/shard_map/jit(_where)/select_n | solution.py:142
  57.0 3.1 %collective-permute-done.12 = f32[4,1153]{1,0:T(4,128)} collective-permute-done((f32[4,1153]{1,0:T(4,128)}, f32[4,1153]{1,0:T(4,128)}, u32[]{:S(2)}, u32[]{:S(2)}) %collective-permute-start.12) | collective-permute-done | bytes 18480 | tf_op jit(solution)/shard_map/ppermute | solution.py:91
  62.2 3.0 %fusion.26 = (bf16[2,2,32,64,128,1]{4,3,2,1,0,5:T(8,128)(2,1)S(1)}, bf16[2,2,32,64,128,1]{4,3,2,1,0,5:T(8,128)(2,1)S(1)}) fusion(f32[1,2,32,64,128]{4,3,2,1,0:T(8,128)} %copy-done.3, f32[1,2,32,64,128]{4,3,2,1,0:T(8,128)} %copy-done.2, f32[2,2,32]{2,1,0:T(2,128)S(1)} %exp.77), kind=kLoop, calls=%fused_computation.39 | loop fusion | flops 6291456 | bytes 8389120 | tf_op jit(solution)/shard_map/convert_element_type | solution.py:281
  65.2 2.0 fusion.31
  67.2 2.1 add_bitcast_fusion
  76.4 2.1 fusion.84
  78.5 4.4 %collective-permute-done.13 = f32[4,4,2,32,64]{4,3,2,1,0:T(8,128)} collective-permute-done((f32[4,4,2,32,64]{4,3,2,1,0:T(8,128)}, f32[4,4,2,32,64]{4,3,2,1,0:T(8,128)}, u32[]{:S(2)}, u32[]{:S(2)}) %collective-permute-start.13) | collective-permute-done | bytes 262176 | tf_op jit(solution)/shard_map/ppermute | solution.py:111
  86.2 5.5 %collective-permute-done.14 = f32[2,4,2,32,64]{4,3,2,1,0:T(8,128)S(1)} collective-permute-done((f32[2,4,2,32,64]{4,3,2,1,0:T(8,128)S(1)}, f32[2,4,2,32,64]{4,3,2,1,0:T(8,128)S(1)}, u32[]{:S(2)}, u32[]{:S(2)}) %collective-permute-start.14) | collective-permute-done | bytes 131104 | tf_op jit(solution)/shard_map/ppermute | solution.py:111
  96.9 7.6 %collective-permute-done.15 = f32[1,4,2,32,64]{4,3,2,1,0:T(8,128)S(1)} collective-permute-done((f32[1,4,2,32,64]{4,3,2,1,0:T(8,128)S(1)}, f32[1,4,2,32,64]{4,3,2,1,0:T(8,128)S(1)}, u32[]{:S(2)}, u32[]{:S(2)}) %collective-permute-start.15) | collective-permute-done | bytes 65568 | tf_op jit(solution)/shard_map/ppermute | solution.py:111
  107.4 2.7 %select_convert_fusion.4 = bf16[2,32,32,128]{3,2,1,0:T(8,128)(2,1)} fusion(bf16[2,32,32,128]{3,2,1,0:T(8,128)(2,1)} %collective-permute-done.4, f32[2,32]{1,0:T(2,128)} %get-tuple-element.42, f32[2,32]{1,0:T(2,128)} %get-tuple-element.45, pred[]{:T(512)S(6)} %eq.47, pred[]{:T(512)S(6)} %eq.46, bf16[2,32,32,128]{3,2,1,0:T(8,128)(2,1)S(1)} %collective-permute-done.3, ...), kind=kLoop, calls=%fused_computation.87 | loop fusion | flops 4718592 | bytes 4195331 | tf_op jit(solution)/shard_map/convert_element_type | solution.py:166
  115.2 6.2 %collective-permute-done.5 = bf16[2,32,32,128]{3,2,1,0:T(8,128)(2,1)} collective-permute-done((bf16[2,32,32,128]{3,2,1,0:T(8,128)(2,1)}, bf16[2,32,32,128]{3,2,1,0:T(8,128)(2,1)}, u32[]{:S(2)}, u32[]{:S(2)}) %collective-permute-start.5) | collective-permute-done | bytes 524320 | tf_op jit(solution)/shard_map/ppermute | solution.py:166
  121.5 3.0 %fusion.45 = bf16[2,32,32,128]{3,2,1,0:T(8,128)(2,1)} fusion(bf16[2,32,32,128]{3,2,1,0:T(8,128)(2,1)} %collective-permute-done.5, bf16[2,32,32,128]{3,2,1,0:T(8,128)(2,1)} %collective-permute-done.4, f32[2,32]{1,0:T(2,128)} %get-tuple-element.42, f32[2,32]{1,0:T(2,128)S(1)} %copy-done.32, pred[]{:T(512)S(6)} %eq.49, pred[]{:T(512)S(6)} %eq.47, pred[]{:T(512)S(6)} %eq.45, ...), kind=kLoop, calls=%fused_computation.73 | loop fusion | flops 5767168 | bytes 4719620 | tf_op jit(solution)/shard_map/convert_element_type | solution.py:166
  124.5 1.9 collective-permute-start.6
  126.5 6.6 %fusion.24 = f32[1,2,32,256,64]{3,4,2,1,0:T(8,128)} fusion(bf16[256,2,32,64]{0,3,2,1:T(8,128)(2,1)S(1)} %bitcast.213, f32[2,32,256]{2,1,0:T(8,128)S(1)} %bitcast.230, f32[2,32,256]{2,1,0:T(8,128)S(1)} %copy-done.28, f32[2,256,256]{2,1,0:T(8,128)S(1)} %copy-done.20, pred[256,256]{1,0:T(8,128)(4,1)S(1)} %copy-done.27), kind=kOutput, calls=%fused_computation.37 | convolution fusion | flops 562036736 | bytes 7012352 | tf_op jit(solution)/shard_map/gkts,sgkp->gktp/dot_general | solution.py:35
  134.4 7.1 %copy.168 = f32[2,256,4096]{1,2,0:T(8,128)} copy(bf16[2,256,4096]{2,1,0:T(8,128)(2,1)} %param.13) | data formatting | bytes 12582912 | tf_op jit(solution)/shard_map/convert_element_type | solution.py:63
  146.3 2.5 %collective-permute-done.18 = bf16[4,4,4096]{2,1,0:T(4,128)(2,1)S(1)} collective-permute-done((bf16[4,4,4096]{2,1,0:T(4,128)(2,1)S(1)}, bf16[4,4,4096]{2,1,0:T(4,128)(2,1)S(1)}, u32[]{:S(2)}, u32[]{:S(2)}) %collective-permute-start.18) | collective-permute-done | bytes 131104 | tf_op jit(solution)/shard_map/ppermute | solution.py:91
  149.0 4.8 %collective-permute-done.7 = bf16[2,32,32,128]{3,2,1,0:T(8,128)(2,1)S(1)} collective-permute-done((bf16[2,32,32,128]{3,2,1,0:T(8,128)(2,1)S(1)}, bf16[2,32,32,128]{3,2,1,0:T(8,128)(2,1)S(1)}, u32[]{:S(2)}, u32[]{:S(2)}) %collective-permute-start.7) | collective-permute-done | bytes 524320 | tf_op jit(solution)/shard_map/ppermute | solution.py:80
  153.9 3.9 %convert_select_fusion.3 = (f32[2,32,32,128]{3,2,1,0:T(8,128)}, f32[2,32,32,128]{3,2,1,0:T(8,128)}, bf16[2,32,32,128]{3,2,1,0:T(8,128)(2,1)S(1)}) fusion(bf16[2,32,32,128]{3,2,1,0:T(8,128)(2,1)S(1)} %collective-permute-done.7, pred[]{:T(512)S(6)} %eq.43, bf16[2,32,32,128]{3,2,1,0:T(8,128)(2,1)S(1)} %collective-permute-done.3, ...), kind=kLoop, calls=%fused_computation.60 | loop fusion | flops 6291456 | bytes 7865094 | tf_op jit(solution)/shard_map/jit(_where)/select_n | solution.py:175
  157.7 6.3 %collective-permute-start.8 = (bf16[2,32,32,128]{3,2,1,0:T(8,128)(2,1)S(1)}, bf16[2,32,32,128]{3,2,1,0:T(8,128)(2,1)S(1)}, u32[]{:S(2)}, u32[]{:S(2)}) collective-permute-start(bf16[2,32,32,128]{3,2,1,0:T(8,128)(2,1)S(1)} %get-tuple-element.24), channel_id=1, source_target_pairs={{8,12},{10,14},{9,13},{11,15},{24,28},{26,30},{25,29},{27,31}} | collective-permute-start | bytes 1572872 | tf_op jit(solution)/shard_map/ppermute | solution.py:166
  164.0 5.5 %fusion.5 = f32[8,4,1024]{2,0,1:T(8,128)} fusion(bf16[4096,1024]{1,0:T(8,128)(2,1)} %param.25, bf16[8,4,4096]{2,1,0:T(4,128)(2,1)S(1)} %maximum_select_fusion), kind=kOutput, calls=%fused_computation.8 | convolution fusion | flops 268435456 | bytes 8781824 | tf_op jit(solution)/shard_map/jup,pd->jud/dot_general | solution.py:316
  171.5 2.4 %select_convert_fusion.1 = bf16[2,32,32,128]{3,2,1,0:T(8,128)(2,1)} fusion(bf16[2,32,32,128]{3,2,1,0:T(8,128)(2,1)} %collective-permute-done.5, bf16[2,32,32,128]{3,2,1,0:T(8,128)(2,1)} %collective-permute-done.6, bf16[2,32,32,128]{3,2,1,0:T(8,128)(2,1)S(1)} %collective-permute-done.8, bf16[2,32,32,128]{3,2,1,0:T(8,128)(2,1)S(1)} %collective-permute-done.1, ...), kind=kLoop, calls=%fused_computation.79 | loop fusion | flops 3145728 | bytes 3670276 | tf_op jit(solution)/shard_map/convert_element_type | solution.py:80
  175.5 5.0 %all-reduce.1 = bf16[8,4,1024]{2,0,1:T(8,128)(2,1)} all-reduce(f32[8,4,1024]{2,0,1:T(8,128)} %fusion.5), channel_id=1, replica_groups=mesh['groups'=2,'ctx'=8,'heads'=2] {'heads'}, use_global_device_ids=true, to_apply=%region_7.8 | all-reduce | flops 32768 | bytes 196608 | tf_op jit(solution)/shard_map/psum | solution.py:322
  183.4 1.9 convert_select_fusion.1
  186.7 4.5 %fusion.22 = f32[2,2,2048,256]{3,2,1,0:T(8,128)} fusion(f32[1,2,2048,128]{3,2,1,0:T(8,128)S(1)} %bitcast.209, f32[1,2,2048,128]{3,2,1,0:T(8,128)S(1)} %bitcast.207, bf16[2,256,256]{2,1,0:T(8,128)(2,1)S(1)} %copy-done.10), kind=kOutput, calls=%fused_computation.36 | convolution fusion | flops 537919488 | bytes 12845056 | tf_op jit(solution)/shard_map/dot_general | solution.py:55
  191.2 4.9 %convolution_add_fusion = f32[2,2,2048,256]{3,2,1,0:T(8,128)S(1)} fusion(f32[2,2,2048,256]{3,2,1,0:T(8,128)} %fusion.22, f32[1,2,2048,128]{3,2,1,0:T(8,128)S(1)} %bitcast.210, f32[1,2,2048,128]{3,2,1,0:T(8,128)S(1)} %bitcast.208, bf16[2,256,256]{2,1,0:T(8,128)(2,1)S(1)} %copy-done.10), kind=kOutput, calls=%fused_computation.27 | convolution fusion | flops 544210944 | bytes 21233664 | tf_op jit(solution)/shard_map/dot_general | solution.py:57
  197.1 6.0 %fusion.4 = bf16[2,256,2,32,64]{1,4,3,2,0:T(8,128)(2,1)} fusion(f32[1,2,32,256,64]{3,4,2,1,0:T(8,128)} %fusion.24, f32[1,2,32,256,64]{3,4,2,1,0:T(8,128)S(1)} %copy-done.9, f32[2,256,2,32,64]{1,4,3,2,0:T(8,128)S(1)} %bitcast.205, f32[2,2,256,32,64]{2,4,3,1,0:T(8,128)S(1)} %bitcast.206, f32[2,32]{1,0:T(2,128)S(1)} %copy-done.37, f32[2,2,256,32]{2,3,1,0:T(8,128)S(1)} %fusion.56), kind=kLoop, calls=%fused_computation.7 | loop fusion | flops 12582912 | bytes 29491456 | tf_op jit(solution)/shard_map/convert_element_type | solution.py:66
  203.1 6.3 %copy.183 = bf16[2,256,4096]{2,1,0:T(8,128)(2,1)} copy(bf16[2,256,4096]{1,2,0:T(8,128)(2,1)} %bitcast.211) | data formatting | bytes 8388608
  (206 shorter events, 73.0 us)
Async XLA Ops:
  0.6 32.7 %copy-start = (bf16[1,4,256]{2,1,0:T(4,128)(2,1)S(1)}, bf16[1,4,256]{2,1,0:T(4,128)(2,1)}, u32[]{:S(2)}) copy-start(bf16[1,4,256]{2,1,0:T(4,128)(2,1)} %param.21) | copy-start | bytes 6148
  0.6 11.2 %copy-start.22 = (bf16[2,256,256]{2,1,0:T(8,128)(2,1)S(1)}, bf16[2,256,256]{2,1,0:T(8,128)(2,1)}, u32[]{:S(2)}) copy-start(bf16[2,256,256]{2,1,0:T(8,128)(2,1)} %param.14) | copy-start | bytes 786436
  3.4 12.7 %copy-start.30 = (f32[64,2]{0,1:T(2,128)}, f32[64,2]{0,1:T(2,128)S(1)}, u32[]{:S(2)}) copy-start(f32[64,2]{0,1:T(2,128)S(1)} %slice.112) | copy-start | bytes 1540
  4.4 91.3 %collective-permute-start = (f32[2,32]{1,0:T(2,128)}, f32[2,32]{1,0:T(2,128)}, u32[]{:S(2)}, u32[]{:S(2)}) collective-permute-start(f32[2,32]{1,0:T(2,128)} %squeeze_stack_reshape_squeeze.4), channel_id=1, source_target_pairs={{0,2},{4,6},{8,10},{12,14},{2,0},{6,4},{10,8},{14,12},{1,3},{5,7},... | collective-permute-start | bytes 776 | tf_op jit(solution)/shard_map/ppermute | solution.py:80
  6.6 78.4 %collective-permute-start.2 = (f32[2,32]{1,0:T(2,128)}, f32[2,32]{1,0:T(2,128)}, u32[]{:S(2)}, u32[]{:S(2)}) collective-permute-start(f32[2,32]{1,0:T(2,128)} %squeeze_stack_reshape_squeeze.5), channel_id=1, source_target_pairs={{0,2},{4,6},{8,10},{12,14},{2,0},{6,4},{10,8},{14,12},{1,3},{5,7},... | collective-permute-start | bytes 776 | tf_op jit(solution)/shard_map/ppermute | solution.py:80
  9.3 39.3 %collective-permute-start.10 = (f32[1,1153]{1,0:T(1,128)}, f32[1,1153]{1,0:T(1,128)}, u32[]{:S(2)}, u32[]{:S(2)}) collective-permute-start(f32[1,1153]{1,0:T(1,128)} %broadcast_in_dim.81), channel_id=1, source_target_pairs={{0,2},{2,0},{4,6},{6,4},{8,10},{10,8},{12,14},{14,12},{1,3},{3,1},... | collective-permute-start | bytes 13844 | tf_op jit(solution)/shard_map/ppermute | solution.py:91
  12.0 9.9 %copy-start.16 = (bf16[1,256,256]{1,2,0:T(8,128)(2,1)}, bf16[1,256,256]{1,2,0:T(8,128)(2,1)S(1)}, u32[]{:S(2)}) copy-start(bf16[1,256,256]{1,2,0:T(8,128)(2,1)S(1)} %copy.209) | copy-start | bytes 393220
  12.1 12.8 %copy-start.15 = (bf16[1,256,256]{1,2,0:T(8,128)(2,1)}, bf16[1,256,256]{1,2,0:T(8,128)(2,1)S(1)}, u32[]{:S(2)}) copy-start(bf16[1,256,256]{1,2,0:T(8,128)(2,1)S(1)} %copy.210) | copy-start | bytes 393220
  27.7 12.6 %copy-start.7 = (bf16[1,256,4096]{1,2,0:T(8,128)(2,1)S(1)}, bf16[1,256,4096]{1,2,0:T(8,128)(2,1)}, u32[]{:S(2)}) copy-start(bf16[1,256,4096]{1,2,0:T(8,128)(2,1)} %copy.150) | copy-start | bytes 6291460
  28.7 78.7 %collective-permute-start.1 = (bf16[2,32,32,128]{3,2,1,0:T(8,128)(2,1)}, bf16[2,32,32,128]{3,2,1,0:T(8,128)(2,1)S(1)}, u32[]{:S(2)}, u32[]{:S(2)}) collective-permute-start(bf16[2,32,32,128]{3,2,1,0:T(8,128)(2,1)} %get-tuple-element.27), channel_id=1, source_target_pairs={{0,2},{4,6},{8,10},{12,14},{2,0},{6,4},{10,8},{14,12},{1,3},{5,7},... | collective-permute-start | bytes 1572872 | tf_op jit(solution)/shard_map/ppermute | solution.py:80
  29.2 62.6 %collective-permute-start.3 = (bf16[2,32,32,128]{3,2,1,0:T(8,128)(2,1)}, bf16[2,32,32,128]{3,2,1,0:T(8,128)(2,1)S(1)}, u32[]{:S(2)}, u32[]{:S(2)}) collective-permute-start(bf16[2,32,32,128]{3,2,1,0:T(8,128)(2,1)} %get-tuple-element.28), channel_id=1, source_target_pairs={{0,2},{4,6},{8,10},{12,14},{2,0},{6,4},{10,8},{14,12},{1,3},{5,7},... | collective-permute-start | bytes 1572872 | tf_op jit(solution)/shard_map/ppermute | solution.py:80
  49.4 4.3 %collective-permute-start.11 = (f32[2,1153]{1,0:T(2,128)S(1)}, f32[2,1153]{1,0:T(2,128)}, u32[]{:S(2)}, u32[]{:S(2)}) collective-permute-start(f32[2,1153]{1,0:T(2,128)S(1)} %maximum_select_fusion.5), channel_id=1, source_target_pairs={{0,4},{2,6},{4,0},{6,2},{8,12},{10,14},{12,8},{14,10},{1,5},{3,7},... | collective-permute-start | bytes 27680 | tf_op jit(solution)/shard_map/ppermute | solution.py:91
  55.2 5.0 %collective-permute-start.12 = (f32[4,1153]{1,0:T(4,128)}, f32[4,1153]{1,0:T(4,128)}, u32[]{:S(2)}, u32[]{:S(2)}) collective-permute-start(f32[4,1153]{1,0:T(4,128)} %maximum_select_fusion.4), channel_id=1, source_target_pairs={{0,8},{2,10},{4,12},{6,14},{8,0},{10,2},{12,4},{14,6},{1,9},{3,11}... | collective-permute-start | bytes 55352 | tf_op jit(solution)/shard_map/ppermute | solution.py:91
  71.7 11.2 %collective-permute-start.13 = (f32[4,4,2,32,64]{4,3,2,1,0:T(8,128)}, f32[4,4,2,32,64]{4,3,2,1,0:T(8,128)}, u32[]{:S(2)}, u32[]{:S(2)}) collective-permute-start(f32[4,4,2,32,64]{4,3,2,1,0:T(8,128)} %select_bitcast_fusion), channel_id=1, source_target_pairs={{0,2},{2,0},{4,6},{6,4},{8,10},{10,8},{12,14},{14,12},{1,3},{3,1},... | collective-permute-start | bytes 786440 | tf_op jit(solution)/shard_map/ppermute | solution.py:111
  74.7 29.9 %copy-start.36 = (f32[2,32]{1,0:T(2,128)}, f32[2,32]{1,0:T(2,128)S(1)}, u32[]{:S(2)}) copy-start(f32[2,32]{1,0:T(2,128)S(1)} %mul.283) | copy-start | bytes 772
  84.4 20.2 %copy-start.17 = (f32[1,4,2,32,64]{4,3,2,1,0:T(8,128)S(1)}, f32[1,4,2,32,64]{4,3,2,1,0:T(8,128)}, u32[]{:S(2)}) copy-start(f32[1,4,2,32,64]{4,3,2,1,0:T(8,128)} %reshape.389) | copy-start | bytes 196612
  84.4 20.2 %copy-start.19 = (f32[4,2,32,64]{3,2,1,0:T(8,128)S(1)}, f32[4,2,32,64]{3,2,1,0:T(8,128)}, u32[]{:S(2)}) copy-start(f32[4,2,32,64]{3,2,1,0:T(8,128)} %multiply_reduce_fusion) | copy-start | bytes 196612
  84.5 7.3 %collective-permute-start.14 = (f32[2,4,2,32,64]{4,3,2,1,0:T(8,128)S(1)}, f32[2,4,2,32,64]{4,3,2,1,0:T(8,128)S(1)}, u32[]{:S(2)}, u32[]{:S(2)}) collective-permute-start(f32[2,4,2,32,64]{4,3,2,1,0:T(8,128)S(1)} %select_bitcast_fusion.1), channel_id=1, source_target_pairs={{0,4},{2,6},{4,0},{6,2},{8,12},{10,14},{12,8},{14,10},{1,5},{3,7},... | collective-permute-start | bytes 393224 | tf_op jit(solution)/shard_map/ppermute | solution.py:111
  92.9 14.4 %collective-permute-start.4 = (bf16[2,32,32,128]{3,2,1,0:T(8,128)(2,1)}, bf16[2,32,32,128]{3,2,1,0:T(8,128)(2,1)}, u32[]{:S(2)}, u32[]{:S(2)}) collective-permute-start(bf16[2,32,32,128]{3,2,1,0:T(8,128)(2,1)} %select_convert_fusion.5), channel_id=1, source_target_pairs={{0,4},{2,6},{1,5},{3,7},{16,20},{18,22},{17,21},{19,23}} | collective-permute-start | bytes 1572872 | tf_op jit(solution)/shard_map/ppermute | solution.py:166
  94.4 10.2 %collective-permute-start.15 = (f32[1,4,2,32,64]{4,3,2,1,0:T(8,128)S(1)}, f32[1,4,2,32,64]{4,3,2,1,0:T(8,128)S(1)}, u32[]{:S(2)}, u32[]{:S(2)}) collective-permute-start(f32[1,4,2,32,64]{4,3,2,1,0:T(8,128)S(1)} %select_bitcast_fusion.2), channel_id=1, source_target_pairs={{0,8},{2,10},{4,12},{6,14},{8,0},{10,2},{12,4},{14,6},{1,9},{3,11}... | collective-permute-start | bytes 196616 | tf_op jit(solution)/shard_map/ppermute | solution.py:111
  106.9 6.8 %collective-permute-start.16 = (bf16[1,4,4096]{2,1,0:T(4,128)(2,1)}, bf16[1,4,4096]{2,1,0:T(4,128)(2,1)}, u32[]{:S(2)}, u32[]{:S(2)}) collective-permute-start(bf16[1,4,4096]{2,1,0:T(4,128)(2,1)} %convert_element_type.188), channel_id=1, source_target_pairs={{0,2},{2,0},{4,6},{6,4},{8,10},{10,8},{12,14},{14,12},{1,3},{3,1},... | collective-permute-start | bytes 98312 | tf_op jit(solution)/shard_map/ppermute | solution.py:91
  107.4 14.1 %copy-start.32 = (f32[2,32]{1,0:T(2,128)S(1)}, f32[2,32]{1,0:T(2,128)}, u32[]{:S(2)}) copy-start(f32[2,32]{1,0:T(2,128)} %get-tuple-element.46) | copy-start | bytes 772
  110.1 11.4 %collective-permute-start.5 = (bf16[2,32,32,128]{3,2,1,0:T(8,128)(2,1)}, bf16[2,32,32,128]{3,2,1,0:T(8,128)(2,1)}, u32[]{:S(2)}, u32[]{:S(2)}) collective-permute-start(bf16[2,32,32,128]{3,2,1,0:T(8,128)(2,1)} %select_convert_fusion.4), channel_id=1, source_target_pairs={{0,4},{4,8},{2,6},{6,10},{1,5},{5,9},{3,7},{7,11},{16,20},{20,24},... | collective-permute-start | bytes 1572872 | tf_op jit(solution)/shard_map/ppermute | solution.py:166
  115.2 26.3 %collective-permute-start.17 = (bf16[2,4,4096]{2,1,0:T(4,128)(2,1)}, bf16[2,4,4096]{2,1,0:T(4,128)(2,1)}, u32[]{:S(2)}, u32[]{:S(2)}) collective-permute-start(bf16[2,4,4096]{2,1,0:T(4,128)(2,1)} %maximum_select_fusion.2), channel_id=1, source_target_pairs={{0,4},{2,6},{4,0},{6,2},{8,12},{10,14},{12,8},{14,10},{1,5},{3,7},... | collective-permute-start | bytes 196616 | tf_op jit(solution)/shard_map/ppermute | solution.py:91
  124.5 18.3 %collective-permute-start.6 = (bf16[2,32,32,128]{3,2,1,0:T(8,128)(2,1)}, bf16[2,32,32,128]{3,2,1,0:T(8,128)(2,1)}, u32[]{:S(2)}, u32[]{:S(2)}) collective-permute-start(bf16[2,32,32,128]{3,2,1,0:T(8,128)(2,1)} %fusion.45), channel_id=1, source_target_pairs={{4,8},{8,12},{6,10},{10,14},{5,9},{9,13},{7,11},{11,15},{20,24},{2... | collective-permute-start | bytes 1572872 | tf_op jit(solution)/shard_map/ppermute | solution.py:166
  142.7 6.0 %collective-permute-start.18 = (bf16[4,4,4096]{2,1,0:T(4,128)(2,1)S(1)}, bf16[4,4,4096]{2,1,0:T(4,128)(2,1)S(1)}, u32[]{:S(2)}, u32[]{:S(2)}) collective-permute-start(bf16[4,4,4096]{2,1,0:T(4,128)(2,1)S(1)} %maximum_select_fusion.1), channel_id=1, source_target_pairs={{0,8},{2,10},{4,12},{6,14},{8,0},{10,2},{12,4},{14,6},{1,9},{3,11}... | collective-permute-start | bytes 393224 | tf_op jit(solution)/shard_map/ppermute | solution.py:91
  144.6 9.2 %collective-permute-start.7 = (bf16[2,32,32,128]{3,2,1,0:T(8,128)(2,1)S(1)}, bf16[2,32,32,128]{3,2,1,0:T(8,128)(2,1)S(1)}, u32[]{:S(2)}, u32[]{:S(2)}) collective-permute-start(bf16[2,32,32,128]{3,2,1,0:T(8,128)(2,1)S(1)} %select_convert_fusion.3), channel_id=1, source_target_pairs={{0,2},{4,6},{8,10},{12,14},{2,0},{6,4},{10,8},{14,12},{1,3},{5,7},... | collective-permute-start | bytes 1572872 | tf_op jit(solution)/shard_map/ppermute | solution.py:80
  157.7 13.8 %copy-start.33 = (f32[2,32]{1,0:T(2,128)S(1)}, f32[2,32]{1,0:T(2,128)}, u32[]{:S(2)}) copy-start(f32[2,32]{1,0:T(2,128)} %get-tuple-element.43) | copy-start | bytes 772
  157.7 12.9 %collective-permute-start.8 = (bf16[2,32,32,128]{3,2,1,0:T(8,128)(2,1)S(1)}, bf16[2,32,32,128]{3,2,1,0:T(8,128)(2,1)S(1)}, u32[]{:S(2)}, u32[]{:S(2)}) collective-permute-start(bf16[2,32,32,128]{3,2,1,0:T(8,128)(2,1)S(1)} %get-tuple-element.24), channel_id=1, source_target_pairs={{8,12},{10,14},{9,13},{11,15},{24,28},{26,30},{25,29},{27,31}} | collective-permute-start | bytes 1572872 | tf_op jit(solution)/shard_map/ppermute | solution.py:166
  169.5 12.6 %copy-start.12 = (bf16[2,32,32,128]{3,2,1,0:T(8,128)(2,1)S(1)}, bf16[2,32,32,128]{3,2,1,0:T(8,128)(2,1)}, u32[]{:S(2)}) copy-start(bf16[2,32,32,128]{3,2,1,0:T(8,128)(2,1)} %copy-done.11) | copy-start | bytes 1572868
  173.9 9.5 %collective-permute-start.9 = (bf16[2,32,32,128]{3,2,1,0:T(8,128)(2,1)}, bf16[2,32,32,128]{3,2,1,0:T(8,128)(2,1)}, u32[]{:S(2)}, u32[]{:S(2)}) collective-permute-start(bf16[2,32,32,128]{3,2,1,0:T(8,128)(2,1)} %select_convert_fusion.1), channel_id=1, source_target_pairs={{0,2},{4,6},{8,10},{12,14},{2,0},{6,4},{10,8},{14,12},{1,3},{5,7},... | collective-permute-start | bytes 1572872 | tf_op jit(solution)/shard_map/ppermute | solution.py:80
  186.7 9.4 %slice-start = ((s8[8388608]{0:T(1024)(128)(4,1)}), s8[4194304]{0:T(1024)(128)(4,1)S(1)}, s32[]{:S(2)}) async-start(s8[8388608]{0:T(1024)(128)(4,1)} %bitcast.203), calls=%async_computation | async-start | bytes 8388608
  (29 other events, 126.1 us)

commit v12 on v9

--- a/solution.py
+++ b/solution.py
@@ -111,6 +111,13 @@
         value = keep + lax.ppermute(give, "ctx", [(i, i ^ reach) for i in range(count)])
         reach *= 2
     return value
+
+
+def exchange_ctx(value, total):
+    count = lax.axis_size("ctx")
+    got = lax.all_to_all(value, "ctx", 0, 0, tiled=True)
+    got = got.reshape((count, value.shape[0] // count) + value.shape[1:])
+    return jnp.sum(got, axis=0) if total else got.reshape(value.shape)
 
 
 def chain_columns(window, window_total, column, columns):
@@ -240,7 +247,7 @@
     for request in range(1, request_count):
         pick = (all_request == request)[:, None, None, None, None]
         contribution = jnp.where(pick, projected[request], contribution)
-    from_prompt = reduce_scatter_ctx(contribution)
+    from_prompt = exchange_ctx(contribution, True)
 
     row_input = new_input.reshape(slots, steps, group_count, per_group, HEAD_DIM).astype(
         jnp.float32
@@ -267,7 +274,7 @@
     new_output = value.reshape(slots, steps, -1).astype(jnp.bfloat16)
     partial_value = jnp.einsum(
         "jup,pd->jud",
-        gather_ctx(new_output),
+        exchange_ctx(jnp.concatenate([new_output] * count, axis=0), False),
         out_weight,
         preferred_element_type=jnp.float32,
     )

time: 198 us -> 191 us (0.965)
  waiting for transfers between devices: 36.3 us -> 16.8 us
  local copies, waits for them, and re-layouts: 47.1 us -> 61 us
  starting transfers between devices: 33.6 us -> 28.4 us
  other arithmetic: 38.3 us -> 40.4 us
    ppermute x3 -> x0, waiting for transfers between devices: 19.5 us -> none  [reduce_scatter_ctx(): lax.ppermute(give, 'ctx', [(i, i ^ reach) for i in range(count)])]
    ppermute x3 -> x0, starting transfers between devices: 14.8 us -> none  [reduce_scatter_ctx(): lax.ppermute(give, 'ctx', [(i, i ^ reach) for i in range(count)])]
    all_to_all x0 -> x2, starting transfers between devices: none -> 13 us  [exchange_ctx(): got = lax.all_to_all(value, 'ctx', 0, 0, tiled=True)]
    unnamed x92 -> x96, local copies, waits for them, and re-layouts: 15.8 us -> 20.8 us
    ppermute x4, starting transfers between devices: 11 us -> 7.2 us  [chain_columns(): lax.ppermute(outgoing.astype(jnp.bfloat16), 'ctx', pairs)]
    ppermute x3, waiting for transfers between devices: 3.78 us -> 0.02 us  [send(): lax.ppermute((value.astype(jnp.bfloat16), total), 'ctx', pairs)]
    all_to_all x0 -> x1, other arithmetic: none -> 3.65 us  [exchange_ctx(): got = lax.all_to_all(value, 'ctx', 0, 0, tiled=True)]
    select_n x6 -> x3, other arithmetic: 3.77 us -> 0.83 us  [gather_ctx(): jnp.where(upper, jnp.concatenate([got, value], axis=0), jnp.concatenate([...]
  transfers between devices with their start and end apart: 16 -> 12, of which waited for: 7 -> 5; matrix products, arithmetic and copies ran while one was open for 45% -> 56% of each run, Pallas kernels for 0% -> 0%
where the time goes in v12:
time: 191 us; the launch traced here: 188 us
  local copies, waits for them, and re-layouts  61 us (32%)
  other arithmetic  40.4 us (21%)
  matrix products  34.4 us (18%)
  starting transfers between devices  28.4 us (15%)
  waiting for transfers between devices  16.8 us (9%)
  blocking collectives  5.02 us (3%)
  between operations  1.96 us (1%)
    unnamed x96, local copies, waits for them, and re-layouts  20.8 us
    dot_general x2, matrix products, block_terms(): jnp.einsum('gkts,sgkp->gktp', mixing, inputs_head, preferred_element_type...  14.5 us
    all_to_all x2, starting transfers between devices, exchange_ctx(): got = lax.all_to_all(value, 'ctx', 0, 0, tiled=True)  13 us
    slice x3, local copies, waits for them, and re-layouts, shards(): ssm_input[request]  10.5 us
    ppermute x4, waiting for transfers between devices, chain_columns(): lax.ppermute(outgoing.astype(jnp.bfloat16), 'ctx', pairs)  10.3 us
    ppermute x4, starting transfers between devices, chain_columns(): lax.ppermute(outgoing.astype(jnp.bfloat16), 'ctx', pairs)  7.2 us
    convert_element_type x1, local copies, waits for them, and re-layouts, finish(): inputs_head = ssm_input.reshape(request_count, block_size, group_count, p...  7.12 us
    ppermute x3, waiting for transfers between devices, gather_ctx(): got = lax.ppermute(value, 'ctx', [(i, i ^ reach) for i in range(count)])  6.44 us
  transfers between devices with their start and end apart: 12, of which 5 were waited for; matrix products, arithmetic and copies ran while one was open for 56% of the time, Pallas kernels for 0%

profile of v12, /device:TPU:18, one launch (start us, length us, event | category | flops | bytes accessed | tf_op | source)
XLA Modules:
  0.0 187.9 jit_solution(5586770124279665061)
XLA Ops:
  10.5 4.0 %fusion.70 = (bf16[1,256,4096]{2,1,0:T(8,128)(2,1)}, bf16[1,256,4096]{2,1,0:T(8,128)(2,1)S(1)}) fusion(bf16[2,256,4096]{2,1,0:T(8,128)(2,1)} %param.13), kind=kLoop, calls=%fused_computation.143 | loop fusion | bytes 8388608 | tf_op jit(solution)/shard_map/slice | solution.py:210
  14.4 4.1 %copy.208 = bf16[1,256,4096]{1,2,0:T(8,128)(2,1)} copy(bf16[1,256,4096]{2,1,0:T(8,128)(2,1)} %get-tuple-element.24) | data formatting | bytes 4194304 | tf_op jit(solution)/shard_map/slice | solution.py:210
  18.5 2.4 %copy.211 = bf16[1,256,4096]{1,2,0:T(8,128)(2,1)} copy(bf16[1,256,4096]{2,1,0:T(8,128)(2,1)S(1)} %get-tuple-element.25) | data formatting | bytes 4194304 | tf_op jit(solution)/shard_map/slice | solution.py:210
  21.0 2.5 %fusion.41 = f32[1,2,32,64,128]{4,3,2,1,0:T(8,128)S(1)} fusion(bf16[256,2,128,1]{0,2,3,1:T(8,128)(2,1)S(1)} %bitcast.186, bf16[256,2,32,64]{0,3,2,1:T(8,128)(2,1)} %bitcast.181, f32[256,2,32]{0,2,1:T(8,128)S(1)} %bitcast.191), kind=kOutput, calls=%fused_computation.63 | convolution fusion | flops 271581184 | bytes 4390912 | tf_op jit(solution)/shard_map/sgkp,sgn->gkpn/dot_general | solution.py:42
  38.3 7.9 %fusion.23 = f32[1,2,32,256,64]{3,4,2,1,0:T(8,128)} fusion(bf16[256,2,32,64]{0,3,2,1:T(8,128)(2,1)} %bitcast.182, f32[2,32,256]{2,1,0:T(8,128)} %bitcast.195, f32[2,32,256]{2,1,0:T(8,128)} %reduce_window_sum.88, f32[2,256,256]{2,1,0:T(8,128)S(1)} %fusion.75, pred[256,256]{1,0:T(8,128)(4,1)S(1)} %copy-done.28), kind=kOutput, calls=%fused_computation.42 | convolution fusion | flops 562036736 | bytes 7012352 | tf_op jit(solution)/shard_map/gkts,sgkp->gktp/dot_general | solution.py:35
  49.9 2.1 %collective-permute-done.8 = f32[2,1153]{1,0:T(2,128)S(1)} collective-permute-done((f32[2,1153]{1,0:T(2,128)S(1)}, f32[2,1153]{1,0:T(2,128)S(1)}, u32[]{:S(2)}, u32[]{:S(2)}) %collective-permute-start.8) | collective-permute-done | bytes 9256 | tf_op jit(solution)/shard_map/ppermute | solution.py:91
  52.4 4.3 %collective-permute-done.9 = f32[4,1153]{1,0:T(4,128)S(1)} collective-permute-done((f32[4,1153]{1,0:T(4,128)S(1)}, f32[4,1153]{1,0:T(4,128)S(1)}, u32[]{:S(2)}, u32[]{:S(2)}) %collective-permute-start.9) | collective-permute-done | bytes 18480 | tf_op jit(solution)/shard_map/ppermute | solution.py:91
  57.1 2.3 %fusion.24 = (bf16[2,2,32,64,128,1]{4,3,2,1,0,5:T(8,128)(2,1)S(1)}, bf16[2,2,32,64,128,1]{4,3,2,1,0,5:T(8,128)(2,1)S(1)}) fusion(f32[1,2,32,64,128]{4,3,2,1,0:T(8,128)} %copy-done.4, f32[1,2,32,64,128]{4,3,2,1,0:T(8,128)S(1)} %fusion.41, f32[2,2,32]{2,1,0:T(2,128)S(1)} %exp.65), kind=kLoop, calls=%fused_computation.43 | loop fusion | flops 6291456 | bytes 8389120 | tf_op jit(solution)/shard_map/convert_element_type | solution.py:240
  59.4 2.0 %fusion.30 = f32[2,8,4,2,32,64]{5,1,4,3,2,0:T(8,128)S(1)} fusion(bf16[2,2,32,64,128,1]{4,3,2,1,0,5:T(8,128)(2,1)S(1)} %get-tuple-element.23, bf16[8,4,2,128,1,1]{3,0,2,1,5,4:T(8,128)(2,1)S(1)} %bitcast.192), kind=kOutput, calls=%fused_computation.50 | convolution fusion | flops 67108864 | bytes 3162112 | tf_op jit(solution)/shard_map/rgkpn,jugn->rjugkp/dot_general | solution.py:245
  64.4 2.0 %add_bitcast_fusion = f32[2,8,4,2,32,64]{5,1,4,0,2,3:T(8,128)S(1)} fusion(f32[2,8,4,2,32,64]{5,1,4,3,2,0:T(8,128)S(1)} %fusion.30, bf16[2,2,32,64,128,1]{4,3,2,1,0,5:T(8,128)(2,1)S(1)} %get-tuple-element.22, bf16[8,4,2,128,1,1]{3,0,2,1,5,4:T(8,128)(2,1)S(1)} %bitcast.193), kind=kOutput, calls=%fused_computation.54 | convolution fusion | flops 67371008 | bytes 4210688 | tf_op jit(solution)/shard_map/rgkpn,jugn->rjugkp/dot_general | solution.py:243
  67.9 2.7 %reshape.359 = f32[8,1,16384]{2,1,0:T(1,128)} reshape(f32[8,2,4,32,64]{4,3,2,1,0:T(8,128)} %bitcast.183) | data formatting | bytes 1048576
  70.6 7.3 %all-to-all-start = ((f32[8,1,16384]{2,1,0:T(1,128)}), f32[8,1,16384]{2,1,0:T(1,128)}, u32[]{:S(2)}, u32[]{:S(2)}) async-start(f32[8,1,16384]{2,1,0:T(1,128)} %reshape.359), calls=%async_computation | async-start | bytes 1048576 | tf_op jit(solution)/shard_map/all_to_all | solution.py:118
  94.5 2.0 %fusion.76 = f32[2,256,256]{2,1,0:T(8,128)} fusion(bf16[256,2,128]{0,2,1:T(8,128)(2,1)} %bitcast.188, bf16[256,2,128]{0,2,1:T(8,128)(2,1)S(1)} %bitcast.185), kind=kOutput, calls=%fused_computation.151 | convolution fusion | flops 33554432 | bytes 786432 | tf_op jit(solution)/shard_map/tgn,sgn->gts/dot_general | solution.py:24
  96.5 1.9 collective-permute-done.3
  98.3 2.0 %select_convert_fusion.3 = bf16[2,32,32,128]{3,2,1,0:T(8,128)(2,1)} fusion(bf16[2,32,32,128]{3,2,1,0:T(8,128)(2,1)S(1)} %collective-permute-done.2, bf16[2,32,32,128]{3,2,1,0:T(8,128)(2,1)S(1)} %collective-permute-done.3, f32[2,2,32,32,128]{4,3,2,1,0:T(8,128)S(1)} %get-tuple-element.18, f32[2,32]{1,0:T(2,128)} %copy-done.37, f32[2,32]{1,0:T(2,128)} %copy-done.35, ...), kind=kLoop, calls=%fused_computation.88 | loop fusion | flops 3407872 | bytes 3670532 | tf_op jit(solution)/shard_map/convert_element_type | solution.py:134
  100.3 2.0 %collective-permute-start.4 = (bf16[2,32,32,128]{3,2,1,0:T(8,128)(2,1)}, bf16[2,32,32,128]{3,2,1,0:T(8,128)(2,1)}, u32[]{:S(2)}, u32[]{:S(2)}) collective-permute-start(bf16[2,32,32,128]{3,2,1,0:T(8,128)(2,1)} %select_convert_fusion.3), channel_id=1, source_target_pairs={{4,8},{8,12},{6,10},{10,14},{5,9},{9,13},{7,11},{11,15},{20,24},{2... | collective-permute-start | bytes 1572872 | tf_op jit(solution)/shard_map/ppermute | solution.py:134
  103.1 3.6 %reduce.16 = f32[8,16384]{1,0:T(8,128)} reduce(f32[8,1,16384]{2,1,0:T(1,128)} %all-to-all-done, f32[]{:T(128)} %broadcast.183), dimensions={1}, to_apply=%all_to_all.6.reduce_sub_computation | reduce | bytes 1048580 | tf_op jit(solution)/shard_map/all_to_all | solution.py:118
  106.8 2.4 %reshape.360 = f32[8,2,4,32,64]{4,3,2,1,0:T(8,128)} reshape(f32[8,16384]{1,0:T(8,128)} %reduce.16) | data formatting | bytes 1048576
  111.4 3.1 %collective-permute-done.4 = bf16[2,32,32,128]{3,2,1,0:T(8,128)(2,1)} collective-permute-done((bf16[2,32,32,128]{3,2,1,0:T(8,128)(2,1)}, bf16[2,32,32,128]{3,2,1,0:T(8,128)(2,1)}, u32[]{:S(2)}, u32[]{:S(2)}) %collective-permute-start.4) | collective-permute-done | bytes 524320 | tf_op jit(solution)/shard_map/ppermute | solution.py:134
  114.6 2.5 %select_convert_fusion.2 = bf16[2,32,32,128]{3,2,1,0:T(8,128)(2,1)} fusion(f32[2,2,32,32,128]{4,3,2,1,0:T(8,128)S(1)} %get-tuple-element.18, bf16[2,32,32,128]{3,2,1,0:T(8,128)(2,1)S(1)} %collective-permute-done.2, bf16[2,32,32,128]{3,2,1,0:T(8,128)(2,1)S(1)} %collective-permute-done.3, bf16[2,32,32,128]{3,2,1,0:T(8,128)(2,1)} %collective-permute-done.4, ...), kind=kLoop, calls=%fused_computation.87 | loop fusion | flops 4194304 | bytes 4194822 | tf_op jit(solution)/shard_map/convert_element_type | solution.py:134
  117.1 3.0 %collective-permute-start.5 = (bf16[2,32,32,128]{3,2,1,0:T(8,128)(2,1)}, bf16[2,32,32,128]{3,2,1,0:T(8,128)(2,1)}, u32[]{:S(2)}, u32[]{:S(2)}) collective-permute-start(bf16[2,32,32,128]{3,2,1,0:T(8,128)(2,1)} %select_convert_fusion.2), channel_id=1, source_target_pairs={{8,12},{10,14},{9,13},{11,15},{24,28},{26,30},{25,29},{27,31}} | collective-permute-start | bytes 1572872 | tf_op jit(solution)/shard_map/ppermute | solution.py:134
  120.9 5.7 %all-to-all-start.1 = ((bf16[8,4,4096]{2,1,0:T(4,128)(2,1)}), bf16[8,4,4096]{2,1,0:T(4,128)(2,1)}, u32[]{:S(2)}, u32[]{:S(2)}) async-start(bf16[8,4,4096]{2,1,0:T(4,128)(2,1)} %concatenate.36), calls=%async_computation.1 | async-start | bytes 524288 | tf_op jit(solution)/shard_map/all_to_all | solution.py:118
  126.6 5.3 %collective-permute-done.5 = bf16[2,32,32,128]{3,2,1,0:T(8,128)(2,1)} collective-permute-done((bf16[2,32,32,128]{3,2,1,0:T(8,128)(2,1)}, bf16[2,32,32,128]{3,2,1,0:T(8,128)(2,1)}, u32[]{:S(2)}, u32[]{:S(2)}) %collective-permute-start.5) | collective-permute-done | bytes 524320 | tf_op jit(solution)/shard_map/ppermute | solution.py:134
  131.9 1.9 %fusion.49 = (f32[1,2,32,32,128]{4,3,2,1,0:T(8,128)S(1)}, f32[1,2,32,32,128]{4,3,2,1,0:T(8,128)S(1)}) fusion(bf16[2,32,32,128]{3,2,1,0:T(8,128)(2,1)} %collective-permute-done.5, bf16[2,32,32,128]{3,2,1,0:T(8,128)(2,1)} %copy-done.12, bf16[2,32,32,128]{3,2,1,0:T(8,128)(2,1)} %copy-done.13, bf16[2,32,32,128]{3,2,1,0:T(8,128)(2,1)} %collective-permute-done.4, ...), kind=kLoop, calls=%fused_computation.80 | loop fusion | flops 3145728 | bytes 4194312 | tf_op jit(solution)/shard_map/stack | solution.py:137
  135.4 2.6 %collective-permute-start.6 = (bf16[2,2,32,32,128]{4,3,2,1,0:T(8,128)(2,1)}, bf16[2,2,32,32,128]{4,3,2,1,0:T(8,128)(2,1)}, u32[]{:S(2)}, u32[]{:S(2)}) collective-permute-start(bf16[2,2,32,32,128]{4,3,2,1,0:T(8,128)(2,1)} %select_convert_fusion), channel_id=1, source_target_pairs={{0,2},{4,6},{8,10},{12,14},{2,0},{6,4},{10,8},{14,12},{1,3},{5,7},... | collective-permute-start | bytes 3145736 | tf_op jit(solution)/shard_map/ppermute | solution.py:80
  138.0 6.6 %fusion.22 = f32[1,2,32,256,64]{3,4,2,1,0:T(8,128)} fusion(bf16[256,2,32,64]{0,3,2,1:T(8,128)(2,1)S(1)} %bitcast.180, f32[2,32,256]{2,1,0:T(8,128)S(1)} %bitcast.194, f32[2,32,256]{2,1,0:T(8,128)S(1)} %copy-done.30, f32[2,256,256]{2,1,0:T(8,128)S(1)} %copy-done.22, pred[256,256]{1,0:T(8,128)(4,1)S(1)} %copy-done.29), kind=kOutput, calls=%fused_computation.41 | convolution fusion | flops 562036736 | bytes 7012352 | tf_op jit(solution)/shard_map/gkts,sgkp->gktp/dot_general | solution.py:35
  146.0 7.1 %copy.226 = f32[2,256,4096]{1,2,0:T(8,128)} copy(bf16[2,256,4096]{2,1,0:T(8,128)(2,1)} %param.13) | data formatting | bytes 12582912 | tf_op jit(solution)/shard_map/convert_element_type | solution.py:63
  154.1 5.6 %fusion.5 = f32[8,4,1024]{2,0,1:T(8,128)} fusion(bf16[4096,1024]{1,0:T(8,128)(2,1)} %param.25, bf16[8,4,4096]{2,1,0:T(4,128)(2,1)} %all-to-all-done.1), kind=kOutput, calls=%fused_computation.8 | convolution fusion | flops 268435456 | bytes 8781824 | tf_op jit(solution)/shard_map/jup,pd->jud/dot_general | solution.py:275
  159.6 5.0 %all-reduce.1 = bf16[8,4,1024]{2,0,1:T(8,128)(2,1)} all-reduce(f32[8,4,1024]{2,0,1:T(8,128)} %fusion.5), channel_id=1, replica_groups=mesh['groups'=2,'ctx'=8,'heads'=2] {'heads'}, use_global_device_ids=true, to_apply=%region_8.9 | all-reduce | flops 32768 | bytes 196608 | tf_op jit(solution)/shard_map/psum | solution.py:281
  166.2 2.5 %convert_select_fusion.1 = (f32[2,2,32,32,128]{4,3,2,1,0:T(8,128)S(1)}, f32[2,2,32,32,128]{4,3,2,1,0:T(8,128)S(1)}) fusion(bf16[2,2,32,32,128]{4,3,2,1,0:T(8,128)(2,1)} %collective-permute-done.6, pred[]{:T(512)S(6)} %eq.51, f32[2,2,32,32,128]{4,3,2,1,0:T(8,128)S(1)} %copy-done.6, bf16[2,2,32,32,128]{4,3,2,1,0:T(8,128)(2,1)} %copy-done.8, ...), kind=kLoop, calls=%fused_computation.38 | loop fusion | flops 4718592 | bytes 10486273 | tf_op jit(solution)/shard_map/jit(_where)/select_n | solution.py:183
  175.6 5.9 %fusion.4 = bf16[2,256,2,32,64]{1,4,3,2,0:T(8,128)(2,1)} fusion(f32[1,2,32,256,64]{3,4,2,1,0:T(8,128)} %fusion.22, f32[1,2,32,256,64]{3,4,2,1,0:T(8,128)S(1)} %copy-done.14, f32[2,256,2,32,64]{1,4,3,2,0:T(8,128)S(1)} %bitcast.177, f32[2,2,256,32,64]{2,4,3,1,0:T(8,128)S(1)} %bitcast.174, f32[2,32]{1,0:T(2,128)S(1)} %copy-done.39, f32[2,2,256,32]{2,3,1,0:T(8,128)S(1)} %fusion.58), kind=kLoop, calls=%fused_computation.7 | loop fusion | flops 12582912 | bytes 29491456 | tf_op jit(solution)/shard_map/convert_element_type | solution.py:66
  181.6 6.3 %copy.244 = bf16[2,256,4096]{2,1,0:T(8,128)(2,1)} copy(bf16[2,256,4096]{1,2,0:T(8,128)(2,1)} %bitcast.178) | data formatting | bytes 8388608
  (192 shorter events, 65.1 us)
Async XLA Ops:
  0.6 31.0 %copy-start = (bf16[1,4,256]{2,1,0:T(4,128)(2,1)S(1)}, bf16[1,4,256]{2,1,0:T(4,128)(2,1)}, u32[]{:S(2)}) copy-start(bf16[1,4,256]{2,1,0:T(4,128)(2,1)} %param.21) | copy-start | bytes 6148
  0.6 9.5 %copy-start.25 = (bf16[2,256,256]{2,1,0:T(8,128)(2,1)S(1)}, bf16[2,256,256]{2,1,0:T(8,128)(2,1)}, u32[]{:S(2)}) copy-start(bf16[2,256,256]{2,1,0:T(8,128)(2,1)} %param.14) | copy-start | bytes 786436
  3.4 11.0 %copy-start.33 = (f32[64,2]{0,1:T(2,128)}, f32[64,2]{0,1:T(2,128)S(1)}, u32[]{:S(2)}) copy-start(f32[64,2]{0,1:T(2,128)S(1)} %slice.100) | copy-start | bytes 1540
  5.0 41.2 %collective-permute-start = (f32[2,2,32]{2,1,0:T(2,128)}, f32[2,2,32]{2,1,0:T(2,128)}, u32[]{:S(2)}, u32[]{:S(2)}) collective-permute-start(f32[2,2,32]{2,1,0:T(2,128)} %constant_dynamic-update-slice_fusion), channel_id=1, source_target_pairs={{0,2},{4,6},{8,10},{12,14},{2,0},{6,4},{10,8},{14,12},{1,3},{5,7},... | collective-permute-start | bytes 1544 | tf_op jit(solution)/shard_map/ppermute | solution.py:80
  8.7 38.8 %collective-permute-start.7 = (f32[1,1153]{1,0:T(1,128)S(1)}, f32[1,1153]{1,0:T(1,128)}, u32[]{:S(2)}, u32[]{:S(2)}) collective-permute-start(f32[1,1153]{1,0:T(1,128)S(1)} %broadcast_in_dim.73), channel_id=1, source_target_pairs={{0,2},{2,0},{4,6},{6,4},{8,10},{10,8},{12,14},{14,12},{1,3},{3,1},... | collective-permute-start | bytes 13844 | tf_op jit(solution)/shard_map/ppermute | solution.py:91
  10.3 10.6 %copy-start.18 = (bf16[1,256,256]{1,2,0:T(8,128)(2,1)}, bf16[1,256,256]{1,2,0:T(8,128)(2,1)S(1)}, u32[]{:S(2)}) copy-start(bf16[1,256,256]{1,2,0:T(8,128)(2,1)S(1)} %copy.271) | copy-start | bytes 393220
  10.5 13.0 %copy-start.16 = (bf16[1,256,256]{1,2,0:T(8,128)(2,1)}, bf16[1,256,256]{1,2,0:T(8,128)(2,1)S(1)}, u32[]{:S(2)}) copy-start(bf16[1,256,256]{1,2,0:T(8,128)(2,1)S(1)} %copy.272) | copy-start | bytes 393220
  23.4 33.6 %copy-start.2 = (f32[1,2,32,64,128]{4,3,2,1,0:T(8,128)}, f32[1,2,32,64,128]{4,3,2,1,0:T(8,128)S(1)}, u32[]{:S(2)}) copy-start(f32[1,2,32,64,128]{4,3,2,1,0:T(8,128)S(1)} %fusion.41) | copy-start | bytes 6291460
  24.2 10.5 %copy-start.15 = (bf16[2,256,256]{2,1,0:T(8,128)(2,1)S(1)}, bf16[2,256,256]{2,1,0:T(8,128)(2,1)}, u32[]{:S(2)}) copy-start(bf16[2,256,256]{2,1,0:T(8,128)(2,1)} %param.15) | copy-start | bytes 786436
  25.9 35.6 %collective-permute-start.1 = (bf16[2,2,32,32,128]{4,3,2,1,0:T(8,128)(2,1)}, bf16[2,2,32,32,128]{4,3,2,1,0:T(8,128)(2,1)S(1)}, u32[]{:S(2)}, u32[]{:S(2)}) collective-permute-start(bf16[2,2,32,32,128]{4,3,2,1,0:T(8,128)(2,1)} %select_convert_fusion.1), channel_id=1, source_target_pairs={{0,2},{4,6},{8,10},{12,14},{2,0},{6,4},{10,8},{14,12},{1,3},{5,7},... | collective-permute-start | bytes 3145736 | tf_op jit(solution)/shard_map/ppermute | solution.py:80
  34.0 12.2 %copy-start.19 = (f32[64,2,128]{2,1,0:T(2,128)}, f32[64,2,128]{2,1,0:T(2,128)S(1)}, u32[]{:S(2)}) copy-start(f32[64,2,128]{2,1,0:T(2,128)S(1)} %copy.205) | copy-start | bytes 196612
  48.3 3.7 %collective-permute-start.8 = (f32[2,1153]{1,0:T(2,128)S(1)}, f32[2,1153]{1,0:T(2,128)S(1)}, u32[]{:S(2)}, u32[]{:S(2)}) collective-permute-start(f32[2,1153]{1,0:T(2,128)S(1)} %maximum_select_fusion.2), channel_id=1, source_target_pairs={{0,4},{2,6},{4,0},{6,2},{8,12},{10,14},{12,8},{14,10},{1,5},{3,7},... | collective-permute-start | bytes 27680 | tf_op jit(solution)/shard_map/ppermute | solution.py:91
  52.0 4.8 %collective-permute-start.9 = (f32[4,1153]{1,0:T(4,128)S(1)}, f32[4,1153]{1,0:T(4,128)S(1)}, u32[]{:S(2)}, u32[]{:S(2)}) collective-permute-start(f32[4,1153]{1,0:T(4,128)S(1)} %maximum_select_fusion.1), channel_id=1, source_target_pairs={{0,8},{2,10},{4,12},{6,14},{8,0},{10,2},{12,4},{14,6},{1,9},{3,11}... | collective-permute-start | bytes 55352 | tf_op jit(solution)/shard_map/ppermute | solution.py:91
  52.4 25.5 %copy-start.35 = (f32[2,32]{1,0:T(2,128)}, f32[2,32]{1,0:T(2,128)S(1)}, u32[]{:S(2)}) copy-start(f32[2,32]{1,0:T(2,128)S(1)} %get-tuple-element.41) | copy-start | bytes 772
  52.4 25.5 %copy-start.37 = (f32[2,32]{1,0:T(2,128)}, f32[2,32]{1,0:T(2,128)S(1)}, u32[]{:S(2)}) copy-start(f32[2,32]{1,0:T(2,128)S(1)} %get-tuple-element.42) | copy-start | bytes 772
  63.7 14.2 %collective-permute-start.2 = (bf16[2,32,32,128]{3,2,1,0:T(8,128)(2,1)S(1)}, bf16[2,32,32,128]{3,2,1,0:T(8,128)(2,1)S(1)}, u32[]{:S(2)}, u32[]{:S(2)}) collective-permute-start(bf16[2,32,32,128]{3,2,1,0:T(8,128)(2,1)S(1)} %select_convert_fusion.4), channel_id=1, source_target_pairs={{0,4},{2,6},{1,5},{3,7},{16,20},{18,22},{17,21},{19,23}} | collective-permute-start | bytes 1572872 | tf_op jit(solution)/shard_map/ppermute | solution.py:134
  70.6 10.6 %copy-start.40 = (f32[1,4,64]{2,1,0:T(4,128)S(1)}, f32[1,4,64]{2,1,0:T(4,128)}, u32[]{:S(2)}) copy-start(f32[1,4,64]{2,1,0:T(4,128)} %param.24) | copy-start | bytes 3076
  70.6 32.0 %all-to-all-start = ((f32[8,1,16384]{2,1,0:T(1,128)}), f32[8,1,16384]{2,1,0:T(1,128)}, u32[]{:S(2)}, u32[]{:S(2)}) async-start(f32[8,1,16384]{2,1,0:T(1,128)} %reshape.359), calls=%async_computation | async-start | bytes 1048576 | tf_op jit(solution)/shard_map/all_to_all | solution.py:118
  77.9 16.5 %copy-start.17 = (bf16[1,256,256]{1,2,0:T(8,128)(2,1)S(1)}, bf16[1,256,256]{1,2,0:T(8,128)(2,1)}, u32[]{:S(2)}) copy-start(bf16[1,256,256]{1,2,0:T(8,128)(2,1)} %copy-done.16) | copy-start | bytes 393220
  77.9 36.7 %copy-start.12 = (bf16[2,32,32,128]{3,2,1,0:T(8,128)(2,1)}, bf16[2,32,32,128]{3,2,1,0:T(8,128)(2,1)S(1)}, u32[]{:S(2)}) copy-start(bf16[2,32,32,128]{3,2,1,0:T(8,128)(2,1)S(1)} %collective-permute-done.2) | copy-start | bytes 1572868
  79.2 19.2 %collective-permute-start.3 = (bf16[2,32,32,128]{3,2,1,0:T(8,128)(2,1)}, bf16[2,32,32,128]{3,2,1,0:T(8,128)(2,1)S(1)}, u32[]{:S(2)}, u32[]{:S(2)}) collective-permute-start(bf16[2,32,32,128]{3,2,1,0:T(8,128)(2,1)} %fusion.47), channel_id=1, source_target_pairs={{0,4},{4,8},{2,6},{6,10},{1,5},{5,9},{3,7},{7,11},{16,20},{20,24},... | collective-permute-start | bytes 1572872 | tf_op jit(solution)/shard_map/ppermute | solution.py:134
  98.3 16.3 %copy-start.13 = (bf16[2,32,32,128]{3,2,1,0:T(8,128)(2,1)}, bf16[2,32,32,128]{3,2,1,0:T(8,128)(2,1)S(1)}, u32[]{:S(2)}) copy-start(bf16[2,32,32,128]{3,2,1,0:T(8,128)(2,1)S(1)} %collective-permute-done.3) | copy-start | bytes 1572868
  100.3 10.2 %copy-start.34 = (f32[4,2,32]{2,0,1:T(4,128)S(1)}, f32[4,2,32]{2,0,1:T(4,128)}, u32[]{:S(2)}) copy-start(f32[4,2,32]{2,0,1:T(4,128)} %exp.63) | copy-start | bytes 3076
  100.3 14.3 %collective-permute-start.4 = (bf16[2,32,32,128]{3,2,1,0:T(8,128)(2,1)}, bf16[2,32,32,128]{3,2,1,0:T(8,128)(2,1)}, u32[]{:S(2)}, u32[]{:S(2)}) collective-permute-start(bf16[2,32,32,128]{3,2,1,0:T(8,128)(2,1)} %select_convert_fusion.3), channel_id=1, source_target_pairs={{4,8},{8,12},{6,10},{10,14},{5,9},{9,13},{7,11},{11,15},{20,24},{2... | collective-permute-start | bytes 1572872 | tf_op jit(solution)/shard_map/ppermute | solution.py:134
  103.1 11.5 %copy-start.36 = (f32[2,32]{1,0:T(2,128)S(1)}, f32[2,32]{1,0:T(2,128)}, u32[]{:S(2)}) copy-start(f32[2,32]{1,0:T(2,128)} %copy-done.35) | copy-start | bytes 772
  103.1 11.5 %copy-start.38 = (f32[2,32]{1,0:T(2,128)S(1)}, f32[2,32]{1,0:T(2,128)}, u32[]{:S(2)}) copy-start(f32[2,32]{1,0:T(2,128)} %copy-done.37) | copy-start | bytes 772
  111.4 8.7 %copy-start.24 = (f32[1,4,4096]{2,1,0:T(4,128)S(1)}, f32[1,4,4096]{2,1,0:T(4,128)}, u32[]{:S(2)}) copy-start(f32[1,4,4096]{2,1,0:T(4,128)} %add.119) | copy-start | bytes 196612
  111.4 8.7 %copy-start.26 = (bf16[1,4,4096]{2,1,0:T(4,128)(2,1)S(1)}, bf16[1,4,4096]{2,1,0:T(4,128)(2,1)}, u32[]{:S(2)}) copy-start(bf16[1,4,4096]{2,1,0:T(4,128)(2,1)} %param.20) | copy-start | bytes 98308
  111.4 8.7 %copy-start.27 = (f32[4096]{0:T(1024)S(1)}, f32[4096]{0:T(1024)}, u32[]{:S(2)}) copy-start(f32[4096]{0:T(1024)} %mul.311) | copy-start | bytes 49156
  117.1 14.8 %collective-permute-start.5 = (bf16[2,32,32,128]{3,2,1,0:T(8,128)(2,1)}, bf16[2,32,32,128]{3,2,1,0:T(8,128)(2,1)}, u32[]{:S(2)}, u32[]{:S(2)}) collective-permute-start(bf16[2,32,32,128]{3,2,1,0:T(8,128)(2,1)} %select_convert_fusion.2), channel_id=1, source_target_pairs={{8,12},{10,14},{9,13},{11,15},{24,28},{26,30},{25,29},{27,31}} | collective-permute-start | bytes 1572872 | tf_op jit(solution)/shard_map/ppermute | solution.py:134
  120.9 33.1 %all-to-all-start.1 = ((bf16[8,4,4096]{2,1,0:T(4,128)(2,1)}), bf16[8,4,4096]{2,1,0:T(4,128)(2,1)}, u32[]{:S(2)}, u32[]{:S(2)}) async-start(bf16[8,4,4096]{2,1,0:T(4,128)(2,1)} %concatenate.36), calls=%async_computation.1 | async-start | bytes 524288 | tf_op jit(solution)/shard_map/all_to_all | solution.py:118
  135.4 30.7 %collective-permute-start.6 = (bf16[2,2,32,32,128]{4,3,2,1,0:T(8,128)(2,1)}, bf16[2,2,32,32,128]{4,3,2,1,0:T(8,128)(2,1)}, u32[]{:S(2)}, u32[]{:S(2)}) collective-permute-start(bf16[2,2,32,32,128]{4,3,2,1,0:T(8,128)(2,1)} %select_convert_fusion), channel_id=1, source_target_pairs={{0,2},{4,6},{8,10},{12,14},{2,0},{6,4},{10,8},{14,12},{1,3},{5,7},... | collective-permute-start | bytes 3145736 | tf_op jit(solution)/shard_map/ppermute | solution.py:80
  (23 other events, 105.7 us)

commit v13 on v12

--- a/solution.py
+++ b/solution.py
@@ -278,7 +278,11 @@
         out_weight,
         preferred_element_type=jnp.float32,
     )
-    decoded = lax.psum(partial_value, "heads").astype(jnp.bfloat16)
+    if lax.axis_size("heads") == 2:
+        other_half = lax.ppermute(partial_value, "heads", [(0, 1), (1, 0)])
+        decoded = (partial_value + other_half).astype(jnp.bfloat16)
+    else:
+        decoded = lax.psum(partial_value, "heads").astype(jnp.bfloat16)
 
     entering = prefix_states(states, totals)
     prefill_out = finish(

time: 191 us -> 184 us (0.963)
  local copies, waits for them, and re-layouts: 61 us -> 52.9 us
  other arithmetic: 40.4 us -> 47.2 us
  blocking collectives: 5.02 us -> 0 us
  waiting for transfers between devices: 16.8 us -> 19.8 us
  matrix products: 34.4 us -> 32.3 us
    ppermute x3, waiting for transfers between devices: 0.02 us -> 5.94 us  [send(): lax.ppermute((value.astype(jnp.bfloat16), total), 'ctx', pairs)]
    psum x1 -> x0, blocking collectives: 5.02 us -> none  [shards(): decoded = lax.psum(partial_value, 'heads').astype(jnp.bfloat16)]
    unnamed x96 -> x106, local copies, waits for them, and re-layouts: 20.8 us -> 17.1 us
    another operation x11, local copies, waits for them, and re-layouts: 6.18 us -> 3.04 us
    add x1, other arithmetic: 1.84 us -> 4.44 us  [prefix_states(): window = scale(jnp.exp(odd_total), even_state) + odd_state]
    mul x2, local copies, waits for them, and re-layouts: 2.78 us -> 0.75 us  [shards(): skip_gain.reshape(group_count, per_group, 1) * row_input]
    another operation x8, other arithmetic: 3.56 us -> 1.63 us
    all_to_all x2, starting transfers between devices: 13 us -> 15 us  [exchange_ctx(): got = lax.all_to_all(value, 'ctx', 0, 0, tiled=True)]
  transfers between devices with their start and end apart: 12 -> 13, of which waited for: 5 -> 6; matrix products, arithmetic and copies ran while one was open for 56% -> 58% of each run, Pallas kernels for 0% -> 0%
where the time goes in v13:
time: 184 us; the launch traced here: 182 us
  local copies, waits for them, and re-layouts  52.9 us (29%)
  other arithmetic  47.2 us (26%)
  matrix products  32.3 us (18%)
  starting transfers between devices  28.2 us (15%)
  waiting for transfers between devices  19.8 us (11%)
  between operations  2 us (1%)
    unnamed x106, local copies, waits for them, and re-layouts  17.1 us
    all_to_all x2, starting transfers between devices, exchange_ctx(): got = lax.all_to_all(value, 'ctx', 0, 0, tiled=True)  15 us
    dot_general x2, matrix products, block_terms(): jnp.einsum('gkts,sgkp->gktp', mixing, inputs_head, preferred_element_type...  14.5 us
    slice x3, local copies, waits for them, and re-layouts, shards(): ssm_input[request]  10.5 us
    ppermute x4, waiting for transfers between devices, chain_columns(): lax.ppermute(outgoing.astype(jnp.bfloat16), 'ctx', pairs)  9.32 us
    convert_element_type x1, local copies, waits for them, and re-layouts, finish(): inputs_head = ssm_input.reshape(request_count, block_size, group_count, p...  7.11 us
    ppermute x4, starting transfers between devices, chain_columns(): lax.ppermute(outgoing.astype(jnp.bfloat16), 'ctx', pairs)  6.14 us
    convert_element_type x4, other arithmetic, chain_columns(): outgoing.astype(jnp.bfloat16)  6.09 us
  transfers between devices with their start and end apart: 13, of which 6 were waited for; matrix products, arithmetic and copies ran while one was open for 58% of the time, Pallas kernels for 0%

profile of v13, /device:TPU:18, one launch (start us, length us, event | category | flops | bytes accessed | tf_op | source)
XLA Modules:
  0.0 182.4 jit_solution(7389976023681781856)
XLA Ops:
  11.2 4.0 %fusion.70 = (bf16[1,256,4096]{2,1,0:T(8,128)(2,1)}, bf16[1,256,4096]{2,1,0:T(8,128)(2,1)S(1)}) fusion(bf16[2,256,4096]{2,1,0:T(8,128)(2,1)} %param.13), kind=kLoop, calls=%fused_computation.144 | loop fusion | bytes 8388608 | tf_op jit(solution)/shard_map/slice | solution.py:210
  15.1 4.1 %copy.208 = bf16[1,256,4096]{1,2,0:T(8,128)(2,1)} copy(bf16[1,256,4096]{2,1,0:T(8,128)(2,1)} %get-tuple-element.24) | data formatting | bytes 4194304 | tf_op jit(solution)/shard_map/slice | solution.py:210
  19.2 2.4 %copy.211 = bf16[1,256,4096]{1,2,0:T(8,128)(2,1)} copy(bf16[1,256,4096]{2,1,0:T(8,128)(2,1)S(1)} %get-tuple-element.25) | data formatting | bytes 4194304 | tf_op jit(solution)/shard_map/slice | solution.py:210
  21.7 2.5 %fusion.41 = f32[1,2,32,64,128]{4,3,2,1,0:T(8,128)S(1)} fusion(bf16[256,2,128,1]{0,2,3,1:T(8,128)(2,1)S(1)} %bitcast.186, bf16[256,2,32,64]{0,3,2,1:T(8,128)(2,1)} %bitcast.181, f32[256,2,32]{0,2,1:T(8,128)S(1)} %bitcast.191), kind=kOutput, calls=%fused_computation.63 | convolution fusion | flops 271581184 | bytes 4390912 | tf_op jit(solution)/shard_map/sgkp,sgn->gkpn/dot_general | solution.py:42
  24.9 1.6 select_convert_fusion.1
  29.3 1.5 fusion.74
  32.4 1.7 copy.274
  35.3 7.9 %fusion.23 = f32[1,2,32,256,64]{3,4,2,1,0:T(8,128)} fusion(bf16[256,2,32,64]{0,3,2,1:T(8,128)(2,1)} %bitcast.182, f32[2,32,256]{2,1,0:T(8,128)} %bitcast.195, f32[2,32,256]{2,1,0:T(8,128)} %reduce_window_sum.88, f32[2,256,256]{2,1,0:T(8,128)S(1)} %fusion.75, pred[256,256]{1,0:T(8,128)(4,1)} %iota_compare_fusion), kind=kOutput, calls=%fused_computation.42 | convolution fusion | flops 562036736 | bytes 7012352 | tf_op jit(solution)/shard_map/gkts,sgkp->gktp/dot_general | solution.py:35
  46.1 1.6 collective-permute-start.8
  50.9 3.7 %collective-permute-done.9 = f32[4,1153]{1,0:T(4,128)S(1)} collective-permute-done((f32[4,1153]{1,0:T(4,128)S(1)}, f32[4,1153]{1,0:T(4,128)S(1)}, u32[]{:S(2)}, u32[]{:S(2)}) %collective-permute-start.9) | collective-permute-done | bytes 18480 | tf_op jit(solution)/shard_map/ppermute | solution.py:91
  57.9 2.3 %fusion.24 = (bf16[2,2,32,64,128,1]{4,3,2,1,0,5:T(8,128)(2,1)S(1)}, bf16[2,2,32,64,128,1]{4,3,2,1,0,5:T(8,128)(2,1)S(1)}) fusion(f32[1,2,32,64,128]{4,3,2,1,0:T(8,128)} %copy-done.3, f32[1,2,32,64,128]{4,3,2,1,0:T(8,128)S(1)} %fusion.41, f32[2,2,32]{2,1,0:T(2,128)} %exp.65), kind=kLoop, calls=%fused_computation.43 | loop fusion | flops 6291456 | bytes 8389120 | tf_op jit(solution)/shard_map/convert_element_type | solution.py:240
  61.1 2.0 %fusion.30 = f32[2,8,4,2,32,64]{5,1,4,3,2,0:T(8,128)S(1)} fusion(bf16[2,2,32,64,128,1]{4,3,2,1,0,5:T(8,128)(2,1)S(1)} %get-tuple-element.23, bf16[8,4,2,128,1,1]{3,0,2,1,5,4:T(8,128)(2,1)S(1)} %bitcast.192), kind=kOutput, calls=%fused_computation.50 | convolution fusion | flops 67108864 | bytes 3162112 | tf_op jit(solution)/shard_map/rgkpn,jugn->rjugkp/dot_general | solution.py:245
  63.1 2.1 %add_bitcast_fusion = f32[2,8,4,2,32,64]{5,1,4,0,2,3:T(8,128)S(1)} fusion(f32[2,8,4,2,32,64]{5,1,4,3,2,0:T(8,128)S(1)} %fusion.30, bf16[2,2,32,64,128,1]{4,3,2,1,0,5:T(8,128)(2,1)S(1)} %get-tuple-element.22, bf16[8,4,2,128,1,1]{3,0,2,1,5,4:T(8,128)(2,1)S(1)} %bitcast.193), kind=kOutput, calls=%fused_computation.54 | convolution fusion | flops 67371008 | bytes 4210688 | tf_op jit(solution)/shard_map/rgkpn,jugn->rjugkp/dot_general | solution.py:243
  67.0 5.3 %all-to-all-start = ((f32[8,1,16384]{2,1,0:T(1,128)}), f32[8,1,16384]{2,1,0:T(1,128)}, u32[]{:S(2)}, u32[]{:S(2)}) async-start(f32[8,1,16384]{2,1,0:T(1,128)} %reshape.359), calls=%async_computation | async-start | bytes 1048576 | tf_op jit(solution)/shard_map/all_to_all | solution.py:118
  72.4 4.4 %fusion.25 = (f32[2,2,32,32,128]{4,3,2,1,0:T(8,128)S(1)}, f32[2,2,32,32,128]{4,3,2,1,0:T(8,128)}) fusion(bf16[2,2,32,32,128]{4,3,2,1,0:T(8,128)(2,1)S(1)} %collective-permute-done.1, f32[2,2,32]{2,1,0:T(2,128)} %get-tuple-element.39, pred[]{:T(512)S(6)} %eq.51, f32[1,2,32,64,128]{4,3,2,1,0:T(8,128)} %copy-done.3, f32[1,2,32,64,128]{4,3,2,1,0:T(8,128)} %copy-done.2), kind=kLoop, calls=%fused_computation.44 | loop fusion | flops 4194304 | bytes 9437697 | tf_op jit(solution)/shard_map/add | solution.py:159
  86.3 3.8 %reduce.16 = f32[8,16384]{1,0:T(8,128)} reduce(f32[8,1,16384]{2,1,0:T(1,128)} %all-to-all-done, f32[]{:T(128)} %broadcast.183), dimensions={1}, to_apply=%all_to_all.6.reduce_sub_computation | reduce | bytes 1048580 | tf_op jit(solution)/shard_map/all_to_all | solution.py:118
  90.1 2.4 %reshape.360 = f32[8,2,4,32,64]{4,3,2,1,0:T(8,128)} reshape(f32[8,16384]{1,0:T(8,128)} %reduce.16) | data formatting | bytes 1048576
  95.5 1.6 add.120
  97.2 4.6 %collective-permute-done.3 = bf16[2,32,32,128]{3,2,1,0:T(8,128)(2,1)S(1)} collective-permute-done((bf16[2,32,32,128]{3,2,1,0:T(8,128)(2,1)}, bf16[2,32,32,128]{3,2,1,0:T(8,128)(2,1)S(1)}, u32[]{:S(2)}, u32[]{:S(2)}) %collective-permute-start.3) | collective-permute-done | bytes 524320 | tf_op jit(solution)/shard_map/ppermute | solution.py:134
  103.1 1.9 %collective-permute-start.4 = (bf16[2,32,32,128]{3,2,1,0:T(8,128)(2,1)}, bf16[2,32,32,128]{3,2,1,0:T(8,128)(2,1)}, u32[]{:S(2)}, u32[]{:S(2)}) collective-permute-start(bf16[2,32,32,128]{3,2,1,0:T(8,128)(2,1)} %select_convert_fusion.3), channel_id=1, source_target_pairs={{4,8},{8,12},{6,10},{10,14},{5,9},{9,13},{7,11},{11,15},{20,24},{2... | collective-permute-start | bytes 1572872 | tf_op jit(solution)/shard_map/ppermute | solution.py:134
  106.6 9.6 %all-to-all-start.1 = ((bf16[8,4,4096]{2,1,0:T(4,128)(2,1)}), bf16[8,4,4096]{2,1,0:T(4,128)(2,1)}, u32[]{:S(2)}, u32[]{:S(2)}) async-start(bf16[8,4,4096]{2,1,0:T(4,128)(2,1)} %concatenate.36), calls=%async_computation.1 | async-start | bytes 524288 | tf_op jit(solution)/shard_map/all_to_all | solution.py:118
  117.0 4.2 %collective-permute-done.4 = bf16[2,32,32,128]{3,2,1,0:T(8,128)(2,1)} collective-permute-done((bf16[2,32,32,128]{3,2,1,0:T(8,128)(2,1)}, bf16[2,32,32,128]{3,2,1,0:T(8,128)(2,1)}, u32[]{:S(2)}, u32[]{:S(2)}) %collective-permute-start.4) | collective-permute-done | bytes 524320 | tf_op jit(solution)/shard_map/ppermute | solution.py:134
  121.2 2.5 %select_convert_fusion.2 = bf16[2,32,32,128]{3,2,1,0:T(8,128)(2,1)} fusion(f32[2,2,32,32,128]{4,3,2,1,0:T(8,128)S(1)} %get-tuple-element.18, bf16[2,32,32,128]{3,2,1,0:T(8,128)(2,1)S(1)} %collective-permute-done.2, bf16[2,32,32,128]{3,2,1,0:T(8,128)(2,1)S(1)} %collective-permute-done.3, bf16[2,32,32,128]{3,2,1,0:T(8,128)(2,1)} %collective-permute-done.4, ...), kind=kLoop, calls=%fused_computation.87 | loop fusion | flops 4194304 | bytes 4194822 | tf_op jit(solution)/shard_map/convert_element_type | solution.py:134
  123.7 2.1 %collective-permute-start.5 = (bf16[2,32,32,128]{3,2,1,0:T(8,128)(2,1)}, bf16[2,32,32,128]{3,2,1,0:T(8,128)(2,1)}, u32[]{:S(2)}, u32[]{:S(2)}) collective-permute-start(bf16[2,32,32,128]{3,2,1,0:T(8,128)(2,1)} %select_convert_fusion.2), channel_id=1, source_target_pairs={{8,12},{10,14},{9,13},{11,15},{24,28},{26,30},{25,29},{27,31}} | collective-permute-start | bytes 1572872 | tf_op jit(solution)/shard_map/ppermute | solution.py:134
  125.8 5.6 %fusion.5 = f32[8,4,1024]{2,0,1:T(8,128)} fusion(bf16[4096,1024]{1,0:T(8,128)(2,1)} %param.25, bf16[8,4,4096]{2,1,0:T(4,128)(2,1)} %all-to-all-done.1), kind=kOutput, calls=%fused_computation.8 | convolution fusion | flops 268435456 | bytes 8781824 | tf_op jit(solution)/shard_map/jup,pd->jud/dot_general | solution.py:275
  132.0 2.0 %fusion.49 = (f32[1,2,32,32,128]{4,3,2,1,0:T(8,128)S(1)}, f32[1,2,32,32,128]{4,3,2,1,0:T(8,128)S(1)}) fusion(bf16[2,32,32,128]{3,2,1,0:T(8,128)(2,1)} %collective-permute-done.5, bf16[2,32,32,128]{3,2,1,0:T(8,128)(2,1)S(1)} %copy-done.11, bf16[2,32,32,128]{3,2,1,0:T(8,128)(2,1)S(1)} %copy-done.13, bf16[2,32,32,128]{3,2,1,0:T(8,128)(2,1)} %collective-permute-done.4, ...), kind=kLoop, calls=%fused_computation.80 | loop fusion | flops 3145728 | bytes 4194312 | tf_op jit(solution)/shard_map/stack | solution.py:137
  137.1 6.6 %fusion.22 = f32[1,2,32,256,64]{3,4,2,1,0:T(8,128)} fusion(bf16[256,2,32,64]{0,3,2,1:T(8,128)(2,1)S(1)} %bitcast.180, f32[2,32,256]{2,1,0:T(8,128)S(1)} %bitcast.194, f32[2,32,256]{2,1,0:T(8,128)S(1)} %copy-done.30, f32[2,256,256]{2,1,0:T(8,128)S(1)} %copy-done.19, pred[256,256]{1,0:T(8,128)(4,1)S(1)} %copy-done.29), kind=kOutput, calls=%fused_computation.41 | convolution fusion | flops 562036736 | bytes 7012352 | tf_op jit(solution)/shard_map/gkts,sgkp->gktp/dot_general | solution.py:35
  145.0 7.1 %copy.226 = f32[2,256,4096]{1,2,0:T(8,128)} copy(bf16[2,256,4096]{2,1,0:T(8,128)(2,1)} %param.13) | data formatting | bytes 12582912 | tf_op jit(solution)/shard_map/convert_element_type | solution.py:63
  154.7 5.9 %collective-permute-done.6 = bf16[2,2,32,32,128]{4,3,2,1,0:T(8,128)(2,1)} collective-permute-done((bf16[2,2,32,32,128]{4,3,2,1,0:T(8,128)(2,1)}, bf16[2,2,32,32,128]{4,3,2,1,0:T(8,128)(2,1)}, u32[]{:S(2)}, u32[]{:S(2)}) %collective-permute-start.6) | collective-permute-done | bytes 1048608 | tf_op jit(solution)/shard_map/ppermute | solution.py:80
  160.7 2.5 %convert_select_fusion.1 = (f32[2,2,32,32,128]{4,3,2,1,0:T(8,128)S(1)}, f32[2,2,32,32,128]{4,3,2,1,0:T(8,128)S(1)}) fusion(bf16[2,2,32,32,128]{4,3,2,1,0:T(8,128)(2,1)} %collective-permute-done.6, pred[]{:T(512)S(6)} %eq.51, f32[2,2,32,32,128]{4,3,2,1,0:T(8,128)S(1)} %copy-done.4, bf16[2,2,32,32,128]{4,3,2,1,0:T(8,128)(2,1)} %copy-done.6, ...), kind=kLoop, calls=%fused_computation.38 | loop fusion | flops 4718592 | bytes 10486273 | tf_op jit(solution)/shard_map/jit(_where)/select_n | solution.py:183
  170.1 6.0 %fusion.4 = bf16[2,256,2,32,64]{1,4,3,2,0:T(8,128)(2,1)} fusion(f32[1,2,32,256,64]{3,4,2,1,0:T(8,128)} %fusion.22, f32[1,2,32,256,64]{3,4,2,1,0:T(8,128)S(1)} %copy-done.14, f32[2,256,2,32,64]{1,4,3,2,0:T(8,128)S(1)} %bitcast.177, f32[2,2,256,32,64]{2,4,3,1,0:T(8,128)S(1)} %bitcast.174, f32[2,32]{1,0:T(2,128)S(1)} %copy-done.40, f32[2,2,256,32]{2,3,1,0:T(8,128)S(1)} %fusion.58), kind=kLoop, calls=%fused_computation.7 | loop fusion | flops 12582912 | bytes 29491456 | tf_op jit(solution)/shard_map/convert_element_type | solution.py:66
  176.1 6.3 %copy.244 = bf16[2,256,4096]{2,1,0:T(8,128)(2,1)} copy(bf16[2,256,4096]{1,2,0:T(8,128)(2,1)} %bitcast.178) | data formatting | bytes 8388608
  (204 shorter events, 58.4 us)
Async XLA Ops:
  0.6 30.2 %copy-start = (bf16[1,4,256]{2,1,0:T(4,128)(2,1)S(1)}, bf16[1,4,256]{2,1,0:T(4,128)(2,1)}, u32[]{:S(2)}) copy-start(bf16[1,4,256]{2,1,0:T(4,128)(2,1)} %param.21) | copy-start | bytes 6148
  0.6 10.2 %copy-start.23 = (bf16[2,256,256]{2,1,0:T(8,128)(2,1)S(1)}, bf16[2,256,256]{2,1,0:T(8,128)(2,1)}, u32[]{:S(2)}) copy-start(bf16[2,256,256]{2,1,0:T(8,128)(2,1)} %param.14) | copy-start | bytes 786436
  3.4 11.7 %copy-start.35 = (f32[64,2]{0,1:T(2,128)}, f32[64,2]{0,1:T(2,128)S(1)}, u32[]{:S(2)}) copy-start(f32[64,2]{0,1:T(2,128)S(1)} %slice.100) | copy-start | bytes 1540
  5.1 42.7 %collective-permute-start = (f32[2,2,32]{2,1,0:T(2,128)}, f32[2,2,32]{2,1,0:T(2,128)}, u32[]{:S(2)}, u32[]{:S(2)}) collective-permute-start(f32[2,2,32]{2,1,0:T(2,128)} %constant_dynamic-update-slice_fusion), channel_id=1, source_target_pairs={{0,2},{4,6},{8,10},{12,14},{2,0},{6,4},{10,8},{14,12},{1,3},{5,7},... | collective-permute-start | bytes 1544 | tf_op jit(solution)/shard_map/ppermute | solution.py:80
  9.4 36.0 %collective-permute-start.7 = (f32[1,1153]{1,0:T(1,128)}, f32[1,1153]{1,0:T(1,128)}, u32[]{:S(2)}, u32[]{:S(2)}) collective-permute-start(f32[1,1153]{1,0:T(1,128)} %broadcast_in_dim.73), channel_id=1, source_target_pairs={{0,2},{2,0},{4,6},{6,4},{8,10},{10,8},{12,14},{14,12},{1,3},{3,1},... | collective-permute-start | bytes 13844 | tf_op jit(solution)/shard_map/ppermute | solution.py:91
  11.0 10.6 %copy-start.18 = (bf16[1,256,256]{1,2,0:T(8,128)(2,1)}, bf16[1,256,256]{1,2,0:T(8,128)(2,1)S(1)}, u32[]{:S(2)}) copy-start(bf16[1,256,256]{1,2,0:T(8,128)(2,1)S(1)} %copy.271) | copy-start | bytes 393220
  11.2 13.0 %copy-start.16 = (bf16[1,256,256]{1,2,0:T(8,128)(2,1)}, bf16[1,256,256]{1,2,0:T(8,128)(2,1)S(1)}, u32[]{:S(2)}) copy-start(bf16[1,256,256]{1,2,0:T(8,128)(2,1)S(1)} %copy.272) | copy-start | bytes 393220
  24.1 33.8 %copy-start.2 = (f32[1,2,32,64,128]{4,3,2,1,0:T(8,128)}, f32[1,2,32,64,128]{4,3,2,1,0:T(8,128)S(1)}, u32[]{:S(2)}) copy-start(f32[1,2,32,64,128]{4,3,2,1,0:T(8,128)S(1)} %fusion.41) | copy-start | bytes 6291460
  24.9 5.9 %copy-start.38 = (bf16[1,4,256]{2,1,0:T(4,128)(2,1)S(1)}, bf16[1,4,256]{2,1,0:T(4,128)(2,1)}, u32[]{:S(2)}) copy-start(bf16[1,4,256]{2,1,0:T(4,128)(2,1)} %param.22) | copy-start | bytes 6148
  24.9 6.8 %copy-start.15 = (bf16[2,256,256]{2,1,0:T(8,128)(2,1)S(1)}, bf16[2,256,256]{2,1,0:T(8,128)(2,1)}, u32[]{:S(2)}) copy-start(bf16[2,256,256]{2,1,0:T(8,128)(2,1)} %param.15) | copy-start | bytes 786436
  26.5 45.8 %collective-permute-start.1 = (bf16[2,2,32,32,128]{4,3,2,1,0:T(8,128)(2,1)}, bf16[2,2,32,32,128]{4,3,2,1,0:T(8,128)(2,1)S(1)}, u32[]{:S(2)}, u32[]{:S(2)}) collective-permute-start(bf16[2,2,32,32,128]{4,3,2,1,0:T(8,128)(2,1)} %select_convert_fusion.1), channel_id=1, source_target_pairs={{0,2},{4,6},{8,10},{12,14},{2,0},{6,4},{10,8},{14,12},{1,3},{5,7},... | collective-permute-start | bytes 3145736 | tf_op jit(solution)/shard_map/ppermute | solution.py:80
  35.3 8.5 %copy-start.43 = (f32[1,4,64]{2,1,0:T(4,128)S(1)}, f32[1,4,64]{2,1,0:T(4,128)}, u32[]{:S(2)}) copy-start(f32[1,4,64]{2,1,0:T(4,128)} %param.23) | copy-start | bytes 3076
  46.1 3.7 %collective-permute-start.8 = (f32[2,1153]{1,0:T(2,128)S(1)}, f32[2,1153]{1,0:T(2,128)S(1)}, u32[]{:S(2)}, u32[]{:S(2)}) collective-permute-start(f32[2,1153]{1,0:T(2,128)S(1)} %maximum_select_fusion.2), channel_id=1, source_target_pairs={{0,4},{2,6},{4,0},{6,2},{8,12},{10,14},{12,8},{14,10},{1,5},{3,7},... | collective-permute-start | bytes 27680 | tf_op jit(solution)/shard_map/ppermute | solution.py:91
  49.9 4.8 %collective-permute-start.9 = (f32[4,1153]{1,0:T(4,128)S(1)}, f32[4,1153]{1,0:T(4,128)S(1)}, u32[]{:S(2)}, u32[]{:S(2)}) collective-permute-start(f32[4,1153]{1,0:T(4,128)S(1)} %maximum_select_fusion.1), channel_id=1, source_target_pairs={{0,8},{2,10},{4,12},{6,14},{8,0},{10,2},{12,4},{14,6},{1,9},{3,11}... | collective-permute-start | bytes 55352 | tf_op jit(solution)/shard_map/ppermute | solution.py:91
  67.0 18.8 %all-to-all-start = ((f32[8,1,16384]{2,1,0:T(1,128)}), f32[8,1,16384]{2,1,0:T(1,128)}, u32[]{:S(2)}, u32[]{:S(2)}) async-start(f32[8,1,16384]{2,1,0:T(1,128)} %reshape.359), calls=%async_computation | async-start | bytes 1048576 | tf_op jit(solution)/shard_map/all_to_all | solution.py:118
  76.9 5.3 %copy-start.34 = (f32[2,2,32]{2,1,0:T(2,128)S(1)}, f32[2,2,32]{2,1,0:T(2,128)}, u32[]{:S(2)}) copy-start(f32[2,2,32]{2,1,0:T(2,128)} %copy-done.33) | copy-start | bytes 1540
  78.0 4.2 %collective-permute-start.2 = (bf16[2,32,32,128]{3,2,1,0:T(8,128)(2,1)}, bf16[2,32,32,128]{3,2,1,0:T(8,128)(2,1)S(1)}, u32[]{:S(2)}, u32[]{:S(2)}) collective-permute-start(bf16[2,32,32,128]{3,2,1,0:T(8,128)(2,1)} %select_convert_fusion.4), channel_id=1, source_target_pairs={{0,4},{2,6},{1,5},{3,7},{16,20},{18,22},{17,21},{19,23}} | collective-permute-start | bytes 1572872 | tf_op jit(solution)/shard_map/ppermute | solution.py:134
  82.2 39.0 %copy-start.10 = (bf16[2,32,32,128]{3,2,1,0:T(8,128)(2,1)}, bf16[2,32,32,128]{3,2,1,0:T(8,128)(2,1)S(1)}, u32[]{:S(2)}) copy-start(bf16[2,32,32,128]{3,2,1,0:T(8,128)(2,1)S(1)} %collective-permute-done.2) | copy-start | bytes 1572868
  83.4 18.4 %collective-permute-start.3 = (bf16[2,32,32,128]{3,2,1,0:T(8,128)(2,1)}, bf16[2,32,32,128]{3,2,1,0:T(8,128)(2,1)S(1)}, u32[]{:S(2)}, u32[]{:S(2)}) collective-permute-start(bf16[2,32,32,128]{3,2,1,0:T(8,128)(2,1)} %fusion.47), channel_id=1, source_target_pairs={{0,4},{4,8},{2,6},{6,10},{1,5},{5,9},{3,7},{7,11},{16,20},{20,24},... | collective-permute-start | bytes 1572872 | tf_op jit(solution)/shard_map/ppermute | solution.py:134
  97.2 7.9 %copy-start.22 = (f32[1,4,4096]{2,1,0:T(4,128)S(1)}, f32[1,4,4096]{2,1,0:T(4,128)}, u32[]{:S(2)}) copy-start(f32[1,4,4096]{2,1,0:T(4,128)} %add.120) | copy-start | bytes 196612
  97.2 7.9 %copy-start.26 = (bf16[1,4,4096]{2,1,0:T(4,128)(2,1)S(1)}, bf16[1,4,4096]{2,1,0:T(4,128)(2,1)}, u32[]{:S(2)}) copy-start(bf16[1,4,4096]{2,1,0:T(4,128)(2,1)} %param.20) | copy-start | bytes 98308
  97.2 19.0 %copy-start.36 = (f32[64,2]{0,1:T(2,128)S(1)}, f32[64,2]{0,1:T(2,128)}, u32[]{:S(2)}) copy-start(f32[64,2]{0,1:T(2,128)} %copy-done.35) | copy-start | bytes 1540
  101.8 19.4 %copy-start.12 = (bf16[2,32,32,128]{3,2,1,0:T(8,128)(2,1)}, bf16[2,32,32,128]{3,2,1,0:T(8,128)(2,1)S(1)}, u32[]{:S(2)}) copy-start(bf16[2,32,32,128]{3,2,1,0:T(8,128)(2,1)S(1)} %collective-permute-done.3) | copy-start | bytes 1572868
  103.1 18.1 %collective-permute-start.4 = (bf16[2,32,32,128]{3,2,1,0:T(8,128)(2,1)}, bf16[2,32,32,128]{3,2,1,0:T(8,128)(2,1)}, u32[]{:S(2)}, u32[]{:S(2)}) collective-permute-start(bf16[2,32,32,128]{3,2,1,0:T(8,128)(2,1)} %select_convert_fusion.3), channel_id=1, source_target_pairs={{4,8},{8,12},{6,10},{10,14},{5,9},{9,13},{7,11},{11,15},{20,24},{2... | collective-permute-start | bytes 1572872 | tf_op jit(solution)/shard_map/ppermute | solution.py:134
  106.6 19.2 %all-to-all-start.1 = ((bf16[8,4,4096]{2,1,0:T(4,128)(2,1)}), bf16[8,4,4096]{2,1,0:T(4,128)(2,1)}, u32[]{:S(2)}, u32[]{:S(2)}) async-start(bf16[8,4,4096]{2,1,0:T(4,128)(2,1)} %concatenate.36), calls=%async_computation.1 | async-start | bytes 524288 | tf_op jit(solution)/shard_map/all_to_all | solution.py:118
  123.7 8.3 %collective-permute-start.5 = (bf16[2,32,32,128]{3,2,1,0:T(8,128)(2,1)}, bf16[2,32,32,128]{3,2,1,0:T(8,128)(2,1)}, u32[]{:S(2)}, u32[]{:S(2)}) collective-permute-start(bf16[2,32,32,128]{3,2,1,0:T(8,128)(2,1)} %select_convert_fusion.2), channel_id=1, source_target_pairs={{8,12},{10,14},{9,13},{11,15},{24,28},{26,30},{25,29},{27,31}} | collective-permute-start | bytes 1572872 | tf_op jit(solution)/shard_map/ppermute | solution.py:134
  125.8 6.2 %copy-start.11 = (bf16[2,32,32,128]{3,2,1,0:T(8,128)(2,1)S(1)}, bf16[2,32,32,128]{3,2,1,0:T(8,128)(2,1)}, u32[]{:S(2)}) copy-start(bf16[2,32,32,128]{3,2,1,0:T(8,128)(2,1)} %copy-done.10) | copy-start | bytes 1572868
  125.8 6.2 %copy-start.13 = (bf16[2,32,32,128]{3,2,1,0:T(8,128)(2,1)S(1)}, bf16[2,32,32,128]{3,2,1,0:T(8,128)(2,1)}, u32[]{:S(2)}) copy-start(bf16[2,32,32,128]{3,2,1,0:T(8,128)(2,1)} %copy-done.12) | copy-start | bytes 1572868
  131.5 21.6 %collective-permute-start.10 = (f32[8,4,1024]{2,0,1:T(8,128)}, f32[8,4,1024]{2,0,1:T(8,128)}, u32[]{:S(2)}, u32[]{:S(2)}) collective-permute-start(f32[8,4,1024]{2,0,1:T(8,128)} %fusion.5), channel_id=1, source_target_pairs={{0,1},{1,0},{2,3},{3,2},{4,5},{5,4},{6,7},{7,6},{8,9},{9,8},{10,11... | collective-permute-start | bytes 393224 | tf_op jit(solution)/shard_map/ppermute | solution.py:282
  135.6 25.1 %collective-permute-start.6 = (bf16[2,2,32,32,128]{4,3,2,1,0:T(8,128)(2,1)}, bf16[2,2,32,32,128]{4,3,2,1,0:T(8,128)(2,1)}, u32[]{:S(2)}, u32[]{:S(2)}) collective-permute-start(bf16[2,2,32,32,128]{4,3,2,1,0:T(8,128)(2,1)} %select_convert_fusion), channel_id=1, source_target_pairs={{0,2},{4,6},{8,10},{12,14},{2,0},{6,4},{10,8},{14,12},{1,3},{5,7},... | collective-permute-start | bytes 3145736 | tf_op jit(solution)/shard_map/ppermute | solution.py:80
  165.5 4.6 %copy-start.14 = (f32[1,2,32,256,64]{3,4,2,1,0:T(8,128)S(1)}, f32[1,2,32,256,64]{3,4,2,1,0:T(8,128)}, u32[]{:S(2)}) copy-start(f32[1,2,32,256,64]{3,4,2,1,0:T(8,128)} %fusion.23) | copy-start | bytes 12582916
  176.1 6.3 %copy-start.1 = (bf16[1,4,256]{2,1,0:T(4,128)(2,1)S(1)}, bf16[1,4,256]{2,1,0:T(4,128)(2,1)}, u32[]{:S(2)}) copy-start(bf16[1,4,256]{2,1,0:T(4,128)(2,1)} %param.21) | copy-start | bytes 6148
  (29 other events, 87.6 us)

commit v14 on v13

--- a/solution.py
+++ b/solution.py
@@ -221,7 +221,7 @@
     slots, steps = new_input.shape[0], new_input.shape[1]
     pieces = [totals, request_of_slot.astype(jnp.float32), new_c.astype(jnp.float32)]
     packed = jnp.concatenate([piece.reshape(-1) for piece in pieces])
-    gathered = gather_ctx(packed[None])
+    gathered = exchange_ctx(jnp.concatenate([packed[None]] * count, axis=0), False)
     unpacked = []
     offset = 0
     for piece in pieces:

time: 184 us -> 188 us (1.022)
  local copies, waits for them, and re-layouts: 52.9 us -> 55.2 us
    ppermute x4, waiting for transfers between devices: 9.32 us -> 14.5 us  [chain_columns(): lax.ppermute(outgoing.astype(jnp.bfloat16), 'ctx', pairs)]
    ppermute x3 -> x0, waiting for transfers between devices: 4.52 us -> none  [gather_ctx(): got = lax.ppermute(value, 'ctx', [(i, i ^ reach) for i in range(count)])]
    all_to_all x2 -> x3, starting transfers between devices: 15 us -> 18.2 us  [exchange_ctx(): got = lax.all_to_all(value, 'ctx', 0, 0, tiled=True)]
    ppermute x3 -> x0, starting transfers between devices: 2.56 us -> none  [gather_ctx(): got = lax.ppermute(value, 'ctx', [(i, i ^ reach) for i in range(count)])]
    unnamed x106 -> x107, local copies, waits for them, and re-layouts: 17.1 us -> 18.5 us
  transfers between devices with their start and end apart: 13 -> 11, of which waited for: 6 -> 4; matrix products, arithmetic and copies ran while one was open for 58% -> 57% of each run, Pallas kernels for 0% -> 0%
where the time goes in v14:
time: 188 us; the launch traced here: 186 us
  local copies, waits for them, and re-layouts  55.2 us (29%)
  other arithmetic  47.1 us (25%)
  matrix products  32.3 us (17%)
  starting transfers between devices  28.8 us (15%)
  waiting for transfers between devices  20.5 us (11%)
  between operations  1.97 us (1%)
    unnamed x107, local copies, waits for them, and re-layouts  18.5 us
    all_to_all x3, starting transfers between devices, exchange_ctx(): got = lax.all_to_all(value, 'ctx', 0, 0, tiled=True)  18.2 us
    ppermute x4, waiting for transfers between devices, chain_columns(): lax.ppermute(outgoing.astype(jnp.bfloat16), 'ctx', pairs)  14.5 us
    dot_general x2, matrix products, block_terms(): jnp.einsum('gkts,sgkp->gktp', mixing, inputs_head, preferred_element_type...  14.5 us
    slice x3, local copies, waits for them, and re-layouts, shards(): ssm_input[request]  10.5 us
    convert_element_type x1, local copies, waits for them, and re-layouts, finish(): inputs_head = ssm_input.reshape(request_count, block_size, group_count, p...  7.12 us
    ppermute x4, starting transfers between devices, chain_columns(): lax.ppermute(outgoing.astype(jnp.bfloat16), 'ctx', pairs)  6.15 us
    convert_element_type x4, other arithmetic, chain_columns(): outgoing.astype(jnp.bfloat16)  6.09 us
  transfers between devices with their start and end apart: 11, of which 4 were waited for; matrix products, arithmetic and copies ran while one was open for 57% of the time, Pallas kernels for 0%

profile of v14, /device:TPU:18, one launch (start us, length us, event | category | flops | bytes accessed | tf_op | source)
XLA Modules:
  0.0 185.8 jit_solution(9856062212358352987)
XLA Ops:
  5.0 1.5 collective-permute-start
  9.4 5.2 %all-to-all-start = ((f32[8,1,1153]{2,1,0:T(1,128)}), f32[8,1,1153]{2,1,0:T(1,128)}, u32[]{:S(2)}, u32[]{:S(2)}) async-start(f32[8,1,1153]{2,1,0:T(1,128)} %concatenate.15), calls=%async_computation | async-start | bytes 81920 | tf_op jit(solution)/shard_map/all_to_all | solution.py:118
  15.9 4.0 %fusion.70 = (bf16[1,256,4096]{2,1,0:T(8,128)(2,1)}, bf16[1,256,4096]{2,1,0:T(8,128)(2,1)S(1)}) fusion(bf16[2,256,4096]{2,1,0:T(8,128)(2,1)} %param.13), kind=kLoop, calls=%fused_computation.142 | loop fusion | bytes 8388608 | tf_op jit(solution)/shard_map/slice | solution.py:210
  19.9 4.1 %copy.208 = bf16[1,256,4096]{1,2,0:T(8,128)(2,1)} copy(bf16[1,256,4096]{2,1,0:T(8,128)(2,1)} %get-tuple-element.24) | data formatting | bytes 4194304 | tf_op jit(solution)/shard_map/slice | solution.py:210
  23.9 2.4 %copy.211 = bf16[1,256,4096]{1,2,0:T(8,128)(2,1)} copy(bf16[1,256,4096]{2,1,0:T(8,128)(2,1)S(1)} %get-tuple-element.25) | data formatting | bytes 4194304 | tf_op jit(solution)/shard_map/slice | solution.py:210
  26.4 2.5 %fusion.41 = f32[1,2,32,64,128]{4,3,2,1,0:T(8,128)S(1)} fusion(bf16[256,2,128,1]{0,2,3,1:T(8,128)(2,1)S(1)} %bitcast.189, bf16[256,2,32,64]{0,3,2,1:T(8,128)(2,1)} %bitcast.184, f32[256,2,32]{0,2,1:T(8,128)S(1)} %bitcast.194), kind=kOutput, calls=%fused_computation.63 | convolution fusion | flops 271581184 | bytes 4390912 | tf_op jit(solution)/shard_map/sgkp,sgn->gkpn/dot_general | solution.py:42
  29.6 1.6 select_convert_fusion.1
  34.7 1.5 fusion.74
  39.2 1.7 copy.275
  42.1 7.9 %fusion.23 = f32[1,2,32,256,64]{3,4,2,1,0:T(8,128)} fusion(bf16[256,2,32,64]{0,3,2,1:T(8,128)(2,1)} %bitcast.185, f32[2,32,256]{2,1,0:T(8,128)} %bitcast.201, f32[2,32,256]{2,1,0:T(8,128)} %reduce_window_sum.88, f32[2,256,256]{2,1,0:T(8,128)S(1)} %fusion.75, pred[256,256]{1,0:T(8,128)(4,1)} %iota_compare_fusion), kind=kOutput, calls=%fused_computation.42 | convolution fusion | flops 562036736 | bytes 7012352 | tf_op jit(solution)/shard_map/gkts,sgkp->gktp/dot_general | solution.py:35
  58.1 2.3 %fusion.24 = (bf16[2,2,32,64,128,1]{4,3,2,1,0,5:T(8,128)(2,1)S(1)}, bf16[2,2,32,64,128,1]{4,3,2,1,0,5:T(8,128)(2,1)S(1)}) fusion(f32[1,2,32,64,128]{4,3,2,1,0:T(8,128)} %copy-done.3, f32[1,2,32,64,128]{4,3,2,1,0:T(8,128)S(1)} %fusion.41, f32[2,2,32]{2,1,0:T(2,128)} %exp.65), kind=kLoop, calls=%fused_computation.43 | loop fusion | flops 6291456 | bytes 8389120 | tf_op jit(solution)/shard_map/convert_element_type | solution.py:240
  61.2 2.0 %fusion.30 = f32[2,8,4,2,32,64]{5,1,4,3,2,0:T(8,128)S(1)} fusion(bf16[2,2,32,64,128,1]{4,3,2,1,0,5:T(8,128)(2,1)S(1)} %get-tuple-element.23, bf16[8,4,2,128,1,1]{3,0,2,1,5,4:T(8,128)(2,1)S(1)} %bitcast.195), kind=kOutput, calls=%fused_computation.50 | convolution fusion | flops 67108864 | bytes 3162112 | tf_op jit(solution)/shard_map/rgkpn,jugn->rjugkp/dot_general | solution.py:245
  63.3 2.1 %add_bitcast_fusion = f32[2,8,4,2,32,64]{5,1,4,0,2,3:T(8,128)S(1)} fusion(f32[2,8,4,2,32,64]{5,1,4,3,2,0:T(8,128)S(1)} %fusion.30, bf16[2,2,32,64,128,1]{4,3,2,1,0,5:T(8,128)(2,1)S(1)} %get-tuple-element.22, bf16[8,4,2,128,1,1]{3,0,2,1,5,4:T(8,128)(2,1)S(1)} %bitcast.196), kind=kOutput, calls=%fused_computation.54 | convolution fusion | flops 67371008 | bytes 4210688 | tf_op jit(solution)/shard_map/rgkpn,jugn->rjugkp/dot_general | solution.py:243
  67.2 5.1 %all-to-all-start.1 = ((f32[8,1,16384]{2,1,0:T(1,128)}), f32[8,1,16384]{2,1,0:T(1,128)}, u32[]{:S(2)}, u32[]{:S(2)}) async-start(f32[8,1,16384]{2,1,0:T(1,128)} %reshape.366), calls=%async_computation.1 | async-start | bytes 1048576 | tf_op jit(solution)/shard_map/all_to_all | solution.py:118
  72.3 4.4 %fusion.25 = (f32[2,2,32,32,128]{4,3,2,1,0:T(8,128)S(1)}, f32[2,2,32,32,128]{4,3,2,1,0:T(8,128)}) fusion(bf16[2,2,32,32,128]{4,3,2,1,0:T(8,128)(2,1)S(1)} %collective-permute-done.1, f32[2,2,32]{2,1,0:T(2,128)} %get-tuple-element.39, pred[]{:T(512)S(6)} %eq.51, f32[1,2,32,64,128]{4,3,2,1,0:T(8,128)} %copy-done.3, f32[1,2,32,64,128]{4,3,2,1,0:T(8,128)} %copy-done.2), kind=kLoop, calls=%fused_computation.44 | loop fusion | flops 4194304 | bytes 9437697 | tf_op jit(solution)/shard_map/add | solution.py:159
  86.2 3.8 %reduce.16 = f32[8,16384]{1,0:T(8,128)} reduce(f32[8,1,16384]{2,1,0:T(1,128)} %all-to-all-done.1, f32[]{:T(128)} %broadcast.187), dimensions={1}, to_apply=%all_to_all.14.reduce_sub_computation | reduce | bytes 1048580 | tf_op jit(solution)/shard_map/all_to_all | solution.py:118
  90.0 2.5 %reshape.367 = f32[8,2,4,32,64]{4,3,2,1,0:T(8,128)} reshape(f32[8,16384]{1,0:T(8,128)} %reduce.16) | data formatting | bytes 1048576
  95.5 1.6 add.120
  97.1 8.1 %collective-permute-done.3 = bf16[2,32,32,128]{3,2,1,0:T(8,128)(2,1)S(1)} collective-permute-done((bf16[2,32,32,128]{3,2,1,0:T(8,128)(2,1)}, bf16[2,32,32,128]{3,2,1,0:T(8,128)(2,1)S(1)}, u32[]{:S(2)}, u32[]{:S(2)}) %collective-permute-start.3) | collective-permute-done | bytes 524320 | tf_op jit(solution)/shard_map/ppermute | solution.py:134
  106.5 1.9 %collective-permute-start.4 = (bf16[2,32,32,128]{3,2,1,0:T(8,128)(2,1)}, bf16[2,32,32,128]{3,2,1,0:T(8,128)(2,1)}, u32[]{:S(2)}, u32[]{:S(2)}) collective-permute-start(bf16[2,32,32,128]{3,2,1,0:T(8,128)(2,1)} %select_convert_fusion.3), channel_id=1, source_target_pairs={{4,8},{8,12},{6,10},{10,14},{5,9},{9,13},{7,11},{11,15},{20,24},{2... | collective-permute-start | bytes 1572872 | tf_op jit(solution)/shard_map/ppermute | solution.py:134
  110.0 7.9 %all-to-all-start.2 = ((bf16[8,4,4096]{2,1,0:T(4,128)(2,1)}), bf16[8,4,4096]{2,1,0:T(4,128)(2,1)}, u32[]{:S(2)}, u32[]{:S(2)}) async-start(bf16[8,4,4096]{2,1,0:T(4,128)(2,1)} %concatenate.16), calls=%async_computation.2 | async-start | bytes 524288 | tf_op jit(solution)/shard_map/all_to_all | solution.py:118
  118.7 5.9 %collective-permute-done.4 = bf16[2,32,32,128]{3,2,1,0:T(8,128)(2,1)} collective-permute-done((bf16[2,32,32,128]{3,2,1,0:T(8,128)(2,1)}, bf16[2,32,32,128]{3,2,1,0:T(8,128)(2,1)}, u32[]{:S(2)}, u32[]{:S(2)}) %collective-permute-start.4) | collective-permute-done | bytes 524320 | tf_op jit(solution)/shard_map/ppermute | solution.py:134
  124.6 2.5 %select_convert_fusion.2 = bf16[2,32,32,128]{3,2,1,0:T(8,128)(2,1)} fusion(f32[2,2,32,32,128]{4,3,2,1,0:T(8,128)S(1)} %get-tuple-element.18, bf16[2,32,32,128]{3,2,1,0:T(8,128)(2,1)S(1)} %collective-permute-done.2, bf16[2,32,32,128]{3,2,1,0:T(8,128)(2,1)S(1)} %collective-permute-done.3, bf16[2,32,32,128]{3,2,1,0:T(8,128)(2,1)} %collective-permute-done.4, ...), kind=kLoop, calls=%fused_computation.87 | loop fusion | flops 4194304 | bytes 4194822 | tf_op jit(solution)/shard_map/convert_element_type | solution.py:134
  127.1 2.1 %collective-permute-start.5 = (bf16[2,32,32,128]{3,2,1,0:T(8,128)(2,1)}, bf16[2,32,32,128]{3,2,1,0:T(8,128)(2,1)}, u32[]{:S(2)}, u32[]{:S(2)}) collective-permute-start(bf16[2,32,32,128]{3,2,1,0:T(8,128)(2,1)} %select_convert_fusion.2), channel_id=1, source_target_pairs={{8,12},{10,14},{9,13},{11,15},{24,28},{26,30},{25,29},{27,31}} | collective-permute-start | bytes 1572872 | tf_op jit(solution)/shard_map/ppermute | solution.py:134
  129.2 5.6 %fusion.5 = f32[8,4,1024]{2,0,1:T(8,128)} fusion(bf16[4096,1024]{1,0:T(8,128)(2,1)} %param.25, bf16[8,4,4096]{2,1,0:T(4,128)(2,1)} %all-to-all-done.2), kind=kOutput, calls=%fused_computation.8 | convolution fusion | flops 268435456 | bytes 8781824 | tf_op jit(solution)/shard_map/jup,pd->jud/dot_general | solution.py:275
  135.4 2.0 %fusion.49 = (f32[1,2,32,32,128]{4,3,2,1,0:T(8,128)S(1)}, f32[1,2,32,32,128]{4,3,2,1,0:T(8,128)S(1)}) fusion(bf16[2,32,32,128]{3,2,1,0:T(8,128)(2,1)} %collective-permute-done.5, bf16[2,32,32,128]{3,2,1,0:T(8,128)(2,1)S(1)} %copy-done.11, bf16[2,32,32,128]{3,2,1,0:T(8,128)(2,1)S(1)} %copy-done.13, bf16[2,32,32,128]{3,2,1,0:T(8,128)(2,1)} %collective-permute-done.4, ...), kind=kLoop, calls=%fused_computation.80 | loop fusion | flops 3145728 | bytes 4194312 | tf_op jit(solution)/shard_map/stack | solution.py:137
  140.5 6.6 %fusion.22 = f32[1,2,32,256,64]{3,4,2,1,0:T(8,128)} fusion(bf16[256,2,32,64]{0,3,2,1:T(8,128)(2,1)S(1)} %bitcast.183, f32[2,32,256]{2,1,0:T(8,128)S(1)} %bitcast.200, f32[2,32,256]{2,1,0:T(8,128)S(1)} %copy-done.30, f32[2,256,256]{2,1,0:T(8,128)S(1)} %copy-done.19, pred[256,256]{1,0:T(8,128)(4,1)S(1)} %copy-done.29), kind=kOutput, calls=%fused_computation.41 | convolution fusion | flops 562036736 | bytes 7012352 | tf_op jit(solution)/shard_map/gkts,sgkp->gktp/dot_general | solution.py:35
  148.4 7.1 %copy.226 = f32[2,256,4096]{1,2,0:T(8,128)} copy(bf16[2,256,4096]{2,1,0:T(8,128)(2,1)} %param.13) | data formatting | bytes 12582912 | tf_op jit(solution)/shard_map/convert_element_type | solution.py:63
  158.1 5.9 %collective-permute-done.6 = bf16[2,2,32,32,128]{4,3,2,1,0:T(8,128)(2,1)} collective-permute-done((bf16[2,2,32,32,128]{4,3,2,1,0:T(8,128)(2,1)}, bf16[2,2,32,32,128]{4,3,2,1,0:T(8,128)(2,1)}, u32[]{:S(2)}, u32[]{:S(2)}) %collective-permute-start.6) | collective-permute-done | bytes 1048608 | tf_op jit(solution)/shard_map/ppermute | solution.py:80
  164.1 2.5 %convert_select_fusion.1 = (f32[2,2,32,32,128]{4,3,2,1,0:T(8,128)S(1)}, f32[2,2,32,32,128]{4,3,2,1,0:T(8,128)S(1)}) fusion(bf16[2,2,32,32,128]{4,3,2,1,0:T(8,128)(2,1)} %collective-permute-done.6, pred[]{:T(512)S(6)} %eq.51, f32[2,2,32,32,128]{4,3,2,1,0:T(8,128)S(1)} %copy-done.4, bf16[2,2,32,32,128]{4,3,2,1,0:T(8,128)(2,1)} %copy-done.6, ...), kind=kLoop, calls=%fused_computation.38 | loop fusion | flops 4718592 | bytes 10486273 | tf_op jit(solution)/shard_map/jit(_where)/select_n | solution.py:183
  173.5 6.0 %fusion.4 = bf16[2,256,2,32,64]{1,4,3,2,0:T(8,128)(2,1)} fusion(f32[1,2,32,256,64]{3,4,2,1,0:T(8,128)} %fusion.22, f32[1,2,32,256,64]{3,4,2,1,0:T(8,128)S(1)} %copy-done.14, f32[2,256,2,32,64]{1,4,3,2,0:T(8,128)S(1)} %bitcast.180, f32[2,2,256,32,64]{2,4,3,1,0:T(8,128)S(1)} %bitcast.177, f32[2,32]{1,0:T(2,128)S(1)} %copy-done.40, f32[2,2,256,32]{2,3,1,0:T(8,128)S(1)} %fusion.58), kind=kLoop, calls=%fused_computation.7 | loop fusion | flops 12582912 | bytes 29491456 | tf_op jit(solution)/shard_map/convert_element_type | solution.py:66
  179.5 6.3 %copy.244 = bf16[2,256,4096]{2,1,0:T(8,128)(2,1)} copy(bf16[2,256,4096]{1,2,0:T(8,128)(2,1)} %bitcast.181) | data formatting | bytes 8388608
  (198 shorter events, 57.2 us)
Async XLA Ops:
  0.6 36.2 %copy-start = (bf16[1,4,256]{2,1,0:T(4,128)(2,1)S(1)}, bf16[1,4,256]{2,1,0:T(4,128)(2,1)}, u32[]{:S(2)}) copy-start(bf16[1,4,256]{2,1,0:T(4,128)(2,1)} %param.21) | copy-start | bytes 6148
  0.6 15.0 %copy-start.23 = (bf16[2,256,256]{2,1,0:T(8,128)(2,1)S(1)}, bf16[2,256,256]{2,1,0:T(8,128)(2,1)}, u32[]{:S(2)}) copy-start(bf16[2,256,256]{2,1,0:T(8,128)(2,1)} %param.14) | copy-start | bytes 786436
  3.4 16.4 %copy-start.35 = (f32[64,2]{0,1:T(2,128)}, f32[64,2]{0,1:T(2,128)S(1)}, u32[]{:S(2)}) copy-start(f32[64,2]{0,1:T(2,128)S(1)} %slice.100) | copy-start | bytes 1540
  5.0 46.6 %collective-permute-start = (f32[2,2,32]{2,1,0:T(2,128)}, f32[2,2,32]{2,1,0:T(2,128)}, u32[]{:S(2)}, u32[]{:S(2)}) collective-permute-start(f32[2,2,32]{2,1,0:T(2,128)} %constant_dynamic-update-slice_fusion), channel_id=1, source_target_pairs={{0,2},{4,6},{8,10},{12,14},{2,0},{6,4},{10,8},{14,12},{1,3},{5,7},... | collective-permute-start | bytes 1544 | tf_op jit(solution)/shard_map/ppermute | solution.py:80
  9.4 44.7 %all-to-all-start = ((f32[8,1,1153]{2,1,0:T(1,128)}), f32[8,1,1153]{2,1,0:T(1,128)}, u32[]{:S(2)}, u32[]{:S(2)}) async-start(f32[8,1,1153]{2,1,0:T(1,128)} %concatenate.15), calls=%async_computation | async-start | bytes 81920 | tf_op jit(solution)/shard_map/all_to_all | solution.py:118
  15.8 10.6 %copy-start.18 = (bf16[1,256,256]{1,2,0:T(8,128)(2,1)}, bf16[1,256,256]{1,2,0:T(8,128)(2,1)S(1)}, u32[]{:S(2)}) copy-start(bf16[1,256,256]{1,2,0:T(8,128)(2,1)S(1)} %copy.272) | copy-start | bytes 393220
  15.9 13.0 %copy-start.16 = (bf16[1,256,256]{1,2,0:T(8,128)(2,1)}, bf16[1,256,256]{1,2,0:T(8,128)(2,1)S(1)}, u32[]{:S(2)}) copy-start(bf16[1,256,256]{1,2,0:T(8,128)(2,1)S(1)} %copy.273) | copy-start | bytes 393220
  28.9 29.2 %copy-start.2 = (f32[1,2,32,64,128]{4,3,2,1,0:T(8,128)}, f32[1,2,32,64,128]{4,3,2,1,0:T(8,128)S(1)}, u32[]{:S(2)}) copy-start(f32[1,2,32,64,128]{4,3,2,1,0:T(8,128)S(1)} %fusion.41) | copy-start | bytes 6291460
  29.6 7.2 %copy-start.38 = (bf16[1,4,256]{2,1,0:T(4,128)(2,1)S(1)}, bf16[1,4,256]{2,1,0:T(4,128)(2,1)}, u32[]{:S(2)}) copy-start(bf16[1,4,256]{2,1,0:T(4,128)(2,1)} %param.22) | copy-start | bytes 6148
  29.6 8.9 %copy-start.15 = (bf16[2,256,256]{2,1,0:T(8,128)(2,1)S(1)}, bf16[2,256,256]{2,1,0:T(8,128)(2,1)}, u32[]{:S(2)}) copy-start(bf16[2,256,256]{2,1,0:T(8,128)(2,1)} %param.15) | copy-start | bytes 786436
  31.3 41.0 %collective-permute-start.1 = (bf16[2,2,32,32,128]{4,3,2,1,0:T(8,128)(2,1)}, bf16[2,2,32,32,128]{4,3,2,1,0:T(8,128)(2,1)S(1)}, u32[]{:S(2)}, u32[]{:S(2)}) collective-permute-start(bf16[2,2,32,32,128]{4,3,2,1,0:T(8,128)(2,1)} %select_convert_fusion.1), channel_id=1, source_target_pairs={{0,2},{4,6},{8,10},{12,14},{2,0},{6,4},{10,8},{14,12},{1,3},{5,7},... | collective-permute-start | bytes 3145736 | tf_op jit(solution)/shard_map/ppermute | solution.py:80
  42.1 8.0 %copy-start.43 = (f32[1,4,64]{2,1,0:T(4,128)S(1)}, f32[1,4,64]{2,1,0:T(4,128)}, u32[]{:S(2)}) copy-start(f32[1,4,64]{2,1,0:T(4,128)} %param.23) | copy-start | bytes 3076
  67.2 18.5 %all-to-all-start.1 = ((f32[8,1,16384]{2,1,0:T(1,128)}), f32[8,1,16384]{2,1,0:T(1,128)}, u32[]{:S(2)}, u32[]{:S(2)}) async-start(f32[8,1,16384]{2,1,0:T(1,128)} %reshape.366), calls=%async_computation.1 | async-start | bytes 1048576 | tf_op jit(solution)/shard_map/all_to_all | solution.py:118
  72.3 4.5 %copy-start.41 = (f32[2,32]{1,0:T(2,128)S(1)}, f32[2,32]{1,0:T(2,128)}, u32[]{:S(2)}) copy-start(f32[2,32]{1,0:T(2,128)} %get-tuple-element.43) | copy-start | bytes 772
  76.8 5.3 %copy-start.34 = (f32[2,2,32]{2,1,0:T(2,128)S(1)}, f32[2,2,32]{2,1,0:T(2,128)}, u32[]{:S(2)}) copy-start(f32[2,2,32]{2,1,0:T(2,128)} %copy-done.33) | copy-start | bytes 1540
  77.9 4.2 %collective-permute-start.2 = (bf16[2,32,32,128]{3,2,1,0:T(8,128)(2,1)}, bf16[2,32,32,128]{3,2,1,0:T(8,128)(2,1)S(1)}, u32[]{:S(2)}, u32[]{:S(2)}) collective-permute-start(bf16[2,32,32,128]{3,2,1,0:T(8,128)(2,1)} %select_convert_fusion.4), channel_id=1, source_target_pairs={{0,4},{2,6},{1,5},{3,7},{16,20},{18,22},{17,21},{19,23}} | collective-permute-start | bytes 1572872 | tf_op jit(solution)/shard_map/ppermute | solution.py:134
  82.1 42.5 %copy-start.10 = (bf16[2,32,32,128]{3,2,1,0:T(8,128)(2,1)}, bf16[2,32,32,128]{3,2,1,0:T(8,128)(2,1)S(1)}, u32[]{:S(2)}) copy-start(bf16[2,32,32,128]{3,2,1,0:T(8,128)(2,1)S(1)} %collective-permute-done.2) | copy-start | bytes 1572868
  83.4 21.8 %collective-permute-start.3 = (bf16[2,32,32,128]{3,2,1,0:T(8,128)(2,1)}, bf16[2,32,32,128]{3,2,1,0:T(8,128)(2,1)S(1)}, u32[]{:S(2)}, u32[]{:S(2)}) collective-permute-start(bf16[2,32,32,128]{3,2,1,0:T(8,128)(2,1)} %fusion.47), channel_id=1, source_target_pairs={{0,4},{4,8},{2,6},{6,10},{1,5},{5,9},{3,7},{7,11},{16,20},{20,24},... | collective-permute-start | bytes 1572872 | tf_op jit(solution)/shard_map/ppermute | solution.py:134
  97.1 11.3 %copy-start.22 = (f32[1,4,4096]{2,1,0:T(4,128)S(1)}, f32[1,4,4096]{2,1,0:T(4,128)}, u32[]{:S(2)}) copy-start(f32[1,4,4096]{2,1,0:T(4,128)} %add.120) | copy-start | bytes 196612
  97.1 11.3 %copy-start.26 = (bf16[1,4,4096]{2,1,0:T(4,128)(2,1)S(1)}, bf16[1,4,4096]{2,1,0:T(4,128)(2,1)}, u32[]{:S(2)}) copy-start(bf16[1,4,4096]{2,1,0:T(4,128)(2,1)} %param.20) | copy-start | bytes 98308
  97.1 20.7 %copy-start.36 = (f32[64,2]{0,1:T(2,128)S(1)}, f32[64,2]{0,1:T(2,128)}, u32[]{:S(2)}) copy-start(f32[64,2]{0,1:T(2,128)} %copy-done.35) | copy-start | bytes 1540
  105.2 19.4 %copy-start.12 = (bf16[2,32,32,128]{3,2,1,0:T(8,128)(2,1)}, bf16[2,32,32,128]{3,2,1,0:T(8,128)(2,1)S(1)}, u32[]{:S(2)}) copy-start(bf16[2,32,32,128]{3,2,1,0:T(8,128)(2,1)S(1)} %collective-permute-done.3) | copy-start | bytes 1572868
  106.5 18.1 %collective-permute-start.4 = (bf16[2,32,32,128]{3,2,1,0:T(8,128)(2,1)}, bf16[2,32,32,128]{3,2,1,0:T(8,128)(2,1)}, u32[]{:S(2)}, u32[]{:S(2)}) collective-permute-start(bf16[2,32,32,128]{3,2,1,0:T(8,128)(2,1)} %select_convert_fusion.3), channel_id=1, source_target_pairs={{4,8},{8,12},{6,10},{10,14},{5,9},{9,13},{7,11},{11,15},{20,24},{2... | collective-permute-start | bytes 1572872 | tf_op jit(solution)/shard_map/ppermute | solution.py:134
  110.0 19.2 %all-to-all-start.2 = ((bf16[8,4,4096]{2,1,0:T(4,128)(2,1)}), bf16[8,4,4096]{2,1,0:T(4,128)(2,1)}, u32[]{:S(2)}, u32[]{:S(2)}) async-start(bf16[8,4,4096]{2,1,0:T(4,128)(2,1)} %concatenate.16), calls=%async_computation.2 | async-start | bytes 524288 | tf_op jit(solution)/shard_map/all_to_all | solution.py:118
  127.1 8.3 %collective-permute-start.5 = (bf16[2,32,32,128]{3,2,1,0:T(8,128)(2,1)}, bf16[2,32,32,128]{3,2,1,0:T(8,128)(2,1)}, u32[]{:S(2)}, u32[]{:S(2)}) collective-permute-start(bf16[2,32,32,128]{3,2,1,0:T(8,128)(2,1)} %select_convert_fusion.2), channel_id=1, source_target_pairs={{8,12},{10,14},{9,13},{11,15},{24,28},{26,30},{25,29},{27,31}} | collective-permute-start | bytes 1572872 | tf_op jit(solution)/shard_map/ppermute | solution.py:134
  129.2 6.2 %copy-start.11 = (bf16[2,32,32,128]{3,2,1,0:T(8,128)(2,1)S(1)}, bf16[2,32,32,128]{3,2,1,0:T(8,128)(2,1)}, u32[]{:S(2)}) copy-start(bf16[2,32,32,128]{3,2,1,0:T(8,128)(2,1)} %copy-done.10) | copy-start | bytes 1572868
  129.2 6.2 %copy-start.13 = (bf16[2,32,32,128]{3,2,1,0:T(8,128)(2,1)S(1)}, bf16[2,32,32,128]{3,2,1,0:T(8,128)(2,1)}, u32[]{:S(2)}) copy-start(bf16[2,32,32,128]{3,2,1,0:T(8,128)(2,1)} %copy-done.12) | copy-start | bytes 1572868
  134.8 21.6 %collective-permute-start.7 = (f32[8,4,1024]{2,0,1:T(8,128)}, f32[8,4,1024]{2,0,1:T(8,128)}, u32[]{:S(2)}, u32[]{:S(2)}) collective-permute-start(f32[8,4,1024]{2,0,1:T(8,128)} %fusion.5), channel_id=1, source_target_pairs={{0,1},{1,0},{2,3},{3,2},{4,5},{5,4},{6,7},{7,6},{8,9},{9,8},{10,11... | collective-permute-start | bytes 393224 | tf_op jit(solution)/shard_map/ppermute | solution.py:282
  139.0 25.1 %collective-permute-start.6 = (bf16[2,2,32,32,128]{4,3,2,1,0:T(8,128)(2,1)}, bf16[2,2,32,32,128]{4,3,2,1,0:T(8,128)(2,1)}, u32[]{:S(2)}, u32[]{:S(2)}) collective-permute-start(bf16[2,2,32,32,128]{4,3,2,1,0:T(8,128)(2,1)} %select_convert_fusion), channel_id=1, source_target_pairs={{0,2},{4,6},{8,10},{12,14},{2,0},{6,4},{10,8},{14,12},{1,3},{5,7},... | collective-permute-start | bytes 3145736 | tf_op jit(solution)/shard_map/ppermute | solution.py:80
  168.9 4.6 %copy-start.14 = (f32[1,2,32,256,64]{3,4,2,1,0:T(8,128)S(1)}, f32[1,2,32,256,64]{3,4,2,1,0:T(8,128)}, u32[]{:S(2)}) copy-start(f32[1,2,32,256,64]{3,4,2,1,0:T(8,128)} %fusion.23) | copy-start | bytes 12582916
  168.9 4.6 %copy-start.40 = (f32[2,32]{1,0:T(2,128)S(1)}, f32[2,32]{1,0:T(2,128)}, u32[]{:S(2)}) copy-start(f32[2,32]{1,0:T(2,128)} %copy-done.39) | copy-start | bytes 772
  179.5 6.3 %copy-start.1 = (bf16[1,4,256]{2,1,0:T(4,128)(2,1)S(1)}, bf16[1,4,256]{2,1,0:T(4,128)(2,1)}, u32[]{:S(2)}) copy-start(bf16[1,4,256]{2,1,0:T(4,128)(2,1)} %param.21) | copy-start | bytes 6148
  (27 other events, 77.2 us)

commit v15 on v13

--- a/solution.py
+++ b/solution.py
@@ -58,11 +58,7 @@
     carried = carried.reshape(request_count, group_count, block_size, per_group, HEAD_DIM)
     growth = jnp.exp(cumulative).reshape(request_count, group_count, per_group, block_size)
     carried = carried * growth.transpose(0, 1, 3, 2)[..., None]
-    inputs_head = ssm_input.reshape(
-        request_count, block_size, group_count, per_group, HEAD_DIM
-    ).astype(jnp.float32)
-    skipped = skip_gain.reshape(group_count, per_group, 1) * inputs_head
-    total = carried.transpose(0, 2, 1, 3, 4) + local_out.transpose(0, 3, 1, 2, 4) + skipped
+    total = carried.transpose(0, 2, 1, 3, 4) + local_out.transpose(0, 3, 1, 2, 4)
     return total.reshape(request_count, block_size, -1).astype(jnp.bfloat16)
 
 
@@ -286,7 +282,11 @@
 
     entering = prefix_states(states, totals)
     prefill_out = finish(
-        jnp.stack([term[2] for term in terms]),
+        jnp.stack([term[2] for term in terms])
+        + skip_gain.reshape(1, group_count, per_group, 1, 1)
+        * ssm_input.reshape(request_count, -1, group_count, per_group, HEAD_DIM)
+        .transpose(0, 2, 3, 1, 4)
+        .astype(jnp.float32),
         jnp.stack([term[0] for term in terms]),
         c_proj,
         entering,

time: 184 us -> 184 us (level)
  transfers between devices with their start and end apart: 13 -> 13, of which waited for: 6 -> 6; matrix products, arithmetic and copies ran while one was open for 58% -> 57% of each run, Pallas kernels for 0% -> 0%
where the time goes in v15:
time: 184 us; the launch traced here: 182 us
  local copies, waits for them, and re-layouts  52.9 us (29%)
  other arithmetic  47.3 us (26%)
  matrix products  32.3 us (18%)
  starting transfers between devices  28.2 us (15%)
  waiting for transfers between devices  19.8 us (11%)
  between operations  2 us (1%)
    unnamed x106, local copies, waits for them, and re-layouts  17.1 us
    all_to_all x2, starting transfers between devices, exchange_ctx(): got = lax.all_to_all(value, 'ctx', 0, 0, tiled=True)  15 us
    dot_general x2, matrix products, block_terms(): jnp.einsum('gkts,sgkp->gktp', mixing, inputs_head, preferred_element_type...  14.5 us
    slice x3, local copies, waits for them, and re-layouts, shards(): ssm_input[request]  10.5 us
    ppermute x4, waiting for transfers between devices, chain_columns(): lax.ppermute(outgoing.astype(jnp.bfloat16), 'ctx', pairs)  9.32 us
    convert_element_type x1, local copies, waits for them, and re-layouts, shards(): prefill_out = finish(jnp.stack([term[2] for term in terms]) + skip_gain.r...  7.11 us
    ppermute x4, starting transfers between devices, chain_columns(): lax.ppermute(outgoing.astype(jnp.bfloat16), 'ctx', pairs)  6.14 us
    convert_element_type x4, other arithmetic, chain_columns(): outgoing.astype(jnp.bfloat16)  6.09 us
  transfers between devices with their start and end apart: 13, of which 6 were waited for; matrix products, arithmetic and copies ran while one was open for 57% of the time, Pallas kernels for 0%

profile of v15, /device:TPU:18, one launch (start us, length us, event | category | flops | bytes accessed | tf_op | source)
XLA Modules:
  0.0 182.5 jit_solution(8492720874828604717)
XLA Ops:
  11.2 4.0 %fusion.70 = (bf16[1,256,4096]{2,1,0:T(8,128)(2,1)}, bf16[1,256,4096]{2,1,0:T(8,128)(2,1)S(1)}) fusion(bf16[2,256,4096]{2,1,0:T(8,128)(2,1)} %param.13), kind=kLoop, calls=%fused_computation.144 | loop fusion | bytes 8388608 | tf_op jit(solution)/shard_map/slice | solution.py:206
  15.1 4.1 %copy.208 = bf16[1,256,4096]{1,2,0:T(8,128)(2,1)} copy(bf16[1,256,4096]{2,1,0:T(8,128)(2,1)} %get-tuple-element.24) | data formatting | bytes 4194304 | tf_op jit(solution)/shard_map/slice | solution.py:206
  19.2 2.4 %copy.211 = bf16[1,256,4096]{1,2,0:T(8,128)(2,1)} copy(bf16[1,256,4096]{2,1,0:T(8,128)(2,1)S(1)} %get-tuple-element.25) | data formatting | bytes 4194304 | tf_op jit(solution)/shard_map/slice | solution.py:206
  21.7 2.5 %fusion.41 = f32[1,2,32,64,128]{4,3,2,1,0:T(8,128)S(1)} fusion(bf16[256,2,128,1]{0,2,3,1:T(8,128)(2,1)S(1)} %bitcast.186, bf16[256,2,32,64]{0,3,2,1:T(8,128)(2,1)} %bitcast.181, f32[256,2,32]{0,2,1:T(8,128)S(1)} %bitcast.191), kind=kOutput, calls=%fused_computation.63 | convolution fusion | flops 271581184 | bytes 4390912 | tf_op jit(solution)/shard_map/sgkp,sgn->gkpn/dot_general | solution.py:42
  24.9 1.6 select_convert_fusion.1
  29.3 1.5 fusion.74
  32.4 1.7 copy.274
  35.3 7.9 %fusion.23 = f32[1,2,32,256,64]{3,4,2,1,0:T(8,128)} fusion(bf16[256,2,32,64]{0,3,2,1:T(8,128)(2,1)} %bitcast.182, f32[2,32,256]{2,1,0:T(8,128)} %bitcast.195, f32[2,32,256]{2,1,0:T(8,128)} %reduce_window_sum.88, f32[2,256,256]{2,1,0:T(8,128)S(1)} %fusion.75, pred[256,256]{1,0:T(8,128)(4,1)} %iota_compare_fusion), kind=kOutput, calls=%fused_computation.42 | convolution fusion | flops 562036736 | bytes 7012352 | tf_op jit(solution)/shard_map/gkts,sgkp->gktp/dot_general | solution.py:35
  46.1 1.6 collective-permute-start.8
  50.9 3.7 %collective-permute-done.9 = f32[4,1153]{1,0:T(4,128)S(1)} collective-permute-done((f32[4,1153]{1,0:T(4,128)S(1)}, f32[4,1153]{1,0:T(4,128)S(1)}, u32[]{:S(2)}, u32[]{:S(2)}) %collective-permute-start.9) | collective-permute-done | bytes 18480 | tf_op jit(solution)/shard_map/ppermute | solution.py:87
  57.9 2.3 %fusion.24 = (bf16[2,2,32,64,128,1]{4,3,2,1,0,5:T(8,128)(2,1)S(1)}, bf16[2,2,32,64,128,1]{4,3,2,1,0,5:T(8,128)(2,1)S(1)}) fusion(f32[1,2,32,64,128]{4,3,2,1,0:T(8,128)} %copy-done.3, f32[1,2,32,64,128]{4,3,2,1,0:T(8,128)S(1)} %fusion.41, f32[2,2,32]{2,1,0:T(2,128)} %exp.65), kind=kLoop, calls=%fused_computation.43 | loop fusion | flops 6291456 | bytes 8389120 | tf_op jit(solution)/shard_map/convert_element_type | solution.py:236
  61.1 2.0 %fusion.30 = f32[2,8,4,2,32,64]{5,1,4,3,2,0:T(8,128)S(1)} fusion(bf16[2,2,32,64,128,1]{4,3,2,1,0,5:T(8,128)(2,1)S(1)} %get-tuple-element.23, bf16[8,4,2,128,1,1]{3,0,2,1,5,4:T(8,128)(2,1)S(1)} %bitcast.192), kind=kOutput, calls=%fused_computation.50 | convolution fusion | flops 67108864 | bytes 3162112 | tf_op jit(solution)/shard_map/rgkpn,jugn->rjugkp/dot_general | solution.py:241
  63.1 2.1 %add_bitcast_fusion = f32[2,8,4,2,32,64]{5,1,4,0,2,3:T(8,128)S(1)} fusion(f32[2,8,4,2,32,64]{5,1,4,3,2,0:T(8,128)S(1)} %fusion.30, bf16[2,2,32,64,128,1]{4,3,2,1,0,5:T(8,128)(2,1)S(1)} %get-tuple-element.22, bf16[8,4,2,128,1,1]{3,0,2,1,5,4:T(8,128)(2,1)S(1)} %bitcast.193), kind=kOutput, calls=%fused_computation.54 | convolution fusion | flops 67371008 | bytes 4210688 | tf_op jit(solution)/shard_map/rgkpn,jugn->rjugkp/dot_general | solution.py:239
  67.0 5.3 %all-to-all-start = ((f32[8,1,16384]{2,1,0:T(1,128)}), f32[8,1,16384]{2,1,0:T(1,128)}, u32[]{:S(2)}, u32[]{:S(2)}) async-start(f32[8,1,16384]{2,1,0:T(1,128)} %reshape.360), calls=%async_computation | async-start | bytes 1048576 | tf_op jit(solution)/shard_map/all_to_all | solution.py:114
  72.4 4.4 %fusion.25 = (f32[2,2,32,32,128]{4,3,2,1,0:T(8,128)S(1)}, f32[2,2,32,32,128]{4,3,2,1,0:T(8,128)}) fusion(bf16[2,2,32,32,128]{4,3,2,1,0:T(8,128)(2,1)S(1)} %collective-permute-done.1, f32[2,2,32]{2,1,0:T(2,128)} %get-tuple-element.39, pred[]{:T(512)S(6)} %eq.51, f32[1,2,32,64,128]{4,3,2,1,0:T(8,128)} %copy-done.3, f32[1,2,32,64,128]{4,3,2,1,0:T(8,128)} %copy-done.2), kind=kLoop, calls=%fused_computation.44 | loop fusion | flops 4194304 | bytes 9437697 | tf_op jit(solution)/shard_map/add | solution.py:155
  86.3 3.8 %reduce.16 = f32[8,16384]{1,0:T(8,128)} reduce(f32[8,1,16384]{2,1,0:T(1,128)} %all-to-all-done, f32[]{:T(128)} %broadcast.184), dimensions={1}, to_apply=%all_to_all.6.reduce_sub_computation | reduce | bytes 1048580 | tf_op jit(solution)/shard_map/all_to_all | solution.py:114
  90.1 2.4 %reshape.361 = f32[8,2,4,32,64]{4,3,2,1,0:T(8,128)} reshape(f32[8,16384]{1,0:T(8,128)} %reduce.16) | data formatting | bytes 1048576
  95.5 1.6 add.120
  97.2 4.6 %collective-permute-done.3 = bf16[2,32,32,128]{3,2,1,0:T(8,128)(2,1)S(1)} collective-permute-done((bf16[2,32,32,128]{3,2,1,0:T(8,128)(2,1)}, bf16[2,32,32,128]{3,2,1,0:T(8,128)(2,1)S(1)}, u32[]{:S(2)}, u32[]{:S(2)}) %collective-permute-start.3) | collective-permute-done | bytes 524320 | tf_op jit(solution)/shard_map/ppermute | solution.py:130
  103.1 1.9 %collective-permute-start.4 = (bf16[2,32,32,128]{3,2,1,0:T(8,128)(2,1)}, bf16[2,32,32,128]{3,2,1,0:T(8,128)(2,1)}, u32[]{:S(2)}, u32[]{:S(2)}) collective-permute-start(bf16[2,32,32,128]{3,2,1,0:T(8,128)(2,1)} %select_convert_fusion.3), channel_id=1, source_target_pairs={{4,8},{8,12},{6,10},{10,14},{5,9},{9,13},{7,11},{11,15},{20,24},{2... | collective-permute-start | bytes 1572872 | tf_op jit(solution)/shard_map/ppermute | solution.py:130
  106.6 9.6 %all-to-all-start.1 = ((bf16[8,4,4096]{2,1,0:T(4,128)(2,1)}), bf16[8,4,4096]{2,1,0:T(4,128)(2,1)}, u32[]{:S(2)}, u32[]{:S(2)}) async-start(bf16[8,4,4096]{2,1,0:T(4,128)(2,1)} %concatenate.36), calls=%async_computation.1 | async-start | bytes 524288 | tf_op jit(solution)/shard_map/all_to_all | solution.py:114
  117.0 4.2 %collective-permute-done.4 = bf16[2,32,32,128]{3,2,1,0:T(8,128)(2,1)} collective-permute-done((bf16[2,32,32,128]{3,2,1,0:T(8,128)(2,1)}, bf16[2,32,32,128]{3,2,1,0:T(8,128)(2,1)}, u32[]{:S(2)}, u32[]{:S(2)}) %collective-permute-start.4) | collective-permute-done | bytes 524320 | tf_op jit(solution)/shard_map/ppermute | solution.py:130
  121.2 2.5 %select_convert_fusion.2 = bf16[2,32,32,128]{3,2,1,0:T(8,128)(2,1)} fusion(f32[2,2,32,32,128]{4,3,2,1,0:T(8,128)S(1)} %get-tuple-element.18, bf16[2,32,32,128]{3,2,1,0:T(8,128)(2,1)S(1)} %collective-permute-done.2, bf16[2,32,32,128]{3,2,1,0:T(8,128)(2,1)S(1)} %collective-permute-done.3, bf16[2,32,32,128]{3,2,1,0:T(8,128)(2,1)} %collective-permute-done.4, ...), kind=kLoop, calls=%fused_computation.87 | loop fusion | flops 4194304 | bytes 4194822 | tf_op jit(solution)/shard_map/convert_element_type | solution.py:130
  123.7 2.1 %collective-permute-start.5 = (bf16[2,32,32,128]{3,2,1,0:T(8,128)(2,1)}, bf16[2,32,32,128]{3,2,1,0:T(8,128)(2,1)}, u32[]{:S(2)}, u32[]{:S(2)}) collective-permute-start(bf16[2,32,32,128]{3,2,1,0:T(8,128)(2,1)} %select_convert_fusion.2), channel_id=1, source_target_pairs={{8,12},{10,14},{9,13},{11,15},{24,28},{26,30},{25,29},{27,31}} | collective-permute-start | bytes 1572872 | tf_op jit(solution)/shard_map/ppermute | solution.py:130
  125.8 5.6 %fusion.5 = f32[8,4,1024]{2,0,1:T(8,128)} fusion(bf16[4096,1024]{1,0:T(8,128)(2,1)} %param.25, bf16[8,4,4096]{2,1,0:T(4,128)(2,1)} %all-to-all-done.1), kind=kOutput, calls=%fused_computation.8 | convolution fusion | flops 268435456 | bytes 8781824 | tf_op jit(solution)/shard_map/jup,pd->jud/dot_general | solution.py:271
  132.0 2.0 %fusion.49 = (f32[1,2,32,32,128]{4,3,2,1,0:T(8,128)S(1)}, f32[1,2,32,32,128]{4,3,2,1,0:T(8,128)S(1)}) fusion(bf16[2,32,32,128]{3,2,1,0:T(8,128)(2,1)} %collective-permute-done.5, bf16[2,32,32,128]{3,2,1,0:T(8,128)(2,1)S(1)} %copy-done.11, bf16[2,32,32,128]{3,2,1,0:T(8,128)(2,1)S(1)} %copy-done.13, bf16[2,32,32,128]{3,2,1,0:T(8,128)(2,1)} %collective-permute-done.4, ...), kind=kLoop, calls=%fused_computation.80 | loop fusion | flops 3145728 | bytes 4194312 | tf_op jit(solution)/shard_map/stack | solution.py:133
  137.1 6.6 %fusion.22 = f32[1,2,32,256,64]{3,4,2,1,0:T(8,128)} fusion(bf16[256,2,32,64]{0,3,2,1:T(8,128)(2,1)S(1)} %bitcast.180, f32[2,32,256]{2,1,0:T(8,128)S(1)} %bitcast.194, f32[2,32,256]{2,1,0:T(8,128)S(1)} %copy-done.30, f32[2,256,256]{2,1,0:T(8,128)S(1)} %copy-done.19, pred[256,256]{1,0:T(8,128)(4,1)S(1)} %copy-done.29), kind=kOutput, calls=%fused_computation.41 | convolution fusion | flops 562036736 | bytes 7012352 | tf_op jit(solution)/shard_map/gkts,sgkp->gktp/dot_general | solution.py:35
  145.0 7.1 %copy.226 = f32[2,256,4096]{1,2,0:T(8,128)} copy(bf16[2,256,4096]{2,1,0:T(8,128)(2,1)} %param.13) | data formatting | bytes 12582912 | tf_op jit(solution)/shard_map/convert_element_type | solution.py:289
  154.7 5.9 %collective-permute-done.6 = bf16[2,2,32,32,128]{4,3,2,1,0:T(8,128)(2,1)} collective-permute-done((bf16[2,2,32,32,128]{4,3,2,1,0:T(8,128)(2,1)}, bf16[2,2,32,32,128]{4,3,2,1,0:T(8,128)(2,1)}, u32[]{:S(2)}, u32[]{:S(2)}) %collective-permute-start.6) | collective-permute-done | bytes 1048608 | tf_op jit(solution)/shard_map/ppermute | solution.py:76
  160.7 2.5 %convert_select_fusion.1 = (f32[2,2,32,32,128]{4,3,2,1,0:T(8,128)S(1)}, f32[2,2,32,32,128]{4,3,2,1,0:T(8,128)S(1)}) fusion(bf16[2,2,32,32,128]{4,3,2,1,0:T(8,128)(2,1)} %collective-permute-done.6, pred[]{:T(512)S(6)} %eq.51, f32[2,2,32,32,128]{4,3,2,1,0:T(8,128)S(1)} %copy-done.4, bf16[2,2,32,32,128]{4,3,2,1,0:T(8,128)(2,1)} %copy-done.6, ...), kind=kLoop, calls=%fused_computation.38 | loop fusion | flops 4718592 | bytes 10486273 | tf_op jit(solution)/shard_map/jit(_where)/select_n | solution.py:179
  170.1 6.0 %fusion.4 = bf16[2,256,2,32,64]{1,4,3,2,0:T(8,128)(2,1)} fusion(f32[1,2,32,256,64]{3,4,2,1,0:T(8,128)} %fusion.22, f32[1,2,32,256,64]{3,4,2,1,0:T(8,128)S(1)} %copy-done.14, f32[2,256,2,32,64]{1,4,3,2,0:T(8,128)S(1)} %bitcast.177, f32[2,2,256,32,64]{2,4,3,1,0:T(8,128)S(1)} %bitcast.174, f32[2,32]{1,0:T(2,128)S(1)} %copy-done.40, f32[2,2,256,32]{2,3,1,0:T(8,128)S(1)} %fusion.58), kind=kLoop, calls=%fused_computation.7 | loop fusion | flops 12582912 | bytes 29491456 | tf_op jit(solution)/shard_map/convert_element_type | solution.py:62
  176.1 6.3 %copy.244 = bf16[2,256,4096]{2,1,0:T(8,128)(2,1)} copy(bf16[2,256,4096]{1,2,0:T(8,128)(2,1)} %bitcast.178) | data formatting | bytes 8388608
  (204 shorter events, 58.4 us)
Async XLA Ops:
  0.6 30.2 %copy-start = (bf16[1,4,256]{2,1,0:T(4,128)(2,1)S(1)}, bf16[1,4,256]{2,1,0:T(4,128)(2,1)}, u32[]{:S(2)}) copy-start(bf16[1,4,256]{2,1,0:T(4,128)(2,1)} %param.21) | copy-start | bytes 6148
  0.6 10.2 %copy-start.23 = (bf16[2,256,256]{2,1,0:T(8,128)(2,1)S(1)}, bf16[2,256,256]{2,1,0:T(8,128)(2,1)}, u32[]{:S(2)}) copy-start(bf16[2,256,256]{2,1,0:T(8,128)(2,1)} %param.14) | copy-start | bytes 786436
  3.4 11.7 %copy-start.35 = (f32[64,2]{0,1:T(2,128)}, f32[64,2]{0,1:T(2,128)S(1)}, u32[]{:S(2)}) copy-start(f32[64,2]{0,1:T(2,128)S(1)} %slice.100) | copy-start | bytes 1540
  5.1 42.7 %collective-permute-start = (f32[2,2,32]{2,1,0:T(2,128)}, f32[2,2,32]{2,1,0:T(2,128)}, u32[]{:S(2)}, u32[]{:S(2)}) collective-permute-start(f32[2,2,32]{2,1,0:T(2,128)} %constant_dynamic-update-slice_fusion), channel_id=1, source_target_pairs={{0,2},{4,6},{8,10},{12,14},{2,0},{6,4},{10,8},{14,12},{1,3},{5,7},... | collective-permute-start | bytes 1544 | tf_op jit(solution)/shard_map/ppermute | solution.py:76
  9.4 36.0 %collective-permute-start.7 = (f32[1,1153]{1,0:T(1,128)}, f32[1,1153]{1,0:T(1,128)}, u32[]{:S(2)}, u32[]{:S(2)}) collective-permute-start(f32[1,1153]{1,0:T(1,128)} %broadcast_in_dim.73), channel_id=1, source_target_pairs={{0,2},{2,0},{4,6},{6,4},{8,10},{10,8},{12,14},{14,12},{1,3},{3,1},... | collective-permute-start | bytes 13844 | tf_op jit(solution)/shard_map/ppermute | solution.py:87
  11.0 10.6 %copy-start.18 = (bf16[1,256,256]{1,2,0:T(8,128)(2,1)}, bf16[1,256,256]{1,2,0:T(8,128)(2,1)S(1)}, u32[]{:S(2)}) copy-start(bf16[1,256,256]{1,2,0:T(8,128)(2,1)S(1)} %copy.271) | copy-start | bytes 393220
  11.2 13.0 %copy-start.16 = (bf16[1,256,256]{1,2,0:T(8,128)(2,1)}, bf16[1,256,256]{1,2,0:T(8,128)(2,1)S(1)}, u32[]{:S(2)}) copy-start(bf16[1,256,256]{1,2,0:T(8,128)(2,1)S(1)} %copy.272) | copy-start | bytes 393220
  24.1 33.8 %copy-start.2 = (f32[1,2,32,64,128]{4,3,2,1,0:T(8,128)}, f32[1,2,32,64,128]{4,3,2,1,0:T(8,128)S(1)}, u32[]{:S(2)}) copy-start(f32[1,2,32,64,128]{4,3,2,1,0:T(8,128)S(1)} %fusion.41) | copy-start | bytes 6291460
  24.9 5.9 %copy-start.38 = (bf16[1,4,256]{2,1,0:T(4,128)(2,1)S(1)}, bf16[1,4,256]{2,1,0:T(4,128)(2,1)}, u32[]{:S(2)}) copy-start(bf16[1,4,256]{2,1,0:T(4,128)(2,1)} %param.22) | copy-start | bytes 6148
  24.9 6.8 %copy-start.15 = (bf16[2,256,256]{2,1,0:T(8,128)(2,1)S(1)}, bf16[2,256,256]{2,1,0:T(8,128)(2,1)}, u32[]{:S(2)}) copy-start(bf16[2,256,256]{2,1,0:T(8,128)(2,1)} %param.15) | copy-start | bytes 786436
  26.5 45.8 %collective-permute-start.1 = (bf16[2,2,32,32,128]{4,3,2,1,0:T(8,128)(2,1)}, bf16[2,2,32,32,128]{4,3,2,1,0:T(8,128)(2,1)S(1)}, u32[]{:S(2)}, u32[]{:S(2)}) collective-permute-start(bf16[2,2,32,32,128]{4,3,2,1,0:T(8,128)(2,1)} %select_convert_fusion.1), channel_id=1, source_target_pairs={{0,2},{4,6},{8,10},{12,14},{2,0},{6,4},{10,8},{14,12},{1,3},{5,7},... | collective-permute-start | bytes 3145736 | tf_op jit(solution)/shard_map/ppermute | solution.py:76
  35.3 8.5 %copy-start.43 = (f32[1,4,64]{2,1,0:T(4,128)S(1)}, f32[1,4,64]{2,1,0:T(4,128)}, u32[]{:S(2)}) copy-start(f32[1,4,64]{2,1,0:T(4,128)} %param.23) | copy-start | bytes 3076
  46.1 3.7 %collective-permute-start.8 = (f32[2,1153]{1,0:T(2,128)S(1)}, f32[2,1153]{1,0:T(2,128)S(1)}, u32[]{:S(2)}, u32[]{:S(2)}) collective-permute-start(f32[2,1153]{1,0:T(2,128)S(1)} %maximum_select_fusion.2), channel_id=1, source_target_pairs={{0,4},{2,6},{4,0},{6,2},{8,12},{10,14},{12,8},{14,10},{1,5},{3,7},... | collective-permute-start | bytes 27680 | tf_op jit(solution)/shard_map/ppermute | solution.py:87
  49.9 4.8 %collective-permute-start.9 = (f32[4,1153]{1,0:T(4,128)S(1)}, f32[4,1153]{1,0:T(4,128)S(1)}, u32[]{:S(2)}, u32[]{:S(2)}) collective-permute-start(f32[4,1153]{1,0:T(4,128)S(1)} %maximum_select_fusion.1), channel_id=1, source_target_pairs={{0,8},{2,10},{4,12},{6,14},{8,0},{10,2},{12,4},{14,6},{1,9},{3,11}... | collective-permute-start | bytes 55352 | tf_op jit(solution)/shard_map/ppermute | solution.py:87
  67.0 18.8 %all-to-all-start = ((f32[8,1,16384]{2,1,0:T(1,128)}), f32[8,1,16384]{2,1,0:T(1,128)}, u32[]{:S(2)}, u32[]{:S(2)}) async-start(f32[8,1,16384]{2,1,0:T(1,128)} %reshape.360), calls=%async_computation | async-start | bytes 1048576 | tf_op jit(solution)/shard_map/all_to_all | solution.py:114
  76.9 5.3 %copy-start.34 = (f32[2,2,32]{2,1,0:T(2,128)S(1)}, f32[2,2,32]{2,1,0:T(2,128)}, u32[]{:S(2)}) copy-start(f32[2,2,32]{2,1,0:T(2,128)} %copy-done.33) | copy-start | bytes 1540
  78.0 4.2 %collective-permute-start.2 = (bf16[2,32,32,128]{3,2,1,0:T(8,128)(2,1)}, bf16[2,32,32,128]{3,2,1,0:T(8,128)(2,1)S(1)}, u32[]{:S(2)}, u32[]{:S(2)}) collective-permute-start(bf16[2,32,32,128]{3,2,1,0:T(8,128)(2,1)} %select_convert_fusion.4), channel_id=1, source_target_pairs={{0,4},{2,6},{1,5},{3,7},{16,20},{18,22},{17,21},{19,23}} | collective-permute-start | bytes 1572872 | tf_op jit(solution)/shard_map/ppermute | solution.py:130
  82.2 39.0 %copy-start.10 = (bf16[2,32,32,128]{3,2,1,0:T(8,128)(2,1)}, bf16[2,32,32,128]{3,2,1,0:T(8,128)(2,1)S(1)}, u32[]{:S(2)}) copy-start(bf16[2,32,32,128]{3,2,1,0:T(8,128)(2,1)S(1)} %collective-permute-done.2) | copy-start | bytes 1572868
  83.4 18.4 %collective-permute-start.3 = (bf16[2,32,32,128]{3,2,1,0:T(8,128)(2,1)}, bf16[2,32,32,128]{3,2,1,0:T(8,128)(2,1)S(1)}, u32[]{:S(2)}, u32[]{:S(2)}) collective-permute-start(bf16[2,32,32,128]{3,2,1,0:T(8,128)(2,1)} %fusion.47), channel_id=1, source_target_pairs={{0,4},{4,8},{2,6},{6,10},{1,5},{5,9},{3,7},{7,11},{16,20},{20,24},... | collective-permute-start | bytes 1572872 | tf_op jit(solution)/shard_map/ppermute | solution.py:130
  97.2 7.9 %copy-start.22 = (f32[1,4,4096]{2,1,0:T(4,128)S(1)}, f32[1,4,4096]{2,1,0:T(4,128)}, u32[]{:S(2)}) copy-start(f32[1,4,4096]{2,1,0:T(4,128)} %add.120) | copy-start | bytes 196612
  97.2 7.9 %copy-start.26 = (bf16[1,4,4096]{2,1,0:T(4,128)(2,1)S(1)}, bf16[1,4,4096]{2,1,0:T(4,128)(2,1)}, u32[]{:S(2)}) copy-start(bf16[1,4,4096]{2,1,0:T(4,128)(2,1)} %param.20) | copy-start | bytes 98308
  97.2 19.0 %copy-start.36 = (f32[64,2]{0,1:T(2,128)S(1)}, f32[64,2]{0,1:T(2,128)}, u32[]{:S(2)}) copy-start(f32[64,2]{0,1:T(2,128)} %copy-done.35) | copy-start | bytes 1540
  101.8 19.4 %copy-start.12 = (bf16[2,32,32,128]{3,2,1,0:T(8,128)(2,1)}, bf16[2,32,32,128]{3,2,1,0:T(8,128)(2,1)S(1)}, u32[]{:S(2)}) copy-start(bf16[2,32,32,128]{3,2,1,0:T(8,128)(2,1)S(1)} %collective-permute-done.3) | copy-start | bytes 1572868
  103.1 18.1 %collective-permute-start.4 = (bf16[2,32,32,128]{3,2,1,0:T(8,128)(2,1)}, bf16[2,32,32,128]{3,2,1,0:T(8,128)(2,1)}, u32[]{:S(2)}, u32[]{:S(2)}) collective-permute-start(bf16[2,32,32,128]{3,2,1,0:T(8,128)(2,1)} %select_convert_fusion.3), channel_id=1, source_target_pairs={{4,8},{8,12},{6,10},{10,14},{5,9},{9,13},{7,11},{11,15},{20,24},{2... | collective-permute-start | bytes 1572872 | tf_op jit(solution)/shard_map/ppermute | solution.py:130
  106.6 19.2 %all-to-all-start.1 = ((bf16[8,4,4096]{2,1,0:T(4,128)(2,1)}), bf16[8,4,4096]{2,1,0:T(4,128)(2,1)}, u32[]{:S(2)}, u32[]{:S(2)}) async-start(bf16[8,4,4096]{2,1,0:T(4,128)(2,1)} %concatenate.36), calls=%async_computation.1 | async-start | bytes 524288 | tf_op jit(solution)/shard_map/all_to_all | solution.py:114
  123.7 8.3 %collective-permute-start.5 = (bf16[2,32,32,128]{3,2,1,0:T(8,128)(2,1)}, bf16[2,32,32,128]{3,2,1,0:T(8,128)(2,1)}, u32[]{:S(2)}, u32[]{:S(2)}) collective-permute-start(bf16[2,32,32,128]{3,2,1,0:T(8,128)(2,1)} %select_convert_fusion.2), channel_id=1, source_target_pairs={{8,12},{10,14},{9,13},{11,15},{24,28},{26,30},{25,29},{27,31}} | collective-permute-start | bytes 1572872 | tf_op jit(solution)/shard_map/ppermute | solution.py:130
  125.8 6.2 %copy-start.11 = (bf16[2,32,32,128]{3,2,1,0:T(8,128)(2,1)S(1)}, bf16[2,32,32,128]{3,2,1,0:T(8,128)(2,1)}, u32[]{:S(2)}) copy-start(bf16[2,32,32,128]{3,2,1,0:T(8,128)(2,1)} %copy-done.10) | copy-start | bytes 1572868
  125.8 6.2 %copy-start.13 = (bf16[2,32,32,128]{3,2,1,0:T(8,128)(2,1)S(1)}, bf16[2,32,32,128]{3,2,1,0:T(8,128)(2,1)}, u32[]{:S(2)}) copy-start(bf16[2,32,32,128]{3,2,1,0:T(8,128)(2,1)} %copy-done.12) | copy-start | bytes 1572868
  131.5 21.6 %collective-permute-start.10 = (f32[8,4,1024]{2,0,1:T(8,128)}, f32[8,4,1024]{2,0,1:T(8,128)}, u32[]{:S(2)}, u32[]{:S(2)}) collective-permute-start(f32[8,4,1024]{2,0,1:T(8,128)} %fusion.5), channel_id=1, source_target_pairs={{0,1},{1,0},{2,3},{3,2},{4,5},{5,4},{6,7},{7,6},{8,9},{9,8},{10,11... | collective-permute-start | bytes 393224 | tf_op jit(solution)/shard_map/ppermute | solution.py:278
  135.6 25.1 %collective-permute-start.6 = (bf16[2,2,32,32,128]{4,3,2,1,0:T(8,128)(2,1)}, bf16[2,2,32,32,128]{4,3,2,1,0:T(8,128)(2,1)}, u32[]{:S(2)}, u32[]{:S(2)}) collective-permute-start(bf16[2,2,32,32,128]{4,3,2,1,0:T(8,128)(2,1)} %select_convert_fusion), channel_id=1, source_target_pairs={{0,2},{4,6},{8,10},{12,14},{2,0},{6,4},{10,8},{14,12},{1,3},{5,7},... | collective-permute-start | bytes 3145736 | tf_op jit(solution)/shard_map/ppermute | solution.py:76
  165.5 4.6 %copy-start.14 = (f32[1,2,32,256,64]{3,4,2,1,0:T(8,128)S(1)}, f32[1,2,32,256,64]{3,4,2,1,0:T(8,128)}, u32[]{:S(2)}) copy-start(f32[1,2,32,256,64]{3,4,2,1,0:T(8,128)} %fusion.23) | copy-start | bytes 12582916
  176.1 6.3 %copy-start.1 = (bf16[1,4,256]{2,1,0:T(4,128)(2,1)S(1)}, bf16[1,4,256]{2,1,0:T(4,128)(2,1)}, u32[]{:S(2)}) copy-start(bf16[1,4,256]{2,1,0:T(4,128)(2,1)} %param.21) | copy-start | bytes 6148
  (29 other events, 87.6 us)

commit v16 on v13

--- a/solution.py
+++ b/solution.py
@@ -53,8 +53,11 @@
     low = (flat - high.astype(jnp.float32)).astype(jnp.bfloat16)
     numbers = (((3,), (3,)), ((0, 2), (0, 1)))
     carried = lax.dot_general(
-        c_groups, high, numbers, preferred_element_type=jnp.float32
-    ) + lax.dot_general(c_groups, low, numbers, preferred_element_type=jnp.float32)
+        jnp.concatenate([c_groups, c_groups], axis=-1),
+        jnp.concatenate([high, low], axis=-1),
+        numbers,
+        preferred_element_type=jnp.float32,
+    )
     carried = carried.reshape(request_count, group_count, block_size, per_group, HEAD_DIM)
     growth = jnp.exp(cumulative).reshape(request_count, group_count, per_group, block_size)
     carried = carried * growth.transpose(0, 1, 3, 2)[..., None]

time: 184 us -> 182 us (0.989)
    unnamed x106 -> x107, local copies, waits for them, and re-layouts: 17.1 us -> 16.2 us
  transfers between devices with their start and end apart: 13 -> 13, of which waited for: 6 -> 6; matrix products, arithmetic and copies ran while one was open for 58% -> 57% of each run, Pallas kernels for 0% -> 0%
where the time goes in v16:
time: 182 us; the launch traced here: 180 us
  local copies, waits for them, and re-layouts  51.4 us (28%)
  other arithmetic  46.9 us (26%)
  matrix products  31.2 us (17%)
  starting transfers between devices  28.8 us (16%)
  waiting for transfers between devices  19.8 us (11%)
  between operations  1.98 us (1%)
    unnamed x107, local copies, waits for them, and re-layouts  16.2 us
    all_to_all x2, starting transfers between devices, exchange_ctx(): got = lax.all_to_all(value, 'ctx', 0, 0, tiled=True)  15.7 us
    dot_general x2, matrix products, block_terms(): jnp.einsum('gkts,sgkp->gktp', mixing, inputs_head, preferred_element_type...  14.5 us
    slice x3, local copies, waits for them, and re-layouts, shards(): ssm_input[request]  10.5 us
    ppermute x4, waiting for transfers between devices, chain_columns(): lax.ppermute(outgoing.astype(jnp.bfloat16), 'ctx', pairs)  8.72 us
    convert_element_type x1, local copies, waits for them, and re-layouts, finish(): inputs_head = ssm_input.reshape(request_count, block_size, group_count, p...  7.16 us
    ppermute x3, waiting for transfers between devices, send(): lax.ppermute((value.astype(jnp.bfloat16), total), 'ctx', pairs)  6.55 us
    ppermute x4, starting transfers between devices, chain_columns(): lax.ppermute(outgoing.astype(jnp.bfloat16), 'ctx', pairs)  6.14 us
  transfers between devices with their start and end apart: 13, of which 6 were waited for; matrix products, arithmetic and copies ran while one was open for 57% of the time, Pallas kernels for 0%

profile of v16, /device:TPU:18, one launch (start us, length us, event | category | flops | bytes accessed | tf_op | source)
XLA Modules:
  0.0 180.1 jit_solution(14278713777187933449)
XLA Ops:
  5.1 1.5 collective-permute-start
  11.2 4.0 %fusion.73 = (bf16[1,256,4096]{2,1,0:T(8,128)(2,1)}, bf16[1,256,4096]{2,1,0:T(8,128)(2,1)S(1)}) fusion(bf16[2,256,4096]{2,1,0:T(8,128)(2,1)} %param.13), kind=kLoop, calls=%fused_computation.146 | loop fusion | bytes 8388608 | tf_op jit(solution)/shard_map/slice | solution.py:213
  15.2 4.1 %copy.220 = bf16[1,256,4096]{1,2,0:T(8,128)(2,1)} copy(bf16[1,256,4096]{2,1,0:T(8,128)(2,1)} %get-tuple-element.24) | data formatting | bytes 4194304 | tf_op jit(solution)/shard_map/slice | solution.py:213
  19.3 2.4 %copy.223 = bf16[1,256,4096]{1,2,0:T(8,128)(2,1)} copy(bf16[1,256,4096]{2,1,0:T(8,128)(2,1)S(1)} %get-tuple-element.25) | data formatting | bytes 4194304 | tf_op jit(solution)/shard_map/slice | solution.py:213
  21.7 2.5 %fusion.45 = f32[1,2,32,64,128]{4,3,2,1,0:T(8,128)S(1)} fusion(bf16[256,2,128,1]{0,2,3,1:T(8,128)(2,1)S(1)} %bitcast.172, bf16[256,2,32,64]{0,3,2,1:T(8,128)(2,1)} %bitcast.166, f32[256,2,32]{0,2,1:T(8,128)S(1)} %bitcast.177), kind=kOutput, calls=%fused_computation.66 | convolution fusion | flops 271581184 | bytes 4390912 | tf_op jit(solution)/shard_map/sgkp,sgn->gkpn/dot_general | solution.py:42
  26.6 1.5 collective-permute-start.1
  33.8 7.9 %fusion.27 = f32[1,2,32,256,64]{3,4,2,1,0:T(8,128)} fusion(bf16[256,2,32,64]{0,3,2,1:T(8,128)(2,1)} %bitcast.167, f32[2,32,256]{2,1,0:T(8,128)} %bitcast.181, f32[2,32,256]{2,1,0:T(8,128)} %reduce_window_sum.88, f32[2,256,256]{2,1,0:T(8,128)S(1)} %fusion.78, pred[256,256]{1,0:T(8,128)(4,1)} %iota_compare_fusion), kind=kOutput, calls=%fused_computation.45 | convolution fusion | flops 562036736 | bytes 7012352 | tf_op jit(solution)/shard_map/gkts,sgkp->gktp/dot_general | solution.py:35
  44.6 1.6 collective-permute-start.8
  49.4 3.8 %collective-permute-done.9 = f32[4,1153]{1,0:T(4,128)S(1)} collective-permute-done((f32[4,1153]{1,0:T(4,128)S(1)}, f32[4,1153]{1,0:T(4,128)S(1)}, u32[]{:S(2)}, u32[]{:S(2)}) %collective-permute-start.9) | collective-permute-done | bytes 18480 | tf_op jit(solution)/shard_map/ppermute | solution.py:94
  56.5 2.3 %fusion.28 = (bf16[2,2,32,64,128,1]{4,3,2,1,0,5:T(8,128)(2,1)S(1)}, bf16[2,2,32,64,128,1]{4,3,2,1,0,5:T(8,128)(2,1)S(1)}) fusion(f32[1,2,32,64,128]{4,3,2,1,0:T(8,128)} %copy-done.3, f32[1,2,32,64,128]{4,3,2,1,0:T(8,128)S(1)} %fusion.45, f32[2,2,32]{2,1,0:T(2,128)} %exp.65), kind=kLoop, calls=%fused_computation.46 | loop fusion | flops 6291456 | bytes 8389120 | tf_op jit(solution)/shard_map/convert_element_type | solution.py:243
  59.6 2.0 %fusion.34 = f32[2,8,4,2,32,64]{5,1,4,3,2,0:T(8,128)S(1)} fusion(bf16[2,2,32,64,128,1]{4,3,2,1,0,5:T(8,128)(2,1)S(1)} %get-tuple-element.23, bf16[8,4,2,128,1,1]{3,0,2,1,5,4:T(8,128)(2,1)S(1)} %bitcast.178), kind=kOutput, calls=%fused_computation.53 | convolution fusion | flops 67108864 | bytes 3162112 | tf_op jit(solution)/shard_map/rgkpn,jugn->rjugkp/dot_general | solution.py:248
  61.6 2.1 %add_bitcast_fusion = f32[2,8,4,2,32,64]{5,1,4,0,2,3:T(8,128)S(1)} fusion(f32[2,8,4,2,32,64]{5,1,4,3,2,0:T(8,128)S(1)} %fusion.34, bf16[2,2,32,64,128,1]{4,3,2,1,0,5:T(8,128)(2,1)S(1)} %get-tuple-element.22, bf16[8,4,2,128,1,1]{3,0,2,1,5,4:T(8,128)(2,1)S(1)} %bitcast.179), kind=kOutput, calls=%fused_computation.57 | convolution fusion | flops 67371008 | bytes 4210688 | tf_op jit(solution)/shard_map/rgkpn,jugn->rjugkp/dot_general | solution.py:246
  65.6 5.3 %all-to-all-start = ((f32[8,1,16384]{2,1,0:T(1,128)}), f32[8,1,16384]{2,1,0:T(1,128)}, u32[]{:S(2)}, u32[]{:S(2)}) async-start(f32[8,1,16384]{2,1,0:T(1,128)} %reshape.359), calls=%async_computation | async-start | bytes 1048576 | tf_op jit(solution)/shard_map/all_to_all | solution.py:121
  70.9 4.4 %fusion.29 = (f32[2,2,32,32,128]{4,3,2,1,0:T(8,128)S(1)}, f32[2,2,32,32,128]{4,3,2,1,0:T(8,128)}) fusion(bf16[2,2,32,32,128]{4,3,2,1,0:T(8,128)(2,1)S(1)} %collective-permute-done.1, f32[2,2,32]{2,1,0:T(2,128)} %get-tuple-element.39, pred[]{:T(512)S(6)} %eq.51, f32[1,2,32,64,128]{4,3,2,1,0:T(8,128)} %copy-done.3, f32[1,2,32,64,128]{4,3,2,1,0:T(8,128)} %copy-done.2), kind=kLoop, calls=%fused_computation.47 | loop fusion | flops 4194304 | bytes 9437697 | tf_op jit(solution)/shard_map/add | solution.py:162
  83.3 1.6 multiply_reduce_fusion
  85.4 3.8 %reduce.16 = f32[8,16384]{1,0:T(8,128)} reduce(f32[8,1,16384]{2,1,0:T(1,128)} %all-to-all-done, f32[]{:T(128)} %broadcast.183), dimensions={1}, to_apply=%all_to_all.6.reduce_sub_computation | reduce | bytes 1048580 | tf_op jit(solution)/shard_map/all_to_all | solution.py:121
  89.2 2.4 %reshape.360 = f32[8,2,4,32,64]{4,3,2,1,0:T(8,128)} reshape(f32[8,16384]{1,0:T(8,128)} %reduce.16) | data formatting | bytes 1048576
  94.6 1.6 add.112
  96.3 4.0 %collective-permute-done.3 = bf16[2,32,32,128]{3,2,1,0:T(8,128)(2,1)S(1)} collective-permute-done((bf16[2,32,32,128]{3,2,1,0:T(8,128)(2,1)}, bf16[2,32,32,128]{3,2,1,0:T(8,128)(2,1)S(1)}, u32[]{:S(2)}, u32[]{:S(2)}) %collective-permute-start.3) | collective-permute-done | bytes 524320 | tf_op jit(solution)/shard_map/ppermute | solution.py:137
  101.6 1.9 %collective-permute-start.4 = (bf16[2,32,32,128]{3,2,1,0:T(8,128)(2,1)}, bf16[2,32,32,128]{3,2,1,0:T(8,128)(2,1)}, u32[]{:S(2)}, u32[]{:S(2)}) collective-permute-start(bf16[2,32,32,128]{3,2,1,0:T(8,128)(2,1)} %select_convert_fusion.3), channel_id=1, source_target_pairs={{4,8},{8,12},{6,10},{10,14},{5,9},{9,13},{7,11},{11,15},{20,24},{2... | collective-permute-start | bytes 1572872 | tf_op jit(solution)/shard_map/ppermute | solution.py:137
  105.1 10.3 %all-to-all-start.1 = ((bf16[8,4,4096]{2,1,0:T(4,128)(2,1)}), bf16[8,4,4096]{2,1,0:T(4,128)(2,1)}, u32[]{:S(2)}, u32[]{:S(2)}) async-start(bf16[8,4,4096]{2,1,0:T(4,128)(2,1)} %concatenate.44), calls=%async_computation.1 | async-start | bytes 524288 | tf_op jit(solution)/shard_map/all_to_all | solution.py:121
  116.2 4.2 %collective-permute-done.4 = bf16[2,32,32,128]{3,2,1,0:T(8,128)(2,1)} collective-permute-done((bf16[2,32,32,128]{3,2,1,0:T(8,128)(2,1)}, bf16[2,32,32,128]{3,2,1,0:T(8,128)(2,1)}, u32[]{:S(2)}, u32[]{:S(2)}) %collective-permute-start.4) | collective-permute-done | bytes 524320 | tf_op jit(solution)/shard_map/ppermute | solution.py:137
  120.4 2.5 %select_convert_fusion.2 = bf16[2,32,32,128]{3,2,1,0:T(8,128)(2,1)} fusion(f32[2,2,32,32,128]{4,3,2,1,0:T(8,128)S(1)} %get-tuple-element.18, bf16[2,32,32,128]{3,2,1,0:T(8,128)(2,1)S(1)} %collective-permute-done.2, bf16[2,32,32,128]{3,2,1,0:T(8,128)(2,1)S(1)} %collective-permute-done.3, bf16[2,32,32,128]{3,2,1,0:T(8,128)(2,1)} %collective-permute-done.4, ...), kind=kLoop, calls=%fused_computation.90 | loop fusion | flops 4194304 | bytes 4194822 | tf_op jit(solution)/shard_map/convert_element_type | solution.py:137
  122.9 2.1 %collective-permute-start.5 = (bf16[2,32,32,128]{3,2,1,0:T(8,128)(2,1)}, bf16[2,32,32,128]{3,2,1,0:T(8,128)(2,1)}, u32[]{:S(2)}, u32[]{:S(2)}) collective-permute-start(bf16[2,32,32,128]{3,2,1,0:T(8,128)(2,1)} %select_convert_fusion.2), channel_id=1, source_target_pairs={{8,12},{10,14},{9,13},{11,15},{24,28},{26,30},{25,29},{27,31}} | collective-permute-start | bytes 1572872 | tf_op jit(solution)/shard_map/ppermute | solution.py:137
  125.0 5.7 %fusion.5 = f32[8,4,1024]{2,0,1:T(8,128)} fusion(bf16[4096,1024]{1,0:T(8,128)(2,1)} %param.25, bf16[8,4,4096]{2,1,0:T(4,128)(2,1)} %all-to-all-done.1), kind=kOutput, calls=%fused_computation.8 | convolution fusion | flops 268435456 | bytes 8781824 | tf_op jit(solution)/shard_map/jup,pd->jud/dot_general | solution.py:278
  131.2 2.0 %fusion.53 = (f32[1,2,32,32,128]{4,3,2,1,0:T(8,128)S(1)}, f32[1,2,32,32,128]{4,3,2,1,0:T(8,128)S(1)}) fusion(bf16[2,32,32,128]{3,2,1,0:T(8,128)(2,1)} %collective-permute-done.5, bf16[2,32,32,128]{3,2,1,0:T(8,128)(2,1)S(1)} %copy-done.11, bf16[2,32,32,128]{3,2,1,0:T(8,128)(2,1)S(1)} %copy-done.13, bf16[2,32,32,128]{3,2,1,0:T(8,128)(2,1)} %collective-permute-done.4, ...), kind=kLoop, calls=%fused_computation.83 | loop fusion | flops 3145728 | bytes 4194312 | tf_op jit(solution)/shard_map/stack | solution.py:140
  136.3 6.6 %fusion.26 = f32[1,2,32,256,64]{3,4,2,1,0:T(8,128)} fusion(bf16[256,2,32,64]{0,3,2,1:T(8,128)(2,1)S(1)} %bitcast.165, f32[2,32,256]{2,1,0:T(8,128)S(1)} %bitcast.180, f32[2,32,256]{2,1,0:T(8,128)S(1)} %copy-done.31, f32[2,256,256]{2,1,0:T(8,128)S(1)} %copy-done.20, pred[256,256]{1,0:T(8,128)(4,1)S(1)} %copy-done.30), kind=kOutput, calls=%fused_computation.44 | convolution fusion | flops 562036736 | bytes 7012352 | tf_op jit(solution)/shard_map/gkts,sgkp->gktp/dot_general | solution.py:35
  143.6 7.2 %copy.237 = f32[2,256,4096]{1,2,0:T(8,128)} copy(bf16[2,256,4096]{2,1,0:T(8,128)(2,1)} %param.13) | data formatting | bytes 12582912 | tf_op jit(solution)/shard_map/convert_element_type | solution.py:66
  153.4 6.5 %collective-permute-done.6 = bf16[2,2,32,32,128]{4,3,2,1,0:T(8,128)(2,1)} collective-permute-done((bf16[2,2,32,32,128]{4,3,2,1,0:T(8,128)(2,1)}, bf16[2,2,32,32,128]{4,3,2,1,0:T(8,128)(2,1)}, u32[]{:S(2)}, u32[]{:S(2)}) %collective-permute-start.6) | collective-permute-done | bytes 1048608 | tf_op jit(solution)/shard_map/ppermute | solution.py:83
  159.9 2.5 %convert_select_fusion.1 = (f32[2,2,32,32,128]{4,3,2,1,0:T(8,128)S(1)}, f32[2,2,32,32,128]{4,3,2,1,0:T(8,128)S(1)}) fusion(bf16[2,2,32,32,128]{4,3,2,1,0:T(8,128)(2,1)} %collective-permute-done.6, pred[]{:T(512)S(6)} %eq.51, f32[2,2,32,32,128]{4,3,2,1,0:T(8,128)S(1)} %copy-done.4, bf16[2,2,32,32,128]{4,3,2,1,0:T(8,128)(2,1)} %copy-done.6, ...), kind=kLoop, calls=%fused_computation.41 | loop fusion | flops 4718592 | bytes 10486273 | tf_op jit(solution)/shard_map/jit(_where)/select_n | solution.py:186
  167.8 6.0 %fusion.4 = bf16[2,256,2,32,64]{1,4,3,2,0:T(8,128)(2,1)} fusion(f32[1,2,32,256,64]{3,4,2,1,0:T(8,128)} %fusion.26, f32[1,2,32,256,64]{3,4,2,1,0:T(8,128)S(1)} %copy-done.14, f32[2,256,2,32,64]{1,4,3,2,0:T(8,128)S(1)} %bitcast.161, f32[2,2,256,32,64]{2,4,3,1,0:T(8,128)S(1)} %bitcast.162, f32[2,32]{1,0:T(2,128)S(1)} %copy-done.41, f32[2,2,256,32]{2,3,1,0:T(8,128)S(1)} %fusion.60), kind=kLoop, calls=%fused_computation.7 | loop fusion | flops 12582912 | bytes 29491456 | tf_op jit(solution)/shard_map/convert_element_type | solution.py:69
  173.8 6.3 %copy.255 = bf16[2,256,4096]{2,1,0:T(8,128)(2,1)} copy(bf16[2,256,4096]{1,2,0:T(8,128)(2,1)} %bitcast.163) | data formatting | bytes 8388608
  (205 shorter events, 55.5 us)
Async XLA Ops:
  0.6 29.3 %copy-start = (bf16[1,4,256]{2,1,0:T(4,128)(2,1)S(1)}, bf16[1,4,256]{2,1,0:T(4,128)(2,1)}, u32[]{:S(2)}) copy-start(bf16[1,4,256]{2,1,0:T(4,128)(2,1)} %param.21) | copy-start | bytes 6148
  0.6 10.3 %copy-start.24 = (bf16[2,256,256]{2,1,0:T(8,128)(2,1)S(1)}, bf16[2,256,256]{2,1,0:T(8,128)(2,1)}, u32[]{:S(2)}) copy-start(bf16[2,256,256]{2,1,0:T(8,128)(2,1)} %param.14) | copy-start | bytes 786436
  3.4 11.7 %copy-start.36 = (f32[64,2]{0,1:T(2,128)}, f32[64,2]{0,1:T(2,128)S(1)}, u32[]{:S(2)}) copy-start(f32[64,2]{0,1:T(2,128)S(1)} %slice.100) | copy-start | bytes 1540
  5.1 41.2 %collective-permute-start = (f32[2,2,32]{2,1,0:T(2,128)}, f32[2,2,32]{2,1,0:T(2,128)}, u32[]{:S(2)}, u32[]{:S(2)}) collective-permute-start(f32[2,2,32]{2,1,0:T(2,128)} %constant_dynamic-update-slice_fusion), channel_id=1, source_target_pairs={{0,2},{4,6},{8,10},{12,14},{2,0},{6,4},{10,8},{14,12},{1,3},{5,7},... | collective-permute-start | bytes 1544 | tf_op jit(solution)/shard_map/ppermute | solution.py:83
  9.4 34.4 %collective-permute-start.7 = (f32[1,1153]{1,0:T(1,128)}, f32[1,1153]{1,0:T(1,128)}, u32[]{:S(2)}, u32[]{:S(2)}) collective-permute-start(f32[1,1153]{1,0:T(1,128)} %broadcast_in_dim.73), channel_id=1, source_target_pairs={{0,2},{2,0},{4,6},{6,4},{8,10},{10,8},{12,14},{14,12},{1,3},{3,1},... | collective-permute-start | bytes 13844 | tf_op jit(solution)/shard_map/ppermute | solution.py:94
  11.1 10.6 %copy-start.17 = (bf16[1,256,256]{1,2,0:T(8,128)(2,1)}, bf16[1,256,256]{1,2,0:T(8,128)(2,1)S(1)}, u32[]{:S(2)}) copy-start(bf16[1,256,256]{1,2,0:T(8,128)(2,1)S(1)} %copy.283) | copy-start | bytes 393220
  11.2 13.0 %copy-start.15 = (bf16[1,256,256]{1,2,0:T(8,128)(2,1)}, bf16[1,256,256]{1,2,0:T(8,128)(2,1)S(1)}, u32[]{:S(2)}) copy-start(bf16[1,256,256]{1,2,0:T(8,128)(2,1)S(1)} %copy.284) | copy-start | bytes 393220
  24.2 32.3 %copy-start.2 = (f32[1,2,32,64,128]{4,3,2,1,0:T(8,128)}, f32[1,2,32,64,128]{4,3,2,1,0:T(8,128)S(1)}, u32[]{:S(2)}) copy-start(f32[1,2,32,64,128]{4,3,2,1,0:T(8,128)S(1)} %fusion.45) | copy-start | bytes 6291460
  24.9 5.0 %copy-start.39 = (bf16[1,4,256]{2,1,0:T(4,128)(2,1)S(1)}, bf16[1,4,256]{2,1,0:T(4,128)(2,1)}, u32[]{:S(2)}) copy-start(bf16[1,4,256]{2,1,0:T(4,128)(2,1)} %param.22) | copy-start | bytes 6148
  26.6 44.3 %collective-permute-start.1 = (bf16[2,2,32,32,128]{4,3,2,1,0:T(8,128)(2,1)}, bf16[2,2,32,32,128]{4,3,2,1,0:T(8,128)(2,1)S(1)}, u32[]{:S(2)}, u32[]{:S(2)}) collective-permute-start(bf16[2,2,32,32,128]{4,3,2,1,0:T(8,128)(2,1)} %select_convert_fusion.1), channel_id=1, source_target_pairs={{0,2},{4,6},{8,10},{12,14},{2,0},{6,4},{10,8},{14,12},{1,3},{5,7},... | collective-permute-start | bytes 3145736 | tf_op jit(solution)/shard_map/ppermute | solution.py:83
  33.8 8.6 %copy-start.44 = (f32[1,4,64]{2,1,0:T(4,128)S(1)}, f32[1,4,64]{2,1,0:T(4,128)}, u32[]{:S(2)}) copy-start(f32[1,4,64]{2,1,0:T(4,128)} %param.23) | copy-start | bytes 3076
  44.6 3.7 %collective-permute-start.8 = (f32[2,1153]{1,0:T(2,128)S(1)}, f32[2,1153]{1,0:T(2,128)S(1)}, u32[]{:S(2)}, u32[]{:S(2)}) collective-permute-start(f32[2,1153]{1,0:T(2,128)S(1)} %maximum_select_fusion.2), channel_id=1, source_target_pairs={{0,4},{2,6},{4,0},{6,2},{8,12},{10,14},{12,8},{14,10},{1,5},{3,7},... | collective-permute-start | bytes 27680 | tf_op jit(solution)/shard_map/ppermute | solution.py:94
  48.4 4.8 %collective-permute-start.9 = (f32[4,1153]{1,0:T(4,128)S(1)}, f32[4,1153]{1,0:T(4,128)S(1)}, u32[]{:S(2)}, u32[]{:S(2)}) collective-permute-start(f32[4,1153]{1,0:T(4,128)S(1)} %maximum_select_fusion.1), channel_id=1, source_target_pairs={{0,8},{2,10},{4,12},{6,14},{8,0},{10,2},{12,4},{14,6},{1,9},{3,11}... | collective-permute-start | bytes 55352 | tf_op jit(solution)/shard_map/ppermute | solution.py:94
  65.6 19.3 %all-to-all-start = ((f32[8,1,16384]{2,1,0:T(1,128)}), f32[8,1,16384]{2,1,0:T(1,128)}, u32[]{:S(2)}, u32[]{:S(2)}) async-start(f32[8,1,16384]{2,1,0:T(1,128)} %reshape.359), calls=%async_computation | async-start | bytes 1048576 | tf_op jit(solution)/shard_map/all_to_all | solution.py:121
  70.9 4.5 %copy-start.42 = (f32[2,32]{1,0:T(2,128)S(1)}, f32[2,32]{1,0:T(2,128)}, u32[]{:S(2)}) copy-start(f32[2,32]{1,0:T(2,128)} %get-tuple-element.43) | copy-start | bytes 772
  75.4 5.2 %copy-start.35 = (f32[2,2,32]{2,1,0:T(2,128)S(1)}, f32[2,2,32]{2,1,0:T(2,128)}, u32[]{:S(2)}) copy-start(f32[2,2,32]{2,1,0:T(2,128)} %copy-done.34) | copy-start | bytes 1540
  76.5 4.1 %collective-permute-start.2 = (bf16[2,32,32,128]{3,2,1,0:T(8,128)(2,1)}, bf16[2,32,32,128]{3,2,1,0:T(8,128)(2,1)S(1)}, u32[]{:S(2)}, u32[]{:S(2)}) collective-permute-start(bf16[2,32,32,128]{3,2,1,0:T(8,128)(2,1)} %select_convert_fusion.4), channel_id=1, source_target_pairs={{0,4},{2,6},{1,5},{3,7},{16,20},{18,22},{17,21},{19,23}} | collective-permute-start | bytes 1572872 | tf_op jit(solution)/shard_map/ppermute | solution.py:137
  80.6 39.8 %copy-start.10 = (bf16[2,32,32,128]{3,2,1,0:T(8,128)(2,1)}, bf16[2,32,32,128]{3,2,1,0:T(8,128)(2,1)S(1)}, u32[]{:S(2)}) copy-start(bf16[2,32,32,128]{3,2,1,0:T(8,128)(2,1)S(1)} %collective-permute-done.2) | copy-start | bytes 1572868
  81.8 18.5 %collective-permute-start.3 = (bf16[2,32,32,128]{3,2,1,0:T(8,128)(2,1)}, bf16[2,32,32,128]{3,2,1,0:T(8,128)(2,1)S(1)}, u32[]{:S(2)}, u32[]{:S(2)}) collective-permute-start(bf16[2,32,32,128]{3,2,1,0:T(8,128)(2,1)} %fusion.51), channel_id=1, source_target_pairs={{0,4},{4,8},{2,6},{6,10},{1,5},{5,9},{3,7},{7,11},{16,20},{20,24},... | collective-permute-start | bytes 1572872 | tf_op jit(solution)/shard_map/ppermute | solution.py:137
  96.3 7.3 %copy-start.23 = (f32[1,4,4096]{2,1,0:T(4,128)S(1)}, f32[1,4,4096]{2,1,0:T(4,128)}, u32[]{:S(2)}) copy-start(f32[1,4,4096]{2,1,0:T(4,128)} %add.112) | copy-start | bytes 196612
  96.3 7.3 %copy-start.28 = (bf16[1,4,4096]{2,1,0:T(4,128)(2,1)S(1)}, bf16[1,4,4096]{2,1,0:T(4,128)(2,1)}, u32[]{:S(2)}) copy-start(bf16[1,4,4096]{2,1,0:T(4,128)(2,1)} %param.20) | copy-start | bytes 98308
  96.3 19.1 %copy-start.37 = (f32[64,2]{0,1:T(2,128)S(1)}, f32[64,2]{0,1:T(2,128)}, u32[]{:S(2)}) copy-start(f32[64,2]{0,1:T(2,128)} %copy-done.36) | copy-start | bytes 1540
  100.3 20.1 %copy-start.12 = (bf16[2,32,32,128]{3,2,1,0:T(8,128)(2,1)}, bf16[2,32,32,128]{3,2,1,0:T(8,128)(2,1)S(1)}, u32[]{:S(2)}) copy-start(bf16[2,32,32,128]{3,2,1,0:T(8,128)(2,1)S(1)} %collective-permute-done.3) | copy-start | bytes 1572868
  101.6 18.8 %collective-permute-start.4 = (bf16[2,32,32,128]{3,2,1,0:T(8,128)(2,1)}, bf16[2,32,32,128]{3,2,1,0:T(8,128)(2,1)}, u32[]{:S(2)}, u32[]{:S(2)}) collective-permute-start(bf16[2,32,32,128]{3,2,1,0:T(8,128)(2,1)} %select_convert_fusion.3), channel_id=1, source_target_pairs={{4,8},{8,12},{6,10},{10,14},{5,9},{9,13},{7,11},{11,15},{20,24},{2... | collective-permute-start | bytes 1572872 | tf_op jit(solution)/shard_map/ppermute | solution.py:137
  105.1 19.9 %all-to-all-start.1 = ((bf16[8,4,4096]{2,1,0:T(4,128)(2,1)}), bf16[8,4,4096]{2,1,0:T(4,128)(2,1)}, u32[]{:S(2)}, u32[]{:S(2)}) async-start(bf16[8,4,4096]{2,1,0:T(4,128)(2,1)} %concatenate.44), calls=%async_computation.1 | async-start | bytes 524288 | tf_op jit(solution)/shard_map/all_to_all | solution.py:121
  122.9 8.3 %collective-permute-start.5 = (bf16[2,32,32,128]{3,2,1,0:T(8,128)(2,1)}, bf16[2,32,32,128]{3,2,1,0:T(8,128)(2,1)}, u32[]{:S(2)}, u32[]{:S(2)}) collective-permute-start(bf16[2,32,32,128]{3,2,1,0:T(8,128)(2,1)} %select_convert_fusion.2), channel_id=1, source_target_pairs={{8,12},{10,14},{9,13},{11,15},{24,28},{26,30},{25,29},{27,31}} | collective-permute-start | bytes 1572872 | tf_op jit(solution)/shard_map/ppermute | solution.py:137
  125.0 6.2 %copy-start.11 = (bf16[2,32,32,128]{3,2,1,0:T(8,128)(2,1)S(1)}, bf16[2,32,32,128]{3,2,1,0:T(8,128)(2,1)}, u32[]{:S(2)}) copy-start(bf16[2,32,32,128]{3,2,1,0:T(8,128)(2,1)} %copy-done.10) | copy-start | bytes 1572868
  125.0 6.2 %copy-start.13 = (bf16[2,32,32,128]{3,2,1,0:T(8,128)(2,1)S(1)}, bf16[2,32,32,128]{3,2,1,0:T(8,128)(2,1)}, u32[]{:S(2)}) copy-start(bf16[2,32,32,128]{3,2,1,0:T(8,128)(2,1)} %copy-done.12) | copy-start | bytes 1572868
  130.7 21.0 %collective-permute-start.10 = (f32[8,4,1024]{2,0,1:T(8,128)}, f32[8,4,1024]{2,0,1:T(8,128)}, u32[]{:S(2)}, u32[]{:S(2)}) collective-permute-start(f32[8,4,1024]{2,0,1:T(8,128)} %fusion.5), channel_id=1, source_target_pairs={{0,1},{1,0},{2,3},{3,2},{4,5},{5,4},{6,7},{7,6},{8,9},{9,8},{10,11... | collective-permute-start | bytes 393224 | tf_op jit(solution)/shard_map/ppermute | solution.py:285
  134.8 25.1 %collective-permute-start.6 = (bf16[2,2,32,32,128]{4,3,2,1,0:T(8,128)(2,1)}, bf16[2,2,32,32,128]{4,3,2,1,0:T(8,128)(2,1)}, u32[]{:S(2)}, u32[]{:S(2)}) collective-permute-start(bf16[2,2,32,32,128]{4,3,2,1,0:T(8,128)(2,1)} %select_convert_fusion), channel_id=1, source_target_pairs={{0,2},{4,6},{8,10},{12,14},{2,0},{6,4},{10,8},{14,12},{1,3},{5,7},... | collective-permute-start | bytes 3145736 | tf_op jit(solution)/shard_map/ppermute | solution.py:83
  143.6 8.0 %copy-start.25 = (f32[1,2,32,256]{3,2,1,0:T(8,128)S(1)}, f32[1,2,32,256]{3,2,1,0:T(8,128)}, u32[]{:S(2)}) copy-start(f32[1,2,32,256]{3,2,1,0:T(8,128)} %reduce_window_sum.86) | copy-start | bytes 196612
  173.8 6.3 %copy-start.1 = (bf16[1,4,256]{2,1,0:T(4,128)(2,1)S(1)}, bf16[1,4,256]{2,1,0:T(4,128)(2,1)}, u32[]{:S(2)}) copy-start(bf16[1,4,256]{2,1,0:T(4,128)(2,1)} %param.21) | copy-start | bytes 6148
  (30 other events, 87.2 us)

commit v17 on v16

--- a/solution.py
+++ b/solution.py
@@ -244,8 +244,11 @@
     low = (weighted_states - high.astype(jnp.float32)).astype(jnp.bfloat16)
     c_rows = all_c.astype(jnp.bfloat16)
     projected = jnp.einsum(
-        "rgkpn,jugn->rjugkp", high, c_rows, preferred_element_type=jnp.float32
-    ) + jnp.einsum("rgkpn,jugn->rjugkp", low, c_rows, preferred_element_type=jnp.float32)
+        "rgkpn,jugn->rjugkp",
+        jnp.concatenate([high, low], axis=-1),
+        jnp.concatenate([c_rows, c_rows], axis=-1),
+        preferred_element_type=jnp.float32,
+    )
     contribution = projected[0]
     for request in range(1, request_count):
         pick = (all_request == request)[:, None, None, None, None]

time: 182 us -> 180 us (0.989)
  matrix products: 31.2 us -> 29.3 us
    dot_general x2 -> x1, matrix products: 4.06 us -> 2.14 us  [shards(): jnp.einsum('rgkpn,jugn->rjugkp', jnp.concatenate([high, low], axis=-1), j...]
where the time goes in v17:
time: 180 us; the launch traced here: 178 us
  local copies, waits for them, and re-layouts  51.4 us (29%)
  other arithmetic  46.9 us (26%)
  matrix products  29.3 us (16%)
  starting transfers between devices  28.8 us (16%)
  waiting for transfers between devices  19.8 us (11%)
  between operations  1.99 us (1%)
    unnamed x107, local copies, waits for them, and re-layouts  16.2 us
    all_to_all x2, starting transfers between devices, exchange_ctx(): got = lax.all_to_all(value, 'ctx', 0, 0, tiled=True)  15.7 us
    dot_general x2, matrix products, block_terms(): jnp.einsum('gkts,sgkp->gktp', mixing, inputs_head, preferred_element_type...  14.5 us
    slice x3, local copies, waits for them, and re-layouts, shards(): ssm_input[request]  10.5 us
    ppermute x4, waiting for transfers between devices, chain_columns(): lax.ppermute(outgoing.astype(jnp.bfloat16), 'ctx', pairs)  8.72 us
    convert_element_type x1, local copies, waits for them, and re-layouts, finish(): inputs_head = ssm_input.reshape(request_count, block_size, group_count, p...  7.16 us
    ppermute x3, waiting for transfers between devices, send(): lax.ppermute((value.astype(jnp.bfloat16), total), 'ctx', pairs)  6.55 us
    ppermute x4, starting transfers between devices, chain_columns(): lax.ppermute(outgoing.astype(jnp.bfloat16), 'ctx', pairs)  6.14 us
  transfers between devices with their start and end apart: 13, of which 6 were waited for; matrix products, arithmetic and copies ran while one was open for 57% of the time, Pallas kernels for 0%

profile of v17, /device:TPU:18, one launch (start us, length us, event | category | flops | bytes accessed | tf_op | source)
XLA Modules:
  0.0 178.2 jit_solution(8387796979867462345)
XLA Ops:
  5.1 1.5 collective-permute-start
  11.2 4.0 %fusion.69 = (bf16[1,256,4096]{2,1,0:T(8,128)(2,1)}, bf16[1,256,4096]{2,1,0:T(8,128)(2,1)S(1)}) fusion(bf16[2,256,4096]{2,1,0:T(8,128)(2,1)} %param.13), kind=kLoop, calls=%fused_computation.143 | loop fusion | bytes 8388608 | tf_op jit(solution)/shard_map/slice | solution.py:213
  15.2 4.1 %copy.214 = bf16[1,256,4096]{1,2,0:T(8,128)(2,1)} copy(bf16[1,256,4096]{2,1,0:T(8,128)(2,1)} %get-tuple-element.24) | data formatting | bytes 4194304 | tf_op jit(solution)/shard_map/slice | solution.py:213
  19.3 2.4 %copy.217 = bf16[1,256,4096]{1,2,0:T(8,128)(2,1)} copy(bf16[1,256,4096]{2,1,0:T(8,128)(2,1)S(1)} %get-tuple-element.25) | data formatting | bytes 4194304 | tf_op jit(solution)/shard_map/slice | solution.py:213
  21.7 2.5 %fusion.42 = f32[1,2,32,64,128]{4,3,2,1,0:T(8,128)S(1)} fusion(bf16[256,2,128,1]{0,2,3,1:T(8,128)(2,1)S(1)} %bitcast.173, bf16[256,2,32,64]{0,3,2,1:T(8,128)(2,1)} %bitcast.167, f32[256,2,32]{0,2,1:T(8,128)S(1)} %bitcast.178), kind=kOutput, calls=%fused_computation.63 | convolution fusion | flops 271581184 | bytes 4390912 | tf_op jit(solution)/shard_map/sgkp,sgn->gkpn/dot_general | solution.py:42
  26.6 1.5 collective-permute-start.1
  33.8 7.9 %fusion.29 = f32[1,2,32,256,64]{3,4,2,1,0:T(8,128)} fusion(bf16[256,2,32,64]{0,3,2,1:T(8,128)(2,1)} %bitcast.168, f32[2,32,256]{2,1,0:T(8,128)} %bitcast.180, f32[2,32,256]{2,1,0:T(8,128)} %reduce_window_sum.88, f32[2,256,256]{2,1,0:T(8,128)S(1)} %fusion.74, pred[256,256]{1,0:T(8,128)(4,1)} %iota_compare_fusion), kind=kOutput, calls=%fused_computation.48 | convolution fusion | flops 562036736 | bytes 7012352 | tf_op jit(solution)/shard_map/gkts,sgkp->gktp/dot_general | solution.py:35
  44.6 1.6 collective-permute-start.8
  49.4 3.8 %collective-permute-done.9 = f32[4,1153]{1,0:T(4,128)S(1)} collective-permute-done((f32[4,1153]{1,0:T(4,128)S(1)}, f32[4,1153]{1,0:T(4,128)S(1)}, u32[]{:S(2)}, u32[]{:S(2)}) %collective-permute-start.9) | collective-permute-done | bytes 18480 | tf_op jit(solution)/shard_map/ppermute | solution.py:94
  57.3 2.3 %fusion.27 = (bf16[2,2,32,64,128]{4,3,2,1,0:T(8,128)(2,1)S(1)}, bf16[2,2,32,64,128]{4,3,2,1,0:T(8,128)(2,1)S(1)}) fusion(f32[1,2,32,64,128]{4,3,2,1,0:T(8,128)} %copy-done.3, f32[1,2,32,64,128]{4,3,2,1,0:T(8,128)S(1)} %fusion.42, f32[2,2,32]{2,1,0:T(2,128)} %exp.65), kind=kLoop, calls=%fused_computation.42 | loop fusion | flops 6291456 | bytes 8389120 | tf_op jit(solution)/shard_map/convert_element_type | solution.py:243
  59.6 2.1 %fusion.38 = f32[2,8,4,2,32,64]{5,1,4,0,2,3:T(8,128)S(1)} fusion(bf16[2,2,32,64,128]{4,3,2,1,0:T(8,128)(2,1)S(1)} %get-tuple-element.23, bf16[2,2,32,64,128]{4,3,2,1,0:T(8,128)(2,1)S(1)} %get-tuple-element.22, bf16[8,4,2,128]{3,0,2,1:T(8,128)(2,1)S(1)} %bitcast.181), kind=kOutput, calls=%fused_computation.61 | convolution fusion | flops 142671872 | bytes 5259264 | tf_op jit(solution)/shard_map/rgkpn,jugn->rjugkp/dot_general | solution.py:246
  63.7 5.3 %all-to-all-start = ((f32[8,1,16384]{2,1,0:T(1,128)}), f32[8,1,16384]{2,1,0:T(1,128)}, u32[]{:S(2)}, u32[]{:S(2)}) async-start(f32[8,1,16384]{2,1,0:T(1,128)} %reshape.357), calls=%async_computation | async-start | bytes 1048576 | tf_op jit(solution)/shard_map/all_to_all | solution.py:121
  69.0 4.4 %fusion.30 = (f32[2,2,32,32,128]{4,3,2,1,0:T(8,128)S(1)}, f32[2,2,32,32,128]{4,3,2,1,0:T(8,128)}) fusion(bf16[2,2,32,32,128]{4,3,2,1,0:T(8,128)(2,1)S(1)} %collective-permute-done.1, f32[2,2,32]{2,1,0:T(2,128)} %get-tuple-element.39, pred[]{:T(512)S(6)} %eq.51, f32[1,2,32,64,128]{4,3,2,1,0:T(8,128)} %copy-done.3, f32[1,2,32,64,128]{4,3,2,1,0:T(8,128)} %copy-done.2), kind=kLoop, calls=%fused_computation.49 | loop fusion | flops 4194304 | bytes 9437697 | tf_op jit(solution)/shard_map/add | solution.py:162
  81.4 1.6 multiply_reduce_fusion
  83.5 3.8 %reduce.16 = f32[8,16384]{1,0:T(8,128)} reduce(f32[8,1,16384]{2,1,0:T(1,128)} %all-to-all-done, f32[]{:T(128)} %broadcast.183), dimensions={1}, to_apply=%all_to_all.6.reduce_sub_computation | reduce | bytes 1048580 | tf_op jit(solution)/shard_map/all_to_all | solution.py:121
  87.3 2.4 %reshape.358 = f32[8,2,4,32,64]{4,3,2,1,0:T(8,128)} reshape(f32[8,16384]{1,0:T(8,128)} %reduce.16) | data formatting | bytes 1048576
  92.7 1.6 add.104
  94.4 4.0 %collective-permute-done.3 = bf16[2,32,32,128]{3,2,1,0:T(8,128)(2,1)S(1)} collective-permute-done((bf16[2,32,32,128]{3,2,1,0:T(8,128)(2,1)}, bf16[2,32,32,128]{3,2,1,0:T(8,128)(2,1)S(1)}, u32[]{:S(2)}, u32[]{:S(2)}) %collective-permute-start.3) | collective-permute-done | bytes 524320 | tf_op jit(solution)/shard_map/ppermute | solution.py:137
  99.7 1.9 %collective-permute-start.4 = (bf16[2,32,32,128]{3,2,1,0:T(8,128)(2,1)}, bf16[2,32,32,128]{3,2,1,0:T(8,128)(2,1)}, u32[]{:S(2)}, u32[]{:S(2)}) collective-permute-start(bf16[2,32,32,128]{3,2,1,0:T(8,128)(2,1)} %select_convert_fusion.3), channel_id=1, source_target_pairs={{4,8},{8,12},{6,10},{10,14},{5,9},{9,13},{7,11},{11,15},{20,24},{2... | collective-permute-start | bytes 1572872 | tf_op jit(solution)/shard_map/ppermute | solution.py:137
  103.2 10.3 %all-to-all-start.1 = ((bf16[8,4,4096]{2,1,0:T(4,128)(2,1)}), bf16[8,4,4096]{2,1,0:T(4,128)(2,1)}, u32[]{:S(2)}, u32[]{:S(2)}) async-start(bf16[8,4,4096]{2,1,0:T(4,128)(2,1)} %concatenate.52), calls=%async_computation.1 | async-start | bytes 524288 | tf_op jit(solution)/shard_map/all_to_all | solution.py:121
  114.3 4.2 %collective-permute-done.4 = bf16[2,32,32,128]{3,2,1,0:T(8,128)(2,1)} collective-permute-done((bf16[2,32,32,128]{3,2,1,0:T(8,128)(2,1)}, bf16[2,32,32,128]{3,2,1,0:T(8,128)(2,1)}, u32[]{:S(2)}, u32[]{:S(2)}) %collective-permute-start.4) | collective-permute-done | bytes 524320 | tf_op jit(solution)/shard_map/ppermute | solution.py:137
  118.5 2.5 %select_convert_fusion.2 = bf16[2,32,32,128]{3,2,1,0:T(8,128)(2,1)} fusion(f32[2,2,32,32,128]{4,3,2,1,0:T(8,128)S(1)} %get-tuple-element.18, bf16[2,32,32,128]{3,2,1,0:T(8,128)(2,1)S(1)} %collective-permute-done.2, bf16[2,32,32,128]{3,2,1,0:T(8,128)(2,1)S(1)} %collective-permute-done.3, bf16[2,32,32,128]{3,2,1,0:T(8,128)(2,1)} %collective-permute-done.4, ...), kind=kLoop, calls=%fused_computation.87 | loop fusion | flops 4194304 | bytes 4194822 | tf_op jit(solution)/shard_map/convert_element_type | solution.py:137
  121.0 2.1 %collective-permute-start.5 = (bf16[2,32,32,128]{3,2,1,0:T(8,128)(2,1)}, bf16[2,32,32,128]{3,2,1,0:T(8,128)(2,1)}, u32[]{:S(2)}, u32[]{:S(2)}) collective-permute-start(bf16[2,32,32,128]{3,2,1,0:T(8,128)(2,1)} %select_convert_fusion.2), channel_id=1, source_target_pairs={{8,12},{10,14},{9,13},{11,15},{24,28},{26,30},{25,29},{27,31}} | collective-permute-start | bytes 1572872 | tf_op jit(solution)/shard_map/ppermute | solution.py:137
  123.1 5.7 %fusion.5 = f32[8,4,1024]{2,0,1:T(8,128)} fusion(bf16[4096,1024]{1,0:T(8,128)(2,1)} %param.25, bf16[8,4,4096]{2,1,0:T(4,128)(2,1)} %all-to-all-done.1), kind=kOutput, calls=%fused_computation.8 | convolution fusion | flops 268435456 | bytes 8781824 | tf_op jit(solution)/shard_map/jup,pd->jud/dot_general | solution.py:281
  129.3 2.0 %fusion.50 = (f32[1,2,32,32,128]{4,3,2,1,0:T(8,128)S(1)}, f32[1,2,32,32,128]{4,3,2,1,0:T(8,128)S(1)}) fusion(bf16[2,32,32,128]{3,2,1,0:T(8,128)(2,1)} %collective-permute-done.5, bf16[2,32,32,128]{3,2,1,0:T(8,128)(2,1)S(1)} %copy-done.11, bf16[2,32,32,128]{3,2,1,0:T(8,128)(2,1)S(1)} %copy-done.13, bf16[2,32,32,128]{3,2,1,0:T(8,128)(2,1)} %collective-permute-done.4, ...), kind=kLoop, calls=%fused_computation.80 | loop fusion | flops 3145728 | bytes 4194312 | tf_op jit(solution)/shard_map/stack | solution.py:140
  131.4 1.5 select_convert_fusion
  134.4 6.6 %fusion.28 = f32[1,2,32,256,64]{3,4,2,1,0:T(8,128)} fusion(bf16[256,2,32,64]{0,3,2,1:T(8,128)(2,1)S(1)} %bitcast.166, f32[2,32,256]{2,1,0:T(8,128)S(1)} %bitcast.179, f32[2,32,256]{2,1,0:T(8,128)S(1)} %copy-done.30, f32[2,256,256]{2,1,0:T(8,128)S(1)} %copy-done.20, pred[256,256]{1,0:T(8,128)(4,1)S(1)} %copy-done.29), kind=kOutput, calls=%fused_computation.47 | convolution fusion | flops 562036736 | bytes 7012352 | tf_op jit(solution)/shard_map/gkts,sgkp->gktp/dot_general | solution.py:35
  141.7 7.2 %copy.231 = f32[2,256,4096]{1,2,0:T(8,128)} copy(bf16[2,256,4096]{2,1,0:T(8,128)(2,1)} %param.13) | data formatting | bytes 12582912 | tf_op jit(solution)/shard_map/convert_element_type | solution.py:66
  151.4 6.5 %collective-permute-done.6 = bf16[2,2,32,32,128]{4,3,2,1,0:T(8,128)(2,1)} collective-permute-done((bf16[2,2,32,32,128]{4,3,2,1,0:T(8,128)(2,1)}, bf16[2,2,32,32,128]{4,3,2,1,0:T(8,128)(2,1)}, u32[]{:S(2)}, u32[]{:S(2)}) %collective-permute-start.6) | collective-permute-done | bytes 1048608 | tf_op jit(solution)/shard_map/ppermute | solution.py:83
  158.0 2.5 %convert_select_fusion.1 = (f32[2,2,32,32,128]{4,3,2,1,0:T(8,128)S(1)}, f32[2,2,32,32,128]{4,3,2,1,0:T(8,128)S(1)}) fusion(bf16[2,2,32,32,128]{4,3,2,1,0:T(8,128)(2,1)} %collective-permute-done.6, pred[]{:T(512)S(6)} %eq.51, f32[2,2,32,32,128]{4,3,2,1,0:T(8,128)S(1)} %copy-done.4, bf16[2,2,32,32,128]{4,3,2,1,0:T(8,128)(2,1)} %copy-done.6, ...), kind=kLoop, calls=%fused_computation.44 | loop fusion | flops 4718592 | bytes 10486273 | tf_op jit(solution)/shard_map/jit(_where)/select_n | solution.py:186
  165.9 6.0 %fusion.4 = bf16[2,256,2,32,64]{1,4,3,2,0:T(8,128)(2,1)} fusion(f32[1,2,32,256,64]{3,4,2,1,0:T(8,128)} %fusion.28, f32[1,2,32,256,64]{3,4,2,1,0:T(8,128)S(1)} %copy-done.14, f32[2,256,2,32,64]{1,4,3,2,0:T(8,128)S(1)} %bitcast.162, f32[2,2,256,32,64]{2,4,3,1,0:T(8,128)S(1)} %bitcast.163, f32[2,32]{1,0:T(2,128)S(1)} %copy-done.41, f32[2,2,256,32]{2,3,1,0:T(8,128)S(1)} %fusion.57), kind=kLoop, calls=%fused_computation.7 | loop fusion | flops 12582912 | bytes 29491456 | tf_op jit(solution)/shard_map/convert_element_type | solution.py:69
  171.9 6.3 %copy.248 = bf16[2,256,4096]{2,1,0:T(8,128)(2,1)} copy(bf16[2,256,4096]{1,2,0:T(8,128)(2,1)} %bitcast.164) | data formatting | bytes 8388608
  (204 shorter events, 54.0 us)
Async XLA Ops:
  0.6 29.3 %copy-start = (bf16[1,4,256]{2,1,0:T(4,128)(2,1)S(1)}, bf16[1,4,256]{2,1,0:T(4,128)(2,1)}, u32[]{:S(2)}) copy-start(bf16[1,4,256]{2,1,0:T(4,128)(2,1)} %param.21) | copy-start | bytes 6148
  0.6 10.3 %copy-start.24 = (bf16[2,256,256]{2,1,0:T(8,128)(2,1)S(1)}, bf16[2,256,256]{2,1,0:T(8,128)(2,1)}, u32[]{:S(2)}) copy-start(bf16[2,256,256]{2,1,0:T(8,128)(2,1)} %param.14) | copy-start | bytes 786436
  3.4 11.7 %copy-start.35 = (f32[64,2]{0,1:T(2,128)}, f32[64,2]{0,1:T(2,128)S(1)}, u32[]{:S(2)}) copy-start(f32[64,2]{0,1:T(2,128)S(1)} %slice.100) | copy-start | bytes 1540
  5.1 41.2 %collective-permute-start = (f32[2,2,32]{2,1,0:T(2,128)}, f32[2,2,32]{2,1,0:T(2,128)}, u32[]{:S(2)}, u32[]{:S(2)}) collective-permute-start(f32[2,2,32]{2,1,0:T(2,128)} %constant_dynamic-update-slice_fusion), channel_id=1, source_target_pairs={{0,2},{4,6},{8,10},{12,14},{2,0},{6,4},{10,8},{14,12},{1,3},{5,7},... | collective-permute-start | bytes 1544 | tf_op jit(solution)/shard_map/ppermute | solution.py:83
  9.4 34.4 %collective-permute-start.7 = (f32[1,1153]{1,0:T(1,128)}, f32[1,1153]{1,0:T(1,128)}, u32[]{:S(2)}, u32[]{:S(2)}) collective-permute-start(f32[1,1153]{1,0:T(1,128)} %broadcast_in_dim.73), channel_id=1, source_target_pairs={{0,2},{2,0},{4,6},{6,4},{8,10},{10,8},{12,14},{14,12},{1,3},{3,1},... | collective-permute-start | bytes 13844 | tf_op jit(solution)/shard_map/ppermute | solution.py:94
  11.1 10.6 %copy-start.17 = (bf16[1,256,256]{1,2,0:T(8,128)(2,1)}, bf16[1,256,256]{1,2,0:T(8,128)(2,1)S(1)}, u32[]{:S(2)}) copy-start(bf16[1,256,256]{1,2,0:T(8,128)(2,1)S(1)} %copy.271) | copy-start | bytes 393220
  11.2 13.0 %copy-start.15 = (bf16[1,256,256]{1,2,0:T(8,128)(2,1)}, bf16[1,256,256]{1,2,0:T(8,128)(2,1)S(1)}, u32[]{:S(2)}) copy-start(bf16[1,256,256]{1,2,0:T(8,128)(2,1)S(1)} %copy.272) | copy-start | bytes 393220
  24.2 33.1 %copy-start.2 = (f32[1,2,32,64,128]{4,3,2,1,0:T(8,128)}, f32[1,2,32,64,128]{4,3,2,1,0:T(8,128)S(1)}, u32[]{:S(2)}) copy-start(f32[1,2,32,64,128]{4,3,2,1,0:T(8,128)S(1)} %fusion.42) | copy-start | bytes 6291460
  24.9 5.0 %copy-start.39 = (bf16[1,4,256]{2,1,0:T(4,128)(2,1)S(1)}, bf16[1,4,256]{2,1,0:T(4,128)(2,1)}, u32[]{:S(2)}) copy-start(bf16[1,4,256]{2,1,0:T(4,128)(2,1)} %param.22) | copy-start | bytes 6148
  26.6 42.4 %collective-permute-start.1 = (bf16[2,2,32,32,128]{4,3,2,1,0:T(8,128)(2,1)}, bf16[2,2,32,32,128]{4,3,2,1,0:T(8,128)(2,1)S(1)}, u32[]{:S(2)}, u32[]{:S(2)}) collective-permute-start(bf16[2,2,32,32,128]{4,3,2,1,0:T(8,128)(2,1)} %select_convert_fusion.1), channel_id=1, source_target_pairs={{0,2},{4,6},{8,10},{12,14},{2,0},{6,4},{10,8},{14,12},{1,3},{5,7},... | collective-permute-start | bytes 3145736 | tf_op jit(solution)/shard_map/ppermute | solution.py:83
  33.8 8.6 %copy-start.44 = (f32[1,4,64]{2,1,0:T(4,128)S(1)}, f32[1,4,64]{2,1,0:T(4,128)}, u32[]{:S(2)}) copy-start(f32[1,4,64]{2,1,0:T(4,128)} %param.23) | copy-start | bytes 3076
  44.6 3.7 %collective-permute-start.8 = (f32[2,1153]{1,0:T(2,128)S(1)}, f32[2,1153]{1,0:T(2,128)S(1)}, u32[]{:S(2)}, u32[]{:S(2)}) collective-permute-start(f32[2,1153]{1,0:T(2,128)S(1)} %maximum_select_fusion.2), channel_id=1, source_target_pairs={{0,4},{2,6},{4,0},{6,2},{8,12},{10,14},{12,8},{14,10},{1,5},{3,7},... | collective-permute-start | bytes 27680 | tf_op jit(solution)/shard_map/ppermute | solution.py:94
  48.4 4.8 %collective-permute-start.9 = (f32[4,1153]{1,0:T(4,128)S(1)}, f32[4,1153]{1,0:T(4,128)S(1)}, u32[]{:S(2)}, u32[]{:S(2)}) collective-permute-start(f32[4,1153]{1,0:T(4,128)S(1)} %maximum_select_fusion.1), channel_id=1, source_target_pairs={{0,8},{2,10},{4,12},{6,14},{8,0},{10,2},{12,4},{14,6},{1,9},{3,11}... | collective-permute-start | bytes 55352 | tf_op jit(solution)/shard_map/ppermute | solution.py:94
  63.7 19.3 %all-to-all-start = ((f32[8,1,16384]{2,1,0:T(1,128)}), f32[8,1,16384]{2,1,0:T(1,128)}, u32[]{:S(2)}, u32[]{:S(2)}) async-start(f32[8,1,16384]{2,1,0:T(1,128)} %reshape.357), calls=%async_computation | async-start | bytes 1048576 | tf_op jit(solution)/shard_map/all_to_all | solution.py:121
  69.0 4.5 %copy-start.42 = (f32[2,32]{1,0:T(2,128)S(1)}, f32[2,32]{1,0:T(2,128)}, u32[]{:S(2)}) copy-start(f32[2,32]{1,0:T(2,128)} %get-tuple-element.43) | copy-start | bytes 772
  73.5 5.2 %copy-start.34 = (f32[2,2,32]{2,1,0:T(2,128)S(1)}, f32[2,2,32]{2,1,0:T(2,128)}, u32[]{:S(2)}) copy-start(f32[2,2,32]{2,1,0:T(2,128)} %copy-done.33) | copy-start | bytes 1540
  74.6 4.1 %collective-permute-start.2 = (bf16[2,32,32,128]{3,2,1,0:T(8,128)(2,1)}, bf16[2,32,32,128]{3,2,1,0:T(8,128)(2,1)S(1)}, u32[]{:S(2)}, u32[]{:S(2)}) collective-permute-start(bf16[2,32,32,128]{3,2,1,0:T(8,128)(2,1)} %select_convert_fusion.4), channel_id=1, source_target_pairs={{0,4},{2,6},{1,5},{3,7},{16,20},{18,22},{17,21},{19,23}} | collective-permute-start | bytes 1572872 | tf_op jit(solution)/shard_map/ppermute | solution.py:137
  78.7 39.8 %copy-start.10 = (bf16[2,32,32,128]{3,2,1,0:T(8,128)(2,1)}, bf16[2,32,32,128]{3,2,1,0:T(8,128)(2,1)S(1)}, u32[]{:S(2)}) copy-start(bf16[2,32,32,128]{3,2,1,0:T(8,128)(2,1)S(1)} %collective-permute-done.2) | copy-start | bytes 1572868
  79.9 18.5 %collective-permute-start.3 = (bf16[2,32,32,128]{3,2,1,0:T(8,128)(2,1)}, bf16[2,32,32,128]{3,2,1,0:T(8,128)(2,1)S(1)}, u32[]{:S(2)}, u32[]{:S(2)}) collective-permute-start(bf16[2,32,32,128]{3,2,1,0:T(8,128)(2,1)} %fusion.48), channel_id=1, source_target_pairs={{0,4},{4,8},{2,6},{6,10},{1,5},{5,9},{3,7},{7,11},{16,20},{20,24},... | collective-permute-start | bytes 1572872 | tf_op jit(solution)/shard_map/ppermute | solution.py:137
  94.4 7.3 %copy-start.23 = (f32[1,4,4096]{2,1,0:T(4,128)S(1)}, f32[1,4,4096]{2,1,0:T(4,128)}, u32[]{:S(2)}) copy-start(f32[1,4,4096]{2,1,0:T(4,128)} %add.104) | copy-start | bytes 196612
  94.4 7.3 %copy-start.27 = (bf16[1,4,4096]{2,1,0:T(4,128)(2,1)S(1)}, bf16[1,4,4096]{2,1,0:T(4,128)(2,1)}, u32[]{:S(2)}) copy-start(bf16[1,4,4096]{2,1,0:T(4,128)(2,1)} %param.20) | copy-start | bytes 98308
  94.4 19.1 %copy-start.36 = (f32[64,2]{0,1:T(2,128)S(1)}, f32[64,2]{0,1:T(2,128)}, u32[]{:S(2)}) copy-start(f32[64,2]{0,1:T(2,128)} %copy-done.35) | copy-start | bytes 1540
  98.4 20.1 %copy-start.12 = (bf16[2,32,32,128]{3,2,1,0:T(8,128)(2,1)}, bf16[2,32,32,128]{3,2,1,0:T(8,128)(2,1)S(1)}, u32[]{:S(2)}) copy-start(bf16[2,32,32,128]{3,2,1,0:T(8,128)(2,1)S(1)} %collective-permute-done.3) | copy-start | bytes 1572868
  99.7 18.8 %collective-permute-start.4 = (bf16[2,32,32,128]{3,2,1,0:T(8,128)(2,1)}, bf16[2,32,32,128]{3,2,1,0:T(8,128)(2,1)}, u32[]{:S(2)}, u32[]{:S(2)}) collective-permute-start(bf16[2,32,32,128]{3,2,1,0:T(8,128)(2,1)} %select_convert_fusion.3), channel_id=1, source_target_pairs={{4,8},{8,12},{6,10},{10,14},{5,9},{9,13},{7,11},{11,15},{20,24},{2... | collective-permute-start | bytes 1572872 | tf_op jit(solution)/shard_map/ppermute | solution.py:137
  103.2 19.9 %all-to-all-start.1 = ((bf16[8,4,4096]{2,1,0:T(4,128)(2,1)}), bf16[8,4,4096]{2,1,0:T(4,128)(2,1)}, u32[]{:S(2)}, u32[]{:S(2)}) async-start(bf16[8,4,4096]{2,1,0:T(4,128)(2,1)} %concatenate.52), calls=%async_computation.1 | async-start | bytes 524288 | tf_op jit(solution)/shard_map/all_to_all | solution.py:121
  121.0 8.3 %collective-permute-start.5 = (bf16[2,32,32,128]{3,2,1,0:T(8,128)(2,1)}, bf16[2,32,32,128]{3,2,1,0:T(8,128)(2,1)}, u32[]{:S(2)}, u32[]{:S(2)}) collective-permute-start(bf16[2,32,32,128]{3,2,1,0:T(8,128)(2,1)} %select_convert_fusion.2), channel_id=1, source_target_pairs={{8,12},{10,14},{9,13},{11,15},{24,28},{26,30},{25,29},{27,31}} | collective-permute-start | bytes 1572872 | tf_op jit(solution)/shard_map/ppermute | solution.py:137
  123.1 6.2 %copy-start.11 = (bf16[2,32,32,128]{3,2,1,0:T(8,128)(2,1)S(1)}, bf16[2,32,32,128]{3,2,1,0:T(8,128)(2,1)}, u32[]{:S(2)}) copy-start(bf16[2,32,32,128]{3,2,1,0:T(8,128)(2,1)} %copy-done.10) | copy-start | bytes 1572868
  123.1 6.2 %copy-start.13 = (bf16[2,32,32,128]{3,2,1,0:T(8,128)(2,1)S(1)}, bf16[2,32,32,128]{3,2,1,0:T(8,128)(2,1)}, u32[]{:S(2)}) copy-start(bf16[2,32,32,128]{3,2,1,0:T(8,128)(2,1)} %copy-done.12) | copy-start | bytes 1572868
  128.8 21.0 %collective-permute-start.10 = (f32[8,4,1024]{2,0,1:T(8,128)}, f32[8,4,1024]{2,0,1:T(8,128)}, u32[]{:S(2)}, u32[]{:S(2)}) collective-permute-start(f32[8,4,1024]{2,0,1:T(8,128)} %fusion.5), channel_id=1, source_target_pairs={{0,1},{1,0},{2,3},{3,2},{4,5},{5,4},{6,7},{7,6},{8,9},{9,8},{10,11... | collective-permute-start | bytes 393224 | tf_op jit(solution)/shard_map/ppermute | solution.py:288
  132.9 25.1 %collective-permute-start.6 = (bf16[2,2,32,32,128]{4,3,2,1,0:T(8,128)(2,1)}, bf16[2,2,32,32,128]{4,3,2,1,0:T(8,128)(2,1)}, u32[]{:S(2)}, u32[]{:S(2)}) collective-permute-start(bf16[2,2,32,32,128]{4,3,2,1,0:T(8,128)(2,1)} %select_convert_fusion), channel_id=1, source_target_pairs={{0,2},{4,6},{8,10},{12,14},{2,0},{6,4},{10,8},{14,12},{1,3},{5,7},... | collective-permute-start | bytes 3145736 | tf_op jit(solution)/shard_map/ppermute | solution.py:83
  141.7 8.0 %copy-start.25 = (f32[1,2,32,256]{3,2,1,0:T(8,128)S(1)}, f32[1,2,32,256]{3,2,1,0:T(8,128)}, u32[]{:S(2)}) copy-start(f32[1,2,32,256]{3,2,1,0:T(8,128)} %reduce_window_sum.86) | copy-start | bytes 196612
  171.9 6.3 %copy-start.1 = (bf16[1,4,256]{2,1,0:T(4,128)(2,1)S(1)}, bf16[1,4,256]{2,1,0:T(4,128)(2,1)}, u32[]{:S(2)}) copy-start(bf16[1,4,256]{2,1,0:T(4,128)(2,1)} %param.21) | copy-start | bytes 6148
  (30 other events, 86.4 us)
